TPU v7x, 32 devices: a whole 2x2x4 slice. The times are simulated.
32 devices in a mesh: tx: 4 (over y, x), ty: 8 (over z, core).
Axes of the slice: x: 2, y: 2, z: 4, core: 2. Of those that a mesh axis runs over, the one named last changes fastest.
Arguments:
- stack: bfloat16 [32, 2, 128, 4096], P('tx', None, None, 'ty'), may hold values from -6 to 6
- filt_re: bfloat16 [32, 32], replicated, may hold values from -0.75 to 0.75
- filt_im: bfloat16 [32, 32], replicated, may hold values from -0.75 to 0.75
- pre_ids: int32 [32], replicated, may hold values from 0 to 15
- post_ids: int32 [32], replicated, may hold values from 16 to 31
Outputs:
- coherence: float32 [32, 128, 4096], P(None, 'ty', 'tx')
- change: float32 [32, 128, 4096], P(None, 'ty', 'tx')
All inputs are finite; a program needn't handle non-finite values.
Results may differ from a plain program's by a relative error of at most 0.0065.
Values may be sent and summed in bfloat16 or wider, within the bound.
No kernel may reach another device: no remote copies, remote signals or barrier semaphores. Data moves between devices by JAX's collectives and lax.ppermute only.
A program may use at most 128 MiB of HBM per device.

v0:
```python
import jax
import jax.numpy as jnp
from jax import lax
from jax.sharding import PartitionSpec as P

RADIUS = 4


def with_halo(block, sides, width):
    for axis, dim in sides:
        count = lax.axis_size(axis)
        forward = [(i, i + 1) for i in range(count - 1)]
        backward = [(target, source) for source, target in forward]
        low = lax.ppermute(
            lax.slice_in_dim(block, block.shape[dim] - width, None, axis=dim), axis, forward
        )
        high = lax.ppermute(lax.slice_in_dim(block, 0, width, axis=dim), axis, backward)
        block = jnp.concatenate([low, block, high], axis=dim)
    return block


def box_mean(fields, tile_rows, tile_cols, radius):
    window = 2 * radius + 1
    out_rows = jnp.arange(tile_rows)[:, None]
    in_rows = jnp.arange(tile_rows + 2 * radius)[None, :]
    row_gap = in_rows - out_rows
    row_band = jnp.where((row_gap >= 0) & (row_gap <= 2 * radius), 1.0, 0.0).astype(jnp.float32)
    in_cols = jnp.arange(tile_cols + 2 * radius)[:, None]
    out_cols = jnp.arange(tile_cols)[None, :]
    col_gap = in_cols - out_cols
    col_band = jnp.where((col_gap >= 0) & (col_gap <= 2 * radius), 1.0, 0.0).astype(jnp.float32)
    rowsum = jnp.einsum("ij,fjw->fiw", row_band, fields, precision=lax.Precision.HIGHEST)
    colsum = jnp.einsum("fiw,wk->fik", rowsum, col_band, precision=lax.Precision.HIGHEST)
    return colsum / float(window * window)


def pair_maps(padded, pre_ids, post_ids, tile_rows, tile_cols, radius):
    widened = padded.astype(jnp.float32)
    power = widened[:, 0] * widened[:, 0] + widened[:, 1] * widened[:, 1]
    pre_side = jnp.take(widened, pre_ids, axis=0)
    post_side = jnp.take(widened, post_ids, axis=0)
    cross_re = pre_side[:, 0] * post_side[:, 0] + pre_side[:, 1] * post_side[:, 1]
    cross_im = pre_side[:, 1] * post_side[:, 0] - pre_side[:, 0] * post_side[:, 1]
    fields = jnp.concatenate([power, cross_re, cross_im], axis=0)
    means = box_mean(fields, tile_rows, tile_cols, radius)
    count_acq = power.shape[0]
    count_pairs = pre_ids.shape[0]
    power_mean = means[:count_acq] + 1e-06
    pre_power = jnp.take(power_mean, pre_ids, axis=0)
    post_power = jnp.take(power_mean, post_ids, axis=0)
    real_mean = means[count_acq : count_acq + count_pairs]
    imag_mean = means[count_acq + count_pairs :]
    coherence = jnp.sqrt(real_mean * real_mean + imag_mean * imag_mean) / jnp.sqrt(
        pre_power * post_power
    )
    change = jnp.log(post_power / pre_power)
    return (coherence, change)


def shards(stack, filt_re, filt_im, pre_ids, post_ids):
    count_acq = filt_re.shape[0]
    mixing = jnp.stack([jnp.stack([filt_re, -filt_im], -1), jnp.stack([filt_im, filt_re], -1)], 1)
    mixing = mixing.reshape(2 * count_acq, 2 * count_acq)
    n_rows = lax.axis_size("ty")
    n_cols = lax.axis_size("tx")
    tile_rows = stack.shape[2] // n_rows
    tile_cols = stack.shape[3] * n_rows // n_cols
    by_rows = lax.all_to_all(stack, "ty", split_axis=2, concat_axis=3, tiled=True)
    piece = lax.all_to_all(by_rows, "tx", split_axis=3, concat_axis=0, tiled=True)
    height = piece.shape[2]
    breadth = piece.shape[3]
    flat = piece.reshape(2 * count_acq, height * breadth)
    result = jnp.dot(mixing, flat, preferred_element_type=jnp.float32)
    filtered = result.astype(jnp.bfloat16).reshape(count_acq, 2, height, breadth)
    padded = with_halo(filtered, (("tx", 3), ("ty", 2)), RADIUS)
    return pair_maps(padded, pre_ids, post_ids, tile_rows, tile_cols, RADIUS)


def solution(mesh):
    in_specs = (P("tx", None, None, "ty"), P(), P(), P(), P())
    out_specs = (P(None, "ty", "tx"), P(None, "ty", "tx"))
    return jax.shard_map(shards, mesh=mesh, in_specs=in_specs, out_specs=out_specs, check_vma=False)
```

profile of v0, /device:TPU:21, one launch (start us, length us, event | category | flops | bytes accessed | tf_op | source)
XLA Modules:
  0.0 292.3 jit_solution(7428069221730173030)
XLA Ops:
  0.6 2.8 copy.47
  3.4 50.5 %all_to_all.33 = bf16[8,2,128,512]{3,0,1,2:T(8,128)(2,1)S(1)} all-to-all(bf16[8,2,128,512]{3,0,1,2:T(8,128)(2,1)S(1)} %copy.47), channel_id=1, replica_groups=mesh['tx'=4,'ty'=8] {'ty'}, dimensions={2} | all-to-all | bytes 4194304 | tf_op jit(solution)/shard_map/all_to_all | solution.py:68
  53.9 20.2 %copy.58 = bf16[8,2,16,8,512]{2,1,0,4,3:T(2,128)(2,1)} copy(bf16[8,2,16,8,512]{4,0,1,2,3:T(8,128)(2,1)S(1)} %bitcast.50) | data formatting | bytes 4194304 | tf_op jit(solution)/shard_map/all_to_all | solution.py:68
  74.1 20.3 %reshape.82 = bf16[4,2,131072]{2,1,0:T(2,128)(2,1)} reshape(bf16[4096,8,2,16]{3,2,1,0:T(2,128)(2,1)} %bitcast.46) | data formatting | bytes 4194304
  94.4 3.9 %all-to-all-start.1 = ((bf16[4,2,131072]{2,1,0:T(2,128)(2,1)}), bf16[4,2,131072]{2,1,0:T(2,128)(2,1)S(1)}, u32[]{:S(2)}, u32[]{:S(2)}) async-start(bf16[4,2,131072]{2,1,0:T(2,128)(2,1)} %reshape.82), calls=%async_computation.1 | async-start | bytes 4194304 | tf_op jit(solution)/shard_map/all_to_all | solution.py:69
  99.8 22.2 %all-to-all-done.1 = bf16[4,2,131072]{2,1,0:T(2,128)(2,1)S(1)} async-done(((bf16[4,2,131072]{2,1,0:T(2,128)(2,1)}), bf16[4,2,131072]{2,1,0:T(2,128)(2,1)S(1)}, u32[]{:S(2)}, u32[]{:S(2)}) %all-to-all-start.1) | async-done | bytes 2097184 | tf_op jit(solution)/shard_map/all_to_all | solution.py:69
  122.0 13.4 %reshape.83 = bf16[4096,8,2,16]{3,2,1,0:T(2,128)(2,1)} reshape(bf16[4,2,131072]{2,1,0:T(2,128)(2,1)S(1)} %all-to-all-done.1) | data formatting | bytes 4194304
  135.4 35.3 %copy.50 = bf16[8,2,16,4,1024]{4,2,1,0,3:T(8,128)(2,1)S(1)} copy(bf16[8,2,16,4,1024]{2,1,0,4,3:T(2,128)(2,1)} %bitcast.47) | data formatting | bytes 4194304 | tf_op jit(solution)/shard_map/all_to_all | solution.py:69
  170.7 1.2 copy.60
  172.6 1.2 copy.61
  174.0 3.0 %collective-permute-start.1 = (bf16[32,2,16,4]{3,2,0,1:T(8,128)(2,1)S(1)}, bf16[32,2,16,4]{3,2,0,1:T(8,128)(2,1)S(1)}, u32[]{:S(2)}, u32[]{:S(2)}) collective-permute-start(bf16[32,2,16,4]{3,2,0,1:T(8,128)(2,1)S(1)} %get-tuple-element.10), channel_id=1, source_target_pairs={{8,0},{16,8},{24,16},{9,1},{17,9},{25,17},{10,2},{18,10},{26,18},{... | collective-permute-start | bytes 24584 | tf_op jit(solution)/shard_map/ppermute | solution.py:17
  177.0 2.3 collective-permute-start
  179.4 1.5 copy.51
  181.8 6.5 %collective-permute-done = bf16[32,2,16,4]{3,2,0,1:T(8,128)(2,1)S(1)} collective-permute-done((bf16[32,2,16,4]{3,2,0,1:T(8,128)(2,1)S(1)}, bf16[32,2,16,4]{3,2,0,1:T(8,128)(2,1)S(1)}, u32[]{:S(2)}, u32[]{:S(2)}) %collective-permute-start) | collective-permute-done | bytes 8224 | tf_op jit(solution)/shard_map/ppermute | solution.py:14
  188.3 4.8 %concatenate.9 = bf16[32,2,16,1032]{3,2,0,1:T(8,128)(2,1)S(1)} concatenate(bf16[32,2,16,4]{3,2,0,1:T(8,128)(2,1)S(1)} %collective-permute-done, bf16[32,2,16,1024]{3,2,0,1:T(8,128)(2,1)} %copy.51, bf16[32,2,16,4]{3,2,0,1:T(8,128)(2,1)S(1)} %collective-permute-done.1), dimensions={3} | concatenate | bytes 4227072 | tf_op jit(solution)/shard_map/concatenate | solution.py:18
  193.6 6.8 %collective-permute-start.2 = (bf16[32,2,4,1032]{3,2,0,1:T(4,128)(2,1)S(1)}, bf16[32,2,4,1032]{3,2,0,1:T(4,128)(2,1)S(1)}, u32[]{:S(2)}, u32[]{:S(2)}) collective-permute-start(bf16[32,2,4,1032]{3,2,0,1:T(4,128)(2,1)S(1)} %get-tuple-element.8), channel_id=1, source_target_pairs={{0,1},{1,2},{2,3},{3,4},{4,5},{5,6},{6,7},{8,9},{9,10},{10,11},{11... | collective-permute-start | bytes 1585160 | tf_op jit(solution)/shard_map/ppermute | solution.py:14
  200.3 2.1 collective-permute-start.3
  202.5 4.6 %collective-permute-done.2 = bf16[32,2,4,1032]{3,2,0,1:T(4,128)(2,1)S(1)} collective-permute-done((bf16[32,2,4,1032]{3,2,0,1:T(4,128)(2,1)S(1)}, bf16[32,2,4,1032]{3,2,0,1:T(4,128)(2,1)S(1)}, u32[]{:S(2)}, u32[]{:S(2)}) %collective-permute-start.2) | collective-permute-done | bytes 528416 | tf_op jit(solution)/shard_map/ppermute | solution.py:14
  207.1 4.4 %collective-permute-done.3 = bf16[32,2,4,1032]{3,2,0,1:T(4,128)(2,1)S(1)} collective-permute-done((bf16[32,2,4,1032]{3,2,0,1:T(4,128)(2,1)S(1)}, bf16[32,2,4,1032]{3,2,0,1:T(4,128)(2,1)S(1)}, u32[]{:S(2)}, u32[]{:S(2)}) %collective-permute-start.3) | collective-permute-done | bytes 528416 | tf_op jit(solution)/shard_map/ppermute | solution.py:17
  211.5 1.6 maximum_convert_fusion
  213.2 2.1 fusion.16
  215.3 3.4 %copy.54 = f32[32,2,24,1032]{3,2,1,0:T(8,128)} copy(f32[32,2,24,1032]{3,2,0,1:T(8,128)S(1)} %maximum_convert_fusion) | data formatting | bytes 12681216 | tf_op jit(solution)/shard_map/convert_element_type | solution.py:38
  218.7 7.0 %gather_fusion.1 = f32[32,2,24,1032]{3,2,1,0:T(8,128)} fusion(f32[32,2,24,1032]{3,2,1,0:T(8,128)} %copy.54, s32[1024]{0:T(1024)S(1)} %pad_clamp_fusion), kind=kCustom, calls=%fused_computation.2.clone | custom fusion | bytes 12681344 | tf_op jit(solution)/shard_map/jit(_take)/gather | solution.py:41
  225.7 6.8 %gather_fusion = f32[32,2,24,1032]{3,2,1,0:T(8,128)} fusion(f32[32,2,24,1032]{3,2,1,0:T(8,128)} %copy.54, s32[1024]{0:T(1024)S(1)} %pad_clamp_fusion.1), kind=kCustom, calls=%fused_computation.clone | custom fusion | bytes 12681344 | tf_op jit(solution)/shard_map/jit(_take)/gather | solution.py:40
  232.5 5.7 %copy_select_fusion = (f32[32,2,24,1032]{3,2,0,1:T(8,128)S(1)}, f32[32,2,24,1032]{3,2,0,1:T(8,128)S(1)}) fusion(f32[32,2,24,1032]{3,2,1,0:T(8,128)} %gather_fusion.1, pred[32]{0:T(512)(128)(4,1)S(1)} %compare_and_fusion, f32[32,2,24,1032]{3,2,1,0:T(8,128)} %gather_fusion, pred[32]{0:T(512)(128)(4,1)S(1)} %compare_and_fusion.1), kind=kLoop, calls=%fused_computation.13 | loop fusion | flops 3170304 | bytes 25362496 | tf_op jit(solution)/shard_map/jit(_take)/select_n | solution.py:41
  238.2 3.6 %add_bitcast_fusion = (f32[32,24,1032]{2,1,0:T(8,128)}, f32[32,24,1032]{2,1,0:T(8,128)}) fusion(f32[32,2,24,1032]{3,2,0,1:T(8,128)S(1)} %get-tuple-element.14, f32[32,2,24,1032]{3,2,0,1:T(8,128)S(1)} %get-tuple-element.15), kind=kLoop, calls=%fused_computation.27 | loop fusion | flops 4755456 | bytes 19021824 | tf_op jit(solution)/shard_map/add | solution.py:42
  241.8 9.5 %fusion = f32[96,1032,16]{1,2,0:T(8,128)S(1)} fusion(f32[32,24,1032]{2,1,0:T(8,128)} %get-tuple-element.5, f32[32,24,1032]{2,1,0:T(8,128)} %get-tuple-element.4, f32[32,24,1032]{2,1,0:T(8,128)} %fusion.16), kind=kOutput, calls=%fused_computation.5 | convolution fusion | flops 461281152 | bytes 15851520 | tf_op jit(solution)/shard_map/ij,fjw->fiw/dot_general | solution.py:32
  251.4 26.9 %broadcast_multiply_fusion = f32[96,16,1024]{2,1,0:T(8,128)S(1)} fusion(f32[96,1032,16]{1,2,0:T(8,128)S(1)} %fusion), kind=kOutput, calls=%fused_computation.28 | convolution fusion | flops 19485204480 | bytes 12632064 | tf_op jit(solution)/shard_map/fiw,wk->fik/dot_general | solution.py:33
  278.3 2.7 copy-done
  281.1 2.0 gather_fusion.3
  283.1 2.0 gather_fusion.2
  285.1 7.1 %divide_log_fusion = (f32[32,16,1024]{2,1,0:T(8,128)}, f32[32,16,1024]{2,1,0:T(8,128)}) fusion(f32[32,16,1024]{2,1,0:T(8,128)} %gather_fusion.3, f32[32,16,1024]{2,1,0:T(8,128)} %gather_fusion.2, pred[32]{0:T(512)(128)(4,1)S(1)} %compare_and_fusion, pred[32]{0:T(512)(128)(4,1)S(1)} %compare_and_fusion.1, f32[96,16,1024]{2,1,0:T(8,128)} %copy-done), kind=kLoop, calls=%fused_computation.39 | loop fusion | flops 4194304 | bytes 12582976 | tf_op jit(solution)/shard_map/log | solution.py:56
  (25 shorter events, 3.8 us)
Async XLA Ops:
  94.4 4.0 %copy-start.1 = (bf16[32,32]{1,0:T(8,128)(2,1)S(1)}, bf16[32,32]{1,0:T(8,128)(2,1)}, u32[]{:S(2)}) copy-start(bf16[32,32]{1,0:T(8,128)(2,1)} %param.11) | copy-start | bytes 6148
  94.4 4.0 %copy-start.2 = (bf16[32,32]{1,0:T(8,128)(2,1)S(1)}, bf16[32,32]{1,0:T(8,128)(2,1)}, u32[]{:S(2)}) copy-start(bf16[32,32]{1,0:T(8,128)(2,1)} %param.10) | copy-start | bytes 6148
  94.4 5.3 %copy-start.3 = (s32[32]{0:T(128)S(1)}, s32[32]{0:T(128)}, u32[]{:S(2)}) copy-start(s32[32]{0:T(128)} %param.12) | copy-start | bytes 388
  94.4 5.3 %copy-start.4 = (s32[32]{0:T(128)S(1)}, s32[32]{0:T(128)}, u32[]{:S(2)}) copy-start(s32[32]{0:T(128)} %param.13) | copy-start | bytes 388
  94.4 27.6 %all-to-all-start.1 = ((bf16[4,2,131072]{2,1,0:T(2,128)(2,1)}), bf16[4,2,131072]{2,1,0:T(2,128)(2,1)S(1)}, u32[]{:S(2)}, u32[]{:S(2)}) async-start(bf16[4,2,131072]{2,1,0:T(2,128)(2,1)} %reshape.82), calls=%async_computation.1 | async-start | bytes 4194304 | tf_op jit(solution)/shard_map/all_to_all | solution.py:69
  174.0 7.7 %collective-permute-start.1 = (bf16[32,2,16,4]{3,2,0,1:T(8,128)(2,1)S(1)}, bf16[32,2,16,4]{3,2,0,1:T(8,128)(2,1)S(1)}, u32[]{:S(2)}, u32[]{:S(2)}) collective-permute-start(bf16[32,2,16,4]{3,2,0,1:T(8,128)(2,1)S(1)} %get-tuple-element.10), channel_id=1, source_target_pairs={{8,0},{16,8},{24,16},{9,1},{17,9},{25,17},{10,2},{18,10},{26,18},{... | collective-permute-start | bytes 24584 | tf_op jit(solution)/shard_map/ppermute | solution.py:17
  177.0 11.2 %collective-permute-start = (bf16[32,2,16,4]{3,2,0,1:T(8,128)(2,1)S(1)}, bf16[32,2,16,4]{3,2,0,1:T(8,128)(2,1)S(1)}, u32[]{:S(2)}, u32[]{:S(2)}) collective-permute-start(bf16[32,2,16,4]{3,2,0,1:T(8,128)(2,1)S(1)} %get-tuple-element.11), channel_id=1, source_target_pairs={{0,8},{8,16},{16,24},{1,9},{9,17},{17,25},{2,10},{10,18},{18,26},{... | collective-permute-start | bytes 24584 | tf_op jit(solution)/shard_map/ppermute | solution.py:14
  193.6 13.6 %collective-permute-start.2 = (bf16[32,2,4,1032]{3,2,0,1:T(4,128)(2,1)S(1)}, bf16[32,2,4,1032]{3,2,0,1:T(4,128)(2,1)S(1)}, u32[]{:S(2)}, u32[]{:S(2)}) collective-permute-start(bf16[32,2,4,1032]{3,2,0,1:T(4,128)(2,1)S(1)} %get-tuple-element.8), channel_id=1, source_target_pairs={{0,1},{1,2},{2,3},{3,4},{4,5},{5,6},{6,7},{8,9},{9,10},{10,11},{11... | collective-permute-start | bytes 1585160 | tf_op jit(solution)/shard_map/ppermute | solution.py:14
  200.3 11.2 %collective-permute-start.3 = (bf16[32,2,4,1032]{3,2,0,1:T(4,128)(2,1)S(1)}, bf16[32,2,4,1032]{3,2,0,1:T(4,128)(2,1)S(1)}, u32[]{:S(2)}, u32[]{:S(2)}) collective-permute-start(bf16[32,2,4,1032]{3,2,0,1:T(4,128)(2,1)S(1)} %get-tuple-element.9), channel_id=1, source_target_pairs={{1,0},{2,1},{3,2},{4,3},{5,4},{6,5},{7,6},{9,8},{10,9},{11,10},{12... | collective-permute-start | bytes 1585160 | tf_op jit(solution)/shard_map/ppermute | solution.py:17
  278.3 2.7 copy-start
where the time goes:
time: 293 us; the launch traced here: 292 us
  local copies, waits for them, and re-layouts  127 us (43%)
  blocking collectives  50.5 us (17%)
  waiting for transfers between devices  38.6 us (13%)
  matrix products  37.1 us (13%)
  other arithmetic  20.5 us (7%)
  starting transfers between devices  18.1 us (6%)
    all_to_all x1, blocking collectives, shards(): lax.all_to_all(stack, 'ty', split_axis=2, concat_axis=3, tiled=True)  50.5 us
    unnamed x15, local copies, waits for them, and re-layouts  41.6 us
    all_to_all x1, local copies, waits for them, and re-layouts, shards(): lax.all_to_all(by_rows, 'tx', split_axis=3, concat_axis=0, tiled=True)  35.3 us
    dot_general x1, matrix products, box_mean(): jnp.einsum('fiw,wk->fik', rowsum, col_band, precision=lax.Precision.HIGHEST)  26.9 us
    all_to_all x1, waiting for transfers between devices, shards(): lax.all_to_all(by_rows, 'tx', split_axis=3, concat_axis=0, tiled=True)  22.2 us
    all_to_all x1, local copies, waits for them, and re-layouts, shards(): lax.all_to_all(stack, 'ty', split_axis=2, concat_axis=3, tiled=True)  20.2 us
    ppermute x2, waiting for transfers between devices, with_halo(): lax.ppermute(lax.slice_in_dim(block, block.shape[dim] - width, None, axis...  11.1 us
    dot_general x1, matrix products, box_mean(): jnp.einsum('ij,fjw->fiw', row_band, fields, precision=lax.Precision.HIGHEST)  9.53 us
  transfers between devices with their start and end apart: 5, of which 5 were waited for; matrix products, arithmetic and copies ran while one was open for 1% of the time, Pallas kernels for 0%

commit v1 on v0

v1 whole, which is shorter than its diff:
```python
import jax
import jax.numpy as jnp
from jax import lax
from jax.sharding import PartitionSpec as P

RADIUS = 4


def with_halo(block, sides, width):
    for axis, dim in sides:
        count = lax.axis_size(axis)
        forward = [(i, i + 1) for i in range(count - 1)]
        backward = [(target, source) for source, target in forward]
        low = lax.ppermute(
            lax.slice_in_dim(block, block.shape[dim] - width, None, axis=dim), axis, forward
        )
        high = lax.ppermute(lax.slice_in_dim(block, 0, width, axis=dim), axis, backward)
        block = jnp.concatenate([low, block, high], axis=dim)
    return block


def box_mean(fields, tile_rows, tile_cols, radius):
    window = 2 * radius + 1
    rowsum = fields[:, 0:tile_rows]
    for offset in range(1, window):
        rowsum = rowsum + fields[:, offset : offset + tile_rows]
    colsum = rowsum[:, :, 0:tile_cols]
    for offset in range(1, window):
        colsum = colsum + rowsum[:, :, offset : offset + tile_cols]
    return colsum / float(window * window)


def shards(stack, filt_re, filt_im, pre_ids, post_ids):
    count_acq = filt_re.shape[0]
    count_pairs = pre_ids.shape[0]
    n_rows = lax.axis_size("ty")
    n_cols = lax.axis_size("tx")
    local_acq, _, height, local_cols = stack.shape
    tile_rows = height // n_rows
    blocks_per_tile = n_rows // n_cols
    tile_cols = local_cols * blocks_per_tile

    x = stack.reshape(local_acq, 2, n_rows, tile_rows, local_cols)
    x = jnp.transpose(x, (2, 0, 1, 3, 4))
    x = lax.all_to_all(x, "ty", 0, 0, tiled=True)
    x = x.reshape(n_cols, blocks_per_tile, local_acq, 2, tile_rows, local_cols)
    x = lax.all_to_all(x, "tx", 0, 0, tiled=True)
    x = jnp.transpose(x, (0, 2, 3, 4, 1, 5))
    x = x.reshape(2 * count_acq, tile_rows, tile_cols)
    x = with_halo(x, (("ty", 1), ("tx", 2)), RADIUS)

    mixing = jnp.stack([jnp.stack([filt_re, -filt_im], -1), jnp.stack([filt_im, filt_re], -1)], 1)
    mixing = mixing.reshape(count_acq, 2, 2 * count_acq)
    wide = jnp.concatenate(
        [mixing, jnp.take(mixing, pre_ids, axis=0), jnp.take(mixing, post_ids, axis=0)], axis=0
    )
    wide = wide.reshape(-1, 2 * count_acq)
    result = jnp.einsum("kc,chw->khw", wide, x, preferred_element_type=jnp.float32)
    filtered = result.astype(jnp.bfloat16).astype(jnp.float32)
    filtered = filtered.reshape(count_acq + 2 * count_pairs, 2, *filtered.shape[1:])

    own = filtered[:count_acq]
    pre_side = filtered[count_acq : count_acq + count_pairs]
    post_side = filtered[count_acq + count_pairs :]
    power = own[:, 0] * own[:, 0] + own[:, 1] * own[:, 1]
    cross_re = pre_side[:, 0] * post_side[:, 0] + pre_side[:, 1] * post_side[:, 1]
    cross_im = pre_side[:, 1] * post_side[:, 0] - pre_side[:, 0] * post_side[:, 1]
    fields = jnp.concatenate([power, cross_re, cross_im], axis=0)
    means = box_mean(fields, tile_rows, tile_cols, RADIUS)
    power_mean = means[:count_acq] + 1e-06
    pre_power = jnp.take(power_mean, pre_ids, axis=0)
    post_power = jnp.take(power_mean, post_ids, axis=0)
    real_mean = means[count_acq : count_acq + count_pairs]
    imag_mean = means[count_acq + count_pairs :]
    coherence = jnp.sqrt(real_mean * real_mean + imag_mean * imag_mean) / jnp.sqrt(
        pre_power * post_power
    )
    change = jnp.log(post_power / pre_power)
    return (coherence, change)


def solution(mesh):
    in_specs = (P("tx", None, None, "ty"), P(), P(), P(), P())
    out_specs = (P(None, "ty", "tx"), P(None, "ty", "tx"))
    return jax.shard_map(shards, mesh=mesh, in_specs=in_specs, out_specs=out_specs, check_vma=False)
```

time: 293 us -> 306 us (1.044)
  other arithmetic: 20.5 us -> 82.8 us
  local copies, waits for them, and re-layouts: 127 us -> 99 us
  matrix products: 37.1 us -> 9.41 us
  waiting for transfers between devices: 38.6 us -> 43 us
    slice x1 -> x7, local copies, waits for them, and re-layouts: 0.46 us -> 76.4 us  [the longest x2 24.3 us: shards(): own = filtered[:count_acq]]
    all_to_all x2 -> x0, local copies, waits for them, and re-layouts: 55.5 us -> none  [the longest x1 35.3 us: shards(): lax.all_to_all(by_rows, 'tx', split_axis=3, concat_axis=0, tiled=True)]
    add x3 -> x4, other arithmetic: 5.95 us -> 52.8 us  [the longest x1 32.5 us: box_mean(): rowsum = rowsum + fields[:, offset:offset + tile_rows]]
    unnamed x15 -> x22, local copies, waits for them, and re-layouts: 41.6 us -> 1 us
    dot_general x3 -> x1, matrix products: 37.1 us -> 9.41 us  [shards(): jnp.einsum('kc,chw->khw', wide, x, preferred_element_type=jnp.float32)]
    div x0 -> x1, other arithmetic: none -> 14.5 us  [box_mean(): return colsum / float(window * window)]
    gather x4, local copies, waits for them, and re-layouts: 17.8 us -> 5.2 us  [the longest x1 2 us: shards(): post_power = jnp.take(power_mean, post_ids, axis=0)]
    concatenate x0 -> x2, other arithmetic: none -> 8.13 us  [the longest x1 7.43 us: shards(): fields = jnp.concatenate([power, cross_re, cross_im], axis=0)]
where the time goes in v1:
time: 306 us; the launch traced here: 303 us
  local copies, waits for them, and re-layouts  99 us (32%)
  other arithmetic  82.8 us (27%)
  blocking collectives  50.6 us (17%)
  waiting for transfers between devices  43 us (14%)
  starting transfers between devices  17.6 us (6%)
  matrix products  9.41 us (3%)
    all_to_all x1, blocking collectives, shards(): x = lax.all_to_all(x, 'ty', 0, 0, tiled=True)  50.6 us
    add x1, other arithmetic, box_mean(): rowsum = rowsum + fields[:, offset:offset + tile_rows]  32.5 us
    slice x2, local copies, waits for them, and re-layouts, shards(): own = filtered[:count_acq]  24.3 us
    all_to_all x1, waiting for transfers between devices, shards(): x = lax.all_to_all(x, 'tx', 0, 0, tiled=True)  23 us
    div x1, other arithmetic, box_mean(): return colsum / float(window * window)  14.5 us
    add x1, other arithmetic, shards(): pre_side[:, 0] * post_side[:, 0] + pre_side[:, 1] * post_side[:, 1]  12.8 us
    slice x1, local copies, waits for them, and re-layouts, shards(): pre_side[:, 0] * post_side[:, 0] + pre_side[:, 1] * post_side[:, 1]  11.5 us
    slice x1, local copies, waits for them, and re-layouts, shards(): power = own[:, 0] * own[:, 0] + own[:, 1] * own[:, 1]  11.5 us
  transfers between devices with their start and end apart: 5, of which 5 were waited for; matrix products, arithmetic and copies ran while one was open for 1% of the time, Pallas kernels for 0%

profile of v1, /device:TPU:21, one launch (start us, length us, event | category | flops | bytes accessed | tf_op | source)
XLA Modules:
  0.0 303.3 jit_solution(9601467351133608838)
XLA Ops:
  0.6 1.8 copy.42
  2.5 50.6 %all_to_all.10 = bf16[8,8,2,16,512]{4,3,2,1,0:T(8,128)(2,1)} all-to-all(bf16[8,8,2,16,512]{4,3,2,1,0:T(8,128)(2,1)S(1)} %copy.42), channel_id=1, replica_groups=mesh['tx'=4,'ty'=8] {'ty'}, dimensions={0} | all-to-all | bytes 4194304 | tf_op jit(solution)/shard_map/all_to_all | solution.py:45
  53.1 3.8 %all-to-all-start.1 = ((bf16[4,2,8,2,16,512]{5,4,3,2,1,0:T(8,128)(2,1)}), bf16[4,2,8,2,16,512]{5,4,3,2,1,0:T(8,128)(2,1)S(1)}, u32[]{:S(2)}, u32[]{:S(2)}) async-start(bf16[4,2,8,2,16,512]{5,4,3,2,1,0:T(8,128)(2,1)} %bitcast.31), calls=%async_computation.1 | async-start | bytes 4194304 | tf_op jit(solution)/shard_map/all_to_all | solution.py:47
  57.4 23.0 %all-to-all-done.1 = bf16[4,2,8,2,16,512]{5,4,3,2,1,0:T(8,128)(2,1)S(1)} async-done(((bf16[4,2,8,2,16,512]{5,4,3,2,1,0:T(8,128)(2,1)}), bf16[4,2,8,2,16,512]{5,4,3,2,1,0:T(8,128)(2,1)S(1)}, u32[]{:S(2)}, u32[]{:S(2)}) %all-to-all-start.1) | async-done | bytes 2097184 | tf_op jit(solution)/shard_map/all_to_all | solution.py:47
  80.4 3.5 %copy.43 = bf16[4,8,2,16,2,512]{5,4,2,1,0,3:T(2,128)(2,1)} copy(bf16[4,8,2,16,2,512]{5,3,2,1,4,0:T(8,128)(2,1)S(1)} %bitcast.30) | data formatting | bytes 4194304 | tf_op jit(solution)/shard_map/transpose | solution.py:48
  83.9 3.2 %reshape.47 = bf16[64,16,1024]{2,0,1:T(8,128)(2,1)S(1)} reshape(bf16[4,8,2,16,2,512]{5,4,2,1,0,3:T(2,128)(2,1)} %copy.43) | data formatting | bytes 4194304 | tf_op jit(solution)/shard_map/reshape | solution.py:49
  88.2 6.4 %collective-permute-start = (bf16[64,4,1024]{2,0,1:T(8,128)(2,1)}, bf16[64,4,1024]{2,0,1:T(8,128)(2,1)S(1)}, u32[]{:S(2)}, u32[]{:S(2)}) collective-permute-start(bf16[64,4,1024]{2,0,1:T(8,128)(2,1)} %get-tuple-element.20), channel_id=1, source_target_pairs={{0,1},{1,2},{2,3},{3,4},{4,5},{5,6},{6,7},{8,9},{9,10},{10,11},{11... | collective-permute-start | bytes 1572872 | tf_op jit(solution)/shard_map/ppermute | solution.py:14
  95.2 1.9 collective-permute-start.1
  98.0 3.1 %collective-permute-done = bf16[64,4,1024]{2,0,1:T(8,128)(2,1)S(1)} collective-permute-done((bf16[64,4,1024]{2,0,1:T(8,128)(2,1)}, bf16[64,4,1024]{2,0,1:T(8,128)(2,1)S(1)}, u32[]{:S(2)}, u32[]{:S(2)}) %collective-permute-start) | collective-permute-done | bytes 524320 | tf_op jit(solution)/shard_map/ppermute | solution.py:14
  101.2 4.7 %collective-permute-done.1 = bf16[64,4,1024]{2,0,1:T(8,128)(2,1)S(1)} collective-permute-done((bf16[64,4,1024]{2,0,1:T(8,128)(2,1)}, bf16[64,4,1024]{2,0,1:T(8,128)(2,1)S(1)}, u32[]{:S(2)}, u32[]{:S(2)}) %collective-permute-start.1) | collective-permute-done | bytes 524320 | tf_op jit(solution)/shard_map/ppermute | solution.py:17
  106.2 3.0 %collective-permute-start.3 = (bf16[64,24,4]{2,0,1:T(8,128)(2,1)S(1)}, bf16[64,24,4]{2,0,1:T(8,128)(2,1)S(1)}, u32[]{:S(2)}, u32[]{:S(2)}) collective-permute-start(bf16[64,24,4]{2,0,1:T(8,128)(2,1)S(1)} %get-tuple-element.17), channel_id=1, source_target_pairs={{8,0},{16,8},{24,16},{9,1},{17,9},{25,17},{10,2},{18,10},{26,18},{... | collective-permute-start | bytes 36872 | tf_op jit(solution)/shard_map/ppermute | solution.py:17
  109.3 2.4 collective-permute-start.2
  112.4 5.8 %collective-permute-done.3 = bf16[64,24,4]{2,0,1:T(8,128)(2,1)S(1)} collective-permute-done((bf16[64,24,4]{2,0,1:T(8,128)(2,1)S(1)}, bf16[64,24,4]{2,0,1:T(8,128)(2,1)S(1)}, u32[]{:S(2)}, u32[]{:S(2)}) %collective-permute-start.3) | collective-permute-done | bytes 12320 | tf_op jit(solution)/shard_map/ppermute | solution.py:17
  119.0 6.5 %collective-permute-done.2 = bf16[64,24,4]{2,0,1:T(8,128)(2,1)} collective-permute-done((bf16[64,24,4]{2,0,1:T(8,128)(2,1)S(1)}, bf16[64,24,4]{2,0,1:T(8,128)(2,1)}, u32[]{:S(2)}, u32[]{:S(2)}) %collective-permute-start.2) | collective-permute-done | bytes 12320 | tf_op jit(solution)/shard_map/ppermute | solution.py:14
  125.5 6.2 %concatenate.15 = bf16[64,24,1032]{2,0,1:T(8,128)(2,1)S(1)} concatenate(bf16[64,24,4]{2,0,1:T(8,128)(2,1)} %collective-permute-done.2, bf16[64,24,1024]{2,0,1:T(8,128)(2,1)} %copy-done.4, bf16[64,24,4]{2,0,1:T(8,128)(2,1)} %copy-done.5), dimensions={2} | concatenate | bytes 6340608 | tf_op jit(solution)/shard_map/concatenate | solution.py:18
  131.6 9.4 %fusion = f32[192,24,1032]{2,0,1:T(8,128)} fusion(bf16[192,64,1]{1,0,2:T(8,128)(2,1)} %bitcast.33, bf16[64,24,1032]{2,0,1:T(8,128)(2,1)S(1)} %concatenate.15), kind=kOutput, calls=%fused_computation.5 | convolution fusion | flops 618209280 | bytes 22216704 | tf_op jit(solution)/shard_map/kc,chw->khw/dot_general | solution.py:58
  141.0 15.0 %fusion.7 = (f32[64,24,1032]{2,0,1:T(8,128)}, f32[64,24,1032]{2,0,1:T(8,128)}, f32[64,24,1032]{2,0,1:T(8,128)}) fusion(f32[192,24,1032]{2,0,1:T(8,128)} %fusion), kind=kLoop, calls=%fused_computation.53 | loop fusion | bytes 38043648 | tf_op jit(solution)/shard_map/slice | solution.py:62
  156.1 9.3 %slice.122 = f32[32,2,24,1032]{3,1,0,2:T(2,128)} reshape(f32[64,24,1032]{2,0,1:T(8,128)} %get-tuple-element.4) | data formatting | bytes 12681216 | tf_op jit(solution)/shard_map/slice | solution.py:62
  165.4 11.5 %fusion.8 = (f32[32,1,24,1032]{3,1,0,2:T(1,128)S(1)}, f32[32,1,24,1032]{3,1,0,2:T(1,128)}) fusion(f32[32,2,24,1032]{3,1,0,2:T(2,128)} %slice.122), kind=kLoop, calls=%fused_computation.54 | loop fusion | bytes 12681216 | tf_op jit(solution)/shard_map/slice | solution.py:65
  176.9 9.3 %slice.129 = f32[32,2,24,1032]{3,1,0,2:T(2,128)} reshape(f32[64,24,1032]{2,0,1:T(8,128)} %get-tuple-element.5) | data formatting | bytes 12681216 | tf_op jit(solution)/shard_map/slice | solution.py:64
  186.2 10.4 %fusion.10 = (f32[32,1,24,1032]{3,1,0,2:T(1,128)}, f32[32,1,24,1032]{3,1,0,2:T(1,128)}) fusion(f32[32,2,24,1032]{3,1,0,2:T(2,128)} %slice.129), kind=kLoop, calls=%fused_computation.56 | loop fusion | bytes 12681216 | tf_op jit(solution)/shard_map/slice | solution.py:66
  196.6 9.3 %slice.126 = f32[32,2,24,1032]{3,1,0,2:T(2,128)} reshape(f32[64,24,1032]{2,0,1:T(8,128)} %get-tuple-element.6) | data formatting | bytes 12681216 | tf_op jit(solution)/shard_map/slice | solution.py:63
  205.9 11.5 %fusion.9 = (f32[32,1,24,1032]{3,1,0,2:T(1,128)S(1)}, f32[32,1,24,1032]{3,1,0,2:T(1,128)}) fusion(f32[32,2,24,1032]{3,1,0,2:T(2,128)} %slice.126), kind=kLoop, calls=%fused_computation.55 | loop fusion | bytes 12681216 | tf_op jit(solution)/shard_map/slice | solution.py:66
  217.5 5.6 %fusion.3 = f32[32,24,1032]{2,1,0:T(8,128)} fusion(f32[32,1,24,1032]{3,1,0,2:T(1,128)S(1)} %copy-done, f32[32,1,24,1032]{3,1,0,2:T(1,128)S(1)} %get-tuple-element.9), kind=kLoop, calls=%fused_computation.26 | loop fusion | flops 2377728 | bytes 9510912 | tf_op jit(solution)/shard_map/add | solution.py:65
  223.1 12.8 %add_bitcast_fusion = (f32[32,24,1032]{2,1,0:T(8,128)}, f32[32,24,1032]{2,1,0:T(8,128)}) fusion(f32[32,1,24,1032]{3,1,0,2:T(1,128)S(1)} %copy-done.2, f32[32,1,24,1032]{3,1,0,2:T(1,128)} %get-tuple-element.12, f32[32,1,24,1032]{3,1,0,2:T(1,128)S(1)} %copy-done.1, f32[32,1,24,1032]{3,1,0,2:T(1,128)S(1)} %get-tuple-element.11), kind=kLoop, calls=%fused_computation.29 | loop fusion | flops 4755456 | bytes 19021824 | tf_op jit(solution)/shard_map/add | solution.py:66
  235.9 7.4 %pad_maximum_fusion = f32[96,24,1032]{2,1,0:T(8,128)} fusion(f32[32,24,1032]{2,1,0:T(8,128)} %get-tuple-element.8, f32[32,24,1032]{2,1,0:T(8,128)} %get-tuple-element.7, f32[32,24,1032]{2,1,0:T(8,128)S(1)} %copy-done.3), kind=kLoop, calls=%fused_computation.6 | loop fusion | flops 4755456 | bytes 19021824 | tf_op jit(solution)/shard_map/concatenate | solution.py:68
  243.3 32.5 %slice_add_fusion = f32[96,16,1032]{2,1,0:T(8,128)S(1)} fusion(f32[96,24,1032]{2,1,0:T(8,128)} %pad_maximum_fusion), kind=kLoop, calls=%fused_computation.7 | loop fusion | flops 12681216 | bytes 63406080 | tf_op jit(solution)/shard_map/add | solution.py:26
  275.9 14.5 %fusion.1 = f32[96,16,1024]{2,1,0:T(8,128)} fusion(f32[96,16,1032]{2,1,0:T(8,128)S(1)} %slice_add_fusion), kind=kLoop, calls=%fused_computation.16 | loop fusion | flops 14155776 | bytes 62914560 | tf_op jit(solution)/shard_map/div | solution.py:30
  290.4 1.8 slice_add_fusion.16
  292.2 2.0 gather_fusion.3
  294.2 2.0 gather_fusion.2
  296.2 7.1 %divide_log_fusion = (f32[32,16,1024]{2,1,0:T(8,128)}, f32[32,16,1024]{2,1,0:T(8,128)}) fusion(f32[32,16,1024]{2,1,0:T(8,128)} %gather_fusion.3, f32[32,16,1024]{2,1,0:T(8,128)} %gather_fusion.2, pred[32]{0:T(512)(128)(4,1)S(1)} %get-tuple-element.25, pred[32]{0:T(512)(128)(4,1)S(1)} %get-tuple-element.26, f32[96,16,1024]{2,1,0:T(8,128)} %fusion.1), kind=kLoop, calls=%fused_computation.36 | loop fusion | flops 4194304 | bytes 12582976 | tf_op jit(solution)/shard_map/log | solution.py:78
  (41 shorter events, 4.9 us)
Async XLA Ops:
  2.4 54.5 %copy-start.6 = (bf16[32,32]{1,0:T(8,128)(2,1)S(1)}, bf16[32,32]{1,0:T(8,128)(2,1)}, u32[]{:S(2)}) copy-start(bf16[32,32]{1,0:T(8,128)(2,1)} %param.11) | copy-start | bytes 6148
  2.4 54.5 %copy-start.7 = (bf16[32,32]{1,0:T(8,128)(2,1)S(1)}, bf16[32,32]{1,0:T(8,128)(2,1)}, u32[]{:S(2)}) copy-start(bf16[32,32]{1,0:T(8,128)(2,1)} %param.10) | copy-start | bytes 6148
  2.4 54.9 %copy-start.9 = (s32[32]{0:T(128)S(1)}, s32[32]{0:T(128)}, u32[]{:S(2)}) copy-start(s32[32]{0:T(128)} %param.12) | copy-start | bytes 388
  2.5 54.9 %copy-start.8 = (s32[32]{0:T(128)S(1)}, s32[32]{0:T(128)}, u32[]{:S(2)}) copy-start(s32[32]{0:T(128)} %param.13) | copy-start | bytes 388
  53.1 27.3 %all-to-all-start.1 = ((bf16[4,2,8,2,16,512]{5,4,3,2,1,0:T(8,128)(2,1)}), bf16[4,2,8,2,16,512]{5,4,3,2,1,0:T(8,128)(2,1)S(1)}, u32[]{:S(2)}, u32[]{:S(2)}) async-start(bf16[4,2,8,2,16,512]{5,4,3,2,1,0:T(8,128)(2,1)} %bitcast.31), calls=%async_computation.1 | async-start | bytes 4194304 | tf_op jit(solution)/shard_map/all_to_all | solution.py:47
  88.2 12.8 %collective-permute-start = (bf16[64,4,1024]{2,0,1:T(8,128)(2,1)}, bf16[64,4,1024]{2,0,1:T(8,128)(2,1)S(1)}, u32[]{:S(2)}, u32[]{:S(2)}) collective-permute-start(bf16[64,4,1024]{2,0,1:T(8,128)(2,1)} %get-tuple-element.20), channel_id=1, source_target_pairs={{0,1},{1,2},{2,3},{3,4},{4,5},{5,6},{6,7},{8,9},{9,10},{10,11},{11... | collective-permute-start | bytes 1572872 | tf_op jit(solution)/shard_map/ppermute | solution.py:14
  95.2 10.7 %collective-permute-start.1 = (bf16[64,4,1024]{2,0,1:T(8,128)(2,1)}, bf16[64,4,1024]{2,0,1:T(8,128)(2,1)S(1)}, u32[]{:S(2)}, u32[]{:S(2)}) collective-permute-start(bf16[64,4,1024]{2,0,1:T(8,128)(2,1)} %get-tuple-element.19), channel_id=1, source_target_pairs={{1,0},{2,1},{3,2},{4,3},{5,4},{6,5},{7,6},{9,8},{10,9},{11,10},{12... | collective-permute-start | bytes 1572872 | tf_op jit(solution)/shard_map/ppermute | solution.py:17
  106.0 12.3 %copy-start.4 = (bf16[64,24,1024]{2,0,1:T(8,128)(2,1)}, bf16[64,24,1024]{2,0,1:T(8,128)(2,1)S(1)}, u32[]{:S(2)}) copy-start(bf16[64,24,1024]{2,0,1:T(8,128)(2,1)S(1)} %constant_dynamic-update-slice_fusion) | copy-start | bytes 9437188
  106.2 12.0 %collective-permute-start.3 = (bf16[64,24,4]{2,0,1:T(8,128)(2,1)S(1)}, bf16[64,24,4]{2,0,1:T(8,128)(2,1)S(1)}, u32[]{:S(2)}, u32[]{:S(2)}) collective-permute-start(bf16[64,24,4]{2,0,1:T(8,128)(2,1)S(1)} %get-tuple-element.17), channel_id=1, source_target_pairs={{8,0},{16,8},{24,16},{9,1},{17,9},{25,17},{10,2},{18,10},{26,18},{... | collective-permute-start | bytes 36872 | tf_op jit(solution)/shard_map/ppermute | solution.py:17
  109.3 16.2 %collective-permute-start.2 = (bf16[64,24,4]{2,0,1:T(8,128)(2,1)S(1)}, bf16[64,24,4]{2,0,1:T(8,128)(2,1)}, u32[]{:S(2)}, u32[]{:S(2)}) collective-permute-start(bf16[64,24,4]{2,0,1:T(8,128)(2,1)S(1)} %get-tuple-element.18), channel_id=1, source_target_pairs={{0,8},{8,16},{16,24},{1,9},{9,17},{17,25},{2,10},{10,18},{18,26},{... | collective-permute-start | bytes 36872 | tf_op jit(solution)/shard_map/ppermute | solution.py:14
  118.2 0.7 copy-start.5
  205.9 11.5 %copy-start = (f32[32,1,24,1032]{3,1,0,2:T(1,128)S(1)}, f32[32,1,24,1032]{3,1,0,2:T(1,128)}, u32[]{:S(2)}) copy-start(f32[32,1,24,1032]{3,1,0,2:T(1,128)} %get-tuple-element.10) | copy-start | bytes 9510916
  217.5 5.6 %copy-start.1 = (f32[32,1,24,1032]{3,1,0,2:T(1,128)S(1)}, f32[32,1,24,1032]{3,1,0,2:T(1,128)}, u32[]{:S(2)}) copy-start(f32[32,1,24,1032]{3,1,0,2:T(1,128)} %get-tuple-element.13) | copy-start | bytes 9510916
  217.5 5.6 %copy-start.2 = (f32[32,1,24,1032]{3,1,0,2:T(1,128)S(1)}, f32[32,1,24,1032]{3,1,0,2:T(1,128)}, u32[]{:S(2)}) copy-start(f32[32,1,24,1032]{3,1,0,2:T(1,128)} %get-tuple-element.14) | copy-start | bytes 9510916
  223.1 12.8 %copy-start.3 = (f32[32,24,1032]{2,1,0:T(8,128)S(1)}, f32[32,24,1032]{2,1,0:T(8,128)}, u32[]{:S(2)}) copy-start(f32[32,24,1032]{2,1,0:T(8,128)} %fusion.3) | copy-start | bytes 9510916

commit v2 on v1

v2 whole, which is shorter than its diff:
```python
import functools

import jax
import jax.numpy as jnp
from jax import lax
from jax.experimental import pallas as pl
from jax.experimental.pallas import tpu as pltpu
from jax.sharding import PartitionSpec as P

RADIUS = 4
LANES = 128
PAIRS_PER_STEP = 2
FIELDS = 4


def with_halo(block, sides, width):
    for axis, dim in sides:
        count = lax.axis_size(axis)
        forward = [(i, i + 1) for i in range(count - 1)]
        backward = [(target, source) for source, target in forward]
        low = lax.ppermute(
            lax.slice_in_dim(block, block.shape[dim] - width, None, axis=dim), axis, forward
        )
        high = lax.ppermute(lax.slice_in_dim(block, 0, width, axis=dim), axis, backward)
        yield low, high
        block = jnp.concatenate([low, block, high], axis=dim)


def pair_kernel(pre_ref, post_ref, *refs, tile_rows, tile_cols):
    del pre_ref, post_ref
    pp = PAIRS_PER_STEP
    sides = refs[: 2 * pp]
    band_ref, coh_ref, chg_ref, field_ref, rows_ref, stack_ref = refs[2 * pp :]
    window = 2 * RADIUS + 1
    padded_cols = tile_cols + LANES
    rows = pp * FIELDS * tile_rows
    blocks = tile_cols // LANES
    for p in range(pp):
        a = sides[2 * p]
        b = sides[2 * p + 1]
        pr = a[0, 0].astype(jnp.float32)
        pi = a[0, 1].astype(jnp.float32)
        qr = b[0, 0].astype(jnp.float32)
        qi = b[0, 1].astype(jnp.float32)
        fields = (pr * pr + pi * pi, qr * qr + qi * qi, pr * qr + pi * qi, pi * qr - pr * qi)
        for f, value in enumerate(fields):
            field_ref[...] = value
            acc = field_ref[pl.ds(0, tile_rows), :]
            for k in range(1, window):
                acc = acc + field_ref[pl.ds(k, tile_rows), :]
            at = (p * FIELDS + f) * tile_rows
            rows_ref[pl.ds(at, tile_rows), pl.ds(LANES, padded_cols)] = acc
            rows_ref[pl.ds(at, tile_rows), pl.ds(0, LANES)] = acc[:, padded_cols - LANES :]
    rowsum = rows_ref[...]
    high = rowsum.astype(jnp.bfloat16)
    low = (rowsum - high.astype(jnp.float32)).astype(jnp.bfloat16)
    width = 3 * LANES
    for j in range(blocks):
        stack_ref[pl.ds(j * rows, rows), pl.ds(0, width)] = high[:, j * LANES : j * LANES + width]
        stack_ref[pl.ds(j * rows, rows), pl.ds(width, width)] = low[:, j * LANES : j * LANES + width]
    sums = jnp.dot(stack_ref[...], band_ref[...], preferred_element_type=jnp.float32)
    means = sums / float(window * window)
    for j in range(blocks):
        for p in range(pp):
            base = j * rows + p * FIELDS * tile_rows
            pre_power = means[base : base + tile_rows] + 1e-06
            post_power = means[base + tile_rows : base + 2 * tile_rows] + 1e-06
            real_mean = means[base + 2 * tile_rows : base + 3 * tile_rows]
            imag_mean = means[base + 3 * tile_rows : base + 4 * tile_rows]
            coh = jnp.sqrt(real_mean * real_mean + imag_mean * imag_mean) / jnp.sqrt(
                pre_power * post_power
            )
            coh_ref[p, :, pl.ds(j * LANES, LANES)] = coh
            chg_ref[p, :, pl.ds(j * LANES, LANES)] = jnp.log(post_power / pre_power)


def pair_maps(filtered, pre_ids, post_ids, tile_rows, tile_cols):
    count_pairs = pre_ids.shape[0]
    pp = PAIRS_PER_STEP
    padded_rows, padded_cols = filtered.shape[2:]
    width = 3 * LANES
    lane_in = jnp.arange(width)[:, None]
    lane_out = jnp.arange(LANES)[None, :]
    gap = lane_in - LANES - lane_out
    band = jnp.where((gap >= -RADIUS) & (gap <= RADIUS), 1.0, 0.0).astype(jnp.bfloat16)
    band = jnp.concatenate([band, band], axis=0)
    block = (1, 2, padded_rows, padded_cols)

    def side_spec(p, which):
        def index(i, pre, post):
            ids = pre if which == 0 else post
            return (ids[i * pp + p], 0, 0, 0)

        return pl.BlockSpec(block, index)

    in_specs = []
    operands = []
    for p in range(pp):
        in_specs += [side_spec(p, 0), side_spec(p, 1)]
        operands += [filtered, filtered]
    in_specs.append(pl.BlockSpec((2 * width, LANES), lambda i, pre, post: (0, 0)))
    operands.append(band)
    out_block = pl.BlockSpec((pp, tile_rows, tile_cols), lambda i, pre, post: (i, 0, 0))
    rows = pp * FIELDS * tile_rows
    blocks = tile_cols // LANES
    grid_spec = pltpu.PrefetchScalarGridSpec(
        num_scalar_prefetch=2,
        grid=(count_pairs // pp,),
        in_specs=in_specs,
        out_specs=[out_block, out_block],
        scratch_shapes=[
            pltpu.VMEM((padded_rows, padded_cols), jnp.float32),
            pltpu.VMEM((rows, padded_cols + LANES), jnp.float32),
            pltpu.VMEM((blocks * rows, 2 * width), jnp.bfloat16),
        ],
    )
    out_shape = jax.ShapeDtypeStruct((count_pairs, tile_rows, tile_cols), jnp.float32)
    kernel = functools.partial(pair_kernel, tile_rows=tile_rows, tile_cols=tile_cols)
    return pl.pallas_call(
        kernel,
        grid_spec=grid_spec,
        out_shape=[out_shape, out_shape],
    )(pre_ids, post_ids, *operands)


def shards(stack, filt_re, filt_im, pre_ids, post_ids):
    count_acq = filt_re.shape[0]
    n_rows = lax.axis_size("ty")
    n_cols = lax.axis_size("tx")
    local_acq, _, height, local_cols = stack.shape
    tile_rows = height // n_rows
    blocks_per_tile = n_rows // n_cols
    tile_cols = local_cols * blocks_per_tile

    x = stack.reshape(local_acq, 2, n_rows, tile_rows, local_cols)
    x = jnp.transpose(x, (2, 0, 1, 3, 4))
    x = lax.all_to_all(x, "ty", 0, 0, tiled=True)
    x = x.reshape(n_cols, blocks_per_tile, local_acq, 2, tile_rows, local_cols)
    x = lax.all_to_all(x, "tx", 0, 0, tiled=True)
    x = jnp.transpose(x, (0, 2, 3, 4, 1, 5))
    x = x.reshape(2 * count_acq, tile_rows, tile_cols)

    halos = with_halo(x, (("ty", 1), ("tx", 2)), RADIUS)
    top, bottom = next(halos)
    x = jnp.concatenate([top, x, bottom], axis=1)
    left, right = next(halos)
    gap = jnp.zeros((2 * count_acq, x.shape[1], LANES - 2 * RADIUS), x.dtype)
    x = jnp.concatenate([x, right, gap, left], axis=2)

    mixing = jnp.stack([jnp.stack([filt_re, -filt_im], -1), jnp.stack([filt_im, filt_re], -1)], 1)
    mixing = mixing.reshape(2 * count_acq, 2 * count_acq)
    result = jnp.einsum("kc,chw->khw", mixing, x, preferred_element_type=jnp.float32)
    filtered = result.astype(jnp.bfloat16).reshape(count_acq, 2, *x.shape[1:])
    return pair_maps(filtered, pre_ids, post_ids, tile_rows, tile_cols)


def solution(mesh):
    in_specs = (P("tx", None, None, "ty"), P(), P(), P(), P())
    out_specs = (P(None, "ty", "tx"), P(None, "ty", "tx"))
    return jax.shard_map(shards, mesh=mesh, in_specs=in_specs, out_specs=out_specs, check_vma=False)
```

time: 306 us -> 161 us (0.53)
  other arithmetic: 82.8 us -> 0.83 us
  local copies, waits for them, and re-layouts: 99 us -> 22.2 us
  Pallas kernels: 0 us -> 22.6 us
  matrix products: 9.41 us -> 1.05 us
    slice x7 -> x1, local copies, waits for them, and re-layouts: 76.4 us -> 0.24 us  [with_halo(): lax.slice_in_dim(block, block.shape[dim] - width, None, axis=dim)]
    add x4 -> x0, other arithmetic: 52.8 us -> none  [the longest x1 32.5 us: box_mean(): rowsum = rowsum + fields[:, offset:offset + tile_rows]]
    pallas_call x0 -> x1, Pallas kernels: none -> 22.6 us  [pair_maps(): pl.pallas_call(kernel, grid_spec=grid_spec, out_shape=[out_shape, out_sha...]
    div x1 -> x0, other arithmetic: 14.5 us -> none  [box_mean(): return colsum / float(window * window)]
    dot_general x1, matrix products: 9.41 us -> 1.05 us  [shards(): jnp.einsum('kc,chw->khw', mixing, x, preferred_element_type=jnp.float32)]
    concatenate x2 -> x1, other arithmetic: 8.13 us -> 0.69 us  [pair_maps(): band = jnp.concatenate([band, band], axis=0)]
    log x1 -> x0, other arithmetic: 7.12 us -> none  [shards(): change = jnp.log(post_power / pre_power)]
    gather x4 -> x0, local copies, waits for them, and re-layouts: 5.2 us -> none  [the longest x1 2 us: shards(): post_power = jnp.take(power_mean, post_ids, axis=0)]
where the time goes in v2:
time: 161 us; the launch traced here: 159 us
  blocking collectives  50.5 us (31%)
  waiting for transfers between devices  43.5 us (27%)
  Pallas kernels  22.6 us (14%)
  local copies, waits for them, and re-layouts  22.2 us (14%)
  starting transfers between devices  17.4 us (11%)
    all_to_all x1, blocking collectives, shards(): x = lax.all_to_all(x, 'ty', 0, 0, tiled=True)  50.5 us
    all_to_all x1, waiting for transfers between devices, shards(): x = lax.all_to_all(x, 'tx', 0, 0, tiled=True)  23.5 us
    pallas_call x1, Pallas kernels, pair_maps(): pl.pallas_call(kernel, grid_spec=grid_spec, out_shape=[out_shape, out_sha...  22.6 us
    ppermute x2, waiting for transfers between devices, with_halo(): lax.ppermute(lax.slice_in_dim(block, block.shape[dim] - width, None, axis...  10.3 us
    ppermute x2, waiting for transfers between devices, with_halo(): lax.ppermute(lax.slice_in_dim(block, 0, width, axis=dim), axis, backward)  9.68 us
    ppermute x2, starting transfers between devices, with_halo(): lax.ppermute(lax.slice_in_dim(block, block.shape[dim] - width, None, axis...  8.63 us
    ppermute x2, starting transfers between devices, with_halo(): lax.ppermute(lax.slice_in_dim(block, 0, width, axis=dim), axis, backward)  4.96 us
    concatenate x1, local copies, waits for them, and re-layouts, shards(): x = jnp.concatenate([x, right, gap, left], axis=2)  4.9 us
  transfers between devices with their start and end apart: 5, of which 5 were waited for; matrix products, arithmetic and copies ran while one was open for 1% of the time, Pallas kernels for 0%

profile of v2, /device:TPU:21, one launch (start us, length us, event | category | flops | bytes accessed | tf_op | source)
XLA Modules:
  0.0 158.9 jit_solution(12181916560959605076)
XLA Ops:
  0.6 1.8 %copy.17 = bf16[8,8,2,16,512]{4,3,2,1,0:T(8,128)(2,1)S(1)} copy(bf16[8,8,2,16,512]{4,3,0,2,1:T(8,128)(2,1)} %bitcast.26) | data formatting | bytes 4194304 | tf_op jit(solution)/shard_map/transpose | solution.py:136
  2.4 50.5 %all_to_all.10 = bf16[8,8,2,16,512]{4,3,2,1,0:T(8,128)(2,1)} all-to-all(bf16[8,8,2,16,512]{4,3,2,1,0:T(8,128)(2,1)S(1)} %copy.17), channel_id=1, replica_groups=mesh['tx'=4,'ty'=8] {'ty'}, dimensions={0} | all-to-all | bytes 4194304 | tf_op jit(solution)/shard_map/all_to_all | solution.py:137
  52.9 3.8 %all-to-all-start.1 = ((bf16[4,2,8,2,16,512]{5,4,3,2,1,0:T(8,128)(2,1)}), bf16[4,2,8,2,16,512]{5,4,3,2,1,0:T(8,128)(2,1)S(1)}, u32[]{:S(2)}, u32[]{:S(2)}) async-start(bf16[4,2,8,2,16,512]{5,4,3,2,1,0:T(8,128)(2,1)} %bitcast.25), calls=%async_computation.1 | async-start | bytes 4194304 | tf_op jit(solution)/shard_map/all_to_all | solution.py:139
  56.7 23.5 %all-to-all-done.1 = bf16[4,2,8,2,16,512]{5,4,3,2,1,0:T(8,128)(2,1)S(1)} async-done(((bf16[4,2,8,2,16,512]{5,4,3,2,1,0:T(8,128)(2,1)}), bf16[4,2,8,2,16,512]{5,4,3,2,1,0:T(8,128)(2,1)S(1)}, u32[]{:S(2)}, u32[]{:S(2)}) %all-to-all-start.1) | async-done | bytes 2097184 | tf_op jit(solution)/shard_map/all_to_all | solution.py:139
  80.2 3.5 %copy.18 = bf16[4,8,2,16,2,512]{5,4,2,1,0,3:T(2,128)(2,1)} copy(bf16[4,8,2,16,2,512]{5,3,2,1,4,0:T(8,128)(2,1)S(1)} %bitcast.24) | data formatting | bytes 4194304 | tf_op jit(solution)/shard_map/transpose | solution.py:140
  83.7 3.3 %reshape.27 = bf16[64,16,1024]{2,0,1:T(8,128)(2,1)S(1)} reshape(bf16[4,8,2,16,2,512]{5,4,2,1,0,3:T(2,128)(2,1)} %copy.18) | data formatting | bytes 4194304 | tf_op jit(solution)/shard_map/reshape | solution.py:141
  87.0 0.1 fusion.4
  87.1 6.4 %collective-permute-start = (bf16[64,4,1024]{2,0,1:T(8,128)(2,1)S(1)}, bf16[64,4,1024]{2,0,1:T(8,128)(2,1)S(1)}, u32[]{:S(2)}, u32[]{:S(2)}) collective-permute-start(bf16[64,4,1024]{2,0,1:T(8,128)(2,1)S(1)} %get-tuple-element.5), channel_id=1, source_target_pairs={{0,1},{1,2},{2,3},{3,4},{4,5},{5,6},{6,7},{8,9},{9,10},{10,11},{11... | collective-permute-start | bytes 1572872 | tf_op jit(solution)/shard_map/ppermute | solution.py:21
  93.5 0.1 select_convert_fusion
  93.6 1.9 %collective-permute-start.1 = (bf16[64,4,1024]{2,0,1:T(8,128)(2,1)S(1)}, bf16[64,4,1024]{2,0,1:T(8,128)(2,1)S(1)}, u32[]{:S(2)}, u32[]{:S(2)}) collective-permute-start(bf16[64,4,1024]{2,0,1:T(8,128)(2,1)S(1)} %get-tuple-element.4), channel_id=1, source_target_pairs={{1,0},{2,1},{3,2},{4,3},{5,4},{6,5},{7,6},{9,8},{10,9},{11,10},{12... | collective-permute-start | bytes 1572872 | tf_op jit(solution)/shard_map/ppermute | solution.py:24
  95.5 0.0 copy-done.3
  95.5 0.0 copy-done.4
  95.6 0.7 pad_maximum_fusion.refs_4_
  96.2 3.3 %collective-permute-done = bf16[64,4,1024]{2,0,1:T(8,128)(2,1)S(1)} collective-permute-done((bf16[64,4,1024]{2,0,1:T(8,128)(2,1)S(1)}, bf16[64,4,1024]{2,0,1:T(8,128)(2,1)S(1)}, u32[]{:S(2)}, u32[]{:S(2)}) %collective-permute-start) | collective-permute-done | bytes 524320 | tf_op jit(solution)/shard_map/ppermute | solution.py:21
  99.6 0.2 constant_dynamic-update-slice_fusion.1
  99.8 4.3 %collective-permute-done.1 = bf16[64,4,1024]{2,0,1:T(8,128)(2,1)S(1)} collective-permute-done((bf16[64,4,1024]{2,0,1:T(8,128)(2,1)S(1)}, bf16[64,4,1024]{2,0,1:T(8,128)(2,1)S(1)}, u32[]{:S(2)}, u32[]{:S(2)}) %collective-permute-start.1) | collective-permute-done | bytes 524320 | tf_op jit(solution)/shard_map/ppermute | solution.py:24
  104.1 0.0 copy-start
  104.1 1.6 %copy-done = bf16[64,24,1024]{2,0,1:T(8,128)(2,1)} copy-done((bf16[64,24,1024]{2,0,1:T(8,128)(2,1)}, bf16[64,24,1024]{2,0,1:T(8,128)(2,1)S(1)}, u32[]{:S(2)}) %copy-start) | copy-done | bytes 3145752
  105.7 0.2 fusion.3
  106.0 3.0 %collective-permute-start.2 = (bf16[64,24,4]{2,0,1:T(8,128)(2,1)S(1)}, bf16[64,24,4]{2,0,1:T(8,128)(2,1)S(1)}, u32[]{:S(2)}, u32[]{:S(2)}) collective-permute-start(bf16[64,24,4]{2,0,1:T(8,128)(2,1)S(1)} %get-tuple-element.3), channel_id=1, source_target_pairs={{8,0},{16,8},{24,16},{9,1},{17,9},{25,17},{10,2},{18,10},{26,18},{... | collective-permute-start | bytes 36872 | tf_op jit(solution)/shard_map/ppermute | solution.py:24
  109.0 2.3 %collective-permute-start.3 = (bf16[64,24,4]{2,0,1:T(8,128)(2,1)S(1)}, bf16[64,24,4]{2,0,1:T(8,128)(2,1)S(1)}, u32[]{:S(2)}, u32[]{:S(2)}) collective-permute-start(bf16[64,24,4]{2,0,1:T(8,128)(2,1)S(1)} %get-tuple-element.2), channel_id=1, source_target_pairs={{0,8},{8,16},{16,24},{1,9},{9,17},{17,25},{2,10},{10,18},{18,26},{... | collective-permute-start | bytes 36872 | tf_op jit(solution)/shard_map/ppermute | solution.py:21
  111.3 0.5 copy.16
  111.8 0.8 reshape.29
  112.6 5.4 %collective-permute-done.2 = bf16[64,24,4]{2,0,1:T(8,128)(2,1)S(1)} collective-permute-done((bf16[64,24,4]{2,0,1:T(8,128)(2,1)S(1)}, bf16[64,24,4]{2,0,1:T(8,128)(2,1)S(1)}, u32[]{:S(2)}, u32[]{:S(2)}) %collective-permute-start.2) | collective-permute-done | bytes 12320 | tf_op jit(solution)/shard_map/ppermute | solution.py:24
  118.0 7.0 %collective-permute-done.3 = bf16[64,24,4]{2,0,1:T(8,128)(2,1)S(1)} collective-permute-done((bf16[64,24,4]{2,0,1:T(8,128)(2,1)S(1)}, bf16[64,24,4]{2,0,1:T(8,128)(2,1)S(1)}, u32[]{:S(2)}, u32[]{:S(2)}) %collective-permute-start.3) | collective-permute-done | bytes 12320 | tf_op jit(solution)/shard_map/ppermute | solution.py:21
  125.0 0.0 copy-done.1
  125.0 0.8 copy-done.2
  125.8 0.8 broadcast_in_dim.13
  126.6 4.9 %concatenate.11 = bf16[64,24,1152]{2,0,1:T(8,128)(2,1)S(1)} concatenate(bf16[64,24,1024]{2,0,1:T(8,128)(2,1)} %copy-done, bf16[64,24,4]{2,0,1:T(8,128)(2,1)} %copy-done.1, bf16[64,24,120]{2,0,1:T(8,128)(2,1)} %broadcast_in_dim.13, bf16[64,24,4]{2,0,1:T(8,128)(2,1)} %copy-done.2), dimensions={2} | concatenate | bytes 7077888 | tf_op jit(solution)/shard_map/concatenate | solution.py:148
  131.5 1.1 convolution_convert_fusion
  132.6 3.7 %copy.19 = bf16[64,24,1152]{2,1,0:T(8,128)(2,1)} copy(bf16[64,24,1152]{2,0,1:T(8,128)(2,1)S(1)} %convolution_convert_fusion) | data formatting | bytes 7077888 | tf_op jit(solution)/shard_map/convert_element_type | solution.py:153
  136.3 22.6 %shard_map.68 = (f32[32,16,1024]{2,1,0:T(8,128)}, f32[32,16,1024]{2,1,0:T(8,128)}) custom-call(s32[32]{0:T(128)} %pre_ref.1, s32[32]{0:T(128)} %post_ref.1, bf16[32,2,24,1152]{3,2,1,0:T(8,128)(2,1)} %bitcast.20, bf16[32,2,24,1152]{3,2,1,0:T(8,128)(2,1)} %bitcast.21, bf16[32,2,24,1152]{3,2,1,0:T(8,128)(2,1)} %bitcast.22, bf16[32,2,24,1152]{3,2,1,0:T(8,128)(2,1)} %bitcast.23, ...), custom_call_target="tpu_custom_call" | custom-call | tf_op jit(solution)/shard_map/pallas_call | solution.py:119
  (10 shorter events, 0.1 us)
Async XLA Ops:
  52.9 27.3 %all-to-all-start.1 = ((bf16[4,2,8,2,16,512]{5,4,3,2,1,0:T(8,128)(2,1)}), bf16[4,2,8,2,16,512]{5,4,3,2,1,0:T(8,128)(2,1)S(1)}, u32[]{:S(2)}, u32[]{:S(2)}) async-start(bf16[4,2,8,2,16,512]{5,4,3,2,1,0:T(8,128)(2,1)} %bitcast.25), calls=%async_computation.1 | async-start | bytes 4194304 | tf_op jit(solution)/shard_map/all_to_all | solution.py:139
  83.7 11.8 %copy-start.3 = (bf16[32,32]{1,0:T(8,128)(2,1)S(1)}, bf16[32,32]{1,0:T(8,128)(2,1)}, u32[]{:S(2)}) copy-start(bf16[32,32]{1,0:T(8,128)(2,1)} %param.7) | copy-start | bytes 6148
  83.7 11.8 %copy-start.4 = (bf16[32,32]{1,0:T(8,128)(2,1)S(1)}, bf16[32,32]{1,0:T(8,128)(2,1)}, u32[]{:S(2)}) copy-start(bf16[32,32]{1,0:T(8,128)(2,1)} %param.6) | copy-start | bytes 6148
  87.1 12.5 %collective-permute-start = (bf16[64,4,1024]{2,0,1:T(8,128)(2,1)S(1)}, bf16[64,4,1024]{2,0,1:T(8,128)(2,1)S(1)}, u32[]{:S(2)}, u32[]{:S(2)}) collective-permute-start(bf16[64,4,1024]{2,0,1:T(8,128)(2,1)S(1)} %get-tuple-element.5), channel_id=1, source_target_pairs={{0,1},{1,2},{2,3},{3,4},{4,5},{5,6},{6,7},{8,9},{9,10},{10,11},{11... | collective-permute-start | bytes 1572872 | tf_op jit(solution)/shard_map/ppermute | solution.py:21
  93.6 10.5 %collective-permute-start.1 = (bf16[64,4,1024]{2,0,1:T(8,128)(2,1)S(1)}, bf16[64,4,1024]{2,0,1:T(8,128)(2,1)S(1)}, u32[]{:S(2)}, u32[]{:S(2)}) collective-permute-start(bf16[64,4,1024]{2,0,1:T(8,128)(2,1)S(1)} %get-tuple-element.4), channel_id=1, source_target_pairs={{1,0},{2,1},{3,2},{4,3},{5,4},{6,5},{7,6},{9,8},{10,9},{11,10},{12... | collective-permute-start | bytes 1572872 | tf_op jit(solution)/shard_map/ppermute | solution.py:24
  104.1 1.6 %copy-start = (bf16[64,24,1024]{2,0,1:T(8,128)(2,1)}, bf16[64,24,1024]{2,0,1:T(8,128)(2,1)S(1)}, u32[]{:S(2)}) copy-start(bf16[64,24,1024]{2,0,1:T(8,128)(2,1)S(1)} %constant_dynamic-update-slice_fusion) | copy-start | bytes 9437188
  106.0 12.0 %collective-permute-start.2 = (bf16[64,24,4]{2,0,1:T(8,128)(2,1)S(1)}, bf16[64,24,4]{2,0,1:T(8,128)(2,1)S(1)}, u32[]{:S(2)}, u32[]{:S(2)}) collective-permute-start(bf16[64,24,4]{2,0,1:T(8,128)(2,1)S(1)} %get-tuple-element.3), channel_id=1, source_target_pairs={{8,0},{16,8},{24,16},{9,1},{17,9},{25,17},{10,2},{18,10},{26,18},{... | collective-permute-start | bytes 36872 | tf_op jit(solution)/shard_map/ppermute | solution.py:24
  109.0 16.0 %collective-permute-start.3 = (bf16[64,24,4]{2,0,1:T(8,128)(2,1)S(1)}, bf16[64,24,4]{2,0,1:T(8,128)(2,1)S(1)}, u32[]{:S(2)}, u32[]{:S(2)}) collective-permute-start(bf16[64,24,4]{2,0,1:T(8,128)(2,1)S(1)} %get-tuple-element.2), channel_id=1, source_target_pairs={{0,8},{8,16},{16,24},{1,9},{9,17},{17,25},{2,10},{10,18},{18,26},{... | collective-permute-start | bytes 36872 | tf_op jit(solution)/shard_map/ppermute | solution.py:21
  118.0 7.0 %copy-start.1 = (bf16[64,24,4]{2,0,1:T(8,128)(2,1)}, bf16[64,24,4]{2,0,1:T(8,128)(2,1)S(1)}, u32[]{:S(2)}) copy-start(bf16[64,24,4]{2,0,1:T(8,128)(2,1)S(1)} %collective-permute-done.2) | copy-start | bytes 36868
  125.0 0.8 copy-start.2

commit v3 on v2

--- a/solution.py
+++ b/solution.py
@@ -132,11 +132,24 @@
     blocks_per_tile = n_rows // n_cols
     tile_cols = local_cols * blocks_per_tile
 
+    me_col = lax.axis_index("tx")
+    me_row = lax.axis_index("ty")
     x = stack.reshape(local_acq, 2, n_rows, tile_rows, local_cols)
     x = jnp.transpose(x, (2, 0, 1, 3, 4))
-    x = lax.all_to_all(x, "ty", 0, 0, tiled=True)
+    start = me_col * blocks_per_tile + me_row % blocks_per_tile
+    received = []
+    for m in range(n_rows):
+        pairs = []
+        for col in range(n_cols):
+            for row in range(n_rows):
+                to_row = (m + col * blocks_per_tile + row % blocks_per_tile) % n_rows
+                pairs.append((col * n_rows + row, (row // blocks_per_tile) * n_rows + to_row))
+        chunk = lax.dynamic_index_in_dim(x, (start + m) % n_rows, axis=0, keepdims=False)
+        received.append(lax.ppermute(chunk, ("tx", "ty"), pairs))
+    received = jnp.stack(received, axis=0)
+    order = (me_row - jnp.arange(n_rows)) % n_rows
+    x = jnp.take(received, order, axis=0)
     x = x.reshape(n_cols, blocks_per_tile, local_acq, 2, tile_rows, local_cols)
-    x = lax.all_to_all(x, "tx", 0, 0, tiled=True)
     x = jnp.transpose(x, (0, 2, 3, 4, 1, 5))
     x = x.reshape(2 * count_acq, tile_rows, tile_cols)
 

time: 161 us -> 143 us (0.89); the launches traced: 159 us -> 143 us
  blocking collectives: 50.5 us -> 0 us
  starting transfers between devices: 17.4 us -> 53.7 us
  waiting for transfers between devices: 43.5 us -> 32.9 us
  local copies, waits for them, and re-layouts: 22.2 us -> 30.2 us
    all_to_all x1 -> x0, blocking collectives: 50.5 us -> none  [shards(): x = lax.all_to_all(x, 'ty', 0, 0, tiled=True)]
    ppermute x0 -> x8, starting transfers between devices: none -> 35.6 us  [shards(): received.append(lax.ppermute(chunk, ('tx', 'ty'), pairs))]
    all_to_all x1 -> x0, waiting for transfers between devices: 23.5 us -> none  [shards(): x = lax.all_to_all(x, 'tx', 0, 0, tiled=True)]
    ppermute x0 -> x8, waiting for transfers between devices: none -> 13.8 us  [shards(): received.append(lax.ppermute(chunk, ('tx', 'ty'), pairs))]
    unnamed x12 -> x19, local copies, waits for them, and re-layouts: 2.6 us -> 7.69 us
    ppermute x2, starting transfers between devices: 4.96 us -> 9.45 us  [with_halo(): lax.ppermute(lax.slice_in_dim(block, 0, width, axis=dim), axis, backward)]
    all_to_all x1 -> x0, starting transfers between devices: 3.8 us -> none  [shards(): x = lax.all_to_all(x, 'tx', 0, 0, tiled=True)]
    gather x0 -> x1, local copies, waits for them, and re-layouts: none -> 2.27 us  [shards(): x = jnp.take(received, order, axis=0)]
  transfers between devices with their start and end apart: 5 -> 12, of which waited for: 5 -> 6; matrix products, arithmetic and copies ran while one was open for 1% -> 5% of each run, Pallas kernels for 0% -> 0%
where the time goes in v3:
time: 143 us
  starting transfers between devices  53.7 us (38%)
  waiting for transfers between devices  32.9 us (23%)
  local copies, waits for them, and re-layouts  30.2 us (21%)
  Pallas kernels  22.7 us (16%)
    ppermute x8, starting transfers between devices, shards(): received.append(lax.ppermute(chunk, ('tx', 'ty'), pairs))  35.6 us
    pallas_call x1, Pallas kernels, pair_maps(): pl.pallas_call(kernel, grid_spec=grid_spec, out_shape=[out_shape, out_sha...  22.7 us
    ppermute x8, waiting for transfers between devices, shards(): received.append(lax.ppermute(chunk, ('tx', 'ty'), pairs))  13.8 us
    ppermute x2, waiting for transfers between devices, with_halo(): lax.ppermute(lax.slice_in_dim(block, 0, width, axis=dim), axis, backward)  10.3 us
    ppermute x2, starting transfers between devices, with_halo(): lax.ppermute(lax.slice_in_dim(block, 0, width, axis=dim), axis, backward)  9.45 us
    ppermute x2, waiting for transfers between devices, with_halo(): lax.ppermute(lax.slice_in_dim(block, block.shape[dim] - width, None, axis...  8.74 us
    ppermute x2, starting transfers between devices, with_halo(): lax.ppermute(lax.slice_in_dim(block, block.shape[dim] - width, None, axis...  8.64 us
    unnamed x19, local copies, waits for them, and re-layouts  7.69 us
  transfers between devices with their start and end apart: 12, of which 6 were waited for; matrix products, arithmetic and copies ran while one was open for 5% of the time, Pallas kernels for 0%

profile of v3, /device:TPU:21, one launch (start us, length us, event | category | flops | bytes accessed | tf_op | source)
XLA Modules:
  0.0 142.6 jit_solution(16820732411714975180)
XLA Ops:
  0.7 1.7 %dynamic-slice_bitcast_fusion = (bf16[8,2,16,512]{3,2,1,0:T(8,128)(2,1)S(1)}, bf16[8,2,16,512]{3,2,1,0:T(8,128)(2,1)S(1)}, bf16[8,2,16,512]{3,2,1,0:T(8,128)(2,1...) fusion(bf16[8,2,8,16,512]{4,3,2,1,0:T(8,128)(2,1)} %bitcast.58,, ...), kind=kLoop, calls=%fused_computation.11 | loop fusion | bytes 4194336 | tf_op jit(solution)/shard_map/jit(dynamic_index_in_dim)/squeeze | solution.py:147
  3.2 4.5 %collective-permute-start.1 = (bf16[8,2,16,512]{3,2,1,0:T(8,128)(2,1)S(1)}, bf16[8,2,16,512]{3,2,1,0:T(8,128)(2,1)S(1)}, u32[]{:S(2)}, u32[]{:S(2)}) collective-permute-start(bf16[8,2,16,512]{3,2,1,0:T(8,128)(2,1)S(1)} %get-tuple-element.12), channel_id=1, source_target_pairs={{0,1},{1,2},{2,9},{3,10},{4,17},{5,18},{6,25},{7,26},{8,3},{9,4},{... | collective-permute-start | bytes 786440 | tf_op jit(solution)/shard_map/ppermute | solution.py:148
  7.7 5.7 %collective-permute-start.3 = (bf16[8,2,16,512]{3,2,1,0:T(8,128)(2,1)S(1)}, bf16[8,2,16,512]{3,2,1,0:T(8,128)(2,1)S(1)}, u32[]{:S(2)}, u32[]{:S(2)}) collective-permute-start(bf16[8,2,16,512]{3,2,1,0:T(8,128)(2,1)S(1)} %get-tuple-element.10), channel_id=1, source_target_pairs={{0,3},{1,4},{2,11},{3,12},{4,19},{5,20},{6,27},{7,28},{8,5},{9,6},... | collective-permute-start | bytes 786440 | tf_op jit(solution)/shard_map/ppermute | solution.py:148
  13.5 19.4 %collective-permute-start.5 = (bf16[8,2,16,512]{3,2,1,0:T(8,128)(2,1)S(1)}, bf16[8,2,16,512]{3,2,1,0:T(8,128)(2,1)S(1)}, u32[]{:S(2)}, u32[]{:S(2)}) collective-permute-start(bf16[8,2,16,512]{3,2,1,0:T(8,128)(2,1)S(1)} %get-tuple-element.8), channel_id=1, source_target_pairs={{0,5},{1,6},{2,13},{3,14},{4,21},{5,22},{6,29},{7,30},{8,7},{9,0},... | collective-permute-start | bytes 786440 | tf_op jit(solution)/shard_map/ppermute | solution.py:148
  32.9 0.7 bitcast_dynamic-update-slice_fusion.7
  33.6 4.4 %collective-permute-start.6 = (bf16[8,2,16,512]{3,2,1,0:T(8,128)(2,1)S(1)}, bf16[8,2,16,512]{3,2,1,0:T(8,128)(2,1)S(1)}, u32[]{:S(2)}, u32[]{:S(2)}) collective-permute-start(bf16[8,2,16,512]{3,2,1,0:T(8,128)(2,1)S(1)} %get-tuple-element.7), channel_id=1, source_target_pairs={{0,6},{1,7},{2,14},{3,15},{4,22},{5,23},{6,30},{7,31},{8,0},{9,1},... | collective-permute-start | bytes 786440 | tf_op jit(solution)/shard_map/ppermute | solution.py:148
  38.0 0.7 bitcast_dynamic-update-slice_fusion.6
  38.7 0.9 collective-permute-start.7
  40.3 0.7 bitcast_dynamic-update-slice_fusion.4
  41.0 0.7 bitcast_dynamic-update-slice_fusion.3
  41.8 8.9 %collective-permute-done.5 = bf16[8,2,16,512]{3,2,1,0:T(8,128)(2,1)S(1)} collective-permute-done((bf16[8,2,16,512]{3,2,1,0:T(8,128)(2,1)S(1)}, bf16[8,2,16,512]{3,2,1,0:T(8,128)(2,1)S(1)}, u32[]{:S(2)}, u32[]{:S(2)}) %collective-permute-start.5) | collective-permute-done | bytes 262176 | tf_op jit(solution)/shard_map/ppermute | solution.py:148
  51.4 4.9 %collective-permute-done.6 = bf16[8,2,16,512]{3,2,1,0:T(8,128)(2,1)S(1)} collective-permute-done((bf16[8,2,16,512]{3,2,1,0:T(8,128)(2,1)S(1)}, bf16[8,2,16,512]{3,2,1,0:T(8,128)(2,1)S(1)}, u32[]{:S(2)}, u32[]{:S(2)}) %collective-permute-start.6) | collective-permute-done | bytes 262176 | tf_op jit(solution)/shard_map/ppermute | solution.py:148
  57.0 0.7 bitcast_dynamic-update-slice_fusion
  57.8 2.3 %gather_fusion = bf16[8,8,2,16,512]{4,3,2,1,0:T(8,128)(2,1)S(1)} fusion(bf16[8,8,2,16,512]{4,3,2,1,0:T(8,128)(2,1)} %bitcast_dynamic-update-slice_fusion, s32[1024]{0:T(1024)S(1)} %pad_clamp_fusion), kind=kCustom, calls=%fused_computation | custom fusion | bytes 4194336 | tf_op jit(solution)/shard_map/jit(_take)/gather | solution.py:151
  60.3 3.5 %copy.10 = bf16[4,8,2,16,2,512]{5,4,2,1,0,3:T(2,128)(2,1)} copy(bf16[4,8,2,16,2,512]{5,3,2,1,4,0:T(8,128)(2,1)S(1)} %select_bitcast_fusion) | data formatting | bytes 4194304 | tf_op jit(solution)/shard_map/transpose | solution.py:153
  63.8 3.2 %reshape.97 = bf16[64,16,1024]{2,0,1:T(8,128)(2,1)S(1)} reshape(bf16[4,8,2,16,2,512]{5,4,2,1,0,3:T(2,128)(2,1)} %copy.10) | data formatting | bytes 4194304 | tf_op jit(solution)/shard_map/reshape | solution.py:154
  67.1 6.7 %collective-permute-start.8 = (bf16[64,4,1024]{2,0,1:T(8,128)(2,1)S(1)}, bf16[64,4,1024]{2,0,1:T(8,128)(2,1)S(1)}, u32[]{:S(2)}, u32[]{:S(2)}) collective-permute-start(bf16[64,4,1024]{2,0,1:T(8,128)(2,1)S(1)} %get-tuple-element.5), channel_id=1, source_target_pairs={{0,1},{1,2},{2,3},{3,4},{4,5},{5,6},{6,7},{8,9},{9,10},{10,11},{11... | collective-permute-start | bytes 1572872 | tf_op jit(solution)/shard_map/ppermute | solution.py:21
  74.0 1.9 %collective-permute-start.9 = (bf16[64,4,1024]{2,0,1:T(8,128)(2,1)S(1)}, bf16[64,4,1024]{2,0,1:T(8,128)(2,1)S(1)}, u32[]{:S(2)}, u32[]{:S(2)}) collective-permute-start(bf16[64,4,1024]{2,0,1:T(8,128)(2,1)S(1)} %get-tuple-element.4), channel_id=1, source_target_pairs={{1,0},{2,1},{3,2},{4,3},{5,4},{6,5},{7,6},{9,8},{10,9},{11,10},{12... | collective-permute-start | bytes 1572872 | tf_op jit(solution)/shard_map/ppermute | solution.py:24
  76.6 3.3 %collective-permute-done.8 = bf16[64,4,1024]{2,0,1:T(8,128)(2,1)S(1)} collective-permute-done((bf16[64,4,1024]{2,0,1:T(8,128)(2,1)S(1)}, bf16[64,4,1024]{2,0,1:T(8,128)(2,1)S(1)}, u32[]{:S(2)}, u32[]{:S(2)}) %collective-permute-start.8) | collective-permute-done | bytes 524320 | tf_op jit(solution)/shard_map/ppermute | solution.py:21
  80.2 5.2 %collective-permute-done.9 = bf16[64,4,1024]{2,0,1:T(8,128)(2,1)S(1)} collective-permute-done((bf16[64,4,1024]{2,0,1:T(8,128)(2,1)S(1)}, bf16[64,4,1024]{2,0,1:T(8,128)(2,1)S(1)}, u32[]{:S(2)}, u32[]{:S(2)}) %collective-permute-start.9) | collective-permute-done | bytes 524320 | tf_op jit(solution)/shard_map/ppermute | solution.py:24
  85.5 1.6 %copy-done = bf16[64,24,1024]{2,0,1:T(8,128)(2,1)} copy-done((bf16[64,24,1024]{2,0,1:T(8,128)(2,1)}, bf16[64,24,1024]{2,0,1:T(8,128)(2,1)S(1)}, u32[]{:S(2)}) %copy-start) | copy-done | bytes 3145752
  87.3 7.5 %collective-permute-start.10 = (bf16[64,24,4]{2,0,1:T(8,128)(2,1)S(1)}, bf16[64,24,4]{2,0,1:T(8,128)(2,1)S(1)}, u32[]{:S(2)}, u32[]{:S(2)}) collective-permute-start(bf16[64,24,4]{2,0,1:T(8,128)(2,1)S(1)} %get-tuple-element.3), channel_id=1, source_target_pairs={{8,0},{16,8},{24,16},{9,1},{17,9},{25,17},{10,2},{18,10},{26,18},{... | collective-permute-start | bytes 36872 | tf_op jit(solution)/shard_map/ppermute | solution.py:24
  94.9 1.9 %collective-permute-start.11 = (bf16[64,24,4]{2,0,1:T(8,128)(2,1)S(1)}, bf16[64,24,4]{2,0,1:T(8,128)(2,1)S(1)}, u32[]{:S(2)}, u32[]{:S(2)}) collective-permute-start(bf16[64,24,4]{2,0,1:T(8,128)(2,1)S(1)} %get-tuple-element.2), channel_id=1, source_target_pairs={{0,8},{8,16},{16,24},{1,9},{9,17},{17,25},{2,10},{10,18},{18,26},{... | collective-permute-start | bytes 36872 | tf_op jit(solution)/shard_map/ppermute | solution.py:21
  97.3 0.8 reshape.107
  98.1 5.1 %collective-permute-done.10 = bf16[64,24,4]{2,0,1:T(8,128)(2,1)S(1)} collective-permute-done((bf16[64,24,4]{2,0,1:T(8,128)(2,1)S(1)}, bf16[64,24,4]{2,0,1:T(8,128)(2,1)S(1)}, u32[]{:S(2)}, u32[]{:S(2)}) %collective-permute-start.10) | collective-permute-done | bytes 12320 | tf_op jit(solution)/shard_map/ppermute | solution.py:24
  103.2 5.4 %collective-permute-done.11 = bf16[64,24,4]{2,0,1:T(8,128)(2,1)S(1)} collective-permute-done((bf16[64,24,4]{2,0,1:T(8,128)(2,1)S(1)}, bf16[64,24,4]{2,0,1:T(8,128)(2,1)S(1)}, u32[]{:S(2)}, u32[]{:S(2)}) %collective-permute-start.11) | collective-permute-done | bytes 12320 | tf_op jit(solution)/shard_map/ppermute | solution.py:21
  108.6 0.8 copy-done.2
  109.4 0.8 broadcast_in_dim.25
  110.2 4.9 %concatenate.11 = bf16[64,24,1152]{2,0,1:T(8,128)(2,1)S(1)} concatenate(bf16[64,24,1024]{2,0,1:T(8,128)(2,1)} %copy-done, bf16[64,24,4]{2,0,1:T(8,128)(2,1)} %copy-done.1, bf16[64,24,120]{2,0,1:T(8,128)(2,1)} %broadcast_in_dim.25, bf16[64,24,4]{2,0,1:T(8,128)(2,1)} %copy-done.2), dimensions={2} | concatenate | bytes 7077888 | tf_op jit(solution)/shard_map/concatenate | solution.py:161
  115.1 1.1 convolution_convert_fusion
  116.2 3.7 %copy.11 = bf16[64,24,1152]{2,1,0:T(8,128)(2,1)} copy(bf16[64,24,1152]{2,0,1:T(8,128)(2,1)S(1)} %convolution_convert_fusion) | data formatting | bytes 7077888 | tf_op jit(solution)/shard_map/convert_element_type | solution.py:166
  119.9 22.7 %shard_map.68 = (f32[32,16,1024]{2,1,0:T(8,128)}, f32[32,16,1024]{2,1,0:T(8,128)}) custom-call(s32[32]{0:T(128)} %pre_ref.1, s32[32]{0:T(128)} %post_ref.1, bf16[32,2,24,1152]{3,2,1,0:T(8,128)(2,1)} %bitcast.53, bf16[32,2,24,1152]{3,2,1,0:T(8,128)(2,1)} %bitcast.54, bf16[32,2,24,1152]{3,2,1,0:T(8,128)(2,1)} %bitcast.55, bf16[32,2,24,1152]{3,2,1,0:T(8,128)(2,1)} %bitcast.56, ...), custom_call_target="tpu_custom_call" | custom-call | tf_op jit(solution)/shard_map/pallas_call | solution.py:119
  (36 shorter events, 5.1 us)
Async XLA Ops:
  2.5 11.0 %collective-permute-start = (bf16[8,2,16,512]{3,2,1,0:T(8,128)(2,1)S(1)}, bf16[8,2,16,512]{3,2,1,0:T(8,128)(2,1)S(1)}, u32[]{:S(2)}, u32[]{:S(2)}) collective-permute-start(bf16[8,2,16,512]{3,2,1,0:T(8,128)(2,1)S(1)} %get-tuple-element.13), channel_id=1, source_target_pairs={{0,0},{1,1},{2,8},{3,9},{4,16},{5,17},{6,24},{7,25},{8,2},{9,3},{1... | collective-permute-start | bytes 786440 | tf_op jit(solution)/shard_map/ppermute | solution.py:148
  3.2 30.4 %collective-permute-start.1 = (bf16[8,2,16,512]{3,2,1,0:T(8,128)(2,1)S(1)}, bf16[8,2,16,512]{3,2,1,0:T(8,128)(2,1)S(1)}, u32[]{:S(2)}, u32[]{:S(2)}) collective-permute-start(bf16[8,2,16,512]{3,2,1,0:T(8,128)(2,1)S(1)} %get-tuple-element.12), channel_id=1, source_target_pairs={{0,1},{1,2},{2,9},{3,10},{4,17},{5,18},{6,25},{7,26},{8,3},{9,4},{... | collective-permute-start | bytes 786440 | tf_op jit(solution)/shard_map/ppermute | solution.py:148
  7.7 31.0 %collective-permute-start.2 = (bf16[8,2,16,512]{3,2,1,0:T(8,128)(2,1)S(1)}, bf16[8,2,16,512]{3,2,1,0:T(8,128)(2,1)S(1)}, u32[]{:S(2)}, u32[]{:S(2)}) collective-permute-start(bf16[8,2,16,512]{3,2,1,0:T(8,128)(2,1)S(1)} %get-tuple-element.11), channel_id=1, source_target_pairs={{0,2},{1,3},{2,10},{3,11},{4,18},{5,19},{6,26},{7,27},{8,4},{9,5},... | collective-permute-start | bytes 786440 | tf_op jit(solution)/shard_map/ppermute | solution.py:148
  7.7 32.6 %collective-permute-start.3 = (bf16[8,2,16,512]{3,2,1,0:T(8,128)(2,1)S(1)}, bf16[8,2,16,512]{3,2,1,0:T(8,128)(2,1)S(1)}, u32[]{:S(2)}, u32[]{:S(2)}) collective-permute-start(bf16[8,2,16,512]{3,2,1,0:T(8,128)(2,1)S(1)} %get-tuple-element.10), channel_id=1, source_target_pairs={{0,3},{1,4},{2,11},{3,12},{4,19},{5,20},{6,27},{7,28},{8,5},{9,6},... | collective-permute-start | bytes 786440 | tf_op jit(solution)/shard_map/ppermute | solution.py:148
  13.4 27.6 %collective-permute-start.4 = (bf16[8,2,16,512]{3,2,1,0:T(8,128)(2,1)S(1)}, bf16[8,2,16,512]{3,2,1,0:T(8,128)(2,1)S(1)}, u32[]{:S(2)}, u32[]{:S(2)}) collective-permute-start(bf16[8,2,16,512]{3,2,1,0:T(8,128)(2,1)S(1)} %get-tuple-element.9), channel_id=1, source_target_pairs={{0,4},{1,5},{2,12},{3,13},{4,20},{5,21},{6,28},{7,29},{8,6},{9,7},... | collective-permute-start | bytes 786440 | tf_op jit(solution)/shard_map/ppermute | solution.py:148
  13.5 37.2 %collective-permute-start.5 = (bf16[8,2,16,512]{3,2,1,0:T(8,128)(2,1)S(1)}, bf16[8,2,16,512]{3,2,1,0:T(8,128)(2,1)S(1)}, u32[]{:S(2)}, u32[]{:S(2)}) collective-permute-start(bf16[8,2,16,512]{3,2,1,0:T(8,128)(2,1)S(1)} %get-tuple-element.8), channel_id=1, source_target_pairs={{0,5},{1,6},{2,13},{3,14},{4,21},{5,22},{6,29},{7,30},{8,7},{9,0},... | collective-permute-start | bytes 786440 | tf_op jit(solution)/shard_map/ppermute | solution.py:148
  33.6 22.7 %collective-permute-start.6 = (bf16[8,2,16,512]{3,2,1,0:T(8,128)(2,1)S(1)}, bf16[8,2,16,512]{3,2,1,0:T(8,128)(2,1)S(1)}, u32[]{:S(2)}, u32[]{:S(2)}) collective-permute-start(bf16[8,2,16,512]{3,2,1,0:T(8,128)(2,1)S(1)} %get-tuple-element.7), channel_id=1, source_target_pairs={{0,6},{1,7},{2,14},{3,15},{4,22},{5,23},{6,30},{7,31},{8,0},{9,1},... | collective-permute-start | bytes 786440 | tf_op jit(solution)/shard_map/ppermute | solution.py:148
  38.7 18.3 %collective-permute-start.7 = (bf16[8,2,16,512]{3,2,1,0:T(8,128)(2,1)S(1)}, bf16[8,2,16,512]{3,2,1,0:T(8,128)(2,1)S(1)}, u32[]{:S(2)}, u32[]{:S(2)}) collective-permute-start(bf16[8,2,16,512]{3,2,1,0:T(8,128)(2,1)S(1)} %get-tuple-element.6), channel_id=1, source_target_pairs={{0,7},{1,0},{2,15},{3,8},{4,23},{5,16},{6,31},{7,24},{8,1},{9,2},{... | collective-permute-start | bytes 786440 | tf_op jit(solution)/shard_map/ppermute | solution.py:148
  67.0 8.9 %copy-start.3 = (bf16[32,32]{1,0:T(8,128)(2,1)S(1)}, bf16[32,32]{1,0:T(8,128)(2,1)}, u32[]{:S(2)}) copy-start(bf16[32,32]{1,0:T(8,128)(2,1)} %param.7) | copy-start | bytes 6148
  67.0 8.9 %copy-start.4 = (bf16[32,32]{1,0:T(8,128)(2,1)S(1)}, bf16[32,32]{1,0:T(8,128)(2,1)}, u32[]{:S(2)}) copy-start(bf16[32,32]{1,0:T(8,128)(2,1)} %param.6) | copy-start | bytes 6148
  67.1 12.8 %collective-permute-start.8 = (bf16[64,4,1024]{2,0,1:T(8,128)(2,1)S(1)}, bf16[64,4,1024]{2,0,1:T(8,128)(2,1)S(1)}, u32[]{:S(2)}, u32[]{:S(2)}) collective-permute-start(bf16[64,4,1024]{2,0,1:T(8,128)(2,1)S(1)} %get-tuple-element.5), channel_id=1, source_target_pairs={{0,1},{1,2},{2,3},{3,4},{4,5},{5,6},{6,7},{8,9},{9,10},{10,11},{11... | collective-permute-start | bytes 1572872 | tf_op jit(solution)/shard_map/ppermute | solution.py:21
  74.0 11.4 %collective-permute-start.9 = (bf16[64,4,1024]{2,0,1:T(8,128)(2,1)S(1)}, bf16[64,4,1024]{2,0,1:T(8,128)(2,1)S(1)}, u32[]{:S(2)}, u32[]{:S(2)}) collective-permute-start(bf16[64,4,1024]{2,0,1:T(8,128)(2,1)S(1)} %get-tuple-element.4), channel_id=1, source_target_pairs={{1,0},{2,1},{3,2},{4,3},{5,4},{6,5},{7,6},{9,8},{10,9},{11,10},{12... | collective-permute-start | bytes 1572872 | tf_op jit(solution)/shard_map/ppermute | solution.py:24
  85.4 1.7 %copy-start = (bf16[64,24,1024]{2,0,1:T(8,128)(2,1)}, bf16[64,24,1024]{2,0,1:T(8,128)(2,1)S(1)}, u32[]{:S(2)}) copy-start(bf16[64,24,1024]{2,0,1:T(8,128)(2,1)S(1)} %constant_dynamic-update-slice_fusion) | copy-start | bytes 9437188
  87.3 15.9 %collective-permute-start.10 = (bf16[64,24,4]{2,0,1:T(8,128)(2,1)S(1)}, bf16[64,24,4]{2,0,1:T(8,128)(2,1)S(1)}, u32[]{:S(2)}, u32[]{:S(2)}) collective-permute-start(bf16[64,24,4]{2,0,1:T(8,128)(2,1)S(1)} %get-tuple-element.3), channel_id=1, source_target_pairs={{8,0},{16,8},{24,16},{9,1},{17,9},{25,17},{10,2},{18,10},{26,18},{... | collective-permute-start | bytes 36872 | tf_op jit(solution)/shard_map/ppermute | solution.py:24
  94.9 13.7 %collective-permute-start.11 = (bf16[64,24,4]{2,0,1:T(8,128)(2,1)S(1)}, bf16[64,24,4]{2,0,1:T(8,128)(2,1)S(1)}, u32[]{:S(2)}, u32[]{:S(2)}) collective-permute-start(bf16[64,24,4]{2,0,1:T(8,128)(2,1)S(1)} %get-tuple-element.2), channel_id=1, source_target_pairs={{0,8},{8,16},{16,24},{1,9},{9,17},{17,25},{2,10},{10,18},{18,26},{... | collective-permute-start | bytes 36872 | tf_op jit(solution)/shard_map/ppermute | solution.py:21
  103.2 5.4 %copy-start.1 = (bf16[64,24,4]{2,0,1:T(8,128)(2,1)}, bf16[64,24,4]{2,0,1:T(8,128)(2,1)S(1)}, u32[]{:S(2)}) copy-start(bf16[64,24,4]{2,0,1:T(8,128)(2,1)S(1)} %collective-permute-done.10) | copy-start | bytes 36868
  108.6 0.8 copy-start.2

commit v4 on v3

v4 whole, which is shorter than its diff:
```python
import functools

import jax
import jax.numpy as jnp
from jax import lax
from jax.experimental import pallas as pl
from jax.experimental.pallas import tpu as pltpu
from jax.sharding import PartitionSpec as P

RADIUS = 4
LANES = 128
PAIRS_PER_STEP = 2
FIELDS = 4


def pair_kernel(pre_ref, post_ref, *refs, tile_rows, tile_cols):
    del pre_ref, post_ref
    pp = PAIRS_PER_STEP
    sides = refs[: 4 * pp]
    band_ref, coh_ref, chg_ref, field_ref, rows_ref, stack_ref = refs[4 * pp :]
    window = 2 * RADIUS + 1
    padded_cols = tile_cols + LANES
    rows = pp * FIELDS * tile_rows
    blocks = tile_cols // LANES
    for p in range(pp):
        a_main, a_edge, b_main, b_edge = sides[4 * p : 4 * p + 4]
        pieces = [(c * a_main.shape[-1], a_main[c, 0], b_main[c, 0]) for c in range(a_main.shape[0])]
        pieces.append((tile_cols, a_edge[0], b_edge[0]))
        for at, a, b in pieces:
            width = a.shape[-1]
            pr = a[0].astype(jnp.float32)
            pi = a[1].astype(jnp.float32)
            qr = b[0].astype(jnp.float32)
            qi = b[1].astype(jnp.float32)
            fields = (pr * pr + pi * pi, qr * qr + qi * qi, pr * qr + pi * qi, pi * qr - pr * qi)
            for f, value in enumerate(fields):
                field_ref[f, :, pl.ds(at, width)] = value
        for f in range(FIELDS):
            acc = field_ref[f, pl.ds(0, tile_rows), :]
            for k in range(1, window):
                acc = acc + field_ref[f, pl.ds(k, tile_rows), :]
            at = (p * FIELDS + f) * tile_rows
            rows_ref[pl.ds(at, tile_rows), pl.ds(LANES, padded_cols)] = acc
            rows_ref[pl.ds(at, tile_rows), pl.ds(0, LANES)] = acc[:, padded_cols - LANES :]
    rowsum = rows_ref[...]
    high = rowsum.astype(jnp.bfloat16)
    low = (rowsum - high.astype(jnp.float32)).astype(jnp.bfloat16)
    width = 3 * LANES
    for j in range(blocks):
        stack_ref[pl.ds(j * rows, rows), pl.ds(0, width)] = high[:, j * LANES : j * LANES + width]
        stack_ref[pl.ds(j * rows, rows), pl.ds(width, width)] = low[:, j * LANES : j * LANES + width]
    sums = jnp.dot(stack_ref[...], band_ref[...], preferred_element_type=jnp.float32)
    means = sums / float(window * window)
    for j in range(blocks):
        for p in range(pp):
            base = j * rows + p * FIELDS * tile_rows
            pre_power = means[base : base + tile_rows] + 1e-06
            post_power = means[base + tile_rows : base + 2 * tile_rows] + 1e-06
            real_mean = means[base + 2 * tile_rows : base + 3 * tile_rows]
            imag_mean = means[base + 3 * tile_rows : base + 4 * tile_rows]
            coh = jnp.sqrt(real_mean * real_mean + imag_mean * imag_mean) / jnp.sqrt(
                pre_power * post_power
            )
            coh_ref[p, :, pl.ds(j * LANES, LANES)] = coh
            chg_ref[p, :, pl.ds(j * LANES, LANES)] = jnp.log(post_power / pre_power)


def pair_maps(main, edge, pre_ids, post_ids, tile_rows, tile_cols):
    count_pairs = pre_ids.shape[0]
    pp = PAIRS_PER_STEP
    blocks_per_tile, _, _, padded_rows, block_cols = main.shape
    width = 3 * LANES
    lane_in = jnp.arange(width)[:, None]
    lane_out = jnp.arange(LANES)[None, :]
    gap = lane_in - LANES - lane_out
    band = jnp.where((gap >= -RADIUS) & (gap <= RADIUS), 1.0, 0.0).astype(jnp.bfloat16)
    band = jnp.concatenate([band, band], axis=0)
    main_block = (blocks_per_tile, 1, 2, padded_rows, block_cols)
    edge_block = (1, 2, padded_rows, LANES)

    def specs(p, which):
        def main_index(i, pre, post):
            ids = pre if which == 0 else post
            return (0, ids[i * pp + p], 0, 0, 0)

        def edge_index(i, pre, post):
            ids = pre if which == 0 else post
            return (ids[i * pp + p], 0, 0, 0)

        return [pl.BlockSpec(main_block, main_index), pl.BlockSpec(edge_block, edge_index)]

    in_specs = []
    operands = []
    for p in range(pp):
        in_specs += specs(p, 0) + specs(p, 1)
        operands += [main, edge, main, edge]
    in_specs.append(pl.BlockSpec((2 * width, LANES), lambda i, pre, post: (0, 0)))
    operands.append(band)
    out_block = pl.BlockSpec((pp, tile_rows, tile_cols), lambda i, pre, post: (i, 0, 0))
    rows = pp * FIELDS * tile_rows
    blocks = tile_cols // LANES
    padded_cols = tile_cols + LANES
    grid_spec = pltpu.PrefetchScalarGridSpec(
        num_scalar_prefetch=2,
        grid=(count_pairs // pp,),
        in_specs=in_specs,
        out_specs=[out_block, out_block],
        scratch_shapes=[
            pltpu.VMEM((FIELDS, padded_rows, padded_cols), jnp.float32),
            pltpu.VMEM((rows, padded_cols + LANES), jnp.float32),
            pltpu.VMEM((blocks * rows, 2 * width), jnp.bfloat16),
        ],
    )
    out_shape = jax.ShapeDtypeStruct((count_pairs, tile_rows, tile_cols), jnp.float32)
    kernel = functools.partial(pair_kernel, tile_rows=tile_rows, tile_cols=tile_cols)
    return pl.pallas_call(
        kernel,
        grid_spec=grid_spec,
        out_shape=[out_shape, out_shape],
    )(pre_ids, post_ids, *operands)


def shards(stack, filt_re, filt_im, pre_ids, post_ids):
    count_acq = filt_re.shape[0]
    n_rows = lax.axis_size("ty")
    n_cols = lax.axis_size("tx")
    local_acq, _, height, local_cols = stack.shape
    tile_rows = height // n_rows
    blocks_per_tile = n_rows // n_cols
    tile_cols = local_cols * blocks_per_tile
    padded_rows = tile_rows + 2 * RADIUS

    me_col = lax.axis_index("tx")
    me_row = lax.axis_index("ty")
    x = jnp.pad(stack, ((0, 0), (0, 0), (RADIUS, RADIUS), (0, 0)))
    start = me_col * blocks_per_tile + me_row % blocks_per_tile
    received = []
    for m in range(n_rows):
        pairs = []
        for col in range(n_cols):
            for row in range(n_rows):
                to_row = (m + col * blocks_per_tile + row % blocks_per_tile) % n_rows
                pairs.append((col * n_rows + row, (row // blocks_per_tile) * n_rows + to_row))
        first = ((start + m) % n_rows) * tile_rows
        chunk = lax.dynamic_slice_in_dim(x, first, padded_rows, axis=2)
        received.append(lax.ppermute(chunk, ("tx", "ty"), pairs))
    received = jnp.stack(received, axis=0)
    source = jnp.arange(blocks_per_tile)[:, None] + blocks_per_tile * jnp.arange(n_cols)[None, :]
    order = (me_row - source) % n_rows
    x = jnp.take(received, order.reshape(-1), axis=0)
    x = x.reshape(blocks_per_tile, 2 * count_acq, padded_rows, local_cols)

    forward = [(i, i + 1) for i in range(n_cols - 1)]
    backward = [(target, source) for source, target in forward]
    left = lax.ppermute(x[blocks_per_tile - 1, :, :, local_cols - RADIUS :], "tx", forward)
    right = lax.ppermute(x[0, :, :, :RADIUS], "tx", backward)
    gap = jnp.zeros((2 * count_acq, padded_rows, LANES - 2 * RADIUS), x.dtype)
    edge = jnp.concatenate([right, gap, left], axis=2)

    mixing = jnp.stack([jnp.stack([filt_re, -filt_im], -1), jnp.stack([filt_im, filt_re], -1)], 1)
    mixing = mixing.reshape(2 * count_acq, 2 * count_acq)
    main = jnp.einsum("kc,bchw->bkhw", mixing, x, preferred_element_type=jnp.float32)
    main = main.astype(jnp.bfloat16).reshape(blocks_per_tile, count_acq, 2, padded_rows, local_cols)
    edge = jnp.einsum("kc,chw->khw", mixing, edge, preferred_element_type=jnp.float32)
    edge = edge.astype(jnp.bfloat16).reshape(count_acq, 2, padded_rows, LANES)
    return pair_maps(main, edge, pre_ids, post_ids, tile_rows, tile_cols)


def solution(mesh):
    in_specs = (P("tx", None, None, "ty"), P(), P(), P(), P())
    out_specs = (P(None, "ty", "tx"), P(None, "ty", "tx"))
    return jax.shard_map(shards, mesh=mesh, in_specs=in_specs, out_specs=out_specs, check_vma=False)
```

time: 143 us -> 145 us (1.014)
  starting transfers between devices: 53.7 us -> 60.4 us
  waiting for transfers between devices: 32.9 us -> 28.4 us
  local copies, waits for them, and re-layouts: 30.2 us -> 26.1 us
    ppermute x8, starting transfers between devices: 35.6 us -> 46.7 us  [shards(): received.append(lax.ppermute(chunk, ('tx', 'ty'), pairs))]
    ppermute x4 -> x2, waiting for transfers between devices: 19 us -> 10.4 us  [the longest x1 8.27 us: shards(): lax.ppermute(x[blocks_per_tile - 1, :, :, local_cols - RADIUS:], 'tx', fo...]
    dynamic_slice x0 -> x1, local copies, waits for them, and re-layouts: none -> 5.06 us  [shards(): chunk = lax.dynamic_slice_in_dim(x, first, padded_rows, axis=2)]
    concatenate x2 -> x1, local copies, waits for them, and re-layouts: 4.93 us -> 0.08 us  [shards(): edge = jnp.concatenate([right, gap, left], axis=2)]
    ppermute x4 -> x2, starting transfers between devices: 18.1 us -> 13.7 us  [the longest x1 11.6 us: shards(): right = lax.ppermute(x[0, :, :, :RADIUS], 'tx', backward)]
    ppermute x8, waiting for transfers between devices: 13.8 us -> 18 us  [shards(): received.append(lax.ppermute(chunk, ('tx', 'ty'), pairs))]
    transpose x1 -> x0, local copies, waits for them, and re-layouts: 3.49 us -> none  [shards(): x = jnp.transpose(x, (0, 2, 3, 4, 1, 5))]
    reshape x1 -> x0, local copies, waits for them, and re-layouts: 3.23 us -> none  [shards(): x = x.reshape(2 * count_acq, tile_rows, tile_cols)]
  transfers between devices with their start and end apart: 12 -> 10, of which waited for: 6 -> 4; matrix products, arithmetic and copies ran while one was open for 5% -> 13% of each run, Pallas kernels for 0% -> 0%
where the time goes in v4:
time: 145 us; the launch traced here: 144 us
  starting transfers between devices  60.4 us (42%)
  waiting for transfers between devices  28.4 us (20%)
  local copies, waits for them, and re-layouts  26.1 us (18%)
  Pallas kernels  23.9 us (16%)
  other arithmetic  2.33 us (2%)
  matrix products  1.75 us (1%)
    ppermute x8, starting transfers between devices, shards(): received.append(lax.ppermute(chunk, ('tx', 'ty'), pairs))  46.7 us
    pallas_call x1, Pallas kernels, pair_maps(): pl.pallas_call(kernel, grid_spec=grid_spec, out_shape=[out_shape, out_sha...  23.9 us
    ppermute x8, waiting for transfers between devices, shards(): received.append(lax.ppermute(chunk, ('tx', 'ty'), pairs))  18 us
    ppermute x1, starting transfers between devices, shards(): right = lax.ppermute(x[0, :, :, :RADIUS], 'tx', backward)  11.6 us
    unnamed x11, local copies, waits for them, and re-layouts  10.4 us
    ppermute x1, waiting for transfers between devices, shards(): lax.ppermute(x[blocks_per_tile - 1, :, :, local_cols - RADIUS:], 'tx', fo...  8.27 us
    dynamic_slice x1, local copies, waits for them, and re-layouts, shards(): chunk = lax.dynamic_slice_in_dim(x, first, padded_rows, axis=2)  5.06 us
    convert_element_type x1, local copies, waits for them, and re-layouts, shards(): main.astype(jnp.bfloat16)  3.39 us
  transfers between devices with their start and end apart: 10, of which 4 were waited for; matrix products, arithmetic and copies ran while one was open for 13% of the time, Pallas kernels for 0%

profile of v4, /device:TPU:21, one launch (start us, length us, event | category | flops | bytes accessed | tf_op | source)
XLA Modules:
  0.0 143.9 jit_solution(17511430672999849508)
XLA Ops:
  0.8 5.1 %pad_dynamic-slice_fusion = (bf16[8,2,24,512]{3,2,1,0:T(8,128)(2,1)S(1)}, bf16[8,2,24,512]{3,2,1,0:T(8,128)(2,1)S(1)}, bf16[8,2,24,512]{3,2,1,0:T(8,128)(2,1)S(1...) fusion(s32[]{:T(128)S(6)} %select_n.137, ...), kind=kLoop, calls=%fused_computation.7 | loop fusion | bytes 5242912 | tf_op jit(solution)/shard_map/dynamic_slice | solution.py:145
  5.8 4.5 %collective-permute-start = (bf16[8,2,24,512]{3,2,1,0:T(8,128)(2,1)}, bf16[8,2,24,512]{3,2,1,0:T(8,128)(2,1)}, u32[]{:S(2)}, u32[]{:S(2)}) collective-permute-start(bf16[8,2,24,512]{3,2,1,0:T(8,128)(2,1)} %get-tuple-element.11), channel_id=1, source_target_pairs={{0,0},{1,1},{2,8},{3,9},{4,16},{5,17},{6,24},{7,25},{8,2},{9,3},{1... | collective-permute-start | bytes 1179656 | tf_op jit(solution)/shard_map/ppermute | solution.py:146
  10.3 0.7 collective-permute-start.1
  11.0 2.4 %collective-permute-start.2 = (bf16[8,2,24,512]{3,2,1,0:T(8,128)(2,1)S(1)}, bf16[8,2,24,512]{3,2,1,0:T(8,128)(2,1)}, u32[]{:S(2)}, u32[]{:S(2)}) collective-permute-start(bf16[8,2,24,512]{3,2,1,0:T(8,128)(2,1)S(1)} %get-tuple-element.6), channel_id=1, source_target_pairs={{0,2},{1,3},{2,10},{3,11},{4,18},{5,19},{6,26},{7,27},{8,4},{9,5},... | collective-permute-start | bytes 1179656 | tf_op jit(solution)/shard_map/ppermute | solution.py:146
  13.4 3.4 %collective-permute-start.3 = (bf16[8,2,24,512]{3,2,1,0:T(8,128)(2,1)S(1)}, bf16[8,2,24,512]{3,2,1,0:T(8,128)(2,1)}, u32[]{:S(2)}, u32[]{:S(2)}) collective-permute-start(bf16[8,2,24,512]{3,2,1,0:T(8,128)(2,1)S(1)} %get-tuple-element.7), channel_id=1, source_target_pairs={{0,3},{1,4},{2,11},{3,12},{4,19},{5,20},{6,27},{7,28},{8,5},{9,6},... | collective-permute-start | bytes 1179656 | tf_op jit(solution)/shard_map/ppermute | solution.py:146
  17.2 0.5 copy.11
  17.7 0.8 reshape.135
  18.5 0.8 reshape.134
  19.6 0.7 pad_maximum_fusion.refs_8_
  20.3 28.9 %collective-permute-start.5 = (bf16[8,2,24,512]{3,2,1,0:T(8,128)(2,1)S(1)}, bf16[8,2,24,512]{3,2,1,0:T(8,128)(2,1)S(1)}, u32[]{:S(2)}, u32[]{:S(2)}) collective-permute-start(bf16[8,2,24,512]{3,2,1,0:T(8,128)(2,1)S(1)} %get-tuple-element.9), channel_id=1, source_target_pairs={{0,5},{1,6},{2,13},{3,14},{4,21},{5,22},{6,29},{7,30},{8,7},{9,0},... | collective-permute-start | bytes 1179656 | tf_op jit(solution)/shard_map/ppermute | solution.py:146
  49.1 1.8 %bitcast_dynamic-update-slice_fusion.7 = bf16[8,8,2,24,512]{4,3,2,1,0:T(8,128)(2,1)} fusion(bf16[8,2,24,512]{3,2,1,0:T(8,128)(2,1)} %collective-permute-done), kind=kLoop, calls=%fused_computation.28 | loop fusion | bytes 786432
  50.9 6.1 %collective-permute-start.6 = (bf16[8,2,24,512]{3,2,1,0:T(8,128)(2,1)S(1)}, bf16[8,2,24,512]{3,2,1,0:T(8,128)(2,1)S(1)}, u32[]{:S(2)}, u32[]{:S(2)}) collective-permute-start(bf16[8,2,24,512]{3,2,1,0:T(8,128)(2,1)S(1)} %get-tuple-element.10), channel_id=1, source_target_pairs={{0,6},{1,7},{2,14},{3,15},{4,22},{5,23},{6,30},{7,31},{8,0},{9,1},... | collective-permute-start | bytes 1179656 | tf_op jit(solution)/shard_map/ppermute | solution.py:146
  57.0 1.8 %bitcast_dynamic-update-slice_fusion.6 = bf16[8,8,2,24,512]{4,3,2,1,0:T(8,128)(2,1)} fusion(bf16[8,8,2,24,512]{4,3,2,1,0:T(8,128)(2,1)} %bitcast_dynamic-update-slice_fusion.7, bf16[8,2,24,512]{3,2,1,0:T(8,128)(2,1)} %collective-permute-done.1), kind=kLoop, calls=%fused_computation.27 | loop fusion | bytes 786432
  58.8 0.9 collective-permute-start.7
  59.6 1.8 %bitcast_dynamic-update-slice_fusion.5 = bf16[8,8,2,24,512]{4,3,2,1,0:T(8,128)(2,1)} fusion(bf16[8,8,2,24,512]{4,3,2,1,0:T(8,128)(2,1)} %bitcast_dynamic-update-slice_fusion.6, bf16[8,2,24,512]{3,2,1,0:T(8,128)(2,1)} %collective-permute-done.2), kind=kLoop, calls=%fused_computation.26 | loop fusion | bytes 786432
  61.4 1.8 %bitcast_dynamic-update-slice_fusion.4 = bf16[8,8,2,24,512]{4,3,2,1,0:T(8,128)(2,1)} fusion(bf16[8,8,2,24,512]{4,3,2,1,0:T(8,128)(2,1)} %bitcast_dynamic-update-slice_fusion.5, bf16[8,2,24,512]{3,2,1,0:T(8,128)(2,1)} %collective-permute-done.3), kind=kLoop, calls=%fused_computation.25 | loop fusion | bytes 786432
  63.2 1.8 %bitcast_dynamic-update-slice_fusion.3 = bf16[8,8,2,24,512]{4,3,2,1,0:T(8,128)(2,1)} fusion(bf16[8,8,2,24,512]{4,3,2,1,0:T(8,128)(2,1)} %bitcast_dynamic-update-slice_fusion.4, bf16[8,2,24,512]{3,2,1,0:T(8,128)(2,1)} %collective-permute-done.4), kind=kLoop, calls=%fused_computation.24 | loop fusion | bytes 786432
  65.0 10.3 %collective-permute-done.5 = bf16[8,2,24,512]{3,2,1,0:T(8,128)(2,1)S(1)} collective-permute-done((bf16[8,2,24,512]{3,2,1,0:T(8,128)(2,1)S(1)}, bf16[8,2,24,512]{3,2,1,0:T(8,128)(2,1)S(1)}, u32[]{:S(2)}, u32[]{:S(2)}) %collective-permute-start.5) | collective-permute-done | bytes 393248 | tf_op jit(solution)/shard_map/ppermute | solution.py:146
  75.3 0.8 bitcast_dynamic-update-slice_fusion.2
  76.1 7.6 %collective-permute-done.6 = bf16[8,2,24,512]{3,2,1,0:T(8,128)(2,1)S(1)} collective-permute-done((bf16[8,2,24,512]{3,2,1,0:T(8,128)(2,1)S(1)}, bf16[8,2,24,512]{3,2,1,0:T(8,128)(2,1)S(1)}, u32[]{:S(2)}, u32[]{:S(2)}) %collective-permute-start.6) | collective-permute-done | bytes 393248 | tf_op jit(solution)/shard_map/ppermute | solution.py:146
  83.7 0.8 bitcast_dynamic-update-slice_fusion.1
  84.5 0.8 bitcast_dynamic-update-slice_fusion
  85.3 2.6 %gather_fusion = bf16[8,8,2,24,512]{4,3,2,1,0:T(8,128)(2,1)S(1)} fusion(bf16[8,8,2,24,512]{4,3,2,1,0:T(8,128)(2,1)} %bitcast_dynamic-update-slice_fusion, s32[1024]{0:T(1024)S(1)} %pad_clamp_fusion), kind=kCustom, calls=%fused_computation | custom fusion | bytes 6291488 | tf_op jit(solution)/shard_map/jit(_take)/gather | solution.py:150
  88.3 1.1 copy_select_fusion
  89.6 11.6 %collective-permute-start.8 = (bf16[64,24,4]{2,0,1:T(8,128)(2,1)S(1)}, bf16[64,24,4]{2,0,1:T(8,128)(2,1)S(1)}, u32[]{:S(2)}, u32[]{:S(2)}) collective-permute-start(bf16[64,24,4]{2,0,1:T(8,128)(2,1)S(1)} %get-tuple-element.2), channel_id=1, source_target_pairs={{8,0},{16,8},{24,16},{9,1},{17,9},{25,17},{10,2},{18,10},{26,18},{... | collective-permute-start | bytes 36872 | tf_op jit(solution)/shard_map/ppermute | solution.py:156
  101.2 2.1 %collective-permute-start.9 = (bf16[64,24,4]{2,0,1:T(8,128)(2,1)S(1)}, bf16[64,24,4]{2,0,1:T(8,128)(2,1)S(1)}, u32[]{:S(2)}, u32[]{:S(2)}) collective-permute-start(bf16[64,24,4]{2,0,1:T(8,128)(2,1)S(1)} %get-tuple-element.3), channel_id=1, source_target_pairs={{0,8},{8,16},{16,24},{1,9},{9,17},{17,25},{2,10},{10,18},{18,26},{... | collective-permute-start | bytes 36872 | tf_op jit(solution)/shard_map/ppermute | solution.py:155
  103.3 1.3 convert_bitcast_fusion
  104.7 3.4 %copy.13 = bf16[2,64,24,512]{3,2,1,0:T(8,128)(2,1)} copy(bf16[2,64,24,512]{3,1,2,0:T(8,128)(2,1)S(1)} %convert_bitcast_fusion) | data formatting | bytes 6291456 | tf_op jit(solution)/shard_map/convert_element_type | solution.py:163
  108.0 2.1 %collective-permute-done.8 = bf16[64,24,4]{2,0,1:T(8,128)(2,1)S(1)} collective-permute-done((bf16[64,24,4]{2,0,1:T(8,128)(2,1)S(1)}, bf16[64,24,4]{2,0,1:T(8,128)(2,1)S(1)}, u32[]{:S(2)}, u32[]{:S(2)}) %collective-permute-start.8) | collective-permute-done | bytes 12320 | tf_op jit(solution)/shard_map/ppermute | solution.py:156
  110.2 8.3 %collective-permute-done.9 = bf16[64,24,4]{2,0,1:T(8,128)(2,1)S(1)} collective-permute-done((bf16[64,24,4]{2,0,1:T(8,128)(2,1)S(1)}, bf16[64,24,4]{2,0,1:T(8,128)(2,1)S(1)}, u32[]{:S(2)}, u32[]{:S(2)}) %collective-permute-start.9) | collective-permute-done | bytes 12320 | tf_op jit(solution)/shard_map/ppermute | solution.py:155
  118.9 1.0 copy.15
  119.9 23.9 %shard_map.68 = (f32[32,16,1024]{2,1,0:T(8,128)}, f32[32,16,1024]{2,1,0:T(8,128)}) custom-call(s32[32]{0:T(128)} %pre_ref.1, s32[32]{0:T(128)} %post_ref.1, bf16[2,32,2,24,512]{4,3,2,1,0:T(8,128)(2,1)} %bitcast.44, bf16[32,2,24,128]{3,2,1,0:T(8,128)(2,1)} %bitcast.50, bf16[2,32,2,24,512]{4,3,2,1,0:T(8,128)(2,1)} %bitcast.45, ...), custom_call_target="tpu_custom_call" | custom-call | tf_op jit(solution)/shard_map/pallas_call | solution.py:116
  (30 shorter events, 1.7 us)
Async XLA Ops:
  0.6 16.3 %copy-start = (bf16[32,32]{1,0:T(8,128)(2,1)S(1)}, bf16[32,32]{1,0:T(8,128)(2,1)}, u32[]{:S(2)}) copy-start(bf16[32,32]{1,0:T(8,128)(2,1)} %param.7) | copy-start | bytes 6148
  0.6 16.5 %copy-start.1 = (bf16[32,32]{1,0:T(8,128)(2,1)S(1)}, bf16[32,32]{1,0:T(8,128)(2,1)}, u32[]{:S(2)}) copy-start(bf16[32,32]{1,0:T(8,128)(2,1)} %param.6) | copy-start | bytes 6148
  5.8 14.4 %collective-permute-start = (bf16[8,2,24,512]{3,2,1,0:T(8,128)(2,1)}, bf16[8,2,24,512]{3,2,1,0:T(8,128)(2,1)}, u32[]{:S(2)}, u32[]{:S(2)}) collective-permute-start(bf16[8,2,24,512]{3,2,1,0:T(8,128)(2,1)} %get-tuple-element.11), channel_id=1, source_target_pairs={{0,0},{1,1},{2,8},{3,9},{4,16},{5,17},{6,24},{7,25},{8,2},{9,3},{1... | collective-permute-start | bytes 1179656 | tf_op jit(solution)/shard_map/ppermute | solution.py:146
  10.3 40.6 %collective-permute-start.1 = (bf16[8,2,24,512]{3,2,1,0:T(8,128)(2,1)S(1)}, bf16[8,2,24,512]{3,2,1,0:T(8,128)(2,1)}, u32[]{:S(2)}, u32[]{:S(2)}) collective-permute-start(bf16[8,2,24,512]{3,2,1,0:T(8,128)(2,1)S(1)} %get-tuple-element.5), channel_id=1, source_target_pairs={{0,1},{1,2},{2,9},{3,10},{4,17},{5,18},{6,25},{7,26},{8,3},{9,4},{... | collective-permute-start | bytes 1179656 | tf_op jit(solution)/shard_map/ppermute | solution.py:146
  11.0 47.8 %collective-permute-start.2 = (bf16[8,2,24,512]{3,2,1,0:T(8,128)(2,1)S(1)}, bf16[8,2,24,512]{3,2,1,0:T(8,128)(2,1)}, u32[]{:S(2)}, u32[]{:S(2)}) collective-permute-start(bf16[8,2,24,512]{3,2,1,0:T(8,128)(2,1)S(1)} %get-tuple-element.6), channel_id=1, source_target_pairs={{0,2},{1,3},{2,10},{3,11},{4,18},{5,19},{6,26},{7,27},{8,4},{9,5},... | collective-permute-start | bytes 1179656 | tf_op jit(solution)/shard_map/ppermute | solution.py:146
  13.4 48.0 %collective-permute-start.3 = (bf16[8,2,24,512]{3,2,1,0:T(8,128)(2,1)S(1)}, bf16[8,2,24,512]{3,2,1,0:T(8,128)(2,1)}, u32[]{:S(2)}, u32[]{:S(2)}) collective-permute-start(bf16[8,2,24,512]{3,2,1,0:T(8,128)(2,1)S(1)} %get-tuple-element.7), channel_id=1, source_target_pairs={{0,3},{1,4},{2,11},{3,12},{4,19},{5,20},{6,27},{7,28},{8,5},{9,6},... | collective-permute-start | bytes 1179656 | tf_op jit(solution)/shard_map/ppermute | solution.py:146
  16.7 46.5 %collective-permute-start.4 = (bf16[8,2,24,512]{3,2,1,0:T(8,128)(2,1)S(1)}, bf16[8,2,24,512]{3,2,1,0:T(8,128)(2,1)}, u32[]{:S(2)}, u32[]{:S(2)}) collective-permute-start(bf16[8,2,24,512]{3,2,1,0:T(8,128)(2,1)S(1)} %get-tuple-element.8), channel_id=1, source_target_pairs={{0,4},{1,5},{2,12},{3,13},{4,20},{5,21},{6,28},{7,29},{8,6},{9,7},... | collective-permute-start | bytes 1179656 | tf_op jit(solution)/shard_map/ppermute | solution.py:146
  20.3 55.0 %collective-permute-start.5 = (bf16[8,2,24,512]{3,2,1,0:T(8,128)(2,1)S(1)}, bf16[8,2,24,512]{3,2,1,0:T(8,128)(2,1)S(1)}, u32[]{:S(2)}, u32[]{:S(2)}) collective-permute-start(bf16[8,2,24,512]{3,2,1,0:T(8,128)(2,1)S(1)} %get-tuple-element.9), channel_id=1, source_target_pairs={{0,5},{1,6},{2,13},{3,14},{4,21},{5,22},{6,29},{7,30},{8,7},{9,0},... | collective-permute-start | bytes 1179656 | tf_op jit(solution)/shard_map/ppermute | solution.py:146
  50.9 32.8 %collective-permute-start.6 = (bf16[8,2,24,512]{3,2,1,0:T(8,128)(2,1)S(1)}, bf16[8,2,24,512]{3,2,1,0:T(8,128)(2,1)S(1)}, u32[]{:S(2)}, u32[]{:S(2)}) collective-permute-start(bf16[8,2,24,512]{3,2,1,0:T(8,128)(2,1)S(1)} %get-tuple-element.10), channel_id=1, source_target_pairs={{0,6},{1,7},{2,14},{3,15},{4,22},{5,23},{6,30},{7,31},{8,0},{9,1},... | collective-permute-start | bytes 1179656 | tf_op jit(solution)/shard_map/ppermute | solution.py:146
  58.8 25.7 %collective-permute-start.7 = (bf16[8,2,24,512]{3,2,1,0:T(8,128)(2,1)S(1)}, bf16[8,2,24,512]{3,2,1,0:T(8,128)(2,1)S(1)}, u32[]{:S(2)}, u32[]{:S(2)}) collective-permute-start(bf16[8,2,24,512]{3,2,1,0:T(8,128)(2,1)S(1)} %get-tuple-element.4), channel_id=1, source_target_pairs={{0,7},{1,0},{2,15},{3,8},{4,23},{5,16},{6,31},{7,24},{8,1},{9,2},{... | collective-permute-start | bytes 1179656 | tf_op jit(solution)/shard_map/ppermute | solution.py:146
  89.6 20.6 %collective-permute-start.8 = (bf16[64,24,4]{2,0,1:T(8,128)(2,1)S(1)}, bf16[64,24,4]{2,0,1:T(8,128)(2,1)S(1)}, u32[]{:S(2)}, u32[]{:S(2)}) collective-permute-start(bf16[64,24,4]{2,0,1:T(8,128)(2,1)S(1)} %get-tuple-element.2), channel_id=1, source_target_pairs={{8,0},{16,8},{24,16},{9,1},{17,9},{25,17},{10,2},{18,10},{26,18},{... | collective-permute-start | bytes 36872 | tf_op jit(solution)/shard_map/ppermute | solution.py:156
  101.2 17.2 %collective-permute-start.9 = (bf16[64,24,4]{2,0,1:T(8,128)(2,1)S(1)}, bf16[64,24,4]{2,0,1:T(8,128)(2,1)S(1)}, u32[]{:S(2)}, u32[]{:S(2)}) collective-permute-start(bf16[64,24,4]{2,0,1:T(8,128)(2,1)S(1)} %get-tuple-element.3), channel_id=1, source_target_pairs={{0,8},{8,16},{16,24},{1,9},{9,17},{17,25},{2,10},{10,18},{18,26},{... | collective-permute-start | bytes 36872 | tf_op jit(solution)/shard_map/ppermute | solution.py:155

commit v5 on v4

--- a/solution.py
+++ b/solution.py
@@ -9,7 +9,7 @@
 
 RADIUS = 4
 LANES = 128
-PAIRS_PER_STEP = 2
+PAIRS_PER_STEP = 4
 FIELDS = 4
 
 

time: 145 us -> 145 us (level)
  no operation moved by 1% of the time
where the time goes in v5:
time: 145 us; the launch traced here: 144 us
  starting transfers between devices  60.4 us (42%)
  waiting for transfers between devices  28.4 us (20%)
  local copies, waits for them, and re-layouts  26.1 us (18%)
  Pallas kernels  23.9 us (16%)
  other arithmetic  2.33 us (2%)
  matrix products  1.75 us (1%)
    ppermute x8, starting transfers between devices, shards(): received.append(lax.ppermute(chunk, ('tx', 'ty'), pairs))  46.7 us
    pallas_call x1, Pallas kernels, pair_maps(): pl.pallas_call(kernel, grid_spec=grid_spec, out_shape=[out_shape, out_sha...  23.9 us
    ppermute x8, waiting for transfers between devices, shards(): received.append(lax.ppermute(chunk, ('tx', 'ty'), pairs))  18 us
    ppermute x1, starting transfers between devices, shards(): right = lax.ppermute(x[0, :, :, :RADIUS], 'tx', backward)  11.6 us
    unnamed x11, local copies, waits for them, and re-layouts  10.4 us
    ppermute x1, waiting for transfers between devices, shards(): lax.ppermute(x[blocks_per_tile - 1, :, :, local_cols - RADIUS:], 'tx', fo...  8.27 us
    dynamic_slice x1, local copies, waits for them, and re-layouts, shards(): chunk = lax.dynamic_slice_in_dim(x, first, padded_rows, axis=2)  5.06 us
    convert_element_type x1, local copies, waits for them, and re-layouts, shards(): main.astype(jnp.bfloat16)  3.39 us
  transfers between devices with their start and end apart: 10, of which 4 were waited for; matrix products, arithmetic and copies ran while one was open for 13% of the time, Pallas kernels for 0%

profile of v5, /device:TPU:21, one launch (start us, length us, event | category | flops | bytes accessed | tf_op | source)
XLA Modules:
  0.0 143.9 jit_solution(3547809183541305121)
XLA Ops:
  0.8 5.1 %pad_dynamic-slice_fusion = (bf16[8,2,24,512]{3,2,1,0:T(8,128)(2,1)S(1)}, bf16[8,2,24,512]{3,2,1,0:T(8,128)(2,1)S(1)}, bf16[8,2,24,512]{3,2,1,0:T(8,128)(2,1)S(1...) fusion(s32[]{:T(128)S(6)} %select_n.137, ...), kind=kLoop, calls=%fused_computation.7 | loop fusion | bytes 5242912 | tf_op jit(solution)/shard_map/dynamic_slice | solution.py:145
  5.8 4.5 %collective-permute-start = (bf16[8,2,24,512]{3,2,1,0:T(8,128)(2,1)}, bf16[8,2,24,512]{3,2,1,0:T(8,128)(2,1)}, u32[]{:S(2)}, u32[]{:S(2)}) collective-permute-start(bf16[8,2,24,512]{3,2,1,0:T(8,128)(2,1)} %get-tuple-element.11), channel_id=1, source_target_pairs={{0,0},{1,1},{2,8},{3,9},{4,16},{5,17},{6,24},{7,25},{8,2},{9,3},{1... | collective-permute-start | bytes 1179656 | tf_op jit(solution)/shard_map/ppermute | solution.py:146
  10.3 0.7 collective-permute-start.1
  11.0 2.4 %collective-permute-start.2 = (bf16[8,2,24,512]{3,2,1,0:T(8,128)(2,1)S(1)}, bf16[8,2,24,512]{3,2,1,0:T(8,128)(2,1)}, u32[]{:S(2)}, u32[]{:S(2)}) collective-permute-start(bf16[8,2,24,512]{3,2,1,0:T(8,128)(2,1)S(1)} %get-tuple-element.6), channel_id=1, source_target_pairs={{0,2},{1,3},{2,10},{3,11},{4,18},{5,19},{6,26},{7,27},{8,4},{9,5},... | collective-permute-start | bytes 1179656 | tf_op jit(solution)/shard_map/ppermute | solution.py:146
  13.4 3.4 %collective-permute-start.3 = (bf16[8,2,24,512]{3,2,1,0:T(8,128)(2,1)S(1)}, bf16[8,2,24,512]{3,2,1,0:T(8,128)(2,1)}, u32[]{:S(2)}, u32[]{:S(2)}) collective-permute-start(bf16[8,2,24,512]{3,2,1,0:T(8,128)(2,1)S(1)} %get-tuple-element.7), channel_id=1, source_target_pairs={{0,3},{1,4},{2,11},{3,12},{4,19},{5,20},{6,27},{7,28},{8,5},{9,6},... | collective-permute-start | bytes 1179656 | tf_op jit(solution)/shard_map/ppermute | solution.py:146
  17.2 0.5 copy.11
  17.7 0.8 reshape.135
  18.5 0.8 reshape.134
  19.6 0.7 pad_maximum_fusion.refs_16_
  20.3 28.9 %collective-permute-start.5 = (bf16[8,2,24,512]{3,2,1,0:T(8,128)(2,1)S(1)}, bf16[8,2,24,512]{3,2,1,0:T(8,128)(2,1)S(1)}, u32[]{:S(2)}, u32[]{:S(2)}) collective-permute-start(bf16[8,2,24,512]{3,2,1,0:T(8,128)(2,1)S(1)} %get-tuple-element.9), channel_id=1, source_target_pairs={{0,5},{1,6},{2,13},{3,14},{4,21},{5,22},{6,29},{7,30},{8,7},{9,0},... | collective-permute-start | bytes 1179656 | tf_op jit(solution)/shard_map/ppermute | solution.py:146
  49.1 1.8 %bitcast_dynamic-update-slice_fusion.7 = bf16[8,8,2,24,512]{4,3,2,1,0:T(8,128)(2,1)} fusion(bf16[8,2,24,512]{3,2,1,0:T(8,128)(2,1)} %collective-permute-done), kind=kLoop, calls=%fused_computation.28 | loop fusion | bytes 786432
  50.9 6.1 %collective-permute-start.6 = (bf16[8,2,24,512]{3,2,1,0:T(8,128)(2,1)S(1)}, bf16[8,2,24,512]{3,2,1,0:T(8,128)(2,1)S(1)}, u32[]{:S(2)}, u32[]{:S(2)}) collective-permute-start(bf16[8,2,24,512]{3,2,1,0:T(8,128)(2,1)S(1)} %get-tuple-element.10), channel_id=1, source_target_pairs={{0,6},{1,7},{2,14},{3,15},{4,22},{5,23},{6,30},{7,31},{8,0},{9,1},... | collective-permute-start | bytes 1179656 | tf_op jit(solution)/shard_map/ppermute | solution.py:146
  57.0 1.8 %bitcast_dynamic-update-slice_fusion.6 = bf16[8,8,2,24,512]{4,3,2,1,0:T(8,128)(2,1)} fusion(bf16[8,8,2,24,512]{4,3,2,1,0:T(8,128)(2,1)} %bitcast_dynamic-update-slice_fusion.7, bf16[8,2,24,512]{3,2,1,0:T(8,128)(2,1)} %collective-permute-done.1), kind=kLoop, calls=%fused_computation.27 | loop fusion | bytes 786432
  58.8 0.9 collective-permute-start.7
  59.6 1.8 %bitcast_dynamic-update-slice_fusion.5 = bf16[8,8,2,24,512]{4,3,2,1,0:T(8,128)(2,1)} fusion(bf16[8,8,2,24,512]{4,3,2,1,0:T(8,128)(2,1)} %bitcast_dynamic-update-slice_fusion.6, bf16[8,2,24,512]{3,2,1,0:T(8,128)(2,1)} %collective-permute-done.2), kind=kLoop, calls=%fused_computation.26 | loop fusion | bytes 786432
  61.4 1.8 %bitcast_dynamic-update-slice_fusion.4 = bf16[8,8,2,24,512]{4,3,2,1,0:T(8,128)(2,1)} fusion(bf16[8,8,2,24,512]{4,3,2,1,0:T(8,128)(2,1)} %bitcast_dynamic-update-slice_fusion.5, bf16[8,2,24,512]{3,2,1,0:T(8,128)(2,1)} %collective-permute-done.3), kind=kLoop, calls=%fused_computation.25 | loop fusion | bytes 786432
  63.2 1.8 %bitcast_dynamic-update-slice_fusion.3 = bf16[8,8,2,24,512]{4,3,2,1,0:T(8,128)(2,1)} fusion(bf16[8,8,2,24,512]{4,3,2,1,0:T(8,128)(2,1)} %bitcast_dynamic-update-slice_fusion.4, bf16[8,2,24,512]{3,2,1,0:T(8,128)(2,1)} %collective-permute-done.4), kind=kLoop, calls=%fused_computation.24 | loop fusion | bytes 786432
  65.0 10.3 %collective-permute-done.5 = bf16[8,2,24,512]{3,2,1,0:T(8,128)(2,1)S(1)} collective-permute-done((bf16[8,2,24,512]{3,2,1,0:T(8,128)(2,1)S(1)}, bf16[8,2,24,512]{3,2,1,0:T(8,128)(2,1)S(1)}, u32[]{:S(2)}, u32[]{:S(2)}) %collective-permute-start.5) | collective-permute-done | bytes 393248 | tf_op jit(solution)/shard_map/ppermute | solution.py:146
  75.3 0.8 bitcast_dynamic-update-slice_fusion.2
  76.1 7.6 %collective-permute-done.6 = bf16[8,2,24,512]{3,2,1,0:T(8,128)(2,1)S(1)} collective-permute-done((bf16[8,2,24,512]{3,2,1,0:T(8,128)(2,1)S(1)}, bf16[8,2,24,512]{3,2,1,0:T(8,128)(2,1)S(1)}, u32[]{:S(2)}, u32[]{:S(2)}) %collective-permute-start.6) | collective-permute-done | bytes 393248 | tf_op jit(solution)/shard_map/ppermute | solution.py:146
  83.7 0.8 bitcast_dynamic-update-slice_fusion.1
  84.5 0.8 bitcast_dynamic-update-slice_fusion
  85.3 2.6 %gather_fusion = bf16[8,8,2,24,512]{4,3,2,1,0:T(8,128)(2,1)S(1)} fusion(bf16[8,8,2,24,512]{4,3,2,1,0:T(8,128)(2,1)} %bitcast_dynamic-update-slice_fusion, s32[1024]{0:T(1024)S(1)} %pad_clamp_fusion), kind=kCustom, calls=%fused_computation | custom fusion | bytes 6291488 | tf_op jit(solution)/shard_map/jit(_take)/gather | solution.py:150
  88.3 1.1 copy_select_fusion
  89.6 11.6 %collective-permute-start.8 = (bf16[64,24,4]{2,0,1:T(8,128)(2,1)S(1)}, bf16[64,24,4]{2,0,1:T(8,128)(2,1)S(1)}, u32[]{:S(2)}, u32[]{:S(2)}) collective-permute-start(bf16[64,24,4]{2,0,1:T(8,128)(2,1)S(1)} %get-tuple-element.2), channel_id=1, source_target_pairs={{8,0},{16,8},{24,16},{9,1},{17,9},{25,17},{10,2},{18,10},{26,18},{... | collective-permute-start | bytes 36872 | tf_op jit(solution)/shard_map/ppermute | solution.py:156
  101.2 2.1 %collective-permute-start.9 = (bf16[64,24,4]{2,0,1:T(8,128)(2,1)S(1)}, bf16[64,24,4]{2,0,1:T(8,128)(2,1)S(1)}, u32[]{:S(2)}, u32[]{:S(2)}) collective-permute-start(bf16[64,24,4]{2,0,1:T(8,128)(2,1)S(1)} %get-tuple-element.3), channel_id=1, source_target_pairs={{0,8},{8,16},{16,24},{1,9},{9,17},{17,25},{2,10},{10,18},{18,26},{... | collective-permute-start | bytes 36872 | tf_op jit(solution)/shard_map/ppermute | solution.py:155
  103.3 1.3 convert_bitcast_fusion
  104.7 3.4 %copy.13 = bf16[2,64,24,512]{3,2,1,0:T(8,128)(2,1)} copy(bf16[2,64,24,512]{3,1,2,0:T(8,128)(2,1)S(1)} %convert_bitcast_fusion) | data formatting | bytes 6291456 | tf_op jit(solution)/shard_map/convert_element_type | solution.py:163
  108.0 2.1 %collective-permute-done.8 = bf16[64,24,4]{2,0,1:T(8,128)(2,1)S(1)} collective-permute-done((bf16[64,24,4]{2,0,1:T(8,128)(2,1)S(1)}, bf16[64,24,4]{2,0,1:T(8,128)(2,1)S(1)}, u32[]{:S(2)}, u32[]{:S(2)}) %collective-permute-start.8) | collective-permute-done | bytes 12320 | tf_op jit(solution)/shard_map/ppermute | solution.py:156
  110.2 8.3 %collective-permute-done.9 = bf16[64,24,4]{2,0,1:T(8,128)(2,1)S(1)} collective-permute-done((bf16[64,24,4]{2,0,1:T(8,128)(2,1)S(1)}, bf16[64,24,4]{2,0,1:T(8,128)(2,1)S(1)}, u32[]{:S(2)}, u32[]{:S(2)}) %collective-permute-start.9) | collective-permute-done | bytes 12320 | tf_op jit(solution)/shard_map/ppermute | solution.py:155
  118.9 1.0 copy.15
  119.9 23.9 %shard_map.68 = (f32[32,16,1024]{2,1,0:T(8,128)}, f32[32,16,1024]{2,1,0:T(8,128)}) custom-call(s32[32]{0:T(128)} %pre_ref.1, s32[32]{0:T(128)} %post_ref.1, bf16[2,32,2,24,512]{4,3,2,1,0:T(8,128)(2,1)} %bitcast.44, bf16[32,2,24,128]{3,2,1,0:T(8,128)(2,1)} %bitcast.52, bf16[2,32,2,24,512]{4,3,2,1,0:T(8,128)(2,1)} %bitcast.45, ...), custom_call_target="tpu_custom_call" | custom-call | tf_op jit(solution)/shard_map/pallas_call | solution.py:116
  (30 shorter events, 1.7 us)
Async XLA Ops:
  0.6 16.3 %copy-start = (bf16[32,32]{1,0:T(8,128)(2,1)S(1)}, bf16[32,32]{1,0:T(8,128)(2,1)}, u32[]{:S(2)}) copy-start(bf16[32,32]{1,0:T(8,128)(2,1)} %param.7) | copy-start | bytes 6148
  0.6 16.5 %copy-start.1 = (bf16[32,32]{1,0:T(8,128)(2,1)S(1)}, bf16[32,32]{1,0:T(8,128)(2,1)}, u32[]{:S(2)}) copy-start(bf16[32,32]{1,0:T(8,128)(2,1)} %param.6) | copy-start | bytes 6148
  5.8 14.4 %collective-permute-start = (bf16[8,2,24,512]{3,2,1,0:T(8,128)(2,1)}, bf16[8,2,24,512]{3,2,1,0:T(8,128)(2,1)}, u32[]{:S(2)}, u32[]{:S(2)}) collective-permute-start(bf16[8,2,24,512]{3,2,1,0:T(8,128)(2,1)} %get-tuple-element.11), channel_id=1, source_target_pairs={{0,0},{1,1},{2,8},{3,9},{4,16},{5,17},{6,24},{7,25},{8,2},{9,3},{1... | collective-permute-start | bytes 1179656 | tf_op jit(solution)/shard_map/ppermute | solution.py:146
  10.3 40.6 %collective-permute-start.1 = (bf16[8,2,24,512]{3,2,1,0:T(8,128)(2,1)S(1)}, bf16[8,2,24,512]{3,2,1,0:T(8,128)(2,1)}, u32[]{:S(2)}, u32[]{:S(2)}) collective-permute-start(bf16[8,2,24,512]{3,2,1,0:T(8,128)(2,1)S(1)} %get-tuple-element.5), channel_id=1, source_target_pairs={{0,1},{1,2},{2,9},{3,10},{4,17},{5,18},{6,25},{7,26},{8,3},{9,4},{... | collective-permute-start | bytes 1179656 | tf_op jit(solution)/shard_map/ppermute | solution.py:146
  11.0 47.8 %collective-permute-start.2 = (bf16[8,2,24,512]{3,2,1,0:T(8,128)(2,1)S(1)}, bf16[8,2,24,512]{3,2,1,0:T(8,128)(2,1)}, u32[]{:S(2)}, u32[]{:S(2)}) collective-permute-start(bf16[8,2,24,512]{3,2,1,0:T(8,128)(2,1)S(1)} %get-tuple-element.6), channel_id=1, source_target_pairs={{0,2},{1,3},{2,10},{3,11},{4,18},{5,19},{6,26},{7,27},{8,4},{9,5},... | collective-permute-start | bytes 1179656 | tf_op jit(solution)/shard_map/ppermute | solution.py:146
  13.4 48.0 %collective-permute-start.3 = (bf16[8,2,24,512]{3,2,1,0:T(8,128)(2,1)S(1)}, bf16[8,2,24,512]{3,2,1,0:T(8,128)(2,1)}, u32[]{:S(2)}, u32[]{:S(2)}) collective-permute-start(bf16[8,2,24,512]{3,2,1,0:T(8,128)(2,1)S(1)} %get-tuple-element.7), channel_id=1, source_target_pairs={{0,3},{1,4},{2,11},{3,12},{4,19},{5,20},{6,27},{7,28},{8,5},{9,6},... | collective-permute-start | bytes 1179656 | tf_op jit(solution)/shard_map/ppermute | solution.py:146
  16.7 46.5 %collective-permute-start.4 = (bf16[8,2,24,512]{3,2,1,0:T(8,128)(2,1)S(1)}, bf16[8,2,24,512]{3,2,1,0:T(8,128)(2,1)}, u32[]{:S(2)}, u32[]{:S(2)}) collective-permute-start(bf16[8,2,24,512]{3,2,1,0:T(8,128)(2,1)S(1)} %get-tuple-element.8), channel_id=1, source_target_pairs={{0,4},{1,5},{2,12},{3,13},{4,20},{5,21},{6,28},{7,29},{8,6},{9,7},... | collective-permute-start | bytes 1179656 | tf_op jit(solution)/shard_map/ppermute | solution.py:146
  20.3 55.0 %collective-permute-start.5 = (bf16[8,2,24,512]{3,2,1,0:T(8,128)(2,1)S(1)}, bf16[8,2,24,512]{3,2,1,0:T(8,128)(2,1)S(1)}, u32[]{:S(2)}, u32[]{:S(2)}) collective-permute-start(bf16[8,2,24,512]{3,2,1,0:T(8,128)(2,1)S(1)} %get-tuple-element.9), channel_id=1, source_target_pairs={{0,5},{1,6},{2,13},{3,14},{4,21},{5,22},{6,29},{7,30},{8,7},{9,0},... | collective-permute-start | bytes 1179656 | tf_op jit(solution)/shard_map/ppermute | solution.py:146
  50.9 32.8 %collective-permute-start.6 = (bf16[8,2,24,512]{3,2,1,0:T(8,128)(2,1)S(1)}, bf16[8,2,24,512]{3,2,1,0:T(8,128)(2,1)S(1)}, u32[]{:S(2)}, u32[]{:S(2)}) collective-permute-start(bf16[8,2,24,512]{3,2,1,0:T(8,128)(2,1)S(1)} %get-tuple-element.10), channel_id=1, source_target_pairs={{0,6},{1,7},{2,14},{3,15},{4,22},{5,23},{6,30},{7,31},{8,0},{9,1},... | collective-permute-start | bytes 1179656 | tf_op jit(solution)/shard_map/ppermute | solution.py:146
  58.8 25.7 %collective-permute-start.7 = (bf16[8,2,24,512]{3,2,1,0:T(8,128)(2,1)S(1)}, bf16[8,2,24,512]{3,2,1,0:T(8,128)(2,1)S(1)}, u32[]{:S(2)}, u32[]{:S(2)}) collective-permute-start(bf16[8,2,24,512]{3,2,1,0:T(8,128)(2,1)S(1)} %get-tuple-element.4), channel_id=1, source_target_pairs={{0,7},{1,0},{2,15},{3,8},{4,23},{5,16},{6,31},{7,24},{8,1},{9,2},{... | collective-permute-start | bytes 1179656 | tf_op jit(solution)/shard_map/ppermute | solution.py:146
  89.6 20.6 %collective-permute-start.8 = (bf16[64,24,4]{2,0,1:T(8,128)(2,1)S(1)}, bf16[64,24,4]{2,0,1:T(8,128)(2,1)S(1)}, u32[]{:S(2)}, u32[]{:S(2)}) collective-permute-start(bf16[64,24,4]{2,0,1:T(8,128)(2,1)S(1)} %get-tuple-element.2), channel_id=1, source_target_pairs={{8,0},{16,8},{24,16},{9,1},{17,9},{25,17},{10,2},{18,10},{26,18},{... | collective-permute-start | bytes 36872 | tf_op jit(solution)/shard_map/ppermute | solution.py:156
  101.2 17.2 %collective-permute-start.9 = (bf16[64,24,4]{2,0,1:T(8,128)(2,1)S(1)}, bf16[64,24,4]{2,0,1:T(8,128)(2,1)S(1)}, u32[]{:S(2)}, u32[]{:S(2)}) collective-permute-start(bf16[64,24,4]{2,0,1:T(8,128)(2,1)S(1)} %get-tuple-element.3), channel_id=1, source_target_pairs={{0,8},{8,16},{16,24},{1,9},{9,17},{17,25},{2,10},{10,18},{18,26},{... | collective-permute-start | bytes 36872 | tf_op jit(solution)/shard_map/ppermute | solution.py:155

commit v6 on v5

v6 whole, which is shorter than its diff:
```python
import functools

import jax
import jax.numpy as jnp
from jax import lax
from jax.experimental import pallas as pl
from jax.experimental.pallas import tpu as pltpu
from jax.sharding import PartitionSpec as P

RADIUS = 4
LANES = 128
PAIRS_PER_STEP = 4
ACQ_PER_STEP = 4
FIELDS = 4


def assemble(field_ref, sides, fields_of, tile_cols):
    count = 0
    for main, edge in sides:
        pieces = [(c * main[0].shape[-1], [m[c, 0] for m in main]) for c in range(main[0].shape[0])]
        pieces.append((tile_cols, [e[0] for e in edge]))
        for at, parts in pieces:
            width = parts[0].shape[-1]
            values = fields_of(*[(part[0].astype(jnp.float32), part[1].astype(jnp.float32)) for part in parts])
            for f, value in enumerate(values):
                field_ref[count + f, :, pl.ds(at, width)] = value
        count += len(values)
    return count


def box_means(field_ref, rows_ref, band_ref, count, tile_rows, tile_cols):
    window = 2 * RADIUS + 1
    padded_cols = tile_cols + LANES
    for f in range(count):
        acc = field_ref[f, pl.ds(0, tile_rows), :]
        for k in range(1, window):
            acc = acc + field_ref[f, pl.ds(k, tile_rows), :]
        rows_ref[pl.ds(f * tile_rows, tile_rows), pl.ds(LANES, padded_cols)] = acc
        rows_ref[pl.ds(f * tile_rows, tile_rows), pl.ds(0, LANES)] = acc[:, padded_cols - LANES :]
    rowsum = rows_ref[pl.ds(0, count * tile_rows), :]
    high = rowsum.astype(jnp.bfloat16)
    low = (rowsum - high.astype(jnp.float32)).astype(jnp.bfloat16)
    band = band_ref[...]
    width = 3 * LANES
    for j in range(tile_cols // LANES):
        sums = jnp.dot(high[:, j * LANES : j * LANES + width], band, preferred_element_type=jnp.float32)
        sums = sums + jnp.dot(low[:, j * LANES : j * LANES + width], band, preferred_element_type=jnp.float32)
        yield j, sums / float(window * window)


def power_fields(side):
    re, im = side
    return (re * re + im * im,)


def cross_fields(pre, post):
    pr, pi = pre
    qr, qi = post
    return (pr * qr + pi * qi, pi * qr - pr * qi)


def power_kernel(main_ref, edge_ref, band_ref, out_ref, field_ref, rows_ref, *, tile_rows, tile_cols):
    step = main_ref.shape[1]
    sides = [([main_ref.at[:, a : a + 1]], [edge_ref.at[a : a + 1]]) for a in range(step)]
    count = assemble(field_ref, sides, power_fields, tile_cols)
    for j, means in box_means(field_ref, rows_ref, band_ref, count, tile_rows, tile_cols):
        for a in range(step):
            out_ref[a, :, pl.ds(j * LANES, LANES)] = means[a * tile_rows : (a + 1) * tile_rows] + 1e-06


def pair_kernel(pre_ref, post_ref, *refs, tile_rows, tile_cols):
    del pre_ref, post_ref
    pp = PAIRS_PER_STEP
    sides = refs[: 6 * pp]
    band_ref, coh_ref, chg_ref, field_ref, rows_ref = refs[6 * pp :]
    count = 0
    for p in range(pp):
        a_main, a_edge, b_main, b_edge = sides[6 * p : 6 * p + 4]
        count += assemble(field_ref.at[count:], [([a_main, b_main], [a_edge, b_edge])], cross_fields, tile_cols)
    for j, means in box_means(field_ref, rows_ref, band_ref, count, tile_rows, tile_cols):
        for p in range(pp):
            pre_power = sides[6 * p + 4][0, :, pl.ds(j * LANES, LANES)]
            post_power = sides[6 * p + 5][0, :, pl.ds(j * LANES, LANES)]
            base = 2 * p * tile_rows
            real_mean = means[base : base + tile_rows]
            imag_mean = means[base + tile_rows : base + 2 * tile_rows]
            coh = jnp.sqrt(real_mean * real_mean + imag_mean * imag_mean) / jnp.sqrt(
                pre_power * post_power
            )
            coh_ref[p, :, pl.ds(j * LANES, LANES)] = coh
            chg_ref[p, :, pl.ds(j * LANES, LANES)] = jnp.log(post_power / pre_power)


def make_band():
    width = 3 * LANES
    lane_in = jnp.arange(width)[:, None]
    lane_out = jnp.arange(LANES)[None, :]
    gap = lane_in - LANES - lane_out
    return jnp.where((gap >= -RADIUS) & (gap <= RADIUS), 1.0, 0.0).astype(jnp.bfloat16)


def pair_maps(main, edge, pre_ids, post_ids, tile_rows, tile_cols):
    count_pairs = pre_ids.shape[0]
    pp = PAIRS_PER_STEP
    blocks_per_tile, count_acq, _, padded_rows, block_cols = main.shape
    band = make_band()
    padded_cols = tile_cols + LANES
    width = 3 * LANES

    ap = ACQ_PER_STEP
    power = pl.pallas_call(
        functools.partial(power_kernel, tile_rows=tile_rows, tile_cols=tile_cols),
        grid=(count_acq // ap,),
        in_specs=[
            pl.BlockSpec((blocks_per_tile, ap, 2, padded_rows, block_cols), lambda i: (0, i, 0, 0, 0)),
            pl.BlockSpec((ap, 2, padded_rows, LANES), lambda i: (i, 0, 0, 0)),
            pl.BlockSpec((width, LANES), lambda i: (0, 0)),
        ],
        out_specs=pl.BlockSpec((ap, tile_rows, tile_cols), lambda i: (i, 0, 0)),
        out_shape=jax.ShapeDtypeStruct((count_acq, tile_rows, tile_cols), jnp.float32),
        scratch_shapes=[
            pltpu.VMEM((ap, padded_rows, padded_cols), jnp.float32),
            pltpu.VMEM((ap * tile_rows, padded_cols + LANES), jnp.float32),
        ],
    )(main, edge, band)

    main_block = (blocks_per_tile, 1, 2, padded_rows, block_cols)
    edge_block = (1, 2, padded_rows, LANES)
    power_block = (1, tile_rows, tile_cols)

    def specs(p):
        return [
            pl.BlockSpec(main_block, lambda i, pre, post: (0, pre[i * pp + p], 0, 0, 0)),
            pl.BlockSpec(edge_block, lambda i, pre, post: (pre[i * pp + p], 0, 0, 0)),
            pl.BlockSpec(main_block, lambda i, pre, post: (0, post[i * pp + p], 0, 0, 0)),
            pl.BlockSpec(edge_block, lambda i, pre, post: (post[i * pp + p], 0, 0, 0)),
            pl.BlockSpec(power_block, lambda i, pre, post: (pre[i * pp + p], 0, 0)),
            pl.BlockSpec(power_block, lambda i, pre, post: (post[i * pp + p], 0, 0)),
        ]

    in_specs = []
    operands = []
    for p in range(pp):
        in_specs += specs(p)
        operands += [main, edge, main, edge, power, power]
    in_specs.append(pl.BlockSpec((width, LANES), lambda i, pre, post: (0, 0)))
    operands.append(band)
    out_block = pl.BlockSpec((pp, tile_rows, tile_cols), lambda i, pre, post: (i, 0, 0))
    grid_spec = pltpu.PrefetchScalarGridSpec(
        num_scalar_prefetch=2,
        grid=(count_pairs // pp,),
        in_specs=in_specs,
        out_specs=[out_block, out_block],
        scratch_shapes=[
            pltpu.VMEM((2 * pp, padded_rows, padded_cols), jnp.float32),
            pltpu.VMEM((2 * pp * tile_rows, padded_cols + LANES), jnp.float32),
        ],
    )
    out_shape = jax.ShapeDtypeStruct((count_pairs, tile_rows, tile_cols), jnp.float32)
    kernel = functools.partial(pair_kernel, tile_rows=tile_rows, tile_cols=tile_cols)
    return pl.pallas_call(
        kernel,
        grid_spec=grid_spec,
        out_shape=[out_shape, out_shape],
    )(pre_ids, post_ids, *operands)


def shards(stack, filt_re, filt_im, pre_ids, post_ids):
    count_acq = filt_re.shape[0]
    n_rows = lax.axis_size("ty")
    n_cols = lax.axis_size("tx")
    local_acq, _, height, local_cols = stack.shape
    tile_rows = height // n_rows
    blocks_per_tile = n_rows // n_cols
    tile_cols = local_cols * blocks_per_tile
    padded_rows = tile_rows + 2 * RADIUS

    me_col = lax.axis_index("tx")
    me_row = lax.axis_index("ty")
    x = jnp.pad(stack, ((0, 0), (0, 0), (RADIUS, RADIUS), (0, 0)))
    start = me_col * blocks_per_tile + me_row % blocks_per_tile
    received = []
    for m in range(n_rows):
        pairs = []
        for col in range(n_cols):
            for row in range(n_rows):
                to_row = (m + col * blocks_per_tile + row % blocks_per_tile) % n_rows
                pairs.append((col * n_rows + row, (row // blocks_per_tile) * n_rows + to_row))
        first = ((start + m) % n_rows) * tile_rows
        chunk = lax.dynamic_slice_in_dim(x, first, padded_rows, axis=2)
        received.append(lax.ppermute(chunk, ("tx", "ty"), pairs))
    received = jnp.stack(received, axis=0)
    source = jnp.arange(blocks_per_tile)[:, None] + blocks_per_tile * jnp.arange(n_cols)[None, :]
    order = (me_row - source) % n_rows
    x = jnp.take(received, order.reshape(-1), axis=0)
    x = x.reshape(blocks_per_tile, 2 * count_acq, padded_rows, local_cols)

    forward = [(i, i + 1) for i in range(n_cols - 1)]
    backward = [(target, source) for source, target in forward]
    left = lax.ppermute(x[blocks_per_tile - 1, :, :, local_cols - RADIUS :], "tx", forward)
    right = lax.ppermute(x[0, :, :, :RADIUS], "tx", backward)
    gap = jnp.zeros((2 * count_acq, padded_rows, LANES - 2 * RADIUS), x.dtype)
    edge = jnp.concatenate([right, gap, left], axis=2)

    mixing = jnp.stack([jnp.stack([filt_re, -filt_im], -1), jnp.stack([filt_im, filt_re], -1)], 1)
    mixing = mixing.reshape(2 * count_acq, 2 * count_acq)
    main = jnp.einsum("kc,bchw->bkhw", mixing, x, preferred_element_type=jnp.float32)
    main = main.astype(jnp.bfloat16).reshape(blocks_per_tile, count_acq, 2, padded_rows, local_cols)
    edge = jnp.einsum("kc,chw->khw", mixing, edge, preferred_element_type=jnp.float32)
    edge = edge.astype(jnp.bfloat16).reshape(count_acq, 2, padded_rows, LANES)
    return pair_maps(main, edge, pre_ids, post_ids, tile_rows, tile_cols)


def solution(mesh):
    in_specs = (P("tx", None, None, "ty"), P(), P(), P(), P())
    out_specs = (P(None, "ty", "tx"), P(None, "ty", "tx"))
    return jax.shard_map(shards, mesh=mesh, in_specs=in_specs, out_specs=out_specs, check_vma=False)
```

time: 145 us -> 184 us (1.27)
  the two profiles are of different devices: /device:TPU:21 before, /device:TPU:30 now
where the time goes in v6:
time: 184 us
  starting transfers between devices  82.3 us (45%)
  waiting for transfers between devices  44.4 us (24%)
  local copies, waits for them, and re-layouts  26.1 us (14%)
  Pallas kernels  25.7 us (14%)
  other arithmetic  2.29 us (1%)
    ppermute x8, starting transfers between devices, shards(): received.append(lax.ppermute(chunk, ('tx', 'ty'), pairs))  73.5 us
    ppermute x1, waiting for transfers between devices, shards(): lax.ppermute(x[blocks_per_tile - 1, :, :, local_cols - RADIUS:], 'tx', fo...  39 us
    pallas_call x1, Pallas kernels, pair_maps(): pl.pallas_call(kernel, grid_spec=grid_spec, out_shape=[out_shape, out_sha...  17.3 us
    unnamed x11, local copies, waits for them, and re-layouts  9.44 us
    pallas_call x1, Pallas kernels, pair_maps(): pl.pallas_call(functools.partial(power_kernel, tile_rows=tile_rows, tile_...  8.36 us
    ppermute x1, starting transfers between devices, shards(): right = lax.ppermute(x[0, :, :, :RADIUS], 'tx', backward)  7.32 us
    dynamic_slice x1, local copies, waits for them, and re-layouts, shards(): chunk = lax.dynamic_slice_in_dim(x, first, padded_rows, axis=2)  5.06 us
    ppermute x8, waiting for transfers between devices, shards(): received.append(lax.ppermute(chunk, ('tx', 'ty'), pairs))  4.56 us
  transfers between devices with their start and end apart: 10, of which 3 were waited for; matrix products, arithmetic and copies ran while one was open for 10% of the time, Pallas kernels for 0%

profile of v6, /device:TPU:30, one launch (start us, length us, event | category | flops | bytes accessed | tf_op | source)
XLA Modules:
  0.0 183.6 jit_solution(8993541819926219347)
XLA Ops:
  0.8 5.1 %pad_dynamic-slice_fusion = (bf16[8,2,24,512]{3,2,1,0:T(8,128)(2,1)S(1)}, bf16[8,2,24,512]{3,2,1,0:T(8,128)(2,1)S(1)}, bf16[8,2,24,512]{3,2,1,0:T(8,128)(2,1)S(1...) fusion(s32[]{:T(128)S(6)} %select_n.137, ...), kind=kLoop, calls=%fused_computation.7 | loop fusion | bytes 5242912 | tf_op jit(solution)/shard_map/dynamic_slice | solution.py:190
  5.8 0.5 collective-permute-start.1
  6.3 5.1 %collective-permute-start.2 = (bf16[8,2,24,512]{3,2,1,0:T(8,128)(2,1)S(1)}, bf16[8,2,24,512]{3,2,1,0:T(8,128)(2,1)}, u32[]{:S(2)}, u32[]{:S(2)}) collective-permute-start(bf16[8,2,24,512]{3,2,1,0:T(8,128)(2,1)S(1)} %get-tuple-element.6), channel_id=1, source_target_pairs={{0,2},{1,3},{2,10},{3,11},{4,18},{5,19},{6,26},{7,27},{8,4},{9,5},... | collective-permute-start | bytes 1179656 | tf_op jit(solution)/shard_map/ppermute | solution.py:191
  11.4 4.5 %collective-permute-start = (bf16[8,2,24,512]{3,2,1,0:T(8,128)(2,1)}, bf16[8,2,24,512]{3,2,1,0:T(8,128)(2,1)}, u32[]{:S(2)}, u32[]{:S(2)}) collective-permute-start(bf16[8,2,24,512]{3,2,1,0:T(8,128)(2,1)} %get-tuple-element.11), channel_id=1, source_target_pairs={{0,0},{1,1},{2,8},{3,9},{4,16},{5,17},{6,24},{7,25},{8,2},{9,3},{1... | collective-permute-start | bytes 1179656 | tf_op jit(solution)/shard_map/ppermute | solution.py:191
  16.1 0.8 select_convert_fusion.band_ref.refs_24_
  16.9 0.5 copy.11
  17.4 0.8 reshape.134
  18.2 0.8 reshape.135
  19.3 36.4 %collective-permute-start.4 = (bf16[8,2,24,512]{3,2,1,0:T(8,128)(2,1)S(1)}, bf16[8,2,24,512]{3,2,1,0:T(8,128)(2,1)S(1)}, u32[]{:S(2)}, u32[]{:S(2)}) collective-permute-start(bf16[8,2,24,512]{3,2,1,0:T(8,128)(2,1)S(1)} %get-tuple-element.8), channel_id=1, source_target_pairs={{0,4},{1,5},{2,12},{3,13},{4,20},{5,21},{6,28},{7,29},{8,6},{9,7},... | collective-permute-start | bytes 1179656 | tf_op jit(solution)/shard_map/ppermute | solution.py:191
  55.7 1.8 bitcast_dynamic-update-slice_fusion.7
  57.5 1.8 bitcast_dynamic-update-slice_fusion.6
  59.3 27.0 %collective-permute-start.6 = (bf16[8,2,24,512]{3,2,1,0:T(8,128)(2,1)S(1)}, bf16[8,2,24,512]{3,2,1,0:T(8,128)(2,1)S(1)}, u32[]{:S(2)}, u32[]{:S(2)}) collective-permute-start(bf16[8,2,24,512]{3,2,1,0:T(8,128)(2,1)S(1)} %get-tuple-element.10), channel_id=1, source_target_pairs={{0,6},{1,7},{2,14},{3,15},{4,22},{5,23},{6,30},{7,31},{8,0},{9,1},... | collective-permute-start | bytes 1179656 | tf_op jit(solution)/shard_map/ppermute | solution.py:191
  86.3 1.8 bitcast_dynamic-update-slice_fusion.5
  88.1 1.8 bitcast_dynamic-update-slice_fusion.4
  89.9 0.8 bitcast_dynamic-update-slice_fusion.3
  90.7 0.8 bitcast_dynamic-update-slice_fusion.2
  91.5 4.5 %collective-permute-done.6 = bf16[8,2,24,512]{3,2,1,0:T(8,128)(2,1)S(1)} collective-permute-done((bf16[8,2,24,512]{3,2,1,0:T(8,128)(2,1)S(1)}, bf16[8,2,24,512]{3,2,1,0:T(8,128)(2,1)S(1)}, u32[]{:S(2)}, u32[]{:S(2)}) %collective-permute-start.6) | collective-permute-done | bytes 393248 | tf_op jit(solution)/shard_map/ppermute | solution.py:191
  96.0 0.8 bitcast_dynamic-update-slice_fusion.1
  96.8 1.8 bitcast_dynamic-update-slice_fusion
  98.6 2.6 %gather_fusion = bf16[8,8,2,24,512]{4,3,2,1,0:T(8,128)(2,1)S(1)} fusion(bf16[8,8,2,24,512]{4,3,2,1,0:T(8,128)(2,1)} %bitcast_dynamic-update-slice_fusion, s32[1024]{0:T(1024)S(1)} %pad_clamp_fusion), kind=kCustom, calls=%fused_computation | custom fusion | bytes 6291488 | tf_op jit(solution)/shard_map/jit(_take)/gather | solution.py:195
  101.2 0.4 broadcast_select_fusion
  101.6 1.1 copy_select_fusion
  102.9 7.3 %collective-permute-start.8 = (bf16[64,24,4]{2,0,1:T(8,128)(2,1)S(1)}, bf16[64,24,4]{2,0,1:T(8,128)(2,1)S(1)}, u32[]{:S(2)}, u32[]{:S(2)}) collective-permute-start(bf16[64,24,4]{2,0,1:T(8,128)(2,1)S(1)} %get-tuple-element.2), channel_id=1, source_target_pairs={{8,0},{16,8},{24,16},{9,1},{17,9},{25,17},{10,2},{18,10},{26,18},{... | collective-permute-start | bytes 36872 | tf_op jit(solution)/shard_map/ppermute | solution.py:201
  110.2 1.5 collective-permute-start.9
  111.7 1.3 convert_bitcast_fusion
  113.0 3.4 %copy.13 = bf16[2,64,24,512]{3,2,1,0:T(8,128)(2,1)} copy(bf16[2,64,24,512]{3,1,2,0:T(8,128)(2,1)S(1)} %convert_bitcast_fusion) | data formatting | bytes 6291456 | tf_op jit(solution)/shard_map/convert_element_type | solution.py:208
  116.4 0.9 collective-permute-done.8
  117.3 39.0 %collective-permute-done.9 = bf16[64,24,4]{2,0,1:T(8,128)(2,1)S(1)} collective-permute-done((bf16[64,24,4]{2,0,1:T(8,128)(2,1)S(1)}, bf16[64,24,4]{2,0,1:T(8,128)(2,1)S(1)}, u32[]{:S(2)}, u32[]{:S(2)}) %collective-permute-start.9) | collective-permute-done | bytes 12320 | tf_op jit(solution)/shard_map/ppermute | solution.py:200
  156.3 0.4 convolution_convert_fusion
  156.7 1.0 copy.15
  157.7 8.4 %shard_map.68.refs_4_.refs_5_.refs_10_.refs_11_.refs_16_.refs_17_.refs_22_.refs_23_ = f32[32,16,1024]{2,1,0:T(8,128)} custom-call(bf16[2,32,2,24,512]{4,3,2,1,0:T(8,128)(2,1)} %bitcast.44, bf16[32,2,24,128]{3,2,1,0:T(8,128)(2,1)} %bitcast.53, bf16[384,128]{1,0:T(8,128)(2,1)} %select_convert_fusion.band_ref.refs_24_), custom_call_target="tpu_custom_call" | custom-call | tf_op jit(solution)/shard_map/pallas_call | solution.py:111
  166.1 17.3 %shard_map.69 = (f32[32,16,1024]{2,1,0:T(8,128)}, f32[32,16,1024]{2,1,0:T(8,128)}) custom-call(s32[32]{0:T(128)} %pre_ref.1, s32[32]{0:T(128)} %post_ref.1, bf16[2,32,2,24,512]{4,3,2,1,0:T(8,128)(2,1)} %bitcast.45, bf16[32,2,24,128]{3,2,1,0:T(8,128)(2,1)} %bitcast.54, bf16[2,32,2,24,512]{4,3,2,1,0:T(8,128)(2,1)} %bitcast.46, ...), custom_call_target="tpu_custom_call" | custom-call | tf_op jit(solution)/shard_map/pallas_call | solution.py:161
  (30 shorter events, 0.8 us)
Async XLA Ops:
  0.6 15.5 %copy-start = (bf16[32,32]{1,0:T(8,128)(2,1)S(1)}, bf16[32,32]{1,0:T(8,128)(2,1)}, u32[]{:S(2)}) copy-start(bf16[32,32]{1,0:T(8,128)(2,1)} %param.7) | copy-start | bytes 6148
  0.6 16.2 %copy-start.1 = (bf16[32,32]{1,0:T(8,128)(2,1)S(1)}, bf16[32,32]{1,0:T(8,128)(2,1)}, u32[]{:S(2)}) copy-start(bf16[32,32]{1,0:T(8,128)(2,1)} %param.6) | copy-start | bytes 6148
  5.8 90.9 %collective-permute-start.7 = (bf16[8,2,24,512]{3,2,1,0:T(8,128)(2,1)S(1)}, bf16[8,2,24,512]{3,2,1,0:T(8,128)(2,1)}, u32[]{:S(2)}, u32[]{:S(2)}) collective-permute-start(bf16[8,2,24,512]{3,2,1,0:T(8,128)(2,1)S(1)} %get-tuple-element.4), channel_id=1, source_target_pairs={{0,7},{1,0},{2,15},{3,8},{4,23},{5,16},{6,31},{7,24},{8,1},{9,2},{... | collective-permute-start | bytes 1179656 | tf_op jit(solution)/shard_map/ppermute | solution.py:191
  5.8 51.7 %collective-permute-start.1 = (bf16[8,2,24,512]{3,2,1,0:T(8,128)(2,1)S(1)}, bf16[8,2,24,512]{3,2,1,0:T(8,128)(2,1)}, u32[]{:S(2)}, u32[]{:S(2)}) collective-permute-start(bf16[8,2,24,512]{3,2,1,0:T(8,128)(2,1)S(1)} %get-tuple-element.5), channel_id=1, source_target_pairs={{0,1},{1,2},{2,9},{3,10},{4,17},{5,18},{6,25},{7,26},{8,3},{9,4},{... | collective-permute-start | bytes 1179656 | tf_op jit(solution)/shard_map/ppermute | solution.py:191
  6.3 52.9 %collective-permute-start.2 = (bf16[8,2,24,512]{3,2,1,0:T(8,128)(2,1)S(1)}, bf16[8,2,24,512]{3,2,1,0:T(8,128)(2,1)}, u32[]{:S(2)}, u32[]{:S(2)}) collective-permute-start(bf16[8,2,24,512]{3,2,1,0:T(8,128)(2,1)S(1)} %get-tuple-element.6), channel_id=1, source_target_pairs={{0,2},{1,3},{2,10},{3,11},{4,18},{5,19},{6,26},{7,27},{8,4},{9,5},... | collective-permute-start | bytes 1179656 | tf_op jit(solution)/shard_map/ppermute | solution.py:191
  11.4 76.7 %collective-permute-start.3 = (bf16[8,2,24,512]{3,2,1,0:T(8,128)(2,1)S(1)}, bf16[8,2,24,512]{3,2,1,0:T(8,128)(2,1)}, u32[]{:S(2)}, u32[]{:S(2)}) collective-permute-start(bf16[8,2,24,512]{3,2,1,0:T(8,128)(2,1)S(1)} %get-tuple-element.7), channel_id=1, source_target_pairs={{0,3},{1,4},{2,11},{3,12},{4,19},{5,20},{6,27},{7,28},{8,5},{9,6},... | collective-permute-start | bytes 1179656 | tf_op jit(solution)/shard_map/ppermute | solution.py:191
  11.4 7.9 %collective-permute-start = (bf16[8,2,24,512]{3,2,1,0:T(8,128)(2,1)}, bf16[8,2,24,512]{3,2,1,0:T(8,128)(2,1)}, u32[]{:S(2)}, u32[]{:S(2)}) collective-permute-start(bf16[8,2,24,512]{3,2,1,0:T(8,128)(2,1)} %get-tuple-element.11), channel_id=1, source_target_pairs={{0,0},{1,1},{2,8},{3,9},{4,16},{5,17},{6,24},{7,25},{8,2},{9,3},{1... | collective-permute-start | bytes 1179656 | tf_op jit(solution)/shard_map/ppermute | solution.py:191
  19.3 70.6 %collective-permute-start.4 = (bf16[8,2,24,512]{3,2,1,0:T(8,128)(2,1)S(1)}, bf16[8,2,24,512]{3,2,1,0:T(8,128)(2,1)S(1)}, u32[]{:S(2)}, u32[]{:S(2)}) collective-permute-start(bf16[8,2,24,512]{3,2,1,0:T(8,128)(2,1)S(1)} %get-tuple-element.8), channel_id=1, source_target_pairs={{0,4},{1,5},{2,12},{3,13},{4,20},{5,21},{6,28},{7,29},{8,6},{9,7},... | collective-permute-start | bytes 1179656 | tf_op jit(solution)/shard_map/ppermute | solution.py:191
  57.5 33.2 %collective-permute-start.5 = (bf16[8,2,24,512]{3,2,1,0:T(8,128)(2,1)S(1)}, bf16[8,2,24,512]{3,2,1,0:T(8,128)(2,1)S(1)}, u32[]{:S(2)}, u32[]{:S(2)}) collective-permute-start(bf16[8,2,24,512]{3,2,1,0:T(8,128)(2,1)S(1)} %get-tuple-element.9), channel_id=1, source_target_pairs={{0,5},{1,6},{2,13},{3,14},{4,21},{5,22},{6,29},{7,30},{8,7},{9,0},... | collective-permute-start | bytes 1179656 | tf_op jit(solution)/shard_map/ppermute | solution.py:191
  59.3 36.7 %collective-permute-start.6 = (bf16[8,2,24,512]{3,2,1,0:T(8,128)(2,1)S(1)}, bf16[8,2,24,512]{3,2,1,0:T(8,128)(2,1)S(1)}, u32[]{:S(2)}, u32[]{:S(2)}) collective-permute-start(bf16[8,2,24,512]{3,2,1,0:T(8,128)(2,1)S(1)} %get-tuple-element.10), channel_id=1, source_target_pairs={{0,6},{1,7},{2,14},{3,15},{4,22},{5,23},{6,30},{7,31},{8,0},{9,1},... | collective-permute-start | bytes 1179656 | tf_op jit(solution)/shard_map/ppermute | solution.py:191
  102.9 14.4 %collective-permute-start.8 = (bf16[64,24,4]{2,0,1:T(8,128)(2,1)S(1)}, bf16[64,24,4]{2,0,1:T(8,128)(2,1)S(1)}, u32[]{:S(2)}, u32[]{:S(2)}) collective-permute-start(bf16[64,24,4]{2,0,1:T(8,128)(2,1)S(1)} %get-tuple-element.2), channel_id=1, source_target_pairs={{8,0},{16,8},{24,16},{9,1},{17,9},{25,17},{10,2},{18,10},{26,18},{... | collective-permute-start | bytes 36872 | tf_op jit(solution)/shard_map/ppermute | solution.py:201
  110.2 46.1 %collective-permute-start.9 = (bf16[64,24,4]{2,0,1:T(8,128)(2,1)S(1)}, bf16[64,24,4]{2,0,1:T(8,128)(2,1)S(1)}, u32[]{:S(2)}, u32[]{:S(2)}) collective-permute-start(bf16[64,24,4]{2,0,1:T(8,128)(2,1)S(1)} %get-tuple-element.3), channel_id=1, source_target_pairs={{0,8},{8,16},{16,24},{1,9},{9,17},{17,25},{2,10},{10,18},{18,26},{... | collective-permute-start | bytes 36872 | tf_op jit(solution)/shard_map/ppermute | solution.py:200

commit v7 on v5

--- a/solution.py
+++ b/solution.py
@@ -133,29 +133,39 @@
     me_col = lax.axis_index("tx")
     me_row = lax.axis_index("ty")
     x = jnp.pad(stack, ((0, 0), (0, 0), (RADIUS, RADIUS), (0, 0)))
+    side = jnp.where(me_row % blocks_per_tile == 0, x[..., :RADIUS], x[..., local_cols - RADIUS :])
     start = me_col * blocks_per_tile + me_row % blocks_per_tile
+    strip_shape = (local_acq * 2 * padded_rows * RADIUS // LANES, LANES)
     received = []
+    strips = []
     for m in range(n_rows):
         pairs = []
+        side_pairs = []
         for col in range(n_cols):
             for row in range(n_rows):
-                to_row = (m + col * blocks_per_tile + row % blocks_per_tile) % n_rows
-                pairs.append((col * n_rows + row, (row // blocks_per_tile) * n_rows + to_row))
+                block = row % blocks_per_tile
+                to_row = (m + col * blocks_per_tile + block) % n_rows
+                source = col * n_rows + row
+                pairs.append((source, (row // blocks_per_tile) * n_rows + to_row))
+                if block == blocks_per_tile - 1 and row // blocks_per_tile + 1 < n_cols:
+                    side_pairs.append((source, (row // blocks_per_tile + 1) * n_rows + to_row))
+                elif block == 0 and row // blocks_per_tile > 0:
+                    side_pairs.append((source, (row // blocks_per_tile - 1) * n_rows + to_row))
         first = ((start + m) % n_rows) * tile_rows
         chunk = lax.dynamic_slice_in_dim(x, first, padded_rows, axis=2)
         received.append(lax.ppermute(chunk, ("tx", "ty"), pairs))
+        piece = lax.dynamic_slice_in_dim(side, first, padded_rows, axis=2).reshape(strip_shape)
+        strips.append(lax.ppermute(piece, ("tx", "ty"), side_pairs))
     received = jnp.stack(received, axis=0)
+    strips = jnp.stack(strips, axis=0)
     source = jnp.arange(blocks_per_tile)[:, None] + blocks_per_tile * jnp.arange(n_cols)[None, :]
     order = (me_row - source) % n_rows
     x = jnp.take(received, order.reshape(-1), axis=0)
     x = x.reshape(blocks_per_tile, 2 * count_acq, padded_rows, local_cols)
-
-    forward = [(i, i + 1) for i in range(n_cols - 1)]
-    backward = [(target, source) for source, target in forward]
-    left = lax.ppermute(x[blocks_per_tile - 1, :, :, local_cols - RADIUS :], "tx", forward)
-    right = lax.ppermute(x[0, :, :, :RADIUS], "tx", backward)
+    strips = jnp.take(strips, order[jnp.array([0, blocks_per_tile - 1])].reshape(-1), axis=0)
+    strips = strips.reshape(2, 2 * count_acq, padded_rows, RADIUS)
     gap = jnp.zeros((2 * count_acq, padded_rows, LANES - 2 * RADIUS), x.dtype)
-    edge = jnp.concatenate([right, gap, left], axis=2)
+    edge = jnp.concatenate([strips[0], gap, strips[1]], axis=2)
 
     mixing = jnp.stack([jnp.stack([filt_re, -filt_im], -1), jnp.stack([filt_im, filt_re], -1)], 1)
     mixing = mixing.reshape(2 * count_acq, 2 * count_acq)

time: 145 us -> 204 us (1.41)
  the two profiles are of different devices: /device:TPU:21 before, /device:TPU:13 now
where the time goes in v7:
time: 204 us; the launch traced here: 203 us
  waiting for transfers between devices  97 us (48%)
  starting transfers between devices  48.6 us (24%)
  local copies, waits for them, and re-layouts  29.1 us (14%)
  Pallas kernels  23.9 us (12%)
    ppermute x8, waiting for transfers between devices, shards(): strips.append(lax.ppermute(piece, ('tx', 'ty'), side_pairs))  55.1 us
    ppermute x8, waiting for transfers between devices, shards(): received.append(lax.ppermute(chunk, ('tx', 'ty'), pairs))  41.9 us
    ppermute x8, starting transfers between devices, shards(): strips.append(lax.ppermute(piece, ('tx', 'ty'), side_pairs))  34.4 us
    pallas_call x1, Pallas kernels, pair_maps(): pl.pallas_call(kernel, grid_spec=grid_spec, out_shape=[out_shape, out_sha...  23.9 us
    ppermute x8, starting transfers between devices, shards(): received.append(lax.ppermute(chunk, ('tx', 'ty'), pairs))  14.2 us
    unnamed x22, local copies, waits for them, and re-layouts  9.54 us
    dynamic_slice x1, local copies, waits for them, and re-layouts, shards(): chunk = lax.dynamic_slice_in_dim(x, first, padded_rows, axis=2)  4.8 us
  transfers between devices with their start and end apart: 16, of which 11 were waited for; matrix products, arithmetic and copies ran while one was open for 10% of the time, Pallas kernels for 0%

profile of v7, /device:TPU:13, one launch (start us, length us, event | category | flops | bytes accessed | tf_op | source)
XLA Modules:
  0.0 203.4 jit_solution(10165258246434373586)
XLA Ops:
  0.8 4.8 %pad_dynamic-slice_fusion = (bf16[8,2,24,512]{3,2,1,0:T(8,128)(2,1)S(1)}, bf16[8,2,24,512]{3,2,1,0:T(8,128)(2,1)}, bf16[8,2,24,512]{3,2,1,0:T(8,128)(2,1)}, bf16...) fusion(s32[]{:T(128)S(6)} %select_n.177, ...), kind=kLoop, calls=%fused_computation.9 | loop fusion | bytes 5242912 | tf_op jit(solution)/shard_map/dynamic_slice | solution.py:155
  5.6 4.2 %collective-permute-start = (bf16[8,2,24,512]{3,2,1,0:T(8,128)(2,1)}, bf16[8,2,24,512]{3,2,1,0:T(8,128)(2,1)}, u32[]{:S(2)}, u32[]{:S(2)}) collective-permute-start(bf16[8,2,24,512]{3,2,1,0:T(8,128)(2,1)} %get-tuple-element.9), channel_id=1, source_target_pairs={{0,0},{1,1},{2,8},{3,9},{4,16},{5,17},{6,24},{7,25},{8,2},{9,3},{1... | collective-permute-start | bytes 1179656 | tf_op jit(solution)/shard_map/ppermute | solution.py:156
  9.8 2.9 %collective-permute-start.1 = (bf16[8,2,24,512]{3,2,1,0:T(8,128)(2,1)}, bf16[8,2,24,512]{3,2,1,0:T(8,128)(2,1)}, u32[]{:S(2)}, u32[]{:S(2)}) collective-permute-start(bf16[8,2,24,512]{3,2,1,0:T(8,128)(2,1)} %get-tuple-element.3), channel_id=1, source_target_pairs={{0,1},{1,2},{2,9},{3,10},{4,17},{5,18},{6,25},{7,26},{8,3},{9,4},{... | collective-permute-start | bytes 1179656 | tf_op jit(solution)/shard_map/ppermute | solution.py:156
  12.7 1.4 collective-permute-start.2
  15.6 5.0 %collective-permute-start.8 = (bf16[12,128]{1,0:T(8,128)(2,1)S(1)}, bf16[12,128]{1,0:T(8,128)(2,1)S(1)}, u32[]{:S(2)}, u32[]{:S(2)}) collective-permute-start(bf16[12,128]{1,0:T(8,128)(2,1)S(1)} %reshape.194), channel_id=1, source_target_pairs={{1,9},{2,0},{3,17},{4,8},{5,25},{6,16},{9,11},{10,2},{11,19},{12,1... | collective-permute-start | bytes 9224 | tf_op jit(solution)/shard_map/ppermute | solution.py:158
  25.8 39.5 %collective-permute-done.8 = bf16[12,128]{1,0:T(8,128)(2,1)S(1)} collective-permute-done((bf16[12,128]{1,0:T(8,128)(2,1)S(1)}, bf16[12,128]{1,0:T(8,128)(2,1)S(1)}, u32[]{:S(2)}, u32[]{:S(2)}) %collective-permute-start.8) | collective-permute-done | bytes 3104 | tf_op jit(solution)/shard_map/ppermute | solution.py:158
  65.4 1.9 collective-permute-start.9
  67.3 5.7 %collective-permute-done.9 = bf16[12,128]{1,0:T(8,128)(2,1)S(1)} collective-permute-done((bf16[12,128]{1,0:T(8,128)(2,1)S(1)}, bf16[12,128]{1,0:T(8,128)(2,1)S(1)}, u32[]{:S(2)}, u32[]{:S(2)}) %collective-permute-start.9) | collective-permute-done | bytes 3104 | tf_op jit(solution)/shard_map/ppermute | solution.py:158
  73.0 1.9 collective-permute-start.10
  74.9 2.4 %collective-permute-done.10 = bf16[12,128]{1,0:T(8,128)(2,1)S(1)} collective-permute-done((bf16[12,128]{1,0:T(8,128)(2,1)S(1)}, bf16[12,128]{1,0:T(8,128)(2,1)S(1)}, u32[]{:S(2)}, u32[]{:S(2)}) %collective-permute-start.10) | collective-permute-done | bytes 3104 | tf_op jit(solution)/shard_map/ppermute | solution.py:158
  77.3 2.1 %collective-permute-start.11 = (bf16[12,128]{1,0:T(8,128)(2,1)S(1)}, bf16[12,128]{1,0:T(8,128)(2,1)S(1)}, u32[]{:S(2)}, u32[]{:S(2)}) collective-permute-start(bf16[12,128]{1,0:T(8,128)(2,1)S(1)} %reshape.197), channel_id=1, source_target_pairs={{1,12},{2,3},{3,20},{4,11},{5,28},{6,19},{9,14},{10,5},{11,22},{12... | collective-permute-start | bytes 9224 | tf_op jit(solution)/shard_map/ppermute | solution.py:158
  79.4 5.1 %collective-permute-done.11 = bf16[12,128]{1,0:T(8,128)(2,1)S(1)} collective-permute-done((bf16[12,128]{1,0:T(8,128)(2,1)S(1)}, bf16[12,128]{1,0:T(8,128)(2,1)S(1)}, u32[]{:S(2)}, u32[]{:S(2)}) %collective-permute-start.11) | collective-permute-done | bytes 3104 | tf_op jit(solution)/shard_map/ppermute | solution.py:158
  84.5 5.4 %collective-permute-start.12 = (bf16[12,128]{1,0:T(8,128)(2,1)S(1)}, bf16[12,128]{1,0:T(8,128)(2,1)S(1)}, u32[]{:S(2)}, u32[]{:S(2)}) collective-permute-start(bf16[12,128]{1,0:T(8,128)(2,1)S(1)} %reshape.198), channel_id=1, source_target_pairs={{1,13},{2,4},{3,21},{4,12},{5,29},{6,20},{9,15},{10,6},{11,23},{12... | collective-permute-start | bytes 9224 | tf_op jit(solution)/shard_map/ppermute | solution.py:158
  90.7 5.8 %collective-permute-start.13 = (bf16[12,128]{1,0:T(8,128)(2,1)S(1)}, bf16[12,128]{1,0:T(8,128)(2,1)S(1)}, u32[]{:S(2)}, u32[]{:S(2)}) collective-permute-start(bf16[12,128]{1,0:T(8,128)(2,1)S(1)} %reshape.199), channel_id=1, source_target_pairs={{1,14},{2,5},{3,22},{4,13},{5,30},{6,21},{9,8},{10,7},{11,16},{12,... | collective-permute-start | bytes 9224 | tf_op jit(solution)/shard_map/ppermute | solution.py:158
  96.5 0.9 collective-permute-done.13
  98.1 11.6 %collective-permute-start.15 = (bf16[12,128]{1,0:T(8,128)(2,1)S(1)}, bf16[12,128]{1,0:T(8,128)(2,1)S(1)}, u32[]{:S(2)}, u32[]{:S(2)}) collective-permute-start(bf16[12,128]{1,0:T(8,128)(2,1)S(1)} %reshape.201), channel_id=1, source_target_pairs={{1,8},{2,7},{3,16},{4,15},{5,24},{6,23},{9,10},{10,1},{11,18},{12,... | collective-permute-start | bytes 9224 | tf_op jit(solution)/shard_map/ppermute | solution.py:158
  111.9 0.9 squeeze.6
  112.8 0.9 squeeze.7
  114.2 1.0 copy.17
  115.2 4.2 %collective-permute-start.5 = (bf16[8,2,24,512]{3,2,1,0:T(8,128)(2,1)S(1)}, bf16[8,2,24,512]{3,2,1,0:T(8,128)(2,1)S(1)}, u32[]{:S(2)}, u32[]{:S(2)}) collective-permute-start(bf16[8,2,24,512]{3,2,1,0:T(8,128)(2,1)S(1)} %get-tuple-element.7), channel_id=1, source_target_pairs={{0,5},{1,6},{2,13},{3,14},{4,21},{5,22},{6,29},{7,30},{8,7},{9,0},... | collective-permute-start | bytes 1179656 | tf_op jit(solution)/shard_map/ppermute | solution.py:156
  119.4 1.8 bitcast_dynamic-update-slice_fusion.7
  121.1 1.8 bitcast_dynamic-update-slice_fusion.6
  123.0 1.8 bitcast_dynamic-update-slice_fusion.5
  124.8 1.8 bitcast_dynamic-update-slice_fusion.4
  126.5 5.9 %collective-permute-done.4 = bf16[8,2,24,512]{3,2,1,0:T(8,128)(2,1)S(1)} collective-permute-done((bf16[8,2,24,512]{3,2,1,0:T(8,128)(2,1)S(1)}, bf16[8,2,24,512]{3,2,1,0:T(8,128)(2,1)S(1)}, u32[]{:S(2)}, u32[]{:S(2)}) %collective-permute-start.4) | collective-permute-done | bytes 393248 | tf_op jit(solution)/shard_map/ppermute | solution.py:156
  133.3 9.3 %collective-permute-done.5 = bf16[8,2,24,512]{3,2,1,0:T(8,128)(2,1)S(1)} collective-permute-done((bf16[8,2,24,512]{3,2,1,0:T(8,128)(2,1)S(1)}, bf16[8,2,24,512]{3,2,1,0:T(8,128)(2,1)S(1)}, u32[]{:S(2)}, u32[]{:S(2)}) %collective-permute-start.5) | collective-permute-done | bytes 393248 | tf_op jit(solution)/shard_map/ppermute | solution.py:156
  143.4 23.4 %collective-permute-done.6 = bf16[8,2,24,512]{3,2,1,0:T(8,128)(2,1)S(1)} collective-permute-done((bf16[8,2,24,512]{3,2,1,0:T(8,128)(2,1)S(1)}, bf16[8,2,24,512]{3,2,1,0:T(8,128)(2,1)S(1)}, u32[]{:S(2)}, u32[]{:S(2)}) %collective-permute-start.6) | collective-permute-done | bytes 393248 | tf_op jit(solution)/shard_map/ppermute | solution.py:156
  167.6 3.2 %collective-permute-done.7 = bf16[8,2,24,512]{3,2,1,0:T(8,128)(2,1)S(1)} collective-permute-done((bf16[8,2,24,512]{3,2,1,0:T(8,128)(2,1)S(1)}, bf16[8,2,24,512]{3,2,1,0:T(8,128)(2,1)S(1)}, u32[]{:S(2)}, u32[]{:S(2)}) %collective-permute-start.7) | collective-permute-done | bytes 393248 | tf_op jit(solution)/shard_map/ppermute | solution.py:156
  171.6 2.6 %gather_fusion = bf16[8,8,2,24,512]{4,3,2,1,0:T(8,128)(2,1)S(1)} fusion(bf16[8,8,2,24,512]{4,3,2,1,0:T(8,128)(2,1)} %bitcast_dynamic-update-slice_fusion, s32[1024]{0:T(1024)S(1)} %pad_clamp_fusion.2), kind=kCustom, calls=%fused_computation | custom fusion | bytes 6291488 | tf_op jit(solution)/shard_map/jit(_take)/gather | solution.py:163
  174.6 1.3 convert_bitcast_fusion
  176.0 3.4 %copy.14 = bf16[2,64,24,512]{3,2,1,0:T(8,128)(2,1)} copy(bf16[2,64,24,512]{3,1,2,0:T(8,128)(2,1)S(1)} %convert_bitcast_fusion) | data formatting | bytes 6291456 | tf_op jit(solution)/shard_map/convert_element_type | solution.py:173
  179.4 23.9 %shard_map.77 = (f32[32,16,1024]{2,1,0:T(8,128)}, f32[32,16,1024]{2,1,0:T(8,128)}) custom-call(s32[32]{0:T(128)} %pre_ref.1, s32[32]{0:T(128)} %post_ref.1, bf16[2,32,2,24,512]{4,3,2,1,0:T(8,128)(2,1)} %bitcast.73, bf16[32,2,24,128]{3,2,1,0:T(8,128)(2,1)} %bitcast.81, bf16[2,32,2,24,512]{4,3,2,1,0:T(8,128)(2,1)} %bitcast.74, ...), custom_call_target="tpu_custom_call" | custom-call | tf_op jit(solution)/shard_map/pallas_call | solution.py:116
  (75 shorter events, 14.4 us)
Async XLA Ops:
  0.6 14.2 %copy-start = (bf16[8,2,128,512]{3,2,1,0:T(8,128)(2,1)S(1)}, bf16[8,2,128,512]{3,2,1,0:T(8,128)(2,1)}, u32[]{:S(2)}) copy-start(bf16[8,2,128,512]{3,2,1,0:T(8,128)(2,1)} %param.6) | copy-start | bytes 6291460
  5.6 16.0 %copy-start.2 = (bf16[32,32]{1,0:T(8,128)(2,1)S(1)}, bf16[32,32]{1,0:T(8,128)(2,1)}, u32[]{:S(2)}) copy-start(bf16[32,32]{1,0:T(8,128)(2,1)} %param.8) | copy-start | bytes 6148
  5.6 16.9 %copy-start.3 = (bf16[32,32]{1,0:T(8,128)(2,1)S(1)}, bf16[32,32]{1,0:T(8,128)(2,1)}, u32[]{:S(2)}) copy-start(bf16[32,32]{1,0:T(8,128)(2,1)} %param.7) | copy-start | bytes 6148
  5.6 109.6 %collective-permute-start = (bf16[8,2,24,512]{3,2,1,0:T(8,128)(2,1)}, bf16[8,2,24,512]{3,2,1,0:T(8,128)(2,1)}, u32[]{:S(2)}, u32[]{:S(2)}) collective-permute-start(bf16[8,2,24,512]{3,2,1,0:T(8,128)(2,1)} %get-tuple-element.9), channel_id=1, source_target_pairs={{0,0},{1,1},{2,8},{3,9},{4,16},{5,17},{6,24},{7,25},{8,2},{9,3},{1... | collective-permute-start | bytes 1179656 | tf_op jit(solution)/shard_map/ppermute | solution.py:156
  9.8 111.4 %collective-permute-start.1 = (bf16[8,2,24,512]{3,2,1,0:T(8,128)(2,1)}, bf16[8,2,24,512]{3,2,1,0:T(8,128)(2,1)}, u32[]{:S(2)}, u32[]{:S(2)}) collective-permute-start(bf16[8,2,24,512]{3,2,1,0:T(8,128)(2,1)} %get-tuple-element.3), channel_id=1, source_target_pairs={{0,1},{1,2},{2,9},{3,10},{4,17},{5,18},{6,25},{7,26},{8,3},{9,4},{... | collective-permute-start | bytes 1179656 | tf_op jit(solution)/shard_map/ppermute | solution.py:156
  12.7 110.2 %collective-permute-start.2 = (bf16[8,2,24,512]{3,2,1,0:T(8,128)(2,1)}, bf16[8,2,24,512]{3,2,1,0:T(8,128)(2,1)}, u32[]{:S(2)}, u32[]{:S(2)}) collective-permute-start(bf16[8,2,24,512]{3,2,1,0:T(8,128)(2,1)} %get-tuple-element.4), channel_id=1, source_target_pairs={{0,2},{1,3},{2,10},{3,11},{4,18},{5,19},{6,26},{7,27},{8,4},{9,5},... | collective-permute-start | bytes 1179656 | tf_op jit(solution)/shard_map/ppermute | solution.py:156
  14.1 110.7 %collective-permute-start.3 = (bf16[8,2,24,512]{3,2,1,0:T(8,128)(2,1)}, bf16[8,2,24,512]{3,2,1,0:T(8,128)(2,1)}, u32[]{:S(2)}, u32[]{:S(2)}) collective-permute-start(bf16[8,2,24,512]{3,2,1,0:T(8,128)(2,1)} %get-tuple-element.5), channel_id=1, source_target_pairs={{0,3},{1,4},{2,11},{3,12},{4,19},{5,20},{6,27},{7,28},{8,5},{9,6},... | collective-permute-start | bytes 1179656 | tf_op jit(solution)/shard_map/ppermute | solution.py:156
  15.3 95.2 %copy-start.1 = (bf16[8,2,24,512]{3,2,1,0:T(8,128)(2,1)S(1)}, bf16[8,2,24,512]{3,2,1,0:T(8,128)(2,1)}, u32[]{:S(2)}) copy-start(bf16[8,2,24,512]{3,2,1,0:T(8,128)(2,1)} %get-tuple-element.6) | copy-start | bytes 1179652
  15.6 49.8 %collective-permute-start.8 = (bf16[12,128]{1,0:T(8,128)(2,1)S(1)}, bf16[12,128]{1,0:T(8,128)(2,1)S(1)}, u32[]{:S(2)}, u32[]{:S(2)}) collective-permute-start(bf16[12,128]{1,0:T(8,128)(2,1)S(1)} %reshape.194), channel_id=1, source_target_pairs={{1,9},{2,0},{3,17},{4,8},{5,25},{6,16},{9,11},{10,2},{11,19},{12,1... | collective-permute-start | bytes 9224 | tf_op jit(solution)/shard_map/ppermute | solution.py:158
  65.4 7.6 %collective-permute-start.9 = (bf16[12,128]{1,0:T(8,128)(2,1)S(1)}, bf16[12,128]{1,0:T(8,128)(2,1)S(1)}, u32[]{:S(2)}, u32[]{:S(2)}) collective-permute-start(bf16[12,128]{1,0:T(8,128)(2,1)S(1)} %reshape.195), channel_id=1, source_target_pairs={{1,10},{2,1},{3,18},{4,9},{5,26},{6,17},{9,12},{10,3},{11,20},{12,... | collective-permute-start | bytes 9224 | tf_op jit(solution)/shard_map/ppermute | solution.py:158
  73.0 4.3 %collective-permute-start.10 = (bf16[12,128]{1,0:T(8,128)(2,1)S(1)}, bf16[12,128]{1,0:T(8,128)(2,1)S(1)}, u32[]{:S(2)}, u32[]{:S(2)}) collective-permute-start(bf16[12,128]{1,0:T(8,128)(2,1)S(1)} %reshape.196), channel_id=1, source_target_pairs={{1,11},{2,2},{3,19},{4,10},{5,27},{6,18},{9,13},{10,4},{11,21},{12... | collective-permute-start | bytes 9224 | tf_op jit(solution)/shard_map/ppermute | solution.py:158
  77.3 7.2 %collective-permute-start.11 = (bf16[12,128]{1,0:T(8,128)(2,1)S(1)}, bf16[12,128]{1,0:T(8,128)(2,1)S(1)}, u32[]{:S(2)}, u32[]{:S(2)}) collective-permute-start(bf16[12,128]{1,0:T(8,128)(2,1)S(1)} %reshape.197), channel_id=1, source_target_pairs={{1,12},{2,3},{3,20},{4,11},{5,28},{6,19},{9,14},{10,5},{11,22},{12... | collective-permute-start | bytes 9224 | tf_op jit(solution)/shard_map/ppermute | solution.py:158
  84.5 6.1 %collective-permute-start.12 = (bf16[12,128]{1,0:T(8,128)(2,1)S(1)}, bf16[12,128]{1,0:T(8,128)(2,1)S(1)}, u32[]{:S(2)}, u32[]{:S(2)}) collective-permute-start(bf16[12,128]{1,0:T(8,128)(2,1)S(1)} %reshape.198), channel_id=1, source_target_pairs={{1,13},{2,4},{3,21},{4,12},{5,29},{6,20},{9,15},{10,6},{11,23},{12... | collective-permute-start | bytes 9224 | tf_op jit(solution)/shard_map/ppermute | solution.py:158
  90.7 6.7 %collective-permute-start.13 = (bf16[12,128]{1,0:T(8,128)(2,1)S(1)}, bf16[12,128]{1,0:T(8,128)(2,1)S(1)}, u32[]{:S(2)}, u32[]{:S(2)}) collective-permute-start(bf16[12,128]{1,0:T(8,128)(2,1)S(1)} %reshape.199), channel_id=1, source_target_pairs={{1,14},{2,5},{3,22},{4,13},{5,30},{6,21},{9,8},{10,7},{11,16},{12,... | collective-permute-start | bytes 9224 | tf_op jit(solution)/shard_map/ppermute | solution.py:158
  97.4 0.7 collective-permute-start.14
  98.1 12.4 %collective-permute-start.15 = (bf16[12,128]{1,0:T(8,128)(2,1)S(1)}, bf16[12,128]{1,0:T(8,128)(2,1)S(1)}, u32[]{:S(2)}, u32[]{:S(2)}) collective-permute-start(bf16[12,128]{1,0:T(8,128)(2,1)S(1)} %reshape.201), channel_id=1, source_target_pairs={{1,8},{2,7},{3,16},{4,15},{5,24},{6,23},{9,10},{10,1},{11,18},{12,... | collective-permute-start | bytes 9224 | tf_op jit(solution)/shard_map/ppermute | solution.py:158
  110.4 22.0 %collective-permute-start.4 = (bf16[8,2,24,512]{3,2,1,0:T(8,128)(2,1)S(1)}, bf16[8,2,24,512]{3,2,1,0:T(8,128)(2,1)S(1)}, u32[]{:S(2)}, u32[]{:S(2)}) collective-permute-start(bf16[8,2,24,512]{3,2,1,0:T(8,128)(2,1)S(1)} %copy-done.1), channel_id=1, source_target_pairs={{0,4},{1,5},{2,12},{3,13},{4,20},{5,21},{6,28},{7,29},{8,6},{9,7},... | collective-permute-start | bytes 1179656 | tf_op jit(solution)/shard_map/ppermute | solution.py:156
  115.2 27.4 %collective-permute-start.5 = (bf16[8,2,24,512]{3,2,1,0:T(8,128)(2,1)S(1)}, bf16[8,2,24,512]{3,2,1,0:T(8,128)(2,1)S(1)}, u32[]{:S(2)}, u32[]{:S(2)}) collective-permute-start(bf16[8,2,24,512]{3,2,1,0:T(8,128)(2,1)S(1)} %get-tuple-element.7), channel_id=1, source_target_pairs={{0,5},{1,6},{2,13},{3,14},{4,21},{5,22},{6,29},{7,30},{8,7},{9,0},... | collective-permute-start | bytes 1179656 | tf_op jit(solution)/shard_map/ppermute | solution.py:156
  121.1 45.7 %collective-permute-start.6 = (bf16[8,2,24,512]{3,2,1,0:T(8,128)(2,1)S(1)}, bf16[8,2,24,512]{3,2,1,0:T(8,128)(2,1)S(1)}, u32[]{:S(2)}, u32[]{:S(2)}) collective-permute-start(bf16[8,2,24,512]{3,2,1,0:T(8,128)(2,1)S(1)} %get-tuple-element.8), channel_id=1, source_target_pairs={{0,6},{1,7},{2,14},{3,15},{4,22},{5,23},{6,30},{7,31},{8,0},{9,1},... | collective-permute-start | bytes 1179656 | tf_op jit(solution)/shard_map/ppermute | solution.py:156
  122.9 47.9 %collective-permute-start.7 = (bf16[8,2,24,512]{3,2,1,0:T(8,128)(2,1)S(1)}, bf16[8,2,24,512]{3,2,1,0:T(8,128)(2,1)S(1)}, u32[]{:S(2)}, u32[]{:S(2)}) collective-permute-start(bf16[8,2,24,512]{3,2,1,0:T(8,128)(2,1)S(1)} %get-tuple-element.2), channel_id=1, source_target_pairs={{0,7},{1,0},{2,15},{3,8},{4,23},{5,16},{6,31},{7,24},{8,1},{9,2},{... | collective-permute-start | bytes 1179656 | tf_op jit(solution)/shard_map/ppermute | solution.py:156

commit v8 on v5

--- a/solution.py
+++ b/solution.py
@@ -152,8 +152,12 @@
 
     forward = [(i, i + 1) for i in range(n_cols - 1)]
     backward = [(target, source) for source, target in forward]
-    left = lax.ppermute(x[blocks_per_tile - 1, :, :, local_cols - RADIUS :], "tx", forward)
-    right = lax.ppermute(x[0, :, :, :RADIUS], "tx", backward)
+    strip_shape = x.shape[1:3] + (RADIUS,)
+    flat = (2 * count_acq * padded_rows * RADIUS // LANES, LANES)
+    left = x[blocks_per_tile - 1, :, :, local_cols - RADIUS :].reshape(flat)
+    right = x[0, :, :, :RADIUS].reshape(flat)
+    left = lax.ppermute(left, "tx", forward).reshape(strip_shape)
+    right = lax.ppermute(right, "tx", backward).reshape(strip_shape)
     gap = jnp.zeros((2 * count_acq, padded_rows, LANES - 2 * RADIUS), x.dtype)
     edge = jnp.concatenate([right, gap, left], axis=2)
 

time: 145 us -> 145 us (level)
  the two profiles are of different devices: /device:TPU:21 before, /device:TPU:26 now
where the time goes in v8:
time: 145 us; the launch traced here: 144 us
  waiting for transfers between devices  67.8 us (47%)
  local copies, waits for them, and re-layouts  29 us (20%)
  Pallas kernels  23.9 us (16%)
  starting transfers between devices  15.7 us (11%)
  matrix products  3.63 us (3%)
  other arithmetic  3.25 us (2%)
    ppermute x8, waiting for transfers between devices, shards(): received.append(lax.ppermute(chunk, ('tx', 'ty'), pairs))  67.8 us
    pallas_call x1, Pallas kernels, pair_maps(): pl.pallas_call(kernel, grid_spec=grid_spec, out_shape=[out_shape, out_sha...  23.9 us
    unnamed x11, local copies, waits for them, and re-layouts  10.4 us
    ppermute x8, starting transfers between devices, shards(): received.append(lax.ppermute(chunk, ('tx', 'ty'), pairs))  8.76 us
    dynamic_slice x1, local copies, waits for them, and re-layouts, shards(): chunk = lax.dynamic_slice_in_dim(x, first, padded_rows, axis=2)  5.06 us
    ppermute x1, starting transfers between devices, shards(): left = lax.ppermute(left, 'tx', forward).reshape(strip_shape)  4.99 us
    convert_element_type x1, local copies, waits for them, and re-layouts, shards(): main.astype(jnp.bfloat16)  3.39 us
    dot_general x1, matrix products, shards(): jnp.einsum('kc,bchw->bkhw', mixing, x, preferred_element_type=jnp.float32)  3.21 us
  transfers between devices with their start and end apart: 10, of which 7 were waited for; matrix products, arithmetic and copies ran while one was open for 15% of the time, Pallas kernels for 0%

profile of v8, /device:TPU:26, one launch (start us, length us, event | category | flops | bytes accessed | tf_op | source)
XLA Modules:
  0.0 144.3 jit_solution(15245762100136836439)
XLA Ops:
  0.8 5.1 %pad_dynamic-slice_fusion = (bf16[8,2,24,512]{3,2,1,0:T(8,128)(2,1)S(1)}, bf16[8,2,24,512]{3,2,1,0:T(8,128)(2,1)S(1)}, bf16[8,2,24,512]{3,2,1,0:T(8,128)(2,1)S(1...) fusion(s32[]{:T(128)S(6)} %select_n.137, ...), kind=kLoop, calls=%fused_computation.7 | loop fusion | bytes 5242912 | tf_op jit(solution)/shard_map/dynamic_slice | solution.py:145
  5.8 3.2 %collective-permute-start = (bf16[8,2,24,512]{3,2,1,0:T(8,128)(2,1)}, bf16[8,2,24,512]{3,2,1,0:T(8,128)(2,1)}, u32[]{:S(2)}, u32[]{:S(2)}) collective-permute-start(bf16[8,2,24,512]{3,2,1,0:T(8,128)(2,1)} %get-tuple-element.11), channel_id=1, source_target_pairs={{0,0},{1,1},{2,8},{3,9},{4,16},{5,17},{6,24},{7,25},{8,2},{9,3},{1... | collective-permute-start | bytes 1179656 | tf_op jit(solution)/shard_map/ppermute | solution.py:146
  9.0 1.7 %collective-permute-start.1 = (bf16[8,2,24,512]{3,2,1,0:T(8,128)(2,1)S(1)}, bf16[8,2,24,512]{3,2,1,0:T(8,128)(2,1)}, u32[]{:S(2)}, u32[]{:S(2)}) collective-permute-start(bf16[8,2,24,512]{3,2,1,0:T(8,128)(2,1)S(1)} %get-tuple-element.5), channel_id=1, source_target_pairs={{0,1},{1,2},{2,9},{3,10},{4,17},{5,18},{6,25},{7,26},{8,3},{9,4},{... | collective-permute-start | bytes 1179656 | tf_op jit(solution)/shard_map/ppermute | solution.py:146
  11.3 3.3 %collective-permute-start.3 = (bf16[8,2,24,512]{3,2,1,0:T(8,128)(2,1)S(1)}, bf16[8,2,24,512]{3,2,1,0:T(8,128)(2,1)}, u32[]{:S(2)}, u32[]{:S(2)}) collective-permute-start(bf16[8,2,24,512]{3,2,1,0:T(8,128)(2,1)S(1)} %get-tuple-element.7), channel_id=1, source_target_pairs={{0,3},{1,4},{2,11},{3,12},{4,19},{5,20},{6,27},{7,28},{8,5},{9,6},... | collective-permute-start | bytes 1179656 | tf_op jit(solution)/shard_map/ppermute | solution.py:146
  15.5 0.8 reshape.143
  16.3 0.8 reshape.142
  17.4 0.7 pad_maximum_fusion.refs_16_
  18.1 15.3 %collective-permute-done = bf16[8,2,24,512]{3,2,1,0:T(8,128)(2,1)} collective-permute-done((bf16[8,2,24,512]{3,2,1,0:T(8,128)(2,1)}, bf16[8,2,24,512]{3,2,1,0:T(8,128)(2,1)}, u32[]{:S(2)}, u32[]{:S(2)}) %collective-permute-start) | collective-permute-done | bytes 393248 | tf_op jit(solution)/shard_map/ppermute | solution.py:146
  33.4 1.8 %bitcast_dynamic-update-slice_fusion.7 = bf16[8,8,2,24,512]{4,3,2,1,0:T(8,128)(2,1)} fusion(bf16[8,2,24,512]{3,2,1,0:T(8,128)(2,1)} %collective-permute-done), kind=kLoop, calls=%fused_computation.26 | loop fusion | bytes 786432
  35.2 23.2 %collective-permute-done.1 = bf16[8,2,24,512]{3,2,1,0:T(8,128)(2,1)} collective-permute-done((bf16[8,2,24,512]{3,2,1,0:T(8,128)(2,1)S(1)}, bf16[8,2,24,512]{3,2,1,0:T(8,128)(2,1)}, u32[]{:S(2)}, u32[]{:S(2)}) %collective-permute-start.1) | collective-permute-done | bytes 393248 | tf_op jit(solution)/shard_map/ppermute | solution.py:146
  58.4 1.8 %bitcast_dynamic-update-slice_fusion.6 = bf16[8,8,2,24,512]{4,3,2,1,0:T(8,128)(2,1)} fusion(bf16[8,8,2,24,512]{4,3,2,1,0:T(8,128)(2,1)} %bitcast_dynamic-update-slice_fusion.7, bf16[8,2,24,512]{3,2,1,0:T(8,128)(2,1)} %collective-permute-done.1), kind=kLoop, calls=%fused_computation.25 | loop fusion | bytes 786432
  60.2 6.7 %collective-permute-done.2 = bf16[8,2,24,512]{3,2,1,0:T(8,128)(2,1)} collective-permute-done((bf16[8,2,24,512]{3,2,1,0:T(8,128)(2,1)S(1)}, bf16[8,2,24,512]{3,2,1,0:T(8,128)(2,1)}, u32[]{:S(2)}, u32[]{:S(2)}) %collective-permute-start.2) | collective-permute-done | bytes 393248 | tf_op jit(solution)/shard_map/ppermute | solution.py:146
  66.9 1.8 %bitcast_dynamic-update-slice_fusion.5 = bf16[8,8,2,24,512]{4,3,2,1,0:T(8,128)(2,1)} fusion(bf16[8,8,2,24,512]{4,3,2,1,0:T(8,128)(2,1)} %bitcast_dynamic-update-slice_fusion.6, bf16[8,2,24,512]{3,2,1,0:T(8,128)(2,1)} %collective-permute-done.2), kind=kLoop, calls=%fused_computation.24 | loop fusion | bytes 786432
  68.9 1.8 %bitcast_dynamic-update-slice_fusion.4 = bf16[8,8,2,24,512]{4,3,2,1,0:T(8,128)(2,1)} fusion(bf16[8,8,2,24,512]{4,3,2,1,0:T(8,128)(2,1)} %bitcast_dynamic-update-slice_fusion.5, bf16[8,2,24,512]{3,2,1,0:T(8,128)(2,1)} %collective-permute-done.3), kind=kLoop, calls=%fused_computation.23 | loop fusion | bytes 786432
  70.7 2.7 %collective-permute-done.4 = bf16[8,2,24,512]{3,2,1,0:T(8,128)(2,1)} collective-permute-done((bf16[8,2,24,512]{3,2,1,0:T(8,128)(2,1)S(1)}, bf16[8,2,24,512]{3,2,1,0:T(8,128)(2,1)}, u32[]{:S(2)}, u32[]{:S(2)}) %collective-permute-start.4) | collective-permute-done | bytes 393248 | tf_op jit(solution)/shard_map/ppermute | solution.py:146
  73.4 1.8 %bitcast_dynamic-update-slice_fusion.3 = bf16[8,8,2,24,512]{4,3,2,1,0:T(8,128)(2,1)} fusion(bf16[8,8,2,24,512]{4,3,2,1,0:T(8,128)(2,1)} %bitcast_dynamic-update-slice_fusion.4, bf16[8,2,24,512]{3,2,1,0:T(8,128)(2,1)} %collective-permute-done.4), kind=kLoop, calls=%fused_computation.22 | loop fusion | bytes 786432
  75.2 0.8 bitcast_dynamic-update-slice_fusion.2
  75.9 3.4 %collective-permute-done.6 = bf16[8,2,24,512]{3,2,1,0:T(8,128)(2,1)S(1)} collective-permute-done((bf16[8,2,24,512]{3,2,1,0:T(8,128)(2,1)S(1)}, bf16[8,2,24,512]{3,2,1,0:T(8,128)(2,1)S(1)}, u32[]{:S(2)}, u32[]{:S(2)}) %collective-permute-start.6) | collective-permute-done | bytes 393248 | tf_op jit(solution)/shard_map/ppermute | solution.py:146
  79.4 0.8 bitcast_dynamic-update-slice_fusion.1
  80.1 16.3 %collective-permute-done.7 = bf16[8,2,24,512]{3,2,1,0:T(8,128)(2,1)S(1)} collective-permute-done((bf16[8,2,24,512]{3,2,1,0:T(8,128)(2,1)S(1)}, bf16[8,2,24,512]{3,2,1,0:T(8,128)(2,1)S(1)}, u32[]{:S(2)}, u32[]{:S(2)}) %collective-permute-start.7) | collective-permute-done | bytes 393248 | tf_op jit(solution)/shard_map/ppermute | solution.py:146
  96.4 0.8 bitcast_dynamic-update-slice_fusion
  97.2 2.6 %gather_fusion = bf16[8,8,2,24,512]{4,3,2,1,0:T(8,128)(2,1)S(1)} fusion(bf16[8,8,2,24,512]{4,3,2,1,0:T(8,128)(2,1)} %bitcast_dynamic-update-slice_fusion, s32[1024]{0:T(1024)S(1)} %pad_clamp_fusion), kind=kCustom, calls=%fused_computation | custom fusion | bytes 6291488 | tf_op jit(solution)/shard_map/jit(_take)/gather | solution.py:150
  99.8 2.0 %broadcast_select_fusion = bf16[8,8,2,24,512]{4,3,2,1,0:T(8,128)(2,1)} fusion(bf16[8,8,2,24,512]{4,3,2,1,0:T(8,128)(2,1)S(1)} %gather_fusion, pred[8]{0:T(512)(128)(4,1)S(1)} %compare_and_fusion), kind=kLoop, calls=%fused_computation.4 | loop fusion | flops 1572864 | bytes 6291464 | tf_op jit(solution)/shard_map/jit(_take)/select_n | solution.py:150
  102.4 0.5 reshape_squeeze.6
  102.9 1.9 %collective-permute-start.8 = (bf16[48,128]{1,0:T(8,128)(2,1)S(1)}, bf16[48,128]{1,0:T(8,128)(2,1)S(1)}, u32[]{:S(2)}, u32[]{:S(2)}) collective-permute-start(bf16[48,128]{1,0:T(8,128)(2,1)S(1)} %reshape_squeeze.6), channel_id=1, source_target_pairs={{8,0},{16,8},{24,16},{9,1},{17,9},{25,17},{10,2},{18,10},{26,18},{... | collective-permute-start | bytes 36872 | tf_op jit(solution)/shard_map/ppermute | solution.py:160
  105.4 5.0 %collective-permute-start.9 = (bf16[48,128]{1,0:T(8,128)(2,1)S(1)}, bf16[48,128]{1,0:T(8,128)(2,1)S(1)}, u32[]{:S(2)}, u32[]{:S(2)}) collective-permute-start(bf16[48,128]{1,0:T(8,128)(2,1)S(1)} %reshape_squeeze.7), channel_id=1, source_target_pairs={{0,8},{8,16},{16,24},{1,9},{9,17},{17,25},{2,10},{10,18},{18,26},{... | collective-permute-start | bytes 36872 | tf_op jit(solution)/shard_map/ppermute | solution.py:159
  110.4 3.2 %convert_bitcast_fusion = bf16[2,64,24,512]{3,1,2,0:T(8,128)(2,1)S(1)} fusion(bf16[2,64,24,512]{3,2,1,0:T(8,128)(2,1)} %bitcast.61, bf16[64,64,1,1]{1,0,2,3:T(8,128)(2,1)S(1)} %reshape.142), kind=kOutput, calls=%fused_computation.3 | convolution fusion | flops 202899456 | bytes 6299648 | tf_op jit(solution)/shard_map/kc,bchw->bkhw/dot_general | solution.py:166
  113.6 3.4 %copy.13 = bf16[2,64,24,512]{3,2,1,0:T(8,128)(2,1)} copy(bf16[2,64,24,512]{3,1,2,0:T(8,128)(2,1)S(1)} %convert_bitcast_fusion) | data formatting | bytes 6291456 | tf_op jit(solution)/shard_map/convert_element_type | solution.py:167
  117.0 0.8 reshape.131
  117.9 0.8 reshape.132
  119.3 1.0 copy.16
  120.3 23.9 %shard_map.68 = (f32[32,16,1024]{2,1,0:T(8,128)}, f32[32,16,1024]{2,1,0:T(8,128)}) custom-call(s32[32]{0:T(128)} %pre_ref.1, s32[32]{0:T(128)} %post_ref.1, bf16[2,32,2,24,512]{4,3,2,1,0:T(8,128)(2,1)} %bitcast.44, bf16[32,2,24,128]{3,2,1,0:T(8,128)(2,1)} %bitcast.52, bf16[2,32,2,24,512]{4,3,2,1,0:T(8,128)(2,1)} %bitcast.45, ...), custom_call_target="tpu_custom_call" | custom-call | tf_op jit(solution)/shard_map/pallas_call | solution.py:116
  (36 shorter events, 3.5 us)
Async XLA Ops:
  0.6 14.2 %copy-start = (bf16[32,32]{1,0:T(8,128)(2,1)S(1)}, bf16[32,32]{1,0:T(8,128)(2,1)}, u32[]{:S(2)}) copy-start(bf16[32,32]{1,0:T(8,128)(2,1)} %param.7) | copy-start | bytes 6148
  0.6 14.3 %copy-start.1 = (bf16[32,32]{1,0:T(8,128)(2,1)S(1)}, bf16[32,32]{1,0:T(8,128)(2,1)}, u32[]{:S(2)}) copy-start(bf16[32,32]{1,0:T(8,128)(2,1)} %param.6) | copy-start | bytes 6148
  5.8 27.6 %collective-permute-start = (bf16[8,2,24,512]{3,2,1,0:T(8,128)(2,1)}, bf16[8,2,24,512]{3,2,1,0:T(8,128)(2,1)}, u32[]{:S(2)}, u32[]{:S(2)}) collective-permute-start(bf16[8,2,24,512]{3,2,1,0:T(8,128)(2,1)} %get-tuple-element.11), channel_id=1, source_target_pairs={{0,0},{1,1},{2,8},{3,9},{4,16},{5,17},{6,24},{7,25},{8,2},{9,3},{1... | collective-permute-start | bytes 1179656 | tf_op jit(solution)/shard_map/ppermute | solution.py:146
  9.0 49.3 %collective-permute-start.1 = (bf16[8,2,24,512]{3,2,1,0:T(8,128)(2,1)S(1)}, bf16[8,2,24,512]{3,2,1,0:T(8,128)(2,1)}, u32[]{:S(2)}, u32[]{:S(2)}) collective-permute-start(bf16[8,2,24,512]{3,2,1,0:T(8,128)(2,1)S(1)} %get-tuple-element.5), channel_id=1, source_target_pairs={{0,1},{1,2},{2,9},{3,10},{4,17},{5,18},{6,25},{7,26},{8,3},{9,4},{... | collective-permute-start | bytes 1179656 | tf_op jit(solution)/shard_map/ppermute | solution.py:146
  10.8 56.1 %collective-permute-start.2 = (bf16[8,2,24,512]{3,2,1,0:T(8,128)(2,1)S(1)}, bf16[8,2,24,512]{3,2,1,0:T(8,128)(2,1)}, u32[]{:S(2)}, u32[]{:S(2)}) collective-permute-start(bf16[8,2,24,512]{3,2,1,0:T(8,128)(2,1)S(1)} %get-tuple-element.6), channel_id=1, source_target_pairs={{0,2},{1,3},{2,10},{3,11},{4,18},{5,19},{6,26},{7,27},{8,4},{9,5},... | collective-permute-start | bytes 1179656 | tf_op jit(solution)/shard_map/ppermute | solution.py:146
  11.3 57.6 %collective-permute-start.3 = (bf16[8,2,24,512]{3,2,1,0:T(8,128)(2,1)S(1)}, bf16[8,2,24,512]{3,2,1,0:T(8,128)(2,1)}, u32[]{:S(2)}, u32[]{:S(2)}) collective-permute-start(bf16[8,2,24,512]{3,2,1,0:T(8,128)(2,1)S(1)} %get-tuple-element.7), channel_id=1, source_target_pairs={{0,3},{1,4},{2,11},{3,12},{4,19},{5,20},{6,27},{7,28},{8,5},{9,6},... | collective-permute-start | bytes 1179656 | tf_op jit(solution)/shard_map/ppermute | solution.py:146
  14.6 58.8 %collective-permute-start.4 = (bf16[8,2,24,512]{3,2,1,0:T(8,128)(2,1)S(1)}, bf16[8,2,24,512]{3,2,1,0:T(8,128)(2,1)}, u32[]{:S(2)}, u32[]{:S(2)}) collective-permute-start(bf16[8,2,24,512]{3,2,1,0:T(8,128)(2,1)S(1)} %get-tuple-element.8), channel_id=1, source_target_pairs={{0,4},{1,5},{2,12},{3,13},{4,20},{5,21},{6,28},{7,29},{8,6},{9,7},... | collective-permute-start | bytes 1179656 | tf_op jit(solution)/shard_map/ppermute | solution.py:146
  33.4 41.7 %collective-permute-start.5 = (bf16[8,2,24,512]{3,2,1,0:T(8,128)(2,1)S(1)}, bf16[8,2,24,512]{3,2,1,0:T(8,128)(2,1)S(1)}, u32[]{:S(2)}, u32[]{:S(2)}) collective-permute-start(bf16[8,2,24,512]{3,2,1,0:T(8,128)(2,1)S(1)} %get-tuple-element.9), channel_id=1, source_target_pairs={{0,5},{1,6},{2,13},{3,14},{4,21},{5,22},{6,29},{7,30},{8,7},{9,0},... | collective-permute-start | bytes 1179656 | tf_op jit(solution)/shard_map/ppermute | solution.py:146
  58.4 21.0 %collective-permute-start.6 = (bf16[8,2,24,512]{3,2,1,0:T(8,128)(2,1)S(1)}, bf16[8,2,24,512]{3,2,1,0:T(8,128)(2,1)S(1)}, u32[]{:S(2)}, u32[]{:S(2)}) collective-permute-start(bf16[8,2,24,512]{3,2,1,0:T(8,128)(2,1)S(1)} %get-tuple-element.10), channel_id=1, source_target_pairs={{0,6},{1,7},{2,14},{3,15},{4,22},{5,23},{6,30},{7,31},{8,0},{9,1},... | collective-permute-start | bytes 1179656 | tf_op jit(solution)/shard_map/ppermute | solution.py:146
  66.9 29.5 %collective-permute-start.7 = (bf16[8,2,24,512]{3,2,1,0:T(8,128)(2,1)S(1)}, bf16[8,2,24,512]{3,2,1,0:T(8,128)(2,1)S(1)}, u32[]{:S(2)}, u32[]{:S(2)}) collective-permute-start(bf16[8,2,24,512]{3,2,1,0:T(8,128)(2,1)S(1)} %get-tuple-element.4), channel_id=1, source_target_pairs={{0,7},{1,0},{2,15},{3,8},{4,23},{5,16},{6,31},{7,24},{8,1},{9,2},{... | collective-permute-start | bytes 1179656 | tf_op jit(solution)/shard_map/ppermute | solution.py:146
  102.9 14.1 %collective-permute-start.8 = (bf16[48,128]{1,0:T(8,128)(2,1)S(1)}, bf16[48,128]{1,0:T(8,128)(2,1)S(1)}, u32[]{:S(2)}, u32[]{:S(2)}) collective-permute-start(bf16[48,128]{1,0:T(8,128)(2,1)S(1)} %reshape_squeeze.6), channel_id=1, source_target_pairs={{8,0},{16,8},{24,16},{9,1},{17,9},{25,17},{10,2},{18,10},{26,18},{... | collective-permute-start | bytes 36872 | tf_op jit(solution)/shard_map/ppermute | solution.py:160
  105.4 12.6 %collective-permute-start.9 = (bf16[48,128]{1,0:T(8,128)(2,1)S(1)}, bf16[48,128]{1,0:T(8,128)(2,1)S(1)}, u32[]{:S(2)}, u32[]{:S(2)}) collective-permute-start(bf16[48,128]{1,0:T(8,128)(2,1)S(1)} %reshape_squeeze.7), channel_id=1, source_target_pairs={{0,8},{8,16},{16,24},{1,9},{9,17},{17,25},{2,10},{10,18},{18,26},{... | collective-permute-start | bytes 36872 | tf_op jit(solution)/shard_map/ppermute | solution.py:159

commit v9 on v8

--- a/solution.py
+++ b/solution.py
@@ -11,6 +11,22 @@
 LANES = 128
 PAIRS_PER_STEP = 4
 FIELDS = 4
+
+
+def window_rows(full, window):
+    count = full.shape[0]
+    total, offset, span, part = None, 0, 1, full
+    remaining = window
+    while remaining:
+        if remaining & 1:
+            shifted = part if offset == 0 else pltpu.roll(part, count - offset, 0)
+            total = shifted if total is None else total + shifted
+            offset += span
+        remaining >>= 1
+        if remaining:
+            part = part + pltpu.roll(part, count - span, 0)
+            span *= 2
+    return total
 
 
 def pair_kernel(pre_ref, post_ref, *refs, tile_rows, tile_cols):
@@ -36,9 +52,7 @@
             for f, value in enumerate(fields):
                 field_ref[f, :, pl.ds(at, width)] = value
         for f in range(FIELDS):
-            acc = field_ref[f, pl.ds(0, tile_rows), :]
-            for k in range(1, window):
-                acc = acc + field_ref[f, pl.ds(k, tile_rows), :]
+            acc = window_rows(field_ref[f], window)[:tile_rows]
             at = (p * FIELDS + f) * tile_rows
             rows_ref[pl.ds(at, tile_rows), pl.ds(LANES, padded_cols)] = acc
             rows_ref[pl.ds(at, tile_rows), pl.ds(0, LANES)] = acc[:, padded_cols - LANES :]

time: 145 us -> 141 us (0.972)
  Pallas kernels: 23.9 us -> 19.5 us
    pallas_call x1, Pallas kernels: 23.9 us -> 19.5 us  [pair_maps(): pl.pallas_call(kernel, grid_spec=grid_spec, out_shape=[out_shape, out_sha...]
  transfers between devices with their start and end apart: 10 -> 10, of which waited for: 7 -> 7; matrix products, arithmetic and copies ran while one was open for 15% -> 16% of each run, Pallas kernels for 0% -> 0%
where the time goes in v9:
time: 141 us; the launch traced here: 140 us
  waiting for transfers between devices  67.8 us (48%)
  local copies, waits for them, and re-layouts  29 us (21%)
  Pallas kernels  19.5 us (14%)
  starting transfers between devices  15.7 us (11%)
  matrix products  3.63 us (3%)
  other arithmetic  3.25 us (2%)
    ppermute x8, waiting for transfers between devices, shards(): received.append(lax.ppermute(chunk, ('tx', 'ty'), pairs))  67.8 us
    pallas_call x1, Pallas kernels, pair_maps(): pl.pallas_call(kernel, grid_spec=grid_spec, out_shape=[out_shape, out_sha...  19.5 us
    unnamed x11, local copies, waits for them, and re-layouts  10.4 us
    ppermute x8, starting transfers between devices, shards(): received.append(lax.ppermute(chunk, ('tx', 'ty'), pairs))  8.76 us
    dynamic_slice x1, local copies, waits for them, and re-layouts, shards(): chunk = lax.dynamic_slice_in_dim(x, first, padded_rows, axis=2)  5.06 us
    ppermute x1, starting transfers between devices, shards(): left = lax.ppermute(left, 'tx', forward).reshape(strip_shape)  4.99 us
    convert_element_type x1, local copies, waits for them, and re-layouts, shards(): main.astype(jnp.bfloat16)  3.39 us
    dot_general x1, matrix products, shards(): jnp.einsum('kc,bchw->bkhw', mixing, x, preferred_element_type=jnp.float32)  3.21 us
  transfers between devices with their start and end apart: 10, of which 7 were waited for; matrix products, arithmetic and copies ran while one was open for 16% of the time, Pallas kernels for 0%

profile of v9, /device:TPU:26, one launch (start us, length us, event | category | flops | bytes accessed | tf_op | source)
XLA Modules:
  0.0 139.9 jit_solution(15328348057581908149)
XLA Ops:
  0.8 5.1 %pad_dynamic-slice_fusion = (bf16[8,2,24,512]{3,2,1,0:T(8,128)(2,1)S(1)}, bf16[8,2,24,512]{3,2,1,0:T(8,128)(2,1)S(1)}, bf16[8,2,24,512]{3,2,1,0:T(8,128)(2,1)S(1...) fusion(s32[]{:T(128)S(6)} %select_n.137, ...), kind=kLoop, calls=%fused_computation.7 | loop fusion | bytes 5242912 | tf_op jit(solution)/shard_map/dynamic_slice | solution.py:159
  5.8 3.2 %collective-permute-start = (bf16[8,2,24,512]{3,2,1,0:T(8,128)(2,1)}, bf16[8,2,24,512]{3,2,1,0:T(8,128)(2,1)}, u32[]{:S(2)}, u32[]{:S(2)}) collective-permute-start(bf16[8,2,24,512]{3,2,1,0:T(8,128)(2,1)} %get-tuple-element.11), channel_id=1, source_target_pairs={{0,0},{1,1},{2,8},{3,9},{4,16},{5,17},{6,24},{7,25},{8,2},{9,3},{1... | collective-permute-start | bytes 1179656 | tf_op jit(solution)/shard_map/ppermute | solution.py:160
  9.0 1.7 %collective-permute-start.1 = (bf16[8,2,24,512]{3,2,1,0:T(8,128)(2,1)S(1)}, bf16[8,2,24,512]{3,2,1,0:T(8,128)(2,1)}, u32[]{:S(2)}, u32[]{:S(2)}) collective-permute-start(bf16[8,2,24,512]{3,2,1,0:T(8,128)(2,1)S(1)} %get-tuple-element.5), channel_id=1, source_target_pairs={{0,1},{1,2},{2,9},{3,10},{4,17},{5,18},{6,25},{7,26},{8,3},{9,4},{... | collective-permute-start | bytes 1179656 | tf_op jit(solution)/shard_map/ppermute | solution.py:160
  11.3 3.3 %collective-permute-start.3 = (bf16[8,2,24,512]{3,2,1,0:T(8,128)(2,1)S(1)}, bf16[8,2,24,512]{3,2,1,0:T(8,128)(2,1)}, u32[]{:S(2)}, u32[]{:S(2)}) collective-permute-start(bf16[8,2,24,512]{3,2,1,0:T(8,128)(2,1)S(1)} %get-tuple-element.7), channel_id=1, source_target_pairs={{0,3},{1,4},{2,11},{3,12},{4,19},{5,20},{6,27},{7,28},{8,5},{9,6},... | collective-permute-start | bytes 1179656 | tf_op jit(solution)/shard_map/ppermute | solution.py:160
  15.5 0.8 reshape.143
  16.3 0.8 reshape.142
  17.4 0.7 pad_maximum_fusion.refs_16_
  18.1 15.3 %collective-permute-done = bf16[8,2,24,512]{3,2,1,0:T(8,128)(2,1)} collective-permute-done((bf16[8,2,24,512]{3,2,1,0:T(8,128)(2,1)}, bf16[8,2,24,512]{3,2,1,0:T(8,128)(2,1)}, u32[]{:S(2)}, u32[]{:S(2)}) %collective-permute-start) | collective-permute-done | bytes 393248 | tf_op jit(solution)/shard_map/ppermute | solution.py:160
  33.4 1.8 %bitcast_dynamic-update-slice_fusion.7 = bf16[8,8,2,24,512]{4,3,2,1,0:T(8,128)(2,1)} fusion(bf16[8,2,24,512]{3,2,1,0:T(8,128)(2,1)} %collective-permute-done), kind=kLoop, calls=%fused_computation.26 | loop fusion | bytes 786432
  35.2 23.2 %collective-permute-done.1 = bf16[8,2,24,512]{3,2,1,0:T(8,128)(2,1)} collective-permute-done((bf16[8,2,24,512]{3,2,1,0:T(8,128)(2,1)S(1)}, bf16[8,2,24,512]{3,2,1,0:T(8,128)(2,1)}, u32[]{:S(2)}, u32[]{:S(2)}) %collective-permute-start.1) | collective-permute-done | bytes 393248 | tf_op jit(solution)/shard_map/ppermute | solution.py:160
  58.4 1.8 %bitcast_dynamic-update-slice_fusion.6 = bf16[8,8,2,24,512]{4,3,2,1,0:T(8,128)(2,1)} fusion(bf16[8,8,2,24,512]{4,3,2,1,0:T(8,128)(2,1)} %bitcast_dynamic-update-slice_fusion.7, bf16[8,2,24,512]{3,2,1,0:T(8,128)(2,1)} %collective-permute-done.1), kind=kLoop, calls=%fused_computation.25 | loop fusion | bytes 786432
  60.2 6.7 %collective-permute-done.2 = bf16[8,2,24,512]{3,2,1,0:T(8,128)(2,1)} collective-permute-done((bf16[8,2,24,512]{3,2,1,0:T(8,128)(2,1)S(1)}, bf16[8,2,24,512]{3,2,1,0:T(8,128)(2,1)}, u32[]{:S(2)}, u32[]{:S(2)}) %collective-permute-start.2) | collective-permute-done | bytes 393248 | tf_op jit(solution)/shard_map/ppermute | solution.py:160
  66.9 1.8 %bitcast_dynamic-update-slice_fusion.5 = bf16[8,8,2,24,512]{4,3,2,1,0:T(8,128)(2,1)} fusion(bf16[8,8,2,24,512]{4,3,2,1,0:T(8,128)(2,1)} %bitcast_dynamic-update-slice_fusion.6, bf16[8,2,24,512]{3,2,1,0:T(8,128)(2,1)} %collective-permute-done.2), kind=kLoop, calls=%fused_computation.24 | loop fusion | bytes 786432
  68.9 1.8 %bitcast_dynamic-update-slice_fusion.4 = bf16[8,8,2,24,512]{4,3,2,1,0:T(8,128)(2,1)} fusion(bf16[8,8,2,24,512]{4,3,2,1,0:T(8,128)(2,1)} %bitcast_dynamic-update-slice_fusion.5, bf16[8,2,24,512]{3,2,1,0:T(8,128)(2,1)} %collective-permute-done.3), kind=kLoop, calls=%fused_computation.23 | loop fusion | bytes 786432
  70.7 2.7 %collective-permute-done.4 = bf16[8,2,24,512]{3,2,1,0:T(8,128)(2,1)} collective-permute-done((bf16[8,2,24,512]{3,2,1,0:T(8,128)(2,1)S(1)}, bf16[8,2,24,512]{3,2,1,0:T(8,128)(2,1)}, u32[]{:S(2)}, u32[]{:S(2)}) %collective-permute-start.4) | collective-permute-done | bytes 393248 | tf_op jit(solution)/shard_map/ppermute | solution.py:160
  73.4 1.8 %bitcast_dynamic-update-slice_fusion.3 = bf16[8,8,2,24,512]{4,3,2,1,0:T(8,128)(2,1)} fusion(bf16[8,8,2,24,512]{4,3,2,1,0:T(8,128)(2,1)} %bitcast_dynamic-update-slice_fusion.4, bf16[8,2,24,512]{3,2,1,0:T(8,128)(2,1)} %collective-permute-done.4), kind=kLoop, calls=%fused_computation.22 | loop fusion | bytes 786432
  75.2 0.8 bitcast_dynamic-update-slice_fusion.2
  75.9 3.4 %collective-permute-done.6 = bf16[8,2,24,512]{3,2,1,0:T(8,128)(2,1)S(1)} collective-permute-done((bf16[8,2,24,512]{3,2,1,0:T(8,128)(2,1)S(1)}, bf16[8,2,24,512]{3,2,1,0:T(8,128)(2,1)S(1)}, u32[]{:S(2)}, u32[]{:S(2)}) %collective-permute-start.6) | collective-permute-done | bytes 393248 | tf_op jit(solution)/shard_map/ppermute | solution.py:160
  79.4 0.8 bitcast_dynamic-update-slice_fusion.1
  80.1 16.3 %collective-permute-done.7 = bf16[8,2,24,512]{3,2,1,0:T(8,128)(2,1)S(1)} collective-permute-done((bf16[8,2,24,512]{3,2,1,0:T(8,128)(2,1)S(1)}, bf16[8,2,24,512]{3,2,1,0:T(8,128)(2,1)S(1)}, u32[]{:S(2)}, u32[]{:S(2)}) %collective-permute-start.7) | collective-permute-done | bytes 393248 | tf_op jit(solution)/shard_map/ppermute | solution.py:160
  96.4 0.8 bitcast_dynamic-update-slice_fusion
  97.2 2.6 %gather_fusion = bf16[8,8,2,24,512]{4,3,2,1,0:T(8,128)(2,1)S(1)} fusion(bf16[8,8,2,24,512]{4,3,2,1,0:T(8,128)(2,1)} %bitcast_dynamic-update-slice_fusion, s32[1024]{0:T(1024)S(1)} %pad_clamp_fusion), kind=kCustom, calls=%fused_computation | custom fusion | bytes 6291488 | tf_op jit(solution)/shard_map/jit(_take)/gather | solution.py:164
  99.8 2.0 %broadcast_select_fusion = bf16[8,8,2,24,512]{4,3,2,1,0:T(8,128)(2,1)} fusion(bf16[8,8,2,24,512]{4,3,2,1,0:T(8,128)(2,1)S(1)} %gather_fusion, pred[8]{0:T(512)(128)(4,1)S(1)} %compare_and_fusion), kind=kLoop, calls=%fused_computation.4 | loop fusion | flops 1572864 | bytes 6291464 | tf_op jit(solution)/shard_map/jit(_take)/select_n | solution.py:164
  102.4 0.5 reshape_squeeze.6
  102.9 1.9 %collective-permute-start.8 = (bf16[48,128]{1,0:T(8,128)(2,1)S(1)}, bf16[48,128]{1,0:T(8,128)(2,1)S(1)}, u32[]{:S(2)}, u32[]{:S(2)}) collective-permute-start(bf16[48,128]{1,0:T(8,128)(2,1)S(1)} %reshape_squeeze.6), channel_id=1, source_target_pairs={{8,0},{16,8},{24,16},{9,1},{17,9},{25,17},{10,2},{18,10},{26,18},{... | collective-permute-start | bytes 36872 | tf_op jit(solution)/shard_map/ppermute | solution.py:174
  105.4 5.0 %collective-permute-start.9 = (bf16[48,128]{1,0:T(8,128)(2,1)S(1)}, bf16[48,128]{1,0:T(8,128)(2,1)S(1)}, u32[]{:S(2)}, u32[]{:S(2)}) collective-permute-start(bf16[48,128]{1,0:T(8,128)(2,1)S(1)} %reshape_squeeze.7), channel_id=1, source_target_pairs={{0,8},{8,16},{16,24},{1,9},{9,17},{17,25},{2,10},{10,18},{18,26},{... | collective-permute-start | bytes 36872 | tf_op jit(solution)/shard_map/ppermute | solution.py:173
  110.4 3.2 %convert_bitcast_fusion = bf16[2,64,24,512]{3,1,2,0:T(8,128)(2,1)S(1)} fusion(bf16[2,64,24,512]{3,2,1,0:T(8,128)(2,1)} %bitcast.61, bf16[64,64,1,1]{1,0,2,3:T(8,128)(2,1)S(1)} %reshape.142), kind=kOutput, calls=%fused_computation.3 | convolution fusion | flops 202899456 | bytes 6299648 | tf_op jit(solution)/shard_map/kc,bchw->bkhw/dot_general | solution.py:180
  113.6 3.4 %copy.13 = bf16[2,64,24,512]{3,2,1,0:T(8,128)(2,1)} copy(bf16[2,64,24,512]{3,1,2,0:T(8,128)(2,1)S(1)} %convert_bitcast_fusion) | data formatting | bytes 6291456 | tf_op jit(solution)/shard_map/convert_element_type | solution.py:181
  117.0 0.8 reshape.131
  117.9 0.8 reshape.132
  119.3 1.0 copy.16
  120.3 19.5 %shard_map.68 = (f32[32,16,1024]{2,1,0:T(8,128)}, f32[32,16,1024]{2,1,0:T(8,128)}) custom-call(s32[32]{0:T(128)} %pre_ref.1, s32[32]{0:T(128)} %post_ref.1, bf16[2,32,2,24,512]{4,3,2,1,0:T(8,128)(2,1)} %bitcast.44, bf16[32,2,24,128]{3,2,1,0:T(8,128)(2,1)} %bitcast.52, bf16[2,32,2,24,512]{4,3,2,1,0:T(8,128)(2,1)} %bitcast.45, ...), custom_call_target="tpu_custom_call" | custom-call | tf_op jit(solution)/shard_map/pallas_call | solution.py:130
  (36 shorter events, 3.5 us)
Async XLA Ops:
  0.6 14.2 %copy-start = (bf16[32,32]{1,0:T(8,128)(2,1)S(1)}, bf16[32,32]{1,0:T(8,128)(2,1)}, u32[]{:S(2)}) copy-start(bf16[32,32]{1,0:T(8,128)(2,1)} %param.7) | copy-start | bytes 6148
  0.6 14.3 %copy-start.1 = (bf16[32,32]{1,0:T(8,128)(2,1)S(1)}, bf16[32,32]{1,0:T(8,128)(2,1)}, u32[]{:S(2)}) copy-start(bf16[32,32]{1,0:T(8,128)(2,1)} %param.6) | copy-start | bytes 6148
  5.8 27.6 %collective-permute-start = (bf16[8,2,24,512]{3,2,1,0:T(8,128)(2,1)}, bf16[8,2,24,512]{3,2,1,0:T(8,128)(2,1)}, u32[]{:S(2)}, u32[]{:S(2)}) collective-permute-start(bf16[8,2,24,512]{3,2,1,0:T(8,128)(2,1)} %get-tuple-element.11), channel_id=1, source_target_pairs={{0,0},{1,1},{2,8},{3,9},{4,16},{5,17},{6,24},{7,25},{8,2},{9,3},{1... | collective-permute-start | bytes 1179656 | tf_op jit(solution)/shard_map/ppermute | solution.py:160
  9.0 49.3 %collective-permute-start.1 = (bf16[8,2,24,512]{3,2,1,0:T(8,128)(2,1)S(1)}, bf16[8,2,24,512]{3,2,1,0:T(8,128)(2,1)}, u32[]{:S(2)}, u32[]{:S(2)}) collective-permute-start(bf16[8,2,24,512]{3,2,1,0:T(8,128)(2,1)S(1)} %get-tuple-element.5), channel_id=1, source_target_pairs={{0,1},{1,2},{2,9},{3,10},{4,17},{5,18},{6,25},{7,26},{8,3},{9,4},{... | collective-permute-start | bytes 1179656 | tf_op jit(solution)/shard_map/ppermute | solution.py:160
  10.8 56.1 %collective-permute-start.2 = (bf16[8,2,24,512]{3,2,1,0:T(8,128)(2,1)S(1)}, bf16[8,2,24,512]{3,2,1,0:T(8,128)(2,1)}, u32[]{:S(2)}, u32[]{:S(2)}) collective-permute-start(bf16[8,2,24,512]{3,2,1,0:T(8,128)(2,1)S(1)} %get-tuple-element.6), channel_id=1, source_target_pairs={{0,2},{1,3},{2,10},{3,11},{4,18},{5,19},{6,26},{7,27},{8,4},{9,5},... | collective-permute-start | bytes 1179656 | tf_op jit(solution)/shard_map/ppermute | solution.py:160
  11.3 57.6 %collective-permute-start.3 = (bf16[8,2,24,512]{3,2,1,0:T(8,128)(2,1)S(1)}, bf16[8,2,24,512]{3,2,1,0:T(8,128)(2,1)}, u32[]{:S(2)}, u32[]{:S(2)}) collective-permute-start(bf16[8,2,24,512]{3,2,1,0:T(8,128)(2,1)S(1)} %get-tuple-element.7), channel_id=1, source_target_pairs={{0,3},{1,4},{2,11},{3,12},{4,19},{5,20},{6,27},{7,28},{8,5},{9,6},... | collective-permute-start | bytes 1179656 | tf_op jit(solution)/shard_map/ppermute | solution.py:160
  14.6 58.8 %collective-permute-start.4 = (bf16[8,2,24,512]{3,2,1,0:T(8,128)(2,1)S(1)}, bf16[8,2,24,512]{3,2,1,0:T(8,128)(2,1)}, u32[]{:S(2)}, u32[]{:S(2)}) collective-permute-start(bf16[8,2,24,512]{3,2,1,0:T(8,128)(2,1)S(1)} %get-tuple-element.8), channel_id=1, source_target_pairs={{0,4},{1,5},{2,12},{3,13},{4,20},{5,21},{6,28},{7,29},{8,6},{9,7},... | collective-permute-start | bytes 1179656 | tf_op jit(solution)/shard_map/ppermute | solution.py:160
  33.4 41.7 %collective-permute-start.5 = (bf16[8,2,24,512]{3,2,1,0:T(8,128)(2,1)S(1)}, bf16[8,2,24,512]{3,2,1,0:T(8,128)(2,1)S(1)}, u32[]{:S(2)}, u32[]{:S(2)}) collective-permute-start(bf16[8,2,24,512]{3,2,1,0:T(8,128)(2,1)S(1)} %get-tuple-element.9), channel_id=1, source_target_pairs={{0,5},{1,6},{2,13},{3,14},{4,21},{5,22},{6,29},{7,30},{8,7},{9,0},... | collective-permute-start | bytes 1179656 | tf_op jit(solution)/shard_map/ppermute | solution.py:160
  58.4 21.0 %collective-permute-start.6 = (bf16[8,2,24,512]{3,2,1,0:T(8,128)(2,1)S(1)}, bf16[8,2,24,512]{3,2,1,0:T(8,128)(2,1)S(1)}, u32[]{:S(2)}, u32[]{:S(2)}) collective-permute-start(bf16[8,2,24,512]{3,2,1,0:T(8,128)(2,1)S(1)} %get-tuple-element.10), channel_id=1, source_target_pairs={{0,6},{1,7},{2,14},{3,15},{4,22},{5,23},{6,30},{7,31},{8,0},{9,1},... | collective-permute-start | bytes 1179656 | tf_op jit(solution)/shard_map/ppermute | solution.py:160
  66.9 29.5 %collective-permute-start.7 = (bf16[8,2,24,512]{3,2,1,0:T(8,128)(2,1)S(1)}, bf16[8,2,24,512]{3,2,1,0:T(8,128)(2,1)S(1)}, u32[]{:S(2)}, u32[]{:S(2)}) collective-permute-start(bf16[8,2,24,512]{3,2,1,0:T(8,128)(2,1)S(1)} %get-tuple-element.4), channel_id=1, source_target_pairs={{0,7},{1,0},{2,15},{3,8},{4,23},{5,16},{6,31},{7,24},{8,1},{9,2},{... | collective-permute-start | bytes 1179656 | tf_op jit(solution)/shard_map/ppermute | solution.py:160
  102.9 14.1 %collective-permute-start.8 = (bf16[48,128]{1,0:T(8,128)(2,1)S(1)}, bf16[48,128]{1,0:T(8,128)(2,1)S(1)}, u32[]{:S(2)}, u32[]{:S(2)}) collective-permute-start(bf16[48,128]{1,0:T(8,128)(2,1)S(1)} %reshape_squeeze.6), channel_id=1, source_target_pairs={{8,0},{16,8},{24,16},{9,1},{17,9},{25,17},{10,2},{18,10},{26,18},{... | collective-permute-start | bytes 36872 | tf_op jit(solution)/shard_map/ppermute | solution.py:174
  105.4 12.6 %collective-permute-start.9 = (bf16[48,128]{1,0:T(8,128)(2,1)S(1)}, bf16[48,128]{1,0:T(8,128)(2,1)S(1)}, u32[]{:S(2)}, u32[]{:S(2)}) collective-permute-start(bf16[48,128]{1,0:T(8,128)(2,1)S(1)} %reshape_squeeze.7), channel_id=1, source_target_pairs={{0,8},{8,16},{16,24},{1,9},{9,17},{17,25},{2,10},{10,18},{18,26},{... | collective-permute-start | bytes 36872 | tf_op jit(solution)/shard_map/ppermute | solution.py:173

commit v10 on v9

--- a/solution.py
+++ b/solution.py
@@ -10,6 +10,7 @@
 RADIUS = 4
 LANES = 128
 PAIRS_PER_STEP = 4
+ACQ_PER_STEP = 8
 FIELDS = 4
 
 
@@ -29,49 +30,73 @@
     return total
 
 
+def box_means(field_ref, rows_ref, stack_ref, band_ref, count, tile_rows, tile_cols):
+    window = 2 * RADIUS + 1
+    padded_cols = tile_cols + LANES
+    rows = count * tile_rows
+    for f in range(count):
+        acc = window_rows(field_ref[f], window)[:tile_rows]
+        rows_ref[pl.ds(f * tile_rows, tile_rows), pl.ds(LANES, padded_cols)] = acc
+        rows_ref[pl.ds(f * tile_rows, tile_rows), pl.ds(0, LANES)] = acc[:, padded_cols - LANES :]
+    rowsum = rows_ref[...]
+    high = rowsum.astype(jnp.bfloat16)
+    low = (rowsum - high.astype(jnp.float32)).astype(jnp.bfloat16)
+    width = 3 * LANES
+    for j in range(tile_cols // LANES):
+        stack_ref[pl.ds(j * rows, rows), pl.ds(0, width)] = high[:, j * LANES : j * LANES + width]
+        stack_ref[pl.ds(j * rows, rows), pl.ds(width, width)] = low[:, j * LANES : j * LANES + width]
+    sums = jnp.dot(stack_ref[...], band_ref[...], preferred_element_type=jnp.float32)
+    return sums / float(window * window)
+
+
+def pieces_of(main_ref, edge_ref, index, tile_cols):
+    block_cols = main_ref.shape[-1]
+    pieces = [(c * block_cols, main_ref[c, index]) for c in range(main_ref.shape[0])]
+    pieces.append((tile_cols, edge_ref[index]))
+    return pieces
+
+
+def power_kernel(main_ref, edge_ref, band_ref, out_ref, field_ref, rows_ref, stack_ref, *, tile_rows, tile_cols):
+    step = main_ref.shape[1]
+    for a in range(step):
+        for at, piece in pieces_of(main_ref, edge_ref, a, tile_cols):
+            re = piece[0].astype(jnp.float32)
+            im = piece[1].astype(jnp.float32)
+            field_ref[a, :, pl.ds(at, piece.shape[-1])] = re * re + im * im
+    means = box_means(field_ref, rows_ref, stack_ref, band_ref, step, tile_rows, tile_cols)
+    rows = step * tile_rows
+    for j in range(tile_cols // LANES):
+        for a in range(step):
+            base = j * rows + a * tile_rows
+            out_ref[a, :, pl.ds(j * LANES, LANES)] = means[base : base + tile_rows] + 1e-06
+
+
 def pair_kernel(pre_ref, post_ref, *refs, tile_rows, tile_cols):
     del pre_ref, post_ref
     pp = PAIRS_PER_STEP
-    sides = refs[: 4 * pp]
-    band_ref, coh_ref, chg_ref, field_ref, rows_ref, stack_ref = refs[4 * pp :]
-    window = 2 * RADIUS + 1
-    padded_cols = tile_cols + LANES
-    rows = pp * FIELDS * tile_rows
-    blocks = tile_cols // LANES
+    sides = refs[: 6 * pp]
+    band_ref, coh_ref, chg_ref, field_ref, rows_ref, stack_ref = refs[6 * pp :]
     for p in range(pp):
-        a_main, a_edge, b_main, b_edge = sides[4 * p : 4 * p + 4]
-        pieces = [(c * a_main.shape[-1], a_main[c, 0], b_main[c, 0]) for c in range(a_main.shape[0])]
-        pieces.append((tile_cols, a_edge[0], b_edge[0]))
-        for at, a, b in pieces:
+        a_main, a_edge, b_main, b_edge = sides[6 * p : 6 * p + 4]
+        a_pieces = pieces_of(a_main, a_edge, 0, tile_cols)
+        b_pieces = pieces_of(b_main, b_edge, 0, tile_cols)
+        for (at, a), (_, b) in zip(a_pieces, b_pieces):
             width = a.shape[-1]
             pr = a[0].astype(jnp.float32)
             pi = a[1].astype(jnp.float32)
             qr = b[0].astype(jnp.float32)
             qi = b[1].astype(jnp.float32)
-            fields = (pr * pr + pi * pi, qr * qr + qi * qi, pr * qr + pi * qi, pi * qr - pr * qi)
-            for f, value in enumerate(fields):
-                field_ref[f, :, pl.ds(at, width)] = value
-        for f in range(FIELDS):
-            acc = window_rows(field_ref[f], window)[:tile_rows]
-            at = (p * FIELDS + f) * tile_rows
-            rows_ref[pl.ds(at, tile_rows), pl.ds(LANES, padded_cols)] = acc
-            rows_ref[pl.ds(at, tile_rows), pl.ds(0, LANES)] = acc[:, padded_cols - LANES :]
-    rowsum = rows_ref[...]
-    high = rowsum.astype(jnp.bfloat16)
-    low = (rowsum - high.astype(jnp.float32)).astype(jnp.bfloat16)
-    width = 3 * LANES
-    for j in range(blocks):
-        stack_ref[pl.ds(j * rows, rows), pl.ds(0, width)] = high[:, j * LANES : j * LANES + width]
-        stack_ref[pl.ds(j * rows, rows), pl.ds(width, width)] = low[:, j * LANES : j * LANES + width]
-    sums = jnp.dot(stack_ref[...], band_ref[...], preferred_element_type=jnp.float32)
-    means = sums / float(window * window)
-    for j in range(blocks):
+            field_ref[2 * p, :, pl.ds(at, width)] = pr * qr + pi * qi
+            field_ref[2 * p + 1, :, pl.ds(at, width)] = pi * qr - pr * qi
+    means = box_means(field_ref, rows_ref, stack_ref, band_ref, 2 * pp, tile_rows, tile_cols)
+    rows = 2 * pp * tile_rows
+    for j in range(tile_cols // LANES):
         for p in range(pp):
-            base = j * rows + p * FIELDS * tile_rows
-            pre_power = means[base : base + tile_rows] + 1e-06
-            post_power = means[base + tile_rows : base + 2 * tile_rows] + 1e-06
-            real_mean = means[base + 2 * tile_rows : base + 3 * tile_rows]
-            imag_mean = means[base + 3 * tile_rows : base + 4 * tile_rows]
+            pre_power = sides[6 * p + 4][0, :, pl.ds(j * LANES, LANES)]
+            post_power = sides[6 * p + 5][0, :, pl.ds(j * LANES, LANES)]
+            base = j * rows + 2 * p * tile_rows
+            real_mean = means[base : base + tile_rows]
+            imag_mean = means[base + tile_rows : base + 2 * tile_rows]
             coh = jnp.sqrt(real_mean * real_mean + imag_mean * imag_mean) / jnp.sqrt(
                 pre_power * post_power
             )
@@ -79,56 +104,73 @@
             chg_ref[p, :, pl.ds(j * LANES, LANES)] = jnp.log(post_power / pre_power)
 
 
+def scratch(count, padded_rows, tile_rows, tile_cols):
+    padded_cols = tile_cols + LANES
+    return [
+        pltpu.VMEM((count, padded_rows, padded_cols), jnp.float32),
+        pltpu.VMEM((count * tile_rows, padded_cols + LANES), jnp.float32),
+        pltpu.VMEM(((tile_cols // LANES) * count * tile_rows, 6 * LANES), jnp.bfloat16),
+    ]
+
+
 def pair_maps(main, edge, pre_ids, post_ids, tile_rows, tile_cols):
     count_pairs = pre_ids.shape[0]
     pp = PAIRS_PER_STEP
-    blocks_per_tile, _, _, padded_rows, block_cols = main.shape
+    ap = ACQ_PER_STEP
+    blocks_per_tile, count_acq, _, padded_rows, block_cols = main.shape
     width = 3 * LANES
     lane_in = jnp.arange(width)[:, None]
     lane_out = jnp.arange(LANES)[None, :]
     gap = lane_in - LANES - lane_out
     band = jnp.where((gap >= -RADIUS) & (gap <= RADIUS), 1.0, 0.0).astype(jnp.bfloat16)
     band = jnp.concatenate([band, band], axis=0)
+    kw = dict(tile_rows=tile_rows, tile_cols=tile_cols)
+
+    power = pl.pallas_call(
+        functools.partial(power_kernel, **kw),
+        grid=(count_acq // ap,),
+        in_specs=[
+            pl.BlockSpec((blocks_per_tile, ap, 2, padded_rows, block_cols), lambda i: (0, i, 0, 0, 0)),
+            pl.BlockSpec((ap, 2, padded_rows, LANES), lambda i: (i, 0, 0, 0)),
+            pl.BlockSpec((2 * width, LANES), lambda i: (0, 0)),
+        ],
+        out_specs=pl.BlockSpec((ap, tile_rows, tile_cols), lambda i: (i, 0, 0)),
+        out_shape=jax.ShapeDtypeStruct((count_acq, tile_rows, tile_cols), jnp.float32),
+        scratch_shapes=scratch(ap, padded_rows, tile_rows, tile_cols),
+    )(main, edge, band)
+
     main_block = (blocks_per_tile, 1, 2, padded_rows, block_cols)
     edge_block = (1, 2, padded_rows, LANES)
-
-    def specs(p, which):
-        def main_index(i, pre, post):
-            ids = pre if which == 0 else post
-            return (0, ids[i * pp + p], 0, 0, 0)
-
-        def edge_index(i, pre, post):
-            ids = pre if which == 0 else post
-            return (ids[i * pp + p], 0, 0, 0)
-
-        return [pl.BlockSpec(main_block, main_index), pl.BlockSpec(edge_block, edge_index)]
+    power_block = (1, tile_rows, tile_cols)
+
+    def specs(p):
+        return [
+            pl.BlockSpec(main_block, lambda i, pre, post: (0, pre[i * pp + p], 0, 0, 0)),
+            pl.BlockSpec(edge_block, lambda i, pre, post: (pre[i * pp + p], 0, 0, 0)),
+            pl.BlockSpec(main_block, lambda i, pre, post: (0, post[i * pp + p], 0, 0, 0)),
+            pl.BlockSpec(edge_block, lambda i, pre, post: (post[i * pp + p], 0, 0, 0)),
+            pl.BlockSpec(power_block, lambda i, pre, post: (pre[i * pp + p], 0, 0)),
+            pl.BlockSpec(power_block, lambda i, pre, post: (post[i * pp + p], 0, 0)),
+        ]
 
     in_specs = []
     operands = []
     for p in range(pp):
-        in_specs += specs(p, 0) + specs(p, 1)
-        operands += [main, edge, main, edge]
+        in_specs += specs(p)
+        operands += [main, edge, main, edge, power, power]
     in_specs.append(pl.BlockSpec((2 * width, LANES), lambda i, pre, post: (0, 0)))
     operands.append(band)
     out_block = pl.BlockSpec((pp, tile_rows, tile_cols), lambda i, pre, post: (i, 0, 0))
-    rows = pp * FIELDS * tile_rows
-    blocks = tile_cols // LANES
-    padded_cols = tile_cols + LANES
     grid_spec = pltpu.PrefetchScalarGridSpec(
         num_scalar_prefetch=2,
         grid=(count_pairs // pp,),
         in_specs=in_specs,
         out_specs=[out_block, out_block],
-        scratch_shapes=[
-            pltpu.VMEM((FIELDS, padded_rows, padded_cols), jnp.float32),
-            pltpu.VMEM((rows, padded_cols + LANES), jnp.float32),
-            pltpu.VMEM((blocks * rows, 2 * width), jnp.bfloat16),
-        ],
+        scratch_shapes=scratch(2 * pp, padded_rows, tile_rows, tile_cols),
     )
     out_shape = jax.ShapeDtypeStruct((count_pairs, tile_rows, tile_cols), jnp.float32)
-    kernel = functools.partial(pair_kernel, tile_rows=tile_rows, tile_cols=tile_cols)
     return pl.pallas_call(
-        kernel,
+        functools.partial(pair_kernel, **kw),
         grid_spec=grid_spec,
         out_shape=[out_shape, out_shape],
     )(pre_ids, post_ids, *operands)

time: 141 us -> 175 us (1.24)
  starting transfers between devices: 15.7 us -> 37.8 us
  waiting for transfers between devices: 67.8 us -> 78.2 us
  Pallas kernels: 19.5 us -> 21.6 us
    ppermute x8, starting transfers between devices: 8.76 us -> 31.8 us  [shards(): received.append(lax.ppermute(chunk, ('tx', 'ty'), pairs))]
    ppermute x8, waiting for transfers between devices: 67.8 us -> 78.2 us  [shards(): received.append(lax.ppermute(chunk, ('tx', 'ty'), pairs))]
    ppermute x1, starting transfers between devices: 4.99 us -> 1.91 us  [shards(): left = lax.ppermute(left, 'tx', forward).reshape(strip_shape)]
    ppermute x1, starting transfers between devices: 1.91 us -> 4.1 us  [shards(): right = lax.ppermute(right, 'tx', backward).reshape(strip_shape)]
    pallas_call x1 -> x2, Pallas kernels: 19.5 us -> 21.6 us  [the longest x1 15.4 us: pair_maps(): pl.pallas_call(functools.partial(pair_kernel, **kw), grid_spec=grid_spec,...]
  transfers between devices with their start and end apart: 10 -> 10, of which waited for: 7 -> 4; matrix products, arithmetic and copies ran while one was open for 16% -> 12% of each run, Pallas kernels for 0% -> 0%
where the time goes in v10:
time: 175 us
  waiting for transfers between devices  78.2 us (45%)
  starting transfers between devices  37.8 us (22%)
  local copies, waits for them, and re-layouts  29 us (17%)
  Pallas kernels  21.6 us (12%)
  matrix products  3.64 us (2%)
  other arithmetic  3.25 us (2%)
    ppermute x8, waiting for transfers between devices, shards(): received.append(lax.ppermute(chunk, ('tx', 'ty'), pairs))  78.2 us
    ppermute x8, starting transfers between devices, shards(): received.append(lax.ppermute(chunk, ('tx', 'ty'), pairs))  31.8 us
    pallas_call x1, Pallas kernels, pair_maps(): pl.pallas_call(functools.partial(pair_kernel, **kw), grid_spec=grid_spec,...  15.4 us
    unnamed x11, local copies, waits for them, and re-layouts  9.44 us
    pallas_call x1, Pallas kernels, pair_maps(): pl.pallas_call(functools.partial(power_kernel, **kw), grid=(count_acq //...  6.17 us
    dynamic_slice x1, local copies, waits for them, and re-layouts, shards(): chunk = lax.dynamic_slice_in_dim(x, first, padded_rows, axis=2)  5.06 us
    ppermute x1, starting transfers between devices, shards(): right = lax.ppermute(right, 'tx', backward).reshape(strip_shape)  4.1 us
  transfers between devices with their start and end apart: 10, of which 4 were waited for; matrix products, arithmetic and copies ran while one was open for 12% of the time, Pallas kernels for 0%

profile of v10, /device:TPU:26, one launch (start us, length us, event | category | flops | bytes accessed | tf_op | source)
XLA Modules:
  0.0 174.6 jit_solution(6627092644042302273)
XLA Ops:
  0.8 5.1 %pad_dynamic-slice_fusion = (bf16[8,2,24,512]{3,2,1,0:T(8,128)(2,1)S(1)}, bf16[8,2,24,512]{3,2,1,0:T(8,128)(2,1)S(1)}, bf16[8,2,24,512]{3,2,1,0:T(8,128)(2,1)S(1...) fusion(s32[]{:T(128)S(6)} %select_n.137, ...), kind=kLoop, calls=%fused_computation.7 | loop fusion | bytes 5242912 | tf_op jit(solution)/shard_map/dynamic_slice | solution.py:201
  5.8 0.6 collective-permute-start.7
  6.4 2.9 %collective-permute-start.1 = (bf16[8,2,24,512]{3,2,1,0:T(8,128)(2,1)S(1)}, bf16[8,2,24,512]{3,2,1,0:T(8,128)(2,1)}, u32[]{:S(2)}, u32[]{:S(2)}) collective-permute-start(bf16[8,2,24,512]{3,2,1,0:T(8,128)(2,1)S(1)} %get-tuple-element.5), channel_id=1, source_target_pairs={{0,1},{1,2},{2,9},{3,10},{4,17},{5,18},{6,25},{7,26},{8,3},{9,4},{... | collective-permute-start | bytes 1179656 | tf_op jit(solution)/shard_map/ppermute | solution.py:202
  9.9 2.5 %collective-permute-start.3 = (bf16[8,2,24,512]{3,2,1,0:T(8,128)(2,1)S(1)}, bf16[8,2,24,512]{3,2,1,0:T(8,128)(2,1)}, u32[]{:S(2)}, u32[]{:S(2)}) collective-permute-start(bf16[8,2,24,512]{3,2,1,0:T(8,128)(2,1)S(1)} %get-tuple-element.7), channel_id=1, source_target_pairs={{0,3},{1,4},{2,11},{3,12},{4,19},{5,20},{6,27},{7,28},{8,5},{9,6},... | collective-permute-start | bytes 1179656 | tf_op jit(solution)/shard_map/ppermute | solution.py:202
  12.4 1.9 %collective-permute-start = (bf16[8,2,24,512]{3,2,1,0:T(8,128)(2,1)}, bf16[8,2,24,512]{3,2,1,0:T(8,128)(2,1)}, u32[]{:S(2)}, u32[]{:S(2)}) collective-permute-start(bf16[8,2,24,512]{3,2,1,0:T(8,128)(2,1)} %get-tuple-element.11), channel_id=1, source_target_pairs={{0,0},{1,1},{2,8},{3,9},{4,16},{5,17},{6,24},{7,25},{8,2},{9,3},{1... | collective-permute-start | bytes 1179656 | tf_op jit(solution)/shard_map/ppermute | solution.py:202
  15.3 0.8 reshape.142
  16.1 0.8 reshape.143
  17.2 0.7 pad_maximum_fusion.band_ref.refs_24_
  17.9 39.3 %collective-permute-done = bf16[8,2,24,512]{3,2,1,0:T(8,128)(2,1)} collective-permute-done((bf16[8,2,24,512]{3,2,1,0:T(8,128)(2,1)}, bf16[8,2,24,512]{3,2,1,0:T(8,128)(2,1)}, u32[]{:S(2)}, u32[]{:S(2)}) %collective-permute-start) | collective-permute-done | bytes 393248 | tf_op jit(solution)/shard_map/ppermute | solution.py:202
  57.1 1.8 %bitcast_dynamic-update-slice_fusion.7 = bf16[8,8,2,24,512]{4,3,2,1,0:T(8,128)(2,1)} fusion(bf16[8,2,24,512]{3,2,1,0:T(8,128)(2,1)} %collective-permute-done), kind=kLoop, calls=%fused_computation.26 | loop fusion | bytes 786432
  58.9 7.0 %collective-permute-done.1 = bf16[8,2,24,512]{3,2,1,0:T(8,128)(2,1)} collective-permute-done((bf16[8,2,24,512]{3,2,1,0:T(8,128)(2,1)S(1)}, bf16[8,2,24,512]{3,2,1,0:T(8,128)(2,1)}, u32[]{:S(2)}, u32[]{:S(2)}) %collective-permute-start.1) | collective-permute-done | bytes 393248 | tf_op jit(solution)/shard_map/ppermute | solution.py:202
  65.9 1.8 %bitcast_dynamic-update-slice_fusion.6 = bf16[8,8,2,24,512]{4,3,2,1,0:T(8,128)(2,1)} fusion(bf16[8,8,2,24,512]{4,3,2,1,0:T(8,128)(2,1)} %bitcast_dynamic-update-slice_fusion.7, bf16[8,2,24,512]{3,2,1,0:T(8,128)(2,1)} %collective-permute-done.1), kind=kLoop, calls=%fused_computation.25 | loop fusion | bytes 786432
  67.7 23.3 %collective-permute-start.6 = (bf16[8,2,24,512]{3,2,1,0:T(8,128)(2,1)S(1)}, bf16[8,2,24,512]{3,2,1,0:T(8,128)(2,1)S(1)}, u32[]{:S(2)}, u32[]{:S(2)}) collective-permute-start(bf16[8,2,24,512]{3,2,1,0:T(8,128)(2,1)S(1)} %get-tuple-element.10), channel_id=1, source_target_pairs={{0,6},{1,7},{2,14},{3,15},{4,22},{5,23},{6,30},{7,31},{8,0},{9,1},... | collective-permute-start | bytes 1179656 | tf_op jit(solution)/shard_map/ppermute | solution.py:202
  91.0 1.8 %bitcast_dynamic-update-slice_fusion.5 = bf16[8,8,2,24,512]{4,3,2,1,0:T(8,128)(2,1)} fusion(bf16[8,8,2,24,512]{4,3,2,1,0:T(8,128)(2,1)} %bitcast_dynamic-update-slice_fusion.6, bf16[8,2,24,512]{3,2,1,0:T(8,128)(2,1)} %collective-permute-done.2), kind=kLoop, calls=%fused_computation.24 | loop fusion | bytes 786432
  92.8 1.8 %bitcast_dynamic-update-slice_fusion.4 = bf16[8,8,2,24,512]{4,3,2,1,0:T(8,128)(2,1)} fusion(bf16[8,8,2,24,512]{4,3,2,1,0:T(8,128)(2,1)} %bitcast_dynamic-update-slice_fusion.5, bf16[8,2,24,512]{3,2,1,0:T(8,128)(2,1)} %collective-permute-done.3), kind=kLoop, calls=%fused_computation.23 | loop fusion | bytes 786432
  94.6 0.8 bitcast_dynamic-update-slice_fusion.3
  95.3 24.2 %collective-permute-done.5 = bf16[8,2,24,512]{3,2,1,0:T(8,128)(2,1)S(1)} collective-permute-done((bf16[8,2,24,512]{3,2,1,0:T(8,128)(2,1)S(1)}, bf16[8,2,24,512]{3,2,1,0:T(8,128)(2,1)S(1)}, u32[]{:S(2)}, u32[]{:S(2)}) %collective-permute-start.5) | collective-permute-done | bytes 393248 | tf_op jit(solution)/shard_map/ppermute | solution.py:202
  119.6 0.8 bitcast_dynamic-update-slice_fusion.2
  120.4 7.7 %collective-permute-done.6 = bf16[8,2,24,512]{3,2,1,0:T(8,128)(2,1)S(1)} collective-permute-done((bf16[8,2,24,512]{3,2,1,0:T(8,128)(2,1)S(1)}, bf16[8,2,24,512]{3,2,1,0:T(8,128)(2,1)S(1)}, u32[]{:S(2)}, u32[]{:S(2)}) %collective-permute-start.6) | collective-permute-done | bytes 393248 | tf_op jit(solution)/shard_map/ppermute | solution.py:202
  128.1 0.8 bitcast_dynamic-update-slice_fusion.1
  128.9 1.8 %bitcast_dynamic-update-slice_fusion = bf16[8,8,2,24,512]{4,3,2,1,0:T(8,128)(2,1)} fusion(bf16[8,8,2,24,512]{4,3,2,1,0:T(8,128)(2,1)} %bitcast_dynamic-update-slice_fusion.1, bf16[8,2,24,512]{3,2,1,0:T(8,128)(2,1)} %collective-permute-done.7), kind=kLoop, calls=%fused_computation.19 | loop fusion | bytes 786432 | tf_op jit(solution)/shard_map/stack | solution.py:203
  130.7 2.6 %gather_fusion = bf16[8,8,2,24,512]{4,3,2,1,0:T(8,128)(2,1)S(1)} fusion(bf16[8,8,2,24,512]{4,3,2,1,0:T(8,128)(2,1)} %bitcast_dynamic-update-slice_fusion, s32[1024]{0:T(1024)S(1)} %pad_clamp_fusion), kind=kCustom, calls=%fused_computation | custom fusion | bytes 6291488 | tf_op jit(solution)/shard_map/jit(_take)/gather | solution.py:206
  133.3 2.0 %broadcast_select_fusion = bf16[8,8,2,24,512]{4,3,2,1,0:T(8,128)(2,1)} fusion(bf16[8,8,2,24,512]{4,3,2,1,0:T(8,128)(2,1)S(1)} %gather_fusion, pred[8]{0:T(512)(128)(4,1)S(1)} %compare_and_fusion), kind=kLoop, calls=%fused_computation.4 | loop fusion | flops 1572864 | bytes 6291464 | tf_op jit(solution)/shard_map/jit(_take)/select_n | solution.py:206
  136.9 1.9 %collective-permute-start.9 = (bf16[48,128]{1,0:T(8,128)(2,1)S(1)}, bf16[48,128]{1,0:T(8,128)(2,1)S(1)}, u32[]{:S(2)}, u32[]{:S(2)}) collective-permute-start(bf16[48,128]{1,0:T(8,128)(2,1)S(1)} %reshape_squeeze.7), channel_id=1, source_target_pairs={{0,8},{8,16},{16,24},{1,9},{9,17},{17,25},{2,10},{10,18},{18,26},{... | collective-permute-start | bytes 36872 | tf_op jit(solution)/shard_map/ppermute | solution.py:215
  138.9 4.1 %collective-permute-start.8 = (bf16[48,128]{1,0:T(8,128)(2,1)S(1)}, bf16[48,128]{1,0:T(8,128)(2,1)S(1)}, u32[]{:S(2)}, u32[]{:S(2)}) collective-permute-start(bf16[48,128]{1,0:T(8,128)(2,1)S(1)} %reshape_squeeze.6), channel_id=1, source_target_pairs={{8,0},{16,8},{24,16},{9,1},{17,9},{25,17},{10,2},{18,10},{26,18},{... | collective-permute-start | bytes 36872 | tf_op jit(solution)/shard_map/ppermute | solution.py:216
  143.0 3.2 %convert_bitcast_fusion = bf16[2,64,24,512]{3,1,2,0:T(8,128)(2,1)S(1)} fusion(bf16[2,64,24,512]{3,2,1,0:T(8,128)(2,1)} %bitcast.63, bf16[64,64,1,1]{1,0,2,3:T(8,128)(2,1)S(1)} %reshape.142), kind=kOutput, calls=%fused_computation.3 | convolution fusion | flops 202899456 | bytes 6299648 | tf_op jit(solution)/shard_map/kc,bchw->bkhw/dot_general | solution.py:222
  146.2 3.4 %copy.13 = bf16[2,64,24,512]{3,2,1,0:T(8,128)(2,1)} copy(bf16[2,64,24,512]{3,1,2,0:T(8,128)(2,1)S(1)} %convert_bitcast_fusion) | data formatting | bytes 6291456 | tf_op jit(solution)/shard_map/convert_element_type | solution.py:223
  149.6 0.8 reshape.131
  150.5 0.8 reshape.132
  151.9 1.0 copy.16
  152.9 6.2 %shard_map.68.refs_4_.refs_5_.refs_10_.refs_11_.refs_16_.refs_17_.refs_22_.refs_23_ = f32[32,16,1024]{2,1,0:T(8,128)} custom-call(bf16[2,32,2,24,512]{4,3,2,1,0:T(8,128)(2,1)} %bitcast.44, bf16[32,2,24,128]{3,2,1,0:T(8,128)(2,1)} %bitcast.53, bf16[768,128]{1,0:T(8,128)(2,1)} %pad_maximum_fusion.band_ref.refs_24_), custom_call_target="tpu_custom_call" | custom-call | tf_op jit(solution)/shard_map/pallas_call | solution.py:129
  159.1 15.4 %shard_map.69 = (f32[32,16,1024]{2,1,0:T(8,128)}, f32[32,16,1024]{2,1,0:T(8,128)}) custom-call(s32[32]{0:T(128)} %pre_ref.1, s32[32]{0:T(128)} %post_ref.1, bf16[2,32,2,24,512]{4,3,2,1,0:T(8,128)(2,1)} %bitcast.45, bf16[32,2,24,128]{3,2,1,0:T(8,128)(2,1)} %bitcast.54, bf16[2,32,2,24,512]{4,3,2,1,0:T(8,128)(2,1)} %bitcast.46, ...), custom_call_target="tpu_custom_call" | custom-call | tf_op jit(solution)/shard_map/pallas_call | solution.py:172
  (37 shorter events, 3.9 us)
Async XLA Ops:
  0.6 13.9 %copy-start = (bf16[32,32]{1,0:T(8,128)(2,1)S(1)}, bf16[32,32]{1,0:T(8,128)(2,1)}, u32[]{:S(2)}) copy-start(bf16[32,32]{1,0:T(8,128)(2,1)} %param.7) | copy-start | bytes 6148
  0.6 14.1 %copy-start.1 = (bf16[32,32]{1,0:T(8,128)(2,1)S(1)}, bf16[32,32]{1,0:T(8,128)(2,1)}, u32[]{:S(2)}) copy-start(bf16[32,32]{1,0:T(8,128)(2,1)} %param.6) | copy-start | bytes 6148
  5.8 123.0 %collective-permute-start.7 = (bf16[8,2,24,512]{3,2,1,0:T(8,128)(2,1)S(1)}, bf16[8,2,24,512]{3,2,1,0:T(8,128)(2,1)}, u32[]{:S(2)}, u32[]{:S(2)}) collective-permute-start(bf16[8,2,24,512]{3,2,1,0:T(8,128)(2,1)S(1)} %get-tuple-element.4), channel_id=1, source_target_pairs={{0,7},{1,0},{2,15},{3,8},{4,23},{5,16},{6,31},{7,24},{8,1},{9,2},{... | collective-permute-start | bytes 1179656 | tf_op jit(solution)/shard_map/ppermute | solution.py:202
  6.4 59.4 %collective-permute-start.1 = (bf16[8,2,24,512]{3,2,1,0:T(8,128)(2,1)S(1)}, bf16[8,2,24,512]{3,2,1,0:T(8,128)(2,1)}, u32[]{:S(2)}, u32[]{:S(2)}) collective-permute-start(bf16[8,2,24,512]{3,2,1,0:T(8,128)(2,1)S(1)} %get-tuple-element.5), channel_id=1, source_target_pairs={{0,1},{1,2},{2,9},{3,10},{4,17},{5,18},{6,25},{7,26},{8,3},{9,4},{... | collective-permute-start | bytes 1179656 | tf_op jit(solution)/shard_map/ppermute | solution.py:202
  9.4 58.3 %collective-permute-start.2 = (bf16[8,2,24,512]{3,2,1,0:T(8,128)(2,1)S(1)}, bf16[8,2,24,512]{3,2,1,0:T(8,128)(2,1)}, u32[]{:S(2)}, u32[]{:S(2)}) collective-permute-start(bf16[8,2,24,512]{3,2,1,0:T(8,128)(2,1)S(1)} %get-tuple-element.6), channel_id=1, source_target_pairs={{0,2},{1,3},{2,10},{3,11},{4,18},{5,19},{6,26},{7,27},{8,4},{9,5},... | collective-permute-start | bytes 1179656 | tf_op jit(solution)/shard_map/ppermute | solution.py:202
  9.9 82.9 %collective-permute-start.3 = (bf16[8,2,24,512]{3,2,1,0:T(8,128)(2,1)S(1)}, bf16[8,2,24,512]{3,2,1,0:T(8,128)(2,1)}, u32[]{:S(2)}, u32[]{:S(2)}) collective-permute-start(bf16[8,2,24,512]{3,2,1,0:T(8,128)(2,1)S(1)} %get-tuple-element.7), channel_id=1, source_target_pairs={{0,3},{1,4},{2,11},{3,12},{4,19},{5,20},{6,27},{7,28},{8,5},{9,6},... | collective-permute-start | bytes 1179656 | tf_op jit(solution)/shard_map/ppermute | solution.py:202
  12.4 44.7 %collective-permute-start = (bf16[8,2,24,512]{3,2,1,0:T(8,128)(2,1)}, bf16[8,2,24,512]{3,2,1,0:T(8,128)(2,1)}, u32[]{:S(2)}, u32[]{:S(2)}) collective-permute-start(bf16[8,2,24,512]{3,2,1,0:T(8,128)(2,1)} %get-tuple-element.11), channel_id=1, source_target_pairs={{0,0},{1,1},{2,8},{3,9},{4,16},{5,17},{6,24},{7,25},{8,2},{9,3},{1... | collective-permute-start | bytes 1179656 | tf_op jit(solution)/shard_map/ppermute | solution.py:202
  57.1 37.4 %collective-permute-start.4 = (bf16[8,2,24,512]{3,2,1,0:T(8,128)(2,1)S(1)}, bf16[8,2,24,512]{3,2,1,0:T(8,128)(2,1)S(1)}, u32[]{:S(2)}, u32[]{:S(2)}) collective-permute-start(bf16[8,2,24,512]{3,2,1,0:T(8,128)(2,1)S(1)} %get-tuple-element.8), channel_id=1, source_target_pairs={{0,4},{1,5},{2,12},{3,13},{4,20},{5,21},{6,28},{7,29},{8,6},{9,7},... | collective-permute-start | bytes 1179656 | tf_op jit(solution)/shard_map/ppermute | solution.py:202
  65.9 53.7 %collective-permute-start.5 = (bf16[8,2,24,512]{3,2,1,0:T(8,128)(2,1)S(1)}, bf16[8,2,24,512]{3,2,1,0:T(8,128)(2,1)S(1)}, u32[]{:S(2)}, u32[]{:S(2)}) collective-permute-start(bf16[8,2,24,512]{3,2,1,0:T(8,128)(2,1)S(1)} %get-tuple-element.9), channel_id=1, source_target_pairs={{0,5},{1,6},{2,13},{3,14},{4,21},{5,22},{6,29},{7,30},{8,7},{9,0},... | collective-permute-start | bytes 1179656 | tf_op jit(solution)/shard_map/ppermute | solution.py:202
  67.7 60.4 %collective-permute-start.6 = (bf16[8,2,24,512]{3,2,1,0:T(8,128)(2,1)S(1)}, bf16[8,2,24,512]{3,2,1,0:T(8,128)(2,1)S(1)}, u32[]{:S(2)}, u32[]{:S(2)}) collective-permute-start(bf16[8,2,24,512]{3,2,1,0:T(8,128)(2,1)S(1)} %get-tuple-element.10), channel_id=1, source_target_pairs={{0,6},{1,7},{2,14},{3,15},{4,22},{5,23},{6,30},{7,31},{8,0},{9,1},... | collective-permute-start | bytes 1179656 | tf_op jit(solution)/shard_map/ppermute | solution.py:202
  136.9 13.6 %collective-permute-start.9 = (bf16[48,128]{1,0:T(8,128)(2,1)S(1)}, bf16[48,128]{1,0:T(8,128)(2,1)S(1)}, u32[]{:S(2)}, u32[]{:S(2)}) collective-permute-start(bf16[48,128]{1,0:T(8,128)(2,1)S(1)} %reshape_squeeze.7), channel_id=1, source_target_pairs={{0,8},{8,16},{16,24},{1,9},{9,17},{17,25},{2,10},{10,18},{18,26},{... | collective-permute-start | bytes 36872 | tf_op jit(solution)/shard_map/ppermute | solution.py:215
  138.9 10.7 %collective-permute-start.8 = (bf16[48,128]{1,0:T(8,128)(2,1)S(1)}, bf16[48,128]{1,0:T(8,128)(2,1)S(1)}, u32[]{:S(2)}, u32[]{:S(2)}) collective-permute-start(bf16[48,128]{1,0:T(8,128)(2,1)S(1)} %reshape_squeeze.6), channel_id=1, source_target_pairs={{8,0},{16,8},{24,16},{9,1},{17,9},{25,17},{10,2},{18,10},{26,18},{... | collective-permute-start | bytes 36872 | tf_op jit(solution)/shard_map/ppermute | solution.py:216

commit v11 on v9

--- a/solution.py
+++ b/solution.py
@@ -157,6 +157,7 @@
                 pairs.append((col * n_rows + row, (row // blocks_per_tile) * n_rows + to_row))
         first = ((start + m) % n_rows) * tile_rows
         chunk = lax.dynamic_slice_in_dim(x, first, padded_rows, axis=2)
+        chunk = chunk.reshape(local_acq * 2 * padded_rows, local_cols)
         received.append(lax.ppermute(chunk, ("tx", "ty"), pairs))
     received = jnp.stack(received, axis=0)
     source = jnp.arange(blocks_per_tile)[:, None] + blocks_per_tile * jnp.arange(n_cols)[None, :]

time: 141 us -> 142 us (level)
  local copies, waits for them, and re-layouts: 29 us -> 34.5 us
  matrix products: 3.63 us -> 1.75 us
  waiting for transfers between devices: 67.8 us -> 66 us
    dot_general x1, matrix products: 3.21 us -> 1.34 us  [shards(): jnp.einsum('kc,bchw->bkhw', mixing, x, preferred_element_type=jnp.float32)]
    ppermute x8, waiting for transfers between devices: 67.8 us -> 66 us  [shards(): received.append(lax.ppermute(chunk, ('tx', 'ty'), pairs))]
    another operation x1, local copies, waits for them, and re-layouts: 0.53 us -> 2.09 us  [shards(): right = x[0, :, :, :RADIUS].reshape(flat)]
    unnamed x11 -> x15, local copies, waits for them, and re-layouts: 10.4 us -> 10.5 us
  transfers between devices with their start and end apart: 10 -> 10, of which waited for: 7 -> 7; matrix products, arithmetic and copies ran while one was open for 16% -> 17% of each run, Pallas kernels for 0% -> 0%
where the time goes in v11:
time: 142 us; the launch traced here: 141 us
  waiting for transfers between devices  66 us (46%)
  local copies, waits for them, and re-layouts  34.5 us (24%)
  Pallas kernels  19.5 us (14%)
  starting transfers between devices  15.8 us (11%)
  other arithmetic  2.63 us (2%)
  matrix products  1.75 us (1%)
    ppermute x8, waiting for transfers between devices, shards(): received.append(lax.ppermute(chunk, ('tx', 'ty'), pairs))  66 us
    pallas_call x1, Pallas kernels, pair_maps(): pl.pallas_call(kernel, grid_spec=grid_spec, out_shape=[out_shape, out_sha...  19.5 us
    unnamed x15, local copies, waits for them, and re-layouts  10.5 us
    ppermute x8, starting transfers between devices, shards(): received.append(lax.ppermute(chunk, ('tx', 'ty'), pairs))  8.76 us
    ppermute x1, starting transfers between devices, shards(): left = lax.ppermute(left, 'tx', forward).reshape(strip_shape)  5.12 us
    dynamic_slice x1, local copies, waits for them, and re-layouts, shards(): chunk = lax.dynamic_slice_in_dim(x, first, padded_rows, axis=2)  5.06 us
    convert_element_type x1, local copies, waits for them, and re-layouts, shards(): main.astype(jnp.bfloat16)  3.41 us
  transfers between devices with their start and end apart: 10, of which 7 were waited for; matrix products, arithmetic and copies ran while one was open for 17% of the time, Pallas kernels for 0%

profile of v11, /device:TPU:26, one launch (start us, length us, event | category | flops | bytes accessed | tf_op | source)
XLA Modules:
  0.0 141.2 jit_solution(15873857117252635665)
XLA Ops:
  0.8 5.1 %pad_dynamic-slice_fusion = (bf16[8,2,24,512]{3,2,1,0:T(8,128)(2,1)S(1)}, bf16[8,2,24,512]{3,2,1,0:T(8,128)(2,1)S(1)}, bf16[8,2,24,512]{3,2,1,0:T(8,128)(2,1)S(1...) fusion(s32[]{:T(128)S(6)} %select_n.139, ...), kind=kLoop, calls=%fused_computation.7 | loop fusion | bytes 5242912 | tf_op jit(solution)/shard_map/dynamic_slice | solution.py:159
  5.8 3.2 %collective-permute-start = (bf16[384,512]{1,0:T(8,128)(2,1)}, bf16[384,512]{1,0:T(8,128)(2,1)}, u32[]{:S(2)}, u32[]{:S(2)}) collective-permute-start(bf16[384,512]{1,0:T(8,128)(2,1)} %bitcast), channel_id=1, source_target_pairs={{0,0},{1,1},{2,8},{3,9},{4,16},{5,17},{6,24},{7,25},{8,2},{9,3},{1... | collective-permute-start | bytes 1179656 | tf_op jit(solution)/shard_map/ppermute | solution.py:161
  9.0 1.7 %collective-permute-start.1 = (bf16[384,512]{1,0:T(8,128)(2,1)S(1)}, bf16[384,512]{1,0:T(8,128)(2,1)}, u32[]{:S(2)}, u32[]{:S(2)}) collective-permute-start(bf16[384,512]{1,0:T(8,128)(2,1)S(1)} %bitcast.76), channel_id=1, source_target_pairs={{0,1},{1,2},{2,9},{3,10},{4,17},{5,18},{6,25},{7,26},{8,3},{9,4},{... | collective-permute-start | bytes 1179656 | tf_op jit(solution)/shard_map/ppermute | solution.py:161
  11.3 3.3 %collective-permute-start.3 = (bf16[384,512]{1,0:T(8,128)(2,1)S(1)}, bf16[384,512]{1,0:T(8,128)(2,1)}, u32[]{:S(2)}, u32[]{:S(2)}) collective-permute-start(bf16[384,512]{1,0:T(8,128)(2,1)S(1)} %bitcast.74), channel_id=1, source_target_pairs={{0,3},{1,4},{2,11},{3,12},{4,19},{5,20},{6,27},{7,28},{8,5},{9,6},... | collective-permute-start | bytes 1179656 | tf_op jit(solution)/shard_map/ppermute | solution.py:161
  15.4 0.8 reshape.176
  16.2 1.4 %reshape.175 = bf16[64,64,1,1]{1,0,2,3:T(8,128)(2,1)} reshape(bf16[32,2,32,2]{3,2,1,0:T(8,128)(2,1)S(1)} %copy.10) | data formatting | bytes 16384 | tf_op jit(solution)/shard_map/reshape | solution.py:180
  20.0 13.5 %collective-permute-done = bf16[384,512]{1,0:T(8,128)(2,1)} collective-permute-done((bf16[384,512]{1,0:T(8,128)(2,1)}, bf16[384,512]{1,0:T(8,128)(2,1)}, u32[]{:S(2)}, u32[]{:S(2)}) %collective-permute-start) | collective-permute-done | bytes 393248 | tf_op jit(solution)/shard_map/ppermute | solution.py:161
  33.4 1.8 %bitcast_dynamic-update-slice_fusion.7 = bf16[8,384,512]{2,1,0:T(8,128)(2,1)} fusion(bf16[384,512]{1,0:T(8,128)(2,1)} %collective-permute-done), kind=kLoop, calls=%fused_computation.26 | loop fusion | bytes 786432
  35.2 23.2 %collective-permute-done.1 = bf16[384,512]{1,0:T(8,128)(2,1)} collective-permute-done((bf16[384,512]{1,0:T(8,128)(2,1)S(1)}, bf16[384,512]{1,0:T(8,128)(2,1)}, u32[]{:S(2)}, u32[]{:S(2)}) %collective-permute-start.1) | collective-permute-done | bytes 393248 | tf_op jit(solution)/shard_map/ppermute | solution.py:161
  58.4 1.8 %bitcast_dynamic-update-slice_fusion.6 = bf16[8,384,512]{2,1,0:T(8,128)(2,1)} fusion(bf16[8,384,512]{2,1,0:T(8,128)(2,1)} %bitcast_dynamic-update-slice_fusion.7, bf16[384,512]{1,0:T(8,128)(2,1)} %collective-permute-done.1), kind=kLoop, calls=%fused_computation.25 | loop fusion | bytes 786432
  60.1 6.7 %collective-permute-done.2 = bf16[384,512]{1,0:T(8,128)(2,1)} collective-permute-done((bf16[384,512]{1,0:T(8,128)(2,1)S(1)}, bf16[384,512]{1,0:T(8,128)(2,1)}, u32[]{:S(2)}, u32[]{:S(2)}) %collective-permute-start.2) | collective-permute-done | bytes 393248 | tf_op jit(solution)/shard_map/ppermute | solution.py:161
  66.9 1.8 %bitcast_dynamic-update-slice_fusion.5 = bf16[8,384,512]{2,1,0:T(8,128)(2,1)} fusion(bf16[8,384,512]{2,1,0:T(8,128)(2,1)} %bitcast_dynamic-update-slice_fusion.6, bf16[384,512]{1,0:T(8,128)(2,1)} %collective-permute-done.2), kind=kLoop, calls=%fused_computation.24 | loop fusion | bytes 786432
  68.9 1.8 %bitcast_dynamic-update-slice_fusion.4 = bf16[8,384,512]{2,1,0:T(8,128)(2,1)} fusion(bf16[8,384,512]{2,1,0:T(8,128)(2,1)} %bitcast_dynamic-update-slice_fusion.5, bf16[384,512]{1,0:T(8,128)(2,1)} %collective-permute-done.3), kind=kLoop, calls=%fused_computation.23 | loop fusion | bytes 786432
  70.7 2.7 %collective-permute-done.4 = bf16[384,512]{1,0:T(8,128)(2,1)} collective-permute-done((bf16[384,512]{1,0:T(8,128)(2,1)S(1)}, bf16[384,512]{1,0:T(8,128)(2,1)}, u32[]{:S(2)}, u32[]{:S(2)}) %collective-permute-start.4) | collective-permute-done | bytes 393248 | tf_op jit(solution)/shard_map/ppermute | solution.py:161
  73.4 1.8 %bitcast_dynamic-update-slice_fusion.3 = bf16[8,384,512]{2,1,0:T(8,128)(2,1)} fusion(bf16[8,384,512]{2,1,0:T(8,128)(2,1)} %bitcast_dynamic-update-slice_fusion.4, bf16[384,512]{1,0:T(8,128)(2,1)} %collective-permute-done.4), kind=kLoop, calls=%fused_computation.22 | loop fusion | bytes 786432
  75.2 0.8 bitcast_dynamic-update-slice_fusion.2
  75.9 3.4 %collective-permute-done.6 = bf16[384,512]{1,0:T(8,128)(2,1)S(1)} collective-permute-done((bf16[384,512]{1,0:T(8,128)(2,1)S(1)}, bf16[384,512]{1,0:T(8,128)(2,1)S(1)}, u32[]{:S(2)}, u32[]{:S(2)}) %collective-permute-start.6) | collective-permute-done | bytes 393248 | tf_op jit(solution)/shard_map/ppermute | solution.py:161
  80.1 16.2 %collective-permute-done.7 = bf16[384,512]{1,0:T(8,128)(2,1)S(1)} collective-permute-done((bf16[384,512]{1,0:T(8,128)(2,1)S(1)}, bf16[384,512]{1,0:T(8,128)(2,1)S(1)}, u32[]{:S(2)}, u32[]{:S(2)}) %collective-permute-start.7) | collective-permute-done | bytes 393248 | tf_op jit(solution)/shard_map/ppermute | solution.py:161
  96.4 0.8 bitcast_dynamic-update-slice_fusion
  97.2 2.6 %gather_fusion = bf16[8,384,512]{2,1,0:T(8,128)(2,1)S(1)} fusion(bf16[8,384,512]{2,1,0:T(8,128)(2,1)} %bitcast_dynamic-update-slice_fusion, s32[1024]{0:T(1024)S(1)} %pad_clamp_fusion), kind=kCustom, calls=%fused_computation | custom fusion | bytes 6291488 | tf_op jit(solution)/shard_map/jit(_take)/gather | solution.py:165
  100.2 0.9 fusion.17
  101.1 2.1 %reshape_squeeze.6 = bf16[48,128]{1,0:T(8,128)(2,1)} reshape(bf16[1,64,24,4]{3,2,1,0:T(8,128)(2,1)} %get-tuple-element.2) | data formatting | bytes 24576 | tf_op jit(solution)/shard_map/reshape;squeeze | solution.py:173
  103.2 1.9 %collective-permute-start.8 = (bf16[48,128]{1,0:T(8,128)(2,1)}, bf16[48,128]{1,0:T(8,128)(2,1)}, u32[]{:S(2)}, u32[]{:S(2)}) collective-permute-start(bf16[48,128]{1,0:T(8,128)(2,1)} %reshape_squeeze.6), channel_id=1, source_target_pairs={{8,0},{16,8},{24,16},{9,1},{17,9},{25,17},{10,2},{18,10},{26,18},{... | collective-permute-start | bytes 36872 | tf_op jit(solution)/shard_map/ppermute | solution.py:175
  105.1 1.1 reshape_squeeze.7
  106.3 5.1 %collective-permute-start.9 = (bf16[48,128]{1,0:T(8,128)(2,1)}, bf16[48,128]{1,0:T(8,128)(2,1)S(1)}, u32[]{:S(2)}, u32[]{:S(2)}) collective-permute-start(bf16[48,128]{1,0:T(8,128)(2,1)} %reshape_squeeze.7), channel_id=1, source_target_pairs={{0,8},{8,16},{16,24},{1,9},{9,17},{17,25},{2,10},{10,18},{18,26},{... | collective-permute-start | bytes 36872 | tf_op jit(solution)/shard_map/ppermute | solution.py:174
  111.4 1.4 broadcast_select_fusion.1
  112.8 1.3 convert_bitcast_fusion
  114.1 3.4 %copy.12 = bf16[2,64,24,512]{3,2,1,0:T(8,128)(2,1)} copy(bf16[2,64,24,512]{3,1,2,0:T(8,128)(2,1)S(1)} %convert_bitcast_fusion) | data formatting | bytes 6291456 | tf_op jit(solution)/shard_map/convert_element_type | solution.py:182
  117.6 1.5 %reshape.164 = bf16[64,24,4]{2,1,0:T(8,128)(2,1)S(1)} reshape(bf16[48,128]{1,0:T(8,128)(2,1)} %collective-permute-done.8) | data formatting | bytes 24576 | tf_op jit(solution)/shard_map/reshape | solution.py:175
  119.2 0.8 reshape.165
  120.6 1.0 copy.15
  121.6 19.5 %shard_map.68 = (f32[32,16,1024]{2,1,0:T(8,128)}, f32[32,16,1024]{2,1,0:T(8,128)}) custom-call(s32[32]{0:T(128)} %pre_ref.1, s32[32]{0:T(128)} %post_ref.1, bf16[2,32,2,24,512]{4,3,2,1,0:T(8,128)(2,1)} %bitcast.52, bf16[32,2,24,128]{3,2,1,0:T(8,128)(2,1)} %bitcast.60, bf16[2,32,2,24,512]{4,3,2,1,0:T(8,128)(2,1)} %bitcast.53, ...), custom_call_target="tpu_custom_call" | custom-call | tf_op jit(solution)/shard_map/pallas_call | solution.py:130
  (41 shorter events, 5.5 us)
Async XLA Ops:
  0.6 14.1 %copy-start.1 = (bf16[32,32]{1,0:T(8,128)(2,1)S(1)}, bf16[32,32]{1,0:T(8,128)(2,1)}, u32[]{:S(2)}) copy-start(bf16[32,32]{1,0:T(8,128)(2,1)} %param.7) | copy-start | bytes 6148
  0.6 14.2 %copy-start.2 = (bf16[32,32]{1,0:T(8,128)(2,1)S(1)}, bf16[32,32]{1,0:T(8,128)(2,1)}, u32[]{:S(2)}) copy-start(bf16[32,32]{1,0:T(8,128)(2,1)} %param.6) | copy-start | bytes 6148
  5.8 27.6 %collective-permute-start = (bf16[384,512]{1,0:T(8,128)(2,1)}, bf16[384,512]{1,0:T(8,128)(2,1)}, u32[]{:S(2)}, u32[]{:S(2)}) collective-permute-start(bf16[384,512]{1,0:T(8,128)(2,1)} %bitcast), channel_id=1, source_target_pairs={{0,0},{1,1},{2,8},{3,9},{4,16},{5,17},{6,24},{7,25},{8,2},{9,3},{1... | collective-permute-start | bytes 1179656 | tf_op jit(solution)/shard_map/ppermute | solution.py:161
  9.0 49.3 %collective-permute-start.1 = (bf16[384,512]{1,0:T(8,128)(2,1)S(1)}, bf16[384,512]{1,0:T(8,128)(2,1)}, u32[]{:S(2)}, u32[]{:S(2)}) collective-permute-start(bf16[384,512]{1,0:T(8,128)(2,1)S(1)} %bitcast.76), channel_id=1, source_target_pairs={{0,1},{1,2},{2,9},{3,10},{4,17},{5,18},{6,25},{7,26},{8,3},{9,4},{... | collective-permute-start | bytes 1179656 | tf_op jit(solution)/shard_map/ppermute | solution.py:161
  10.8 56.1 %collective-permute-start.2 = (bf16[384,512]{1,0:T(8,128)(2,1)S(1)}, bf16[384,512]{1,0:T(8,128)(2,1)}, u32[]{:S(2)}, u32[]{:S(2)}) collective-permute-start(bf16[384,512]{1,0:T(8,128)(2,1)S(1)} %bitcast.75), channel_id=1, source_target_pairs={{0,2},{1,3},{2,10},{3,11},{4,18},{5,19},{6,26},{7,27},{8,4},{9,5},... | collective-permute-start | bytes 1179656 | tf_op jit(solution)/shard_map/ppermute | solution.py:161
  11.3 57.6 %collective-permute-start.3 = (bf16[384,512]{1,0:T(8,128)(2,1)S(1)}, bf16[384,512]{1,0:T(8,128)(2,1)}, u32[]{:S(2)}, u32[]{:S(2)}) collective-permute-start(bf16[384,512]{1,0:T(8,128)(2,1)S(1)} %bitcast.74), channel_id=1, source_target_pairs={{0,3},{1,4},{2,11},{3,12},{4,19},{5,20},{6,27},{7,28},{8,5},{9,6},... | collective-permute-start | bytes 1179656 | tf_op jit(solution)/shard_map/ppermute | solution.py:161
  14.6 58.8 %collective-permute-start.4 = (bf16[384,512]{1,0:T(8,128)(2,1)S(1)}, bf16[384,512]{1,0:T(8,128)(2,1)}, u32[]{:S(2)}, u32[]{:S(2)}) collective-permute-start(bf16[384,512]{1,0:T(8,128)(2,1)S(1)} %bitcast.73), channel_id=1, source_target_pairs={{0,4},{1,5},{2,12},{3,13},{4,20},{5,21},{6,28},{7,29},{8,6},{9,7},... | collective-permute-start | bytes 1179656 | tf_op jit(solution)/shard_map/ppermute | solution.py:161
  33.4 41.7 %collective-permute-start.5 = (bf16[384,512]{1,0:T(8,128)(2,1)S(1)}, bf16[384,512]{1,0:T(8,128)(2,1)S(1)}, u32[]{:S(2)}, u32[]{:S(2)}) collective-permute-start(bf16[384,512]{1,0:T(8,128)(2,1)S(1)} %bitcast.72), channel_id=1, source_target_pairs={{0,5},{1,6},{2,13},{3,14},{4,21},{5,22},{6,29},{7,30},{8,7},{9,0},... | collective-permute-start | bytes 1179656 | tf_op jit(solution)/shard_map/ppermute | solution.py:161
  58.4 21.0 %collective-permute-start.6 = (bf16[384,512]{1,0:T(8,128)(2,1)S(1)}, bf16[384,512]{1,0:T(8,128)(2,1)S(1)}, u32[]{:S(2)}, u32[]{:S(2)}) collective-permute-start(bf16[384,512]{1,0:T(8,128)(2,1)S(1)} %bitcast.71), channel_id=1, source_target_pairs={{0,6},{1,7},{2,14},{3,15},{4,22},{5,23},{6,30},{7,31},{8,0},{9,1},... | collective-permute-start | bytes 1179656 | tf_op jit(solution)/shard_map/ppermute | solution.py:161
  66.9 29.5 %collective-permute-start.7 = (bf16[384,512]{1,0:T(8,128)(2,1)S(1)}, bf16[384,512]{1,0:T(8,128)(2,1)S(1)}, u32[]{:S(2)}, u32[]{:S(2)}) collective-permute-start(bf16[384,512]{1,0:T(8,128)(2,1)S(1)} %bitcast.70), channel_id=1, source_target_pairs={{0,7},{1,0},{2,15},{3,8},{4,23},{5,16},{6,31},{7,24},{8,1},{9,2},{... | collective-permute-start | bytes 1179656 | tf_op jit(solution)/shard_map/ppermute | solution.py:161
  103.2 14.3 %collective-permute-start.8 = (bf16[48,128]{1,0:T(8,128)(2,1)}, bf16[48,128]{1,0:T(8,128)(2,1)}, u32[]{:S(2)}, u32[]{:S(2)}) collective-permute-start(bf16[48,128]{1,0:T(8,128)(2,1)} %reshape_squeeze.6), channel_id=1, source_target_pairs={{8,0},{16,8},{24,16},{9,1},{17,9},{25,17},{10,2},{18,10},{26,18},{... | collective-permute-start | bytes 36872 | tf_op jit(solution)/shard_map/ppermute | solution.py:175
  106.3 6.5 %copy-start = (bf16[64,64,1,1]{1,0,2,3:T(8,128)(2,1)S(1)}, bf16[64,64,1,1]{1,0,2,3:T(8,128)(2,1)}, u32[]{:S(2)}) copy-start(bf16[64,64,1,1]{1,0,2,3:T(8,128)(2,1)} %reshape.175) | copy-start | bytes 24580
  106.3 12.9 %collective-permute-start.9 = (bf16[48,128]{1,0:T(8,128)(2,1)}, bf16[48,128]{1,0:T(8,128)(2,1)S(1)}, u32[]{:S(2)}, u32[]{:S(2)}) collective-permute-start(bf16[48,128]{1,0:T(8,128)(2,1)} %reshape_squeeze.7), channel_id=1, source_target_pairs={{0,8},{8,16},{16,24},{1,9},{9,17},{17,25},{2,10},{10,18},{18,26},{... | collective-permute-start | bytes 36872 | tf_op jit(solution)/shard_map/ppermute | solution.py:174
  114.1 6.0 %copy-start.3 = (bf16[128]{0:T(256)(128)(2,1)S(1)}, bf16[128]{0:T(256)(128)(2,1)}, u32[]{:S(2)}) copy-start(bf16[128]{0:T(256)(128)(2,1)} %pad.8.clone) | copy-start | bytes 772

commit v12 on v11

--- a/solution.py
+++ b/solution.py
@@ -167,14 +167,11 @@
 
     forward = [(i, i + 1) for i in range(n_cols - 1)]
     backward = [(target, source) for source, target in forward]
-    strip_shape = x.shape[1:3] + (RADIUS,)
-    flat = (2 * count_acq * padded_rows * RADIUS // LANES, LANES)
-    left = x[blocks_per_tile - 1, :, :, local_cols - RADIUS :].reshape(flat)
-    right = x[0, :, :, :RADIUS].reshape(flat)
-    left = lax.ppermute(left, "tx", forward).reshape(strip_shape)
-    right = lax.ppermute(right, "tx", backward).reshape(strip_shape)
-    gap = jnp.zeros((2 * count_acq, padded_rows, LANES - 2 * RADIUS), x.dtype)
-    edge = jnp.concatenate([right, gap, left], axis=2)
+    left = lax.ppermute(x[blocks_per_tile - 1, :, :, local_cols - LANES :], "tx", forward)
+    right = lax.ppermute(x[0, :, :, :LANES], "tx", backward)
+    lane = lax.broadcasted_iota(jnp.int32, right.shape, 2)
+    zeros = jnp.zeros_like(right)
+    edge = jnp.where(lane < RADIUS, right, jnp.where(lane >= LANES - RADIUS, left, zeros))
 
     mixing = jnp.stack([jnp.stack([filt_re, -filt_im], -1), jnp.stack([filt_im, filt_re], -1)], 1)
     mixing = mixing.reshape(2 * count_acq, 2 * count_acq)

time: 142 us -> 139 us (0.979)
  the two profiles are of different devices: /device:TPU:26 before, /device:TPU:21 now
where the time goes in v12:
time: 139 us; the launch traced here: 138 us
  starting transfers between devices  60.4 us (43%)
  waiting for transfers between devices  27.6 us (20%)
  local copies, waits for them, and re-layouts  26 us (19%)
  Pallas kernels  19.5 us (14%)
  other arithmetic  2.01 us (1%)
  matrix products  1.64 us (1%)
    ppermute x8, starting transfers between devices, shards(): received.append(lax.ppermute(chunk, ('tx', 'ty'), pairs))  46.7 us
    pallas_call x1, Pallas kernels, pair_maps(): pl.pallas_call(kernel, grid_spec=grid_spec, out_shape=[out_shape, out_sha...  19.5 us
    ppermute x8, waiting for transfers between devices, shards(): received.append(lax.ppermute(chunk, ('tx', 'ty'), pairs))  18 us
    ppermute x1, starting transfers between devices, shards(): right = lax.ppermute(x[0, :, :, :LANES], 'tx', backward)  11.6 us
    unnamed x11, local copies, waits for them, and re-layouts  10.4 us
    ppermute x1, waiting for transfers between devices, shards(): lax.ppermute(x[blocks_per_tile - 1, :, :, local_cols - LANES:], 'tx', for...  8.27 us
    dynamic_slice x1, local copies, waits for them, and re-layouts, shards(): chunk = lax.dynamic_slice_in_dim(x, first, padded_rows, axis=2)  5.06 us
    convert_element_type x1, local copies, waits for them, and re-layouts, shards(): main.astype(jnp.bfloat16)  3.4 us
  transfers between devices with their start and end apart: 10, of which 4 were waited for; matrix products, arithmetic and copies ran while one was open for 14% of the time, Pallas kernels for 0%

profile of v12, /device:TPU:21, one launch (start us, length us, event | category | flops | bytes accessed | tf_op | source)
XLA Modules:
  0.0 138.2 jit_solution(4250769877139477717)
XLA Ops:
  0.8 5.1 %pad_dynamic-slice_fusion = (bf16[8,2,24,512]{3,2,1,0:T(8,128)(2,1)S(1)}, bf16[8,2,24,512]{3,2,1,0:T(8,128)(2,1)S(1)}, bf16[8,2,24,512]{3,2,1,0:T(8,128)(2,1)S(1...) fusion(s32[]{:T(128)S(6)} %select_n.146, ...), kind=kLoop, calls=%fused_computation.7 | loop fusion | bytes 5242912 | tf_op jit(solution)/shard_map/dynamic_slice | solution.py:159
  5.8 4.5 %collective-permute-start = (bf16[384,512]{1,0:T(8,128)(2,1)}, bf16[384,512]{1,0:T(8,128)(2,1)}, u32[]{:S(2)}, u32[]{:S(2)}) collective-permute-start(bf16[384,512]{1,0:T(8,128)(2,1)} %bitcast), channel_id=1, source_target_pairs={{0,0},{1,1},{2,8},{3,9},{4,16},{5,17},{6,24},{7,25},{8,2},{9,3},{1... | collective-permute-start | bytes 1179656 | tf_op jit(solution)/shard_map/ppermute | solution.py:161
  10.3 0.7 collective-permute-start.1
  11.0 2.3 %collective-permute-start.2 = (bf16[384,512]{1,0:T(8,128)(2,1)S(1)}, bf16[384,512]{1,0:T(8,128)(2,1)}, u32[]{:S(2)}, u32[]{:S(2)}) collective-permute-start(bf16[384,512]{1,0:T(8,128)(2,1)S(1)} %bitcast.75), channel_id=1, source_target_pairs={{0,2},{1,3},{2,10},{3,11},{4,18},{5,19},{6,26},{7,27},{8,4},{9,5},... | collective-permute-start | bytes 1179656 | tf_op jit(solution)/shard_map/ppermute | solution.py:161
  13.4 3.4 %collective-permute-start.3 = (bf16[384,512]{1,0:T(8,128)(2,1)S(1)}, bf16[384,512]{1,0:T(8,128)(2,1)}, u32[]{:S(2)}, u32[]{:S(2)}) collective-permute-start(bf16[384,512]{1,0:T(8,128)(2,1)S(1)} %bitcast.74), channel_id=1, source_target_pairs={{0,3},{1,4},{2,11},{3,12},{4,19},{5,20},{6,27},{7,28},{8,5},{9,6},... | collective-permute-start | bytes 1179656 | tf_op jit(solution)/shard_map/ppermute | solution.py:161
  17.1 0.5 copy.10
  17.6 0.8 reshape.168
  18.4 0.8 reshape.167
  19.6 0.7 pad_maximum_fusion.refs_16_
  20.3 28.9 %collective-permute-start.5 = (bf16[384,512]{1,0:T(8,128)(2,1)S(1)}, bf16[384,512]{1,0:T(8,128)(2,1)S(1)}, u32[]{:S(2)}, u32[]{:S(2)}) collective-permute-start(bf16[384,512]{1,0:T(8,128)(2,1)S(1)} %bitcast.72), channel_id=1, source_target_pairs={{0,5},{1,6},{2,13},{3,14},{4,21},{5,22},{6,29},{7,30},{8,7},{9,0},... | collective-permute-start | bytes 1179656 | tf_op jit(solution)/shard_map/ppermute | solution.py:161
  49.1 1.8 %bitcast_dynamic-update-slice_fusion.7 = bf16[8,384,512]{2,1,0:T(8,128)(2,1)} fusion(bf16[384,512]{1,0:T(8,128)(2,1)} %collective-permute-done), kind=kLoop, calls=%fused_computation.24 | loop fusion | bytes 786432
  50.9 6.1 %collective-permute-start.6 = (bf16[384,512]{1,0:T(8,128)(2,1)S(1)}, bf16[384,512]{1,0:T(8,128)(2,1)S(1)}, u32[]{:S(2)}, u32[]{:S(2)}) collective-permute-start(bf16[384,512]{1,0:T(8,128)(2,1)S(1)} %bitcast.71), channel_id=1, source_target_pairs={{0,6},{1,7},{2,14},{3,15},{4,22},{5,23},{6,30},{7,31},{8,0},{9,1},... | collective-permute-start | bytes 1179656 | tf_op jit(solution)/shard_map/ppermute | solution.py:161
  57.0 1.8 %bitcast_dynamic-update-slice_fusion.6 = bf16[8,384,512]{2,1,0:T(8,128)(2,1)} fusion(bf16[8,384,512]{2,1,0:T(8,128)(2,1)} %bitcast_dynamic-update-slice_fusion.7, bf16[384,512]{1,0:T(8,128)(2,1)} %collective-permute-done.1), kind=kLoop, calls=%fused_computation.23 | loop fusion | bytes 786432
  58.8 0.9 collective-permute-start.7
  59.6 1.8 %bitcast_dynamic-update-slice_fusion.5 = bf16[8,384,512]{2,1,0:T(8,128)(2,1)} fusion(bf16[8,384,512]{2,1,0:T(8,128)(2,1)} %bitcast_dynamic-update-slice_fusion.6, bf16[384,512]{1,0:T(8,128)(2,1)} %collective-permute-done.2), kind=kLoop, calls=%fused_computation.22 | loop fusion | bytes 786432
  61.4 1.8 %bitcast_dynamic-update-slice_fusion.4 = bf16[8,384,512]{2,1,0:T(8,128)(2,1)} fusion(bf16[8,384,512]{2,1,0:T(8,128)(2,1)} %bitcast_dynamic-update-slice_fusion.5, bf16[384,512]{1,0:T(8,128)(2,1)} %collective-permute-done.3), kind=kLoop, calls=%fused_computation.21 | loop fusion | bytes 786432
  63.2 1.8 %bitcast_dynamic-update-slice_fusion.3 = bf16[8,384,512]{2,1,0:T(8,128)(2,1)} fusion(bf16[8,384,512]{2,1,0:T(8,128)(2,1)} %bitcast_dynamic-update-slice_fusion.4, bf16[384,512]{1,0:T(8,128)(2,1)} %collective-permute-done.4), kind=kLoop, calls=%fused_computation.20 | loop fusion | bytes 786432
  65.0 10.3 %collective-permute-done.5 = bf16[384,512]{1,0:T(8,128)(2,1)S(1)} collective-permute-done((bf16[384,512]{1,0:T(8,128)(2,1)S(1)}, bf16[384,512]{1,0:T(8,128)(2,1)S(1)}, u32[]{:S(2)}, u32[]{:S(2)}) %collective-permute-start.5) | collective-permute-done | bytes 393248 | tf_op jit(solution)/shard_map/ppermute | solution.py:161
  75.3 0.8 bitcast_dynamic-update-slice_fusion.2
  76.1 7.7 %collective-permute-done.6 = bf16[384,512]{1,0:T(8,128)(2,1)S(1)} collective-permute-done((bf16[384,512]{1,0:T(8,128)(2,1)S(1)}, bf16[384,512]{1,0:T(8,128)(2,1)S(1)}, u32[]{:S(2)}, u32[]{:S(2)}) %collective-permute-start.6) | collective-permute-done | bytes 393248 | tf_op jit(solution)/shard_map/ppermute | solution.py:161
  83.7 0.8 bitcast_dynamic-update-slice_fusion.1
  84.5 0.8 bitcast_dynamic-update-slice_fusion
  85.3 2.6 %gather_fusion = bf16[8,384,512]{2,1,0:T(8,128)(2,1)S(1)} fusion(bf16[8,384,512]{2,1,0:T(8,128)(2,1)} %bitcast_dynamic-update-slice_fusion, s32[1024]{0:T(1024)S(1)} %pad_clamp_fusion), kind=kCustom, calls=%fused_computation | custom fusion | bytes 6291488 | tf_op jit(solution)/shard_map/jit(_take)/gather | solution.py:165
  88.5 11.6 %collective-permute-start.8 = (bf16[64,24,128]{2,1,0:T(8,128)(2,1)S(1)}, bf16[64,24,128]{2,1,0:T(8,128)(2,1)S(1)}, u32[]{:S(2)}, u32[]{:S(2)}) collective-permute-start(bf16[64,24,128]{2,1,0:T(8,128)(2,1)S(1)} %get-tuple-element.3), channel_id=1, source_target_pairs={{8,0},{16,8},{24,16},{9,1},{17,9},{25,17},{10,2},{18,10},{26,18},{... | collective-permute-start | bytes 1179656 | tf_op jit(solution)/shard_map/ppermute | solution.py:171
  100.0 2.1 %collective-permute-start.9 = (bf16[64,24,128]{2,1,0:T(8,128)(2,1)S(1)}, bf16[64,24,128]{2,1,0:T(8,128)(2,1)S(1)}, u32[]{:S(2)}, u32[]{:S(2)}) collective-permute-start(bf16[64,24,128]{2,1,0:T(8,128)(2,1)S(1)} %get-tuple-element.2), channel_id=1, source_target_pairs={{0,8},{8,16},{16,24},{1,9},{9,17},{17,25},{2,10},{10,18},{18,26},{... | collective-permute-start | bytes 1179656 | tf_op jit(solution)/shard_map/ppermute | solution.py:170
  102.1 0.7 broadcast_select_fusion.1
  102.9 1.4 convert_bitcast_fusion
  104.2 3.4 %copy.12 = bf16[2,64,24,512]{3,2,1,0:T(8,128)(2,1)} copy(bf16[2,64,24,512]{3,1,2,0:T(8,128)(2,1)S(1)} %convert_bitcast_fusion) | data formatting | bytes 6291456 | tf_op jit(solution)/shard_map/convert_element_type | solution.py:179
  107.6 1.4 collective-permute-done.8
  109.0 8.3 %collective-permute-done.9 = bf16[64,24,128]{2,1,0:T(8,128)(2,1)S(1)} collective-permute-done((bf16[64,24,128]{2,1,0:T(8,128)(2,1)S(1)}, bf16[64,24,128]{2,1,0:T(8,128)(2,1)S(1)}, u32[]{:S(2)}, u32[]{:S(2)}) %collective-permute-start.9) | collective-permute-done | bytes 393248 | tf_op jit(solution)/shard_map/ppermute | solution.py:170
  117.6 1.0 copy.14
  118.6 19.5 %shard_map.68 = (f32[32,16,1024]{2,1,0:T(8,128)}, f32[32,16,1024]{2,1,0:T(8,128)}) custom-call(s32[32]{0:T(128)} %pre_ref.1, s32[32]{0:T(128)} %post_ref.1, bf16[2,32,2,24,512]{4,3,2,1,0:T(8,128)(2,1)} %bitcast.52, bf16[32,2,24,128]{3,2,1,0:T(8,128)(2,1)} %bitcast.60, bf16[2,32,2,24,512]{4,3,2,1,0:T(8,128)(2,1)} %bitcast.53, ...), custom_call_target="tpu_custom_call" | custom-call | tf_op jit(solution)/shard_map/pallas_call | solution.py:130
  (31 shorter events, 1.5 us)
Async XLA Ops:
  0.6 16.3 %copy-start = (bf16[32,32]{1,0:T(8,128)(2,1)S(1)}, bf16[32,32]{1,0:T(8,128)(2,1)}, u32[]{:S(2)}) copy-start(bf16[32,32]{1,0:T(8,128)(2,1)} %param.7) | copy-start | bytes 6148
  0.6 16.4 %copy-start.1 = (bf16[32,32]{1,0:T(8,128)(2,1)S(1)}, bf16[32,32]{1,0:T(8,128)(2,1)}, u32[]{:S(2)}) copy-start(bf16[32,32]{1,0:T(8,128)(2,1)} %param.6) | copy-start | bytes 6148
  5.8 14.4 %collective-permute-start = (bf16[384,512]{1,0:T(8,128)(2,1)}, bf16[384,512]{1,0:T(8,128)(2,1)}, u32[]{:S(2)}, u32[]{:S(2)}) collective-permute-start(bf16[384,512]{1,0:T(8,128)(2,1)} %bitcast), channel_id=1, source_target_pairs={{0,0},{1,1},{2,8},{3,9},{4,16},{5,17},{6,24},{7,25},{8,2},{9,3},{1... | collective-permute-start | bytes 1179656 | tf_op jit(solution)/shard_map/ppermute | solution.py:161
  10.3 40.6 %collective-permute-start.1 = (bf16[384,512]{1,0:T(8,128)(2,1)S(1)}, bf16[384,512]{1,0:T(8,128)(2,1)}, u32[]{:S(2)}, u32[]{:S(2)}) collective-permute-start(bf16[384,512]{1,0:T(8,128)(2,1)S(1)} %bitcast.76), channel_id=1, source_target_pairs={{0,1},{1,2},{2,9},{3,10},{4,17},{5,18},{6,25},{7,26},{8,3},{9,4},{... | collective-permute-start | bytes 1179656 | tf_op jit(solution)/shard_map/ppermute | solution.py:161
  11.0 47.7 %collective-permute-start.2 = (bf16[384,512]{1,0:T(8,128)(2,1)S(1)}, bf16[384,512]{1,0:T(8,128)(2,1)}, u32[]{:S(2)}, u32[]{:S(2)}) collective-permute-start(bf16[384,512]{1,0:T(8,128)(2,1)S(1)} %bitcast.75), channel_id=1, source_target_pairs={{0,2},{1,3},{2,10},{3,11},{4,18},{5,19},{6,26},{7,27},{8,4},{9,5},... | collective-permute-start | bytes 1179656 | tf_op jit(solution)/shard_map/ppermute | solution.py:161
  13.4 48.0 %collective-permute-start.3 = (bf16[384,512]{1,0:T(8,128)(2,1)S(1)}, bf16[384,512]{1,0:T(8,128)(2,1)}, u32[]{:S(2)}, u32[]{:S(2)}) collective-permute-start(bf16[384,512]{1,0:T(8,128)(2,1)S(1)} %bitcast.74), channel_id=1, source_target_pairs={{0,3},{1,4},{2,11},{3,12},{4,19},{5,20},{6,27},{7,28},{8,5},{9,6},... | collective-permute-start | bytes 1179656 | tf_op jit(solution)/shard_map/ppermute | solution.py:161
  16.7 46.5 %collective-permute-start.4 = (bf16[384,512]{1,0:T(8,128)(2,1)S(1)}, bf16[384,512]{1,0:T(8,128)(2,1)}, u32[]{:S(2)}, u32[]{:S(2)}) collective-permute-start(bf16[384,512]{1,0:T(8,128)(2,1)S(1)} %bitcast.73), channel_id=1, source_target_pairs={{0,4},{1,5},{2,12},{3,13},{4,20},{5,21},{6,28},{7,29},{8,6},{9,7},... | collective-permute-start | bytes 1179656 | tf_op jit(solution)/shard_map/ppermute | solution.py:161
  20.3 55.0 %collective-permute-start.5 = (bf16[384,512]{1,0:T(8,128)(2,1)S(1)}, bf16[384,512]{1,0:T(8,128)(2,1)S(1)}, u32[]{:S(2)}, u32[]{:S(2)}) collective-permute-start(bf16[384,512]{1,0:T(8,128)(2,1)S(1)} %bitcast.72), channel_id=1, source_target_pairs={{0,5},{1,6},{2,13},{3,14},{4,21},{5,22},{6,29},{7,30},{8,7},{9,0},... | collective-permute-start | bytes 1179656 | tf_op jit(solution)/shard_map/ppermute | solution.py:161
  50.9 32.8 %collective-permute-start.6 = (bf16[384,512]{1,0:T(8,128)(2,1)S(1)}, bf16[384,512]{1,0:T(8,128)(2,1)S(1)}, u32[]{:S(2)}, u32[]{:S(2)}) collective-permute-start(bf16[384,512]{1,0:T(8,128)(2,1)S(1)} %bitcast.71), channel_id=1, source_target_pairs={{0,6},{1,7},{2,14},{3,15},{4,22},{5,23},{6,30},{7,31},{8,0},{9,1},... | collective-permute-start | bytes 1179656 | tf_op jit(solution)/shard_map/ppermute | solution.py:161
  58.8 25.7 %collective-permute-start.7 = (bf16[384,512]{1,0:T(8,128)(2,1)S(1)}, bf16[384,512]{1,0:T(8,128)(2,1)S(1)}, u32[]{:S(2)}, u32[]{:S(2)}) collective-permute-start(bf16[384,512]{1,0:T(8,128)(2,1)S(1)} %bitcast.70), channel_id=1, source_target_pairs={{0,7},{1,0},{2,15},{3,8},{4,23},{5,16},{6,31},{7,24},{8,1},{9,2},{... | collective-permute-start | bytes 1179656 | tf_op jit(solution)/shard_map/ppermute | solution.py:161
  88.5 20.6 %collective-permute-start.8 = (bf16[64,24,128]{2,1,0:T(8,128)(2,1)S(1)}, bf16[64,24,128]{2,1,0:T(8,128)(2,1)S(1)}, u32[]{:S(2)}, u32[]{:S(2)}) collective-permute-start(bf16[64,24,128]{2,1,0:T(8,128)(2,1)S(1)} %get-tuple-element.3), channel_id=1, source_target_pairs={{8,0},{16,8},{24,16},{9,1},{17,9},{25,17},{10,2},{18,10},{26,18},{... | collective-permute-start | bytes 1179656 | tf_op jit(solution)/shard_map/ppermute | solution.py:171
  100.0 17.2 %collective-permute-start.9 = (bf16[64,24,128]{2,1,0:T(8,128)(2,1)S(1)}, bf16[64,24,128]{2,1,0:T(8,128)(2,1)S(1)}, u32[]{:S(2)}, u32[]{:S(2)}) collective-permute-start(bf16[64,24,128]{2,1,0:T(8,128)(2,1)S(1)} %get-tuple-element.2), channel_id=1, source_target_pairs={{0,8},{8,16},{16,24},{1,9},{9,17},{17,25},{2,10},{10,18},{18,26},{... | collective-permute-start | bytes 1179656 | tf_op jit(solution)/shard_map/ppermute | solution.py:170

commit v13 on v12

--- a/solution.py
+++ b/solution.py
@@ -167,18 +167,16 @@
 
     forward = [(i, i + 1) for i in range(n_cols - 1)]
     backward = [(target, source) for source, target in forward]
-    left = lax.ppermute(x[blocks_per_tile - 1, :, :, local_cols - LANES :], "tx", forward)
-    right = lax.ppermute(x[0, :, :, :LANES], "tx", backward)
-    lane = lax.broadcasted_iota(jnp.int32, right.shape, 2)
-    zeros = jnp.zeros_like(right)
-    edge = jnp.where(lane < RADIUS, right, jnp.where(lane >= LANES - RADIUS, left, zeros))
-
     mixing = jnp.stack([jnp.stack([filt_re, -filt_im], -1), jnp.stack([filt_im, filt_re], -1)], 1)
     mixing = mixing.reshape(2 * count_acq, 2 * count_acq)
     main = jnp.einsum("kc,bchw->bkhw", mixing, x, preferred_element_type=jnp.float32)
     main = main.astype(jnp.bfloat16).reshape(blocks_per_tile, count_acq, 2, padded_rows, local_cols)
-    edge = jnp.einsum("kc,chw->khw", mixing, edge, preferred_element_type=jnp.float32)
-    edge = edge.astype(jnp.bfloat16).reshape(count_acq, 2, padded_rows, LANES)
+
+    left = lax.ppermute(main[blocks_per_tile - 1, :, :, :, local_cols - LANES :], "tx", forward)
+    right = lax.ppermute(main[0, :, :, :, :LANES], "tx", backward)
+    lane = lax.broadcasted_iota(jnp.int32, right.shape, 3)
+    zeros = jnp.zeros_like(right)
+    edge = jnp.where(lane < RADIUS, right, jnp.where(lane >= LANES - RADIUS, left, zeros))
     return pair_maps(main, edge, pre_ids, post_ids, tile_rows, tile_cols)
 
 

time: 139 us -> 142 us (1.022)
  waiting for transfers between devices: 27.6 us -> 32.5 us
  local copies, waits for them, and re-layouts: 26 us -> 22.6 us
    ppermute x2, waiting for transfers between devices: 9.64 us -> 14.5 us  [the longest x1 8.28 us: shards(): lax.ppermute(main[blocks_per_tile - 1, :, :, :, local_cols - LANES:], 'tx...]
    convert_element_type x1, local copies, waits for them, and re-layouts: 3.4 us -> 1.76 us  [shards(): main.astype(jnp.bfloat16)]
    ppermute x8, starting transfers between devices: 46.7 us -> 48.4 us  [shards(): received.append(lax.ppermute(chunk, ('tx', 'ty'), pairs))]
    unnamed x11 -> x13, local copies, waits for them, and re-layouts: 10.4 us -> 10.5 us
  transfers between devices with their start and end apart: 10 -> 10, of which waited for: 4 -> 4; matrix products, arithmetic and copies ran while one was open for 14% -> 9% of each run, Pallas kernels for 0% -> 0%
where the time goes in v13:
time: 142 us; the launch traced here: 141 us
  starting transfers between devices  61.8 us (44%)
  waiting for transfers between devices  32.5 us (23%)
  local copies, waits for them, and re-layouts  22.6 us (16%)
  Pallas kernels  19.5 us (14%)
  other arithmetic  2.39 us (2%)
    ppermute x8, starting transfers between devices, shards(): received.append(lax.ppermute(chunk, ('tx', 'ty'), pairs))  48.4 us
    pallas_call x1, Pallas kernels, pair_maps(): pl.pallas_call(kernel, grid_spec=grid_spec, out_shape=[out_shape, out_sha...  19.5 us
    ppermute x8, waiting for transfers between devices, shards(): received.append(lax.ppermute(chunk, ('tx', 'ty'), pairs))  18 us
    ppermute x1, starting transfers between devices, shards(): right = lax.ppermute(main[0, :, :, :, :LANES], 'tx', backward)  11.6 us
    unnamed x13, local copies, waits for them, and re-layouts  10.5 us
    ppermute x1, waiting for transfers between devices, shards(): lax.ppermute(main[blocks_per_tile - 1, :, :, :, local_cols - LANES:], 'tx...  8.28 us
    ppermute x1, waiting for transfers between devices, shards(): right = lax.ppermute(main[0, :, :, :, :LANES], 'tx', backward)  6.23 us
    dynamic_slice x1, local copies, waits for them, and re-layouts, shards(): chunk = lax.dynamic_slice_in_dim(x, first, padded_rows, axis=2)  5.06 us
  transfers between devices with their start and end apart: 10, of which 4 were waited for; matrix products, arithmetic and copies ran while one was open for 9% of the time, Pallas kernels for 0%

profile of v13, /device:TPU:21, one launch (start us, length us, event | category | flops | bytes accessed | tf_op | source)
XLA Modules:
  0.0 141.0 jit_solution(3831119709205551935)
XLA Ops:
  0.8 5.1 %pad_dynamic-slice_fusion = (bf16[8,2,24,512]{3,2,1,0:T(8,128)(2,1)S(1)}, bf16[8,2,24,512]{3,2,1,0:T(8,128)(2,1)S(1)}, bf16[8,2,24,512]{3,2,1,0:T(8,128)(2,1)S(1...) fusion(s32[]{:T(128)S(6)} %select_n.144, ...), kind=kLoop, calls=%fused_computation.5 | loop fusion | bytes 5242912 | tf_op jit(solution)/shard_map/dynamic_slice | solution.py:159
  5.8 4.5 %collective-permute-start = (bf16[384,512]{1,0:T(8,128)(2,1)}, bf16[384,512]{1,0:T(8,128)(2,1)}, u32[]{:S(2)}, u32[]{:S(2)}) collective-permute-start(bf16[384,512]{1,0:T(8,128)(2,1)} %bitcast), channel_id=1, source_target_pairs={{0,0},{1,1},{2,8},{3,9},{4,16},{5,17},{6,24},{7,25},{8,2},{9,3},{1... | collective-permute-start | bytes 1179656 | tf_op jit(solution)/shard_map/ppermute | solution.py:161
  10.3 0.7 collective-permute-start.1
  11.0 2.4 %collective-permute-start.2 = (bf16[384,512]{1,0:T(8,128)(2,1)S(1)}, bf16[384,512]{1,0:T(8,128)(2,1)}, u32[]{:S(2)}, u32[]{:S(2)}) collective-permute-start(bf16[384,512]{1,0:T(8,128)(2,1)S(1)} %bitcast.62), channel_id=1, source_target_pairs={{0,2},{1,3},{2,10},{3,11},{4,18},{5,19},{6,26},{7,27},{8,4},{9,5},... | collective-permute-start | bytes 1179656 | tf_op jit(solution)/shard_map/ppermute | solution.py:161
  13.4 3.3 %collective-permute-start.3 = (bf16[384,512]{1,0:T(8,128)(2,1)S(1)}, bf16[384,512]{1,0:T(8,128)(2,1)}, u32[]{:S(2)}, u32[]{:S(2)}) collective-permute-start(bf16[384,512]{1,0:T(8,128)(2,1)S(1)} %bitcast.61), channel_id=1, source_target_pairs={{0,3},{1,4},{2,11},{3,12},{4,19},{5,20},{6,27},{7,28},{8,5},{9,6},... | collective-permute-start | bytes 1179656 | tf_op jit(solution)/shard_map/ppermute | solution.py:161
  17.3 0.5 copy.9
  17.8 0.8 reshape.163
  18.6 30.5 %collective-permute-start.5 = (bf16[384,512]{1,0:T(8,128)(2,1)S(1)}, bf16[384,512]{1,0:T(8,128)(2,1)S(1)}, u32[]{:S(2)}, u32[]{:S(2)}) collective-permute-start(bf16[384,512]{1,0:T(8,128)(2,1)S(1)} %bitcast.59), channel_id=1, source_target_pairs={{0,5},{1,6},{2,13},{3,14},{4,21},{5,22},{6,29},{7,30},{8,7},{9,0},... | collective-permute-start | bytes 1179656 | tf_op jit(solution)/shard_map/ppermute | solution.py:161
  49.1 1.8 %bitcast_dynamic-update-slice_fusion.7 = bf16[8,384,512]{2,1,0:T(8,128)(2,1)} fusion(bf16[384,512]{1,0:T(8,128)(2,1)} %collective-permute-done), kind=kLoop, calls=%fused_computation.22 | loop fusion | bytes 786432
  50.9 6.1 %collective-permute-start.6 = (bf16[384,512]{1,0:T(8,128)(2,1)S(1)}, bf16[384,512]{1,0:T(8,128)(2,1)S(1)}, u32[]{:S(2)}, u32[]{:S(2)}) collective-permute-start(bf16[384,512]{1,0:T(8,128)(2,1)S(1)} %bitcast.58), channel_id=1, source_target_pairs={{0,6},{1,7},{2,14},{3,15},{4,22},{5,23},{6,30},{7,31},{8,0},{9,1},... | collective-permute-start | bytes 1179656 | tf_op jit(solution)/shard_map/ppermute | solution.py:161
  57.0 1.8 %bitcast_dynamic-update-slice_fusion.6 = bf16[8,384,512]{2,1,0:T(8,128)(2,1)} fusion(bf16[8,384,512]{2,1,0:T(8,128)(2,1)} %bitcast_dynamic-update-slice_fusion.7, bf16[384,512]{1,0:T(8,128)(2,1)} %collective-permute-done.1), kind=kLoop, calls=%fused_computation.21 | loop fusion | bytes 786432
  58.8 0.9 collective-permute-start.7
  59.6 1.8 %bitcast_dynamic-update-slice_fusion.5 = bf16[8,384,512]{2,1,0:T(8,128)(2,1)} fusion(bf16[8,384,512]{2,1,0:T(8,128)(2,1)} %bitcast_dynamic-update-slice_fusion.6, bf16[384,512]{1,0:T(8,128)(2,1)} %collective-permute-done.2), kind=kLoop, calls=%fused_computation.20 | loop fusion | bytes 786432
  61.4 1.8 %bitcast_dynamic-update-slice_fusion.4 = bf16[8,384,512]{2,1,0:T(8,128)(2,1)} fusion(bf16[8,384,512]{2,1,0:T(8,128)(2,1)} %bitcast_dynamic-update-slice_fusion.5, bf16[384,512]{1,0:T(8,128)(2,1)} %collective-permute-done.3), kind=kLoop, calls=%fused_computation.19 | loop fusion | bytes 786432
  63.2 1.8 %bitcast_dynamic-update-slice_fusion.3 = bf16[8,384,512]{2,1,0:T(8,128)(2,1)} fusion(bf16[8,384,512]{2,1,0:T(8,128)(2,1)} %bitcast_dynamic-update-slice_fusion.4, bf16[384,512]{1,0:T(8,128)(2,1)} %collective-permute-done.4), kind=kLoop, calls=%fused_computation.18 | loop fusion | bytes 786432
  65.0 10.3 %collective-permute-done.5 = bf16[384,512]{1,0:T(8,128)(2,1)S(1)} collective-permute-done((bf16[384,512]{1,0:T(8,128)(2,1)S(1)}, bf16[384,512]{1,0:T(8,128)(2,1)S(1)}, u32[]{:S(2)}, u32[]{:S(2)}) %collective-permute-start.5) | collective-permute-done | bytes 393248 | tf_op jit(solution)/shard_map/ppermute | solution.py:161
  75.3 0.8 bitcast_dynamic-update-slice_fusion.2
  76.1 7.6 %collective-permute-done.6 = bf16[384,512]{1,0:T(8,128)(2,1)S(1)} collective-permute-done((bf16[384,512]{1,0:T(8,128)(2,1)S(1)}, bf16[384,512]{1,0:T(8,128)(2,1)S(1)}, u32[]{:S(2)}, u32[]{:S(2)}) %collective-permute-start.6) | collective-permute-done | bytes 393248 | tf_op jit(solution)/shard_map/ppermute | solution.py:161
  83.7 0.8 bitcast_dynamic-update-slice_fusion.1
  84.5 0.8 bitcast_dynamic-update-slice_fusion
  85.3 2.6 %gather_fusion = bf16[8,384,512]{2,1,0:T(8,128)(2,1)S(1)} fusion(bf16[8,384,512]{2,1,0:T(8,128)(2,1)} %bitcast_dynamic-update-slice_fusion, s32[1024]{0:T(1024)S(1)} %pad_clamp_fusion), kind=kCustom, calls=%fused_computation | custom fusion | bytes 6291488 | tf_op jit(solution)/shard_map/jit(_take)/gather | solution.py:165
  87.9 0.7 broadcast_select_fusion
  88.6 1.4 convert_bitcast_fusion
  90.0 1.8 %copy.11 = bf16[2,64,24,512]{3,2,1,0:T(8,128)(2,1)S(1)} copy(bf16[2,64,24,512]{3,1,2,0:T(8,128)(2,1)S(1)} %convert_bitcast_fusion) | data formatting | bytes 6291456 | tf_op jit(solution)/shard_map/convert_element_type | solution.py:173
  91.8 0.1 slice_bitcast_fusion
  92.0 11.6 %collective-permute-start.8 = (bf16[32,2,24,128]{3,2,1,0:T(8,128)(2,1)S(1)}, bf16[32,2,24,128]{3,2,1,0:T(8,128)(2,1)S(1)}, u32[]{:S(2)}, u32[]{:S(2)}) collective-permute-start(bf16[32,2,24,128]{3,2,1,0:T(8,128)(2,1)S(1)} %get-tuple-element.3), channel_id=1, source_target_pairs={{8,0},{16,8},{24,16},{9,1},{17,9},{25,17},{10,2},{18,10},{26,18},{... | collective-permute-start | bytes 1179656 | tf_op jit(solution)/shard_map/ppermute | solution.py:176
  103.5 1.9 %collective-permute-start.9 = (bf16[32,2,24,128]{3,2,1,0:T(8,128)(2,1)S(1)}, bf16[32,2,24,128]{3,2,1,0:T(8,128)(2,1)S(1)}, u32[]{:S(2)}, u32[]{:S(2)}) collective-permute-start(bf16[32,2,24,128]{3,2,1,0:T(8,128)(2,1)S(1)} %get-tuple-element.2), channel_id=1, source_target_pairs={{0,8},{8,16},{16,24},{1,9},{9,17},{17,25},{2,10},{10,18},{18,26},{... | collective-permute-start | bytes 1179656 | tf_op jit(solution)/shard_map/ppermute | solution.py:175
  105.6 0.7 pad_maximum_fusion.refs_16_
  106.3 6.2 %collective-permute-done.8 = bf16[32,2,24,128]{3,2,1,0:T(8,128)(2,1)S(1)} collective-permute-done((bf16[32,2,24,128]{3,2,1,0:T(8,128)(2,1)S(1)}, bf16[32,2,24,128]{3,2,1,0:T(8,128)(2,1)S(1)}, u32[]{:S(2)}, u32[]{:S(2)}) %collective-permute-start.8) | collective-permute-done | bytes 393248 | tf_op jit(solution)/shard_map/ppermute | solution.py:176
  112.5 8.3 %collective-permute-done.9 = bf16[32,2,24,128]{3,2,1,0:T(8,128)(2,1)S(1)} collective-permute-done((bf16[32,2,24,128]{3,2,1,0:T(8,128)(2,1)S(1)}, bf16[32,2,24,128]{3,2,1,0:T(8,128)(2,1)S(1)}, u32[]{:S(2)}, u32[]{:S(2)}) %collective-permute-start.9) | collective-permute-done | bytes 393248 | tf_op jit(solution)/shard_map/ppermute | solution.py:175
  120.8 0.8 select_select_fusion.refs_1_.refs_3_.refs_5_.refs_7_.refs_9_.refs_11_.refs_13_.refs_15_
  121.6 19.5 %shard_map.68 = (f32[32,16,1024]{2,1,0:T(8,128)}, f32[32,16,1024]{2,1,0:T(8,128)}) custom-call(s32[32]{0:T(128)} %pre_ref.1, s32[32]{0:T(128)} %post_ref.1, bf16[2,32,2,24,512]{4,3,2,1,0:T(8,128)(2,1)} %bitcast.48, bf16[32,2,24,128]{3,2,1,0:T(8,128)(2,1)} %select_select_fusion.refs_1_.refs_3_.refs_5_.refs_7_.refs_9_.refs_11_.refs_13_.refs_15_, ...), custom_call_target="tpu_custom_call" | custom-call | tf_op jit(solution)/shard_map/pallas_call | solution.py:130
  (29 shorter events, 0.7 us)
Async XLA Ops:
  0.6 16.2 %copy-start.1 = (bf16[32,32]{1,0:T(8,128)(2,1)S(1)}, bf16[32,32]{1,0:T(8,128)(2,1)}, u32[]{:S(2)}) copy-start(bf16[32,32]{1,0:T(8,128)(2,1)} %param.7) | copy-start | bytes 6148
  0.6 16.2 %copy-start.2 = (bf16[32,32]{1,0:T(8,128)(2,1)S(1)}, bf16[32,32]{1,0:T(8,128)(2,1)}, u32[]{:S(2)}) copy-start(bf16[32,32]{1,0:T(8,128)(2,1)} %param.6) | copy-start | bytes 6148
  5.8 12.8 %collective-permute-start = (bf16[384,512]{1,0:T(8,128)(2,1)}, bf16[384,512]{1,0:T(8,128)(2,1)}, u32[]{:S(2)}, u32[]{:S(2)}) collective-permute-start(bf16[384,512]{1,0:T(8,128)(2,1)} %bitcast), channel_id=1, source_target_pairs={{0,0},{1,1},{2,8},{3,9},{4,16},{5,17},{6,24},{7,25},{8,2},{9,3},{1... | collective-permute-start | bytes 1179656 | tf_op jit(solution)/shard_map/ppermute | solution.py:161
  10.3 40.6 %collective-permute-start.1 = (bf16[384,512]{1,0:T(8,128)(2,1)S(1)}, bf16[384,512]{1,0:T(8,128)(2,1)}, u32[]{:S(2)}, u32[]{:S(2)}) collective-permute-start(bf16[384,512]{1,0:T(8,128)(2,1)S(1)} %bitcast.63), channel_id=1, source_target_pairs={{0,1},{1,2},{2,9},{3,10},{4,17},{5,18},{6,25},{7,26},{8,3},{9,4},{... | collective-permute-start | bytes 1179656 | tf_op jit(solution)/shard_map/ppermute | solution.py:161
  11.0 47.7 %collective-permute-start.2 = (bf16[384,512]{1,0:T(8,128)(2,1)S(1)}, bf16[384,512]{1,0:T(8,128)(2,1)}, u32[]{:S(2)}, u32[]{:S(2)}) collective-permute-start(bf16[384,512]{1,0:T(8,128)(2,1)S(1)} %bitcast.62), channel_id=1, source_target_pairs={{0,2},{1,3},{2,10},{3,11},{4,18},{5,19},{6,26},{7,27},{8,4},{9,5},... | collective-permute-start | bytes 1179656 | tf_op jit(solution)/shard_map/ppermute | solution.py:161
  13.4 48.0 %collective-permute-start.3 = (bf16[384,512]{1,0:T(8,128)(2,1)S(1)}, bf16[384,512]{1,0:T(8,128)(2,1)}, u32[]{:S(2)}, u32[]{:S(2)}) collective-permute-start(bf16[384,512]{1,0:T(8,128)(2,1)S(1)} %bitcast.61), channel_id=1, source_target_pairs={{0,3},{1,4},{2,11},{3,12},{4,19},{5,20},{6,27},{7,28},{8,5},{9,6},... | collective-permute-start | bytes 1179656 | tf_op jit(solution)/shard_map/ppermute | solution.py:161
  16.7 46.5 %collective-permute-start.4 = (bf16[384,512]{1,0:T(8,128)(2,1)S(1)}, bf16[384,512]{1,0:T(8,128)(2,1)}, u32[]{:S(2)}, u32[]{:S(2)}) collective-permute-start(bf16[384,512]{1,0:T(8,128)(2,1)S(1)} %bitcast.60), channel_id=1, source_target_pairs={{0,4},{1,5},{2,12},{3,13},{4,20},{5,21},{6,28},{7,29},{8,6},{9,7},... | collective-permute-start | bytes 1179656 | tf_op jit(solution)/shard_map/ppermute | solution.py:161
  18.6 56.7 %collective-permute-start.5 = (bf16[384,512]{1,0:T(8,128)(2,1)S(1)}, bf16[384,512]{1,0:T(8,128)(2,1)S(1)}, u32[]{:S(2)}, u32[]{:S(2)}) collective-permute-start(bf16[384,512]{1,0:T(8,128)(2,1)S(1)} %bitcast.59), channel_id=1, source_target_pairs={{0,5},{1,6},{2,13},{3,14},{4,21},{5,22},{6,29},{7,30},{8,7},{9,0},... | collective-permute-start | bytes 1179656 | tf_op jit(solution)/shard_map/ppermute | solution.py:161
  50.9 32.8 %collective-permute-start.6 = (bf16[384,512]{1,0:T(8,128)(2,1)S(1)}, bf16[384,512]{1,0:T(8,128)(2,1)S(1)}, u32[]{:S(2)}, u32[]{:S(2)}) collective-permute-start(bf16[384,512]{1,0:T(8,128)(2,1)S(1)} %bitcast.58), channel_id=1, source_target_pairs={{0,6},{1,7},{2,14},{3,15},{4,22},{5,23},{6,30},{7,31},{8,0},{9,1},... | collective-permute-start | bytes 1179656 | tf_op jit(solution)/shard_map/ppermute | solution.py:161
  58.8 25.7 %collective-permute-start.7 = (bf16[384,512]{1,0:T(8,128)(2,1)S(1)}, bf16[384,512]{1,0:T(8,128)(2,1)S(1)}, u32[]{:S(2)}, u32[]{:S(2)}) collective-permute-start(bf16[384,512]{1,0:T(8,128)(2,1)S(1)} %bitcast.57), channel_id=1, source_target_pairs={{0,7},{1,0},{2,15},{3,8},{4,23},{5,16},{6,31},{7,24},{8,1},{9,2},{... | collective-permute-start | bytes 1179656 | tf_op jit(solution)/shard_map/ppermute | solution.py:161
  91.8 29.8 %copy-start = (bf16[2,64,24,512]{3,2,1,0:T(8,128)(2,1)}, bf16[2,64,24,512]{3,2,1,0:T(8,128)(2,1)S(1)}, u32[]{:S(2)}) copy-start(bf16[2,64,24,512]{3,2,1,0:T(8,128)(2,1)S(1)} %copy.11) | copy-start | bytes 9437188
  92.0 20.5 %collective-permute-start.8 = (bf16[32,2,24,128]{3,2,1,0:T(8,128)(2,1)S(1)}, bf16[32,2,24,128]{3,2,1,0:T(8,128)(2,1)S(1)}, u32[]{:S(2)}, u32[]{:S(2)}) collective-permute-start(bf16[32,2,24,128]{3,2,1,0:T(8,128)(2,1)S(1)} %get-tuple-element.3), channel_id=1, source_target_pairs={{8,0},{16,8},{24,16},{9,1},{17,9},{25,17},{10,2},{18,10},{26,18},{... | collective-permute-start | bytes 1179656 | tf_op jit(solution)/shard_map/ppermute | solution.py:176
  103.5 17.3 %collective-permute-start.9 = (bf16[32,2,24,128]{3,2,1,0:T(8,128)(2,1)S(1)}, bf16[32,2,24,128]{3,2,1,0:T(8,128)(2,1)S(1)}, u32[]{:S(2)}, u32[]{:S(2)}) collective-permute-start(bf16[32,2,24,128]{3,2,1,0:T(8,128)(2,1)S(1)} %get-tuple-element.2), channel_id=1, source_target_pairs={{0,8},{8,16},{16,24},{1,9},{9,17},{17,25},{2,10},{10,18},{18,26},{... | collective-permute-start | bytes 1179656 | tf_op jit(solution)/shard_map/ppermute | solution.py:175

commit v14 on v12

--- a/solution.py
+++ b/solution.py
@@ -143,6 +143,7 @@
     blocks_per_tile = n_rows // n_cols
     tile_cols = local_cols * blocks_per_tile
     padded_rows = tile_rows + 2 * RADIUS
+    sent_rows = tile_rows + RADIUS
 
     me_col = lax.axis_index("tx")
     me_row = lax.axis_index("ty")
@@ -155,15 +156,22 @@
             for row in range(n_rows):
                 to_row = (m + col * blocks_per_tile + row % blocks_per_tile) % n_rows
                 pairs.append((col * n_rows + row, (row // blocks_per_tile) * n_rows + to_row))
-        first = ((start + m) % n_rows) * tile_rows
-        chunk = lax.dynamic_slice_in_dim(x, first, padded_rows, axis=2)
-        chunk = chunk.reshape(local_acq * 2 * padded_rows, local_cols)
+        to_block = (start + m) % n_rows
+        first = to_block * tile_rows + RADIUS * (to_block % 2)
+        chunk = lax.dynamic_slice_in_dim(x, first, sent_rows, axis=2)
+        chunk = chunk.reshape(local_acq * 2 * sent_rows, local_cols)
         received.append(lax.ppermute(chunk, ("tx", "ty"), pairs))
     received = jnp.stack(received, axis=0)
     source = jnp.arange(blocks_per_tile)[:, None] + blocks_per_tile * jnp.arange(n_cols)[None, :]
     order = (me_row - source) % n_rows
     x = jnp.take(received, order.reshape(-1), axis=0)
-    x = x.reshape(blocks_per_tile, 2 * count_acq, padded_rows, local_cols)
+    x = x.reshape(blocks_per_tile, 2 * count_acq, sent_rows, local_cols)
+    even = me_row % 2 == 0
+    share = jnp.where(even, x[:, :, sent_rows - RADIUS :], x[:, :, :RADIUS])
+    share_shape = share.shape
+    partners = [(i, i + 1 - 2 * (i % 2)) for i in range(n_rows)]
+    share = lax.ppermute(share.reshape(-1, local_cols), "ty", partners).reshape(share_shape)
+    x = jnp.where(even, jnp.concatenate([x, share], axis=2), jnp.concatenate([share, x], axis=2))
 
     forward = [(i, i + 1) for i in range(n_cols - 1)]
     backward = [(target, source) for source, target in forward]

time: 139 us -> 144 us (1.036)
  the two profiles are of different devices: /device:TPU:21 before, /device:TPU:0 now
where the time goes in v14:
time: 144 us
  starting transfers between devices  69.2 us (48%)
  local copies, waits for them, and re-layouts  32.7 us (23%)
  Pallas kernels  19.5 us (14%)
  waiting for transfers between devices  9.73 us (7%)
  other arithmetic  7.78 us (5%)
  matrix products  3.46 us (2%)
    ppermute x8, starting transfers between devices, shards(): received.append(lax.ppermute(chunk, ('tx', 'ty'), pairs))  42 us
    ppermute x1, starting transfers between devices, shards(): lax.ppermute(share.reshape(-1, local_cols), 'ty', partners)  20.9 us
    pallas_call x1, Pallas kernels, pair_maps(): pl.pallas_call(kernel, grid_spec=grid_spec, out_shape=[out_shape, out_sha...  19.5 us
    unnamed x13, local copies, waits for them, and re-layouts  8.82 us
    ppermute x1, waiting for transfers between devices, shards(): right = lax.ppermute(x[0, :, :, :LANES], 'tx', backward)  7.56 us
    ppermute x1, starting transfers between devices, shards(): lax.ppermute(x[blocks_per_tile - 1, :, :, local_cols - LANES:], 'tx', for...  4.83 us
    gather x2, local copies, waits for them, and re-layouts, shards(): x = jnp.take(received, order.reshape(-1), axis=0)  4.79 us
    dynamic_slice x1, local copies, waits for them, and re-layouts, shards(): chunk = lax.dynamic_slice_in_dim(x, first, sent_rows, axis=2)  4.77 us
  transfers between devices with their start and end apart: 11, of which 4 were waited for; matrix products, arithmetic and copies ran while one was open for 13% of the time, Pallas kernels for 0%

profile of v14, /device:TPU:0, one launch (start us, length us, event | category | flops | bytes accessed | tf_op | source)
XLA Modules:
  0.0 143.6 jit_solution(12482255337008419534)
XLA Ops:
  0.9 4.8 %pad_dynamic-slice_fusion = (bf16[8,2,20,512]{3,2,1,0:T(8,128)(2,1)S(1)}, bf16[8,2,20,512]{3,2,1,0:T(8,128)(2,1)S(1)}, bf16[8,2,20,512]{3,2,1,0:T(8,128)(2,1)S(1...) fusion(s32[]{:T(128)S(6)} %select_n.194, ...), kind=kLoop, calls=%fused_computation.7 | loop fusion | bytes 4718624 | tf_op jit(solution)/shard_map/dynamic_slice | solution.py:161
  5.7 0.8 reshape.134
  6.5 4.0 %collective-permute-start = (bf16[320,512]{1,0:T(8,128)(2,1)}, bf16[320,512]{1,0:T(8,128)(2,1)}, u32[]{:S(2)}, u32[]{:S(2)}) collective-permute-start(bf16[320,512]{1,0:T(8,128)(2,1)} %reshape.134), channel_id=1, source_target_pairs={{0,0},{1,1},{2,8},{3,9},{4,16},{5,17},{6,24},{7,25},{8,2},{9,3},{1... | collective-permute-start | bytes 983048 | tf_op jit(solution)/shard_map/ppermute | solution.py:163
  10.5 5.3 %collective-permute-start.6 = (bf16[320,512]{1,0:T(8,128)(2,1)S(1)}, bf16[320,512]{1,0:T(8,128)(2,1)S(1)}, u32[]{:S(2)}, u32[]{:S(2)}) collective-permute-start(bf16[320,512]{1,0:T(8,128)(2,1)S(1)} %reshape.140), channel_id=1, source_target_pairs={{0,6},{1,7},{2,14},{3,15},{4,22},{5,23},{6,30},{7,31},{8,0},{9,1},... | collective-permute-start | bytes 983048 | tf_op jit(solution)/shard_map/ppermute | solution.py:163
  15.9 0.8 reshape.138
  16.7 0.8 collective-permute-start.4
  18.3 2.2 %collective-permute-start.1 = (bf16[320,512]{1,0:T(8,128)(2,1)}, bf16[320,512]{1,0:T(8,128)(2,1)}, u32[]{:S(2)}, u32[]{:S(2)}) collective-permute-start(bf16[320,512]{1,0:T(8,128)(2,1)} %reshape.135), channel_id=1, source_target_pairs={{0,1},{1,2},{2,9},{3,10},{4,17},{5,18},{6,25},{7,26},{8,3},{9,4},{... | collective-permute-start | bytes 983048 | tf_op jit(solution)/shard_map/ppermute | solution.py:163
  21.1 14.5 %collective-permute-start.2 = (bf16[320,512]{1,0:T(8,128)(2,1)S(1)}, bf16[320,512]{1,0:T(8,128)(2,1)S(1)}, u32[]{:S(2)}, u32[]{:S(2)}) collective-permute-start(bf16[320,512]{1,0:T(8,128)(2,1)S(1)} %reshape.136), channel_id=1, source_target_pairs={{0,2},{1,3},{2,10},{3,11},{4,18},{5,19},{6,26},{7,27},{8,4},{9,5},... | collective-permute-start | bytes 983048 | tf_op jit(solution)/shard_map/ppermute | solution.py:163
  35.7 1.7 %bitcast_dynamic-update-slice_fusion.7 = bf16[8,320,512]{2,1,0:T(8,128)(2,1)} fusion(bf16[320,512]{1,0:T(8,128)(2,1)} %collective-permute-done), kind=kLoop, calls=%fused_computation.27 | loop fusion | bytes 655360
  37.4 5.6 %collective-permute-start.3 = (bf16[320,512]{1,0:T(8,128)(2,1)S(1)}, bf16[320,512]{1,0:T(8,128)(2,1)S(1)}, u32[]{:S(2)}, u32[]{:S(2)}) collective-permute-start(bf16[320,512]{1,0:T(8,128)(2,1)S(1)} %reshape.137), channel_id=1, source_target_pairs={{0,3},{1,4},{2,11},{3,12},{4,19},{5,20},{6,27},{7,28},{8,5},{9,6},... | collective-permute-start | bytes 983048 | tf_op jit(solution)/shard_map/ppermute | solution.py:163
  43.0 1.7 %bitcast_dynamic-update-slice_fusion.6 = bf16[8,320,512]{2,1,0:T(8,128)(2,1)} fusion(bf16[8,320,512]{2,1,0:T(8,128)(2,1)} %bitcast_dynamic-update-slice_fusion.7, bf16[320,512]{1,0:T(8,128)(2,1)} %collective-permute-done.1), kind=kLoop, calls=%fused_computation.26 | loop fusion | bytes 655360
  45.0 9.5 %collective-permute-start.7 = (bf16[320,512]{1,0:T(8,128)(2,1)S(1)}, bf16[320,512]{1,0:T(8,128)(2,1)S(1)}, u32[]{:S(2)}, u32[]{:S(2)}) collective-permute-start(bf16[320,512]{1,0:T(8,128)(2,1)S(1)} %reshape.141), channel_id=1, source_target_pairs={{0,7},{1,0},{2,15},{3,8},{4,23},{5,16},{6,31},{7,24},{8,1},{9,2},{... | collective-permute-start | bytes 983048 | tf_op jit(solution)/shard_map/ppermute | solution.py:163
  58.2 0.8 collective-permute-done.7
  59.8 2.5 %gather_fusion = bf16[8,320,512]{2,1,0:T(8,128)(2,1)S(1)} fusion(bf16[8,320,512]{2,1,0:T(8,128)(2,1)} %bitcast_dynamic-update-slice_fusion, s32[1024]{0:T(1024)S(1)} %pad_clamp_fusion), kind=kCustom, calls=%fused_computation | custom fusion | bytes 5242912 | tf_op jit(solution)/shard_map/jit(_take)/gather | solution.py:167
  62.3 2.3 %gather.7 = bf16[2,64,20,512]{3,2,1,0:T(8,128)(2,1)} reshape(bf16[8,320,512]{2,1,0:T(8,128)(2,1)S(1)} %gather_fusion) | data formatting | bytes 5242880 | tf_op jit(solution)/shard_map/jit(_take)/gather | solution.py:167
  64.6 2.2 %broadcast_select_fusion = bf16[2,64,20,512]{3,2,1,0:T(8,128)(2,1)S(1)} fusion(bf16[2,64,20,512]{3,2,1,0:T(8,128)(2,1)} %gather.7, pred[2,64]{1,0:T(4,128)(4,1)S(1)} %broadcast_in_dim.30), kind=kLoop, calls=%fused_computation.5 | loop fusion | flops 1310720 | bytes 5243008 | tf_op jit(solution)/shard_map/jit(_take)/select_n | solution.py:167
  66.8 1.0 slice_select_fusion
  67.8 2.0 %reshape.142 = bf16[512,512]{1,0:T(8,128)(2,1)} reshape(bf16[2,64,4,512]{3,2,1,0:T(4,128)(2,1)} %slice_select_fusion) | data formatting | bytes 1048576 | tf_op jit(solution)/shard_map/reshape | solution.py:173
  69.8 20.9 %collective-permute-start.8 = (bf16[512,512]{1,0:T(8,128)(2,1)}, bf16[512,512]{1,0:T(8,128)(2,1)}, u32[]{:S(2)}, u32[]{:S(2)}) collective-permute-start(bf16[512,512]{1,0:T(8,128)(2,1)} %reshape.142), channel_id=1, source_target_pairs={{0,1},{1,0},{2,3},{3,2},{4,5},{5,4},{6,7},{7,6},{8,9},{9,8},{10,11... | collective-permute-start | bytes 1572872 | tf_op jit(solution)/shard_map/ppermute | solution.py:173
  91.5 1.1 collective-permute-done.8
  92.6 2.0 %reshape.143 = bf16[2,64,4,512]{3,2,1,0:T(4,128)(2,1)} reshape(bf16[512,512]{1,0:T(8,128)(2,1)} %collective-permute-done.8) | data formatting | bytes 1048576 | tf_op jit(solution)/shard_map/reshape | solution.py:173
  94.5 3.6 %maximum_select_fusion = bf16[2,64,24,512]{3,2,1,0:T(8,128)(2,1)S(1)} fusion(bf16[2,64,4,512]{3,2,1,0:T(4,128)(2,1)} %reshape.143, bf16[2,64,20,512]{3,2,1,0:T(8,128)(2,1)S(1)} %broadcast_select_fusion, pred[]{:T(512)S(6)} %eq.24), kind=kLoop, calls=%fused_computation.1 | loop fusion | flops 14155776 | bytes 6291457 | tf_op jit(solution)/shard_map/jit(_where)/select_n | solution.py:174
  98.2 1.6 %copy-done = bf16[2,64,24,512]{3,2,1,0:T(8,128)(2,1)} copy-done((bf16[2,64,24,512]{3,2,1,0:T(8,128)(2,1)}, bf16[2,64,24,512]{3,2,1,0:T(8,128)(2,1)S(1)}, u32[]{:S(2)}) %copy-start) | copy-done | bytes 3145752
  100.0 4.8 %collective-permute-start.10 = (bf16[64,24,128]{2,1,0:T(8,128)(2,1)S(1)}, bf16[64,24,128]{2,1,0:T(8,128)(2,1)S(1)}, u32[]{:S(2)}, u32[]{:S(2)}) collective-permute-start(bf16[64,24,128]{2,1,0:T(8,128)(2,1)S(1)} %get-tuple-element.2), channel_id=1, source_target_pairs={{0,8},{8,16},{16,24},{1,9},{9,17},{17,25},{2,10},{10,18},{18,26},{... | collective-permute-start | bytes 1179656 | tf_op jit(solution)/shard_map/ppermute | solution.py:178
  104.8 1.5 %collective-permute-start.9 = (bf16[64,24,128]{2,1,0:T(8,128)(2,1)S(1)}, bf16[64,24,128]{2,1,0:T(8,128)(2,1)S(1)}, u32[]{:S(2)}, u32[]{:S(2)}) collective-permute-start(bf16[64,24,128]{2,1,0:T(8,128)(2,1)S(1)} %get-tuple-element.3), channel_id=1, source_target_pairs={{8,0},{16,8},{24,16},{9,1},{17,9},{25,17},{10,2},{18,10},{26,18},{... | collective-permute-start | bytes 1179656 | tf_op jit(solution)/shard_map/ppermute | solution.py:179
  106.8 0.8 reshape.155
  107.6 0.8 reshape.156
  108.4 3.2 %convert_bitcast_fusion = bf16[2,64,24,512]{3,1,2,0:T(8,128)(2,1)S(1)} fusion(bf16[2,64,24,512]{3,2,1,0:T(8,128)(2,1)} %copy-done, bf16[64,64,1,1]{1,0,2,3:T(8,128)(2,1)S(1)} %reshape.155), kind=kOutput, calls=%fused_computation.4 | convolution fusion | flops 202899456 | bytes 6299648 | tf_op jit(solution)/shard_map/kc,bchw->bkhw/dot_general | solution.py:186
  111.7 3.4 %copy.12 = bf16[2,64,24,512]{3,2,1,0:T(8,128)(2,1)} copy(bf16[2,64,24,512]{3,1,2,0:T(8,128)(2,1)S(1)} %convert_bitcast_fusion) | data formatting | bytes 6291456 | tf_op jit(solution)/shard_map/convert_element_type | solution.py:187
  115.1 7.6 %collective-permute-done.9 = bf16[64,24,128]{2,1,0:T(8,128)(2,1)S(1)} collective-permute-done((bf16[64,24,128]{2,1,0:T(8,128)(2,1)S(1)}, bf16[64,24,128]{2,1,0:T(8,128)(2,1)S(1)}, u32[]{:S(2)}, u32[]{:S(2)}) %collective-permute-start.9) | collective-permute-done | bytes 393248 | tf_op jit(solution)/shard_map/ppermute | solution.py:179
  122.9 1.0 copy.14
  123.9 19.5 %shard_map.68 = (f32[32,16,1024]{2,1,0:T(8,128)}, f32[32,16,1024]{2,1,0:T(8,128)}) custom-call(s32[32]{0:T(128)} %pre_ref.1, s32[32]{0:T(128)} %post_ref.1, bf16[2,32,2,24,512]{4,3,2,1,0:T(8,128)(2,1)} %bitcast.42, bf16[32,2,24,128]{3,2,1,0:T(8,128)(2,1)} %bitcast.50, bf16[2,32,2,24,512]{4,3,2,1,0:T(8,128)(2,1)} %bitcast.43, ...), custom_call_target="tpu_custom_call" | custom-call | tf_op jit(solution)/shard_map/pallas_call | solution.py:130
  (45 shorter events, 8.0 us)
Async XLA Ops:
  5.7 15.2 %copy-start.1 = (bf16[32,32]{1,0:T(8,128)(2,1)S(1)}, bf16[32,32]{1,0:T(8,128)(2,1)}, u32[]{:S(2)}) copy-start(bf16[32,32]{1,0:T(8,128)(2,1)} %param.7) | copy-start | bytes 6148
  6.5 14.6 %copy-start.2 = (bf16[32,32]{1,0:T(8,128)(2,1)S(1)}, bf16[32,32]{1,0:T(8,128)(2,1)}, u32[]{:S(2)}) copy-start(bf16[32,32]{1,0:T(8,128)(2,1)} %param.6) | copy-start | bytes 6148
  6.5 14.7 %collective-permute-start = (bf16[320,512]{1,0:T(8,128)(2,1)}, bf16[320,512]{1,0:T(8,128)(2,1)}, u32[]{:S(2)}, u32[]{:S(2)}) collective-permute-start(bf16[320,512]{1,0:T(8,128)(2,1)} %reshape.134), channel_id=1, source_target_pairs={{0,0},{1,1},{2,8},{3,9},{4,16},{5,17},{6,24},{7,25},{8,2},{9,3},{1... | collective-permute-start | bytes 983048 | tf_op jit(solution)/shard_map/ppermute | solution.py:163
  10.5 46.9 %collective-permute-start.6 = (bf16[320,512]{1,0:T(8,128)(2,1)S(1)}, bf16[320,512]{1,0:T(8,128)(2,1)S(1)}, u32[]{:S(2)}, u32[]{:S(2)}) collective-permute-start(bf16[320,512]{1,0:T(8,128)(2,1)S(1)} %reshape.140), channel_id=1, source_target_pairs={{0,6},{1,7},{2,14},{3,15},{4,22},{5,23},{6,30},{7,31},{8,0},{9,1},... | collective-permute-start | bytes 983048 | tf_op jit(solution)/shard_map/ppermute | solution.py:163
  15.8 40.9 %collective-permute-start.5 = (bf16[320,512]{1,0:T(8,128)(2,1)S(1)}, bf16[320,512]{1,0:T(8,128)(2,1)S(1)}, u32[]{:S(2)}, u32[]{:S(2)}) collective-permute-start(bf16[320,512]{1,0:T(8,128)(2,1)S(1)} %reshape.139), channel_id=1, source_target_pairs={{0,5},{1,6},{2,13},{3,14},{4,21},{5,22},{6,29},{7,30},{8,7},{9,0},... | collective-permute-start | bytes 983048 | tf_op jit(solution)/shard_map/ppermute | solution.py:163
  16.7 39.2 %collective-permute-start.4 = (bf16[320,512]{1,0:T(8,128)(2,1)}, bf16[320,512]{1,0:T(8,128)(2,1)S(1)}, u32[]{:S(2)}, u32[]{:S(2)}) collective-permute-start(bf16[320,512]{1,0:T(8,128)(2,1)} %reshape.138), channel_id=1, source_target_pairs={{0,4},{1,5},{2,12},{3,13},{4,20},{5,21},{6,28},{7,29},{8,6},{9,7},... | collective-permute-start | bytes 983048 | tf_op jit(solution)/shard_map/ppermute | solution.py:163
  18.3 19.1 %collective-permute-start.1 = (bf16[320,512]{1,0:T(8,128)(2,1)}, bf16[320,512]{1,0:T(8,128)(2,1)}, u32[]{:S(2)}, u32[]{:S(2)}) collective-permute-start(bf16[320,512]{1,0:T(8,128)(2,1)} %reshape.135), channel_id=1, source_target_pairs={{0,1},{1,2},{2,9},{3,10},{4,17},{5,18},{6,25},{7,26},{8,3},{9,4},{... | collective-permute-start | bytes 983048 | tf_op jit(solution)/shard_map/ppermute | solution.py:163
  21.1 23.9 %collective-permute-start.2 = (bf16[320,512]{1,0:T(8,128)(2,1)S(1)}, bf16[320,512]{1,0:T(8,128)(2,1)S(1)}, u32[]{:S(2)}, u32[]{:S(2)}) collective-permute-start(bf16[320,512]{1,0:T(8,128)(2,1)S(1)} %reshape.136), channel_id=1, source_target_pairs={{0,2},{1,3},{2,10},{3,11},{4,18},{5,19},{6,26},{7,27},{8,4},{9,5},... | collective-permute-start | bytes 983048 | tf_op jit(solution)/shard_map/ppermute | solution.py:163
  37.4 17.8 %collective-permute-start.3 = (bf16[320,512]{1,0:T(8,128)(2,1)S(1)}, bf16[320,512]{1,0:T(8,128)(2,1)S(1)}, u32[]{:S(2)}, u32[]{:S(2)}) collective-permute-start(bf16[320,512]{1,0:T(8,128)(2,1)S(1)} %reshape.137), channel_id=1, source_target_pairs={{0,3},{1,4},{2,11},{3,12},{4,19},{5,20},{6,27},{7,28},{8,5},{9,6},... | collective-permute-start | bytes 983048 | tf_op jit(solution)/shard_map/ppermute | solution.py:163
  45.0 14.1 %collective-permute-start.7 = (bf16[320,512]{1,0:T(8,128)(2,1)S(1)}, bf16[320,512]{1,0:T(8,128)(2,1)S(1)}, u32[]{:S(2)}, u32[]{:S(2)}) collective-permute-start(bf16[320,512]{1,0:T(8,128)(2,1)S(1)} %reshape.141), channel_id=1, source_target_pairs={{0,7},{1,0},{2,15},{3,8},{4,23},{5,16},{6,31},{7,24},{8,1},{9,2},{... | collective-permute-start | bytes 983048 | tf_op jit(solution)/shard_map/ppermute | solution.py:163
  69.8 22.8 %collective-permute-start.8 = (bf16[512,512]{1,0:T(8,128)(2,1)}, bf16[512,512]{1,0:T(8,128)(2,1)}, u32[]{:S(2)}, u32[]{:S(2)}) collective-permute-start(bf16[512,512]{1,0:T(8,128)(2,1)} %reshape.142), channel_id=1, source_target_pairs={{0,1},{1,0},{2,3},{3,2},{4,5},{5,4},{6,7},{7,6},{8,9},{9,8},{10,11... | collective-permute-start | bytes 1572872 | tf_op jit(solution)/shard_map/ppermute | solution.py:173
  98.2 1.7 %copy-start = (bf16[2,64,24,512]{3,2,1,0:T(8,128)(2,1)}, bf16[2,64,24,512]{3,2,1,0:T(8,128)(2,1)S(1)}, u32[]{:S(2)}) copy-start(bf16[2,64,24,512]{3,2,1,0:T(8,128)(2,1)S(1)} %maximum_select_fusion) | copy-start | bytes 9437188
  100.0 15.1 %collective-permute-start.10 = (bf16[64,24,128]{2,1,0:T(8,128)(2,1)S(1)}, bf16[64,24,128]{2,1,0:T(8,128)(2,1)S(1)}, u32[]{:S(2)}, u32[]{:S(2)}) collective-permute-start(bf16[64,24,128]{2,1,0:T(8,128)(2,1)S(1)} %get-tuple-element.2), channel_id=1, source_target_pairs={{0,8},{8,16},{16,24},{1,9},{9,17},{17,25},{2,10},{10,18},{18,26},{... | collective-permute-start | bytes 1179656 | tf_op jit(solution)/shard_map/ppermute | solution.py:178
  104.8 17.8 %collective-permute-start.9 = (bf16[64,24,128]{2,1,0:T(8,128)(2,1)S(1)}, bf16[64,24,128]{2,1,0:T(8,128)(2,1)S(1)}, u32[]{:S(2)}, u32[]{:S(2)}) collective-permute-start(bf16[64,24,128]{2,1,0:T(8,128)(2,1)S(1)} %get-tuple-element.3), channel_id=1, source_target_pairs={{8,0},{16,8},{24,16},{9,1},{17,9},{25,17},{10,2},{18,10},{26,18},{... | collective-permute-start | bytes 1179656 | tf_op jit(solution)/shard_map/ppermute | solution.py:179

commit v15 on v14

--- a/solution.py
+++ b/solution.py
@@ -29,7 +29,7 @@
     return total
 
 
-def pair_kernel(pre_ref, post_ref, *refs, tile_rows, tile_cols):
+def pair_kernel(pre_ref, post_ref, odd_ref, *refs, tile_rows, tile_cols):
     del pre_ref, post_ref
     pp = PAIRS_PER_STEP
     sides = refs[: 4 * pp]
@@ -52,7 +52,9 @@
             for f, value in enumerate(fields):
                 field_ref[f, :, pl.ds(at, width)] = value
         for f in range(FIELDS):
-            acc = window_rows(field_ref[f], window)[:tile_rows]
+            cyclic = window_rows(field_ref[f], window)
+            rotated = pltpu.roll(cyclic, RADIUS, 0)
+            acc = jnp.where(odd_ref[0] == 0, cyclic[:tile_rows], rotated[:tile_rows])
             at = (p * FIELDS + f) * tile_rows
             rows_ref[pl.ds(at, tile_rows), pl.ds(LANES, padded_cols)] = acc
             rows_ref[pl.ds(at, tile_rows), pl.ds(0, LANES)] = acc[:, padded_cols - LANES :]
@@ -79,7 +81,7 @@
             chg_ref[p, :, pl.ds(j * LANES, LANES)] = jnp.log(post_power / pre_power)
 
 
-def pair_maps(main, edge, pre_ids, post_ids, tile_rows, tile_cols):
+def pair_maps(main, edge, pre_ids, post_ids, odd, tile_rows, tile_cols):
     count_pairs = pre_ids.shape[0]
     pp = PAIRS_PER_STEP
     blocks_per_tile, _, _, padded_rows, block_cols = main.shape
@@ -93,11 +95,11 @@
     edge_block = (1, 2, padded_rows, LANES)
 
     def specs(p, which):
-        def main_index(i, pre, post):
+        def main_index(i, pre, post, odd):
             ids = pre if which == 0 else post
             return (0, ids[i * pp + p], 0, 0, 0)
 
-        def edge_index(i, pre, post):
+        def edge_index(i, pre, post, odd):
             ids = pre if which == 0 else post
             return (ids[i * pp + p], 0, 0, 0)
 
@@ -108,14 +110,14 @@
     for p in range(pp):
         in_specs += specs(p, 0) + specs(p, 1)
         operands += [main, edge, main, edge]
-    in_specs.append(pl.BlockSpec((2 * width, LANES), lambda i, pre, post: (0, 0)))
+    in_specs.append(pl.BlockSpec((2 * width, LANES), lambda i, pre, post, odd: (0, 0)))
     operands.append(band)
-    out_block = pl.BlockSpec((pp, tile_rows, tile_cols), lambda i, pre, post: (i, 0, 0))
+    out_block = pl.BlockSpec((pp, tile_rows, tile_cols), lambda i, pre, post, odd: (i, 0, 0))
     rows = pp * FIELDS * tile_rows
     blocks = tile_cols // LANES
     padded_cols = tile_cols + LANES
     grid_spec = pltpu.PrefetchScalarGridSpec(
-        num_scalar_prefetch=2,
+        num_scalar_prefetch=3,
         grid=(count_pairs // pp,),
         in_specs=in_specs,
         out_specs=[out_block, out_block],
@@ -131,7 +133,7 @@
         kernel,
         grid_spec=grid_spec,
         out_shape=[out_shape, out_shape],
-    )(pre_ids, post_ids, *operands)
+    )(pre_ids, post_ids, odd, *operands)
 
 
 def shards(stack, filt_re, filt_im, pre_ids, post_ids):
@@ -166,12 +168,12 @@
     order = (me_row - source) % n_rows
     x = jnp.take(received, order.reshape(-1), axis=0)
     x = x.reshape(blocks_per_tile, 2 * count_acq, sent_rows, local_cols)
-    even = me_row % 2 == 0
-    share = jnp.where(even, x[:, :, sent_rows - RADIUS :], x[:, :, :RADIUS])
+    odd = me_row % 2
+    share = lax.dynamic_slice_in_dim(x, (1 - odd) * tile_rows, RADIUS, axis=2)
     share_shape = share.shape
     partners = [(i, i + 1 - 2 * (i % 2)) for i in range(n_rows)]
     share = lax.ppermute(share.reshape(-1, local_cols), "ty", partners).reshape(share_shape)
-    x = jnp.where(even, jnp.concatenate([x, share], axis=2), jnp.concatenate([share, x], axis=2))
+    x = jnp.concatenate([x, share], axis=2)
 
     forward = [(i, i + 1) for i in range(n_cols - 1)]
     backward = [(target, source) for source, target in forward]
@@ -187,7 +189,7 @@
     main = main.astype(jnp.bfloat16).reshape(blocks_per_tile, count_acq, 2, padded_rows, local_cols)
     edge = jnp.einsum("kc,chw->khw", mixing, edge, preferred_element_type=jnp.float32)
     edge = edge.astype(jnp.bfloat16).reshape(count_acq, 2, padded_rows, LANES)
-    return pair_maps(main, edge, pre_ids, post_ids, tile_rows, tile_cols)
+    return pair_maps(main, edge, pre_ids, post_ids, odd.reshape(1).astype(jnp.int32), tile_rows, tile_cols)
 
 
 def solution(mesh):

time: 144 us -> 140 us (0.972)
  other arithmetic: 7.78 us -> 3.89 us
  waiting for transfers between devices: 9.73 us -> 13.4 us
  local copies, waits for them, and re-layouts: 32.7 us -> 29.7 us
  matrix products: 3.46 us -> 1.23 us
  Pallas kernels: 19.5 us -> 21 us
    select_n x3 -> x0, other arithmetic: 4.67 us -> none  [the longest x1 3.64 us: shards(): jnp.where(even, jnp.concatenate([x, share], axis=2), jnp.concatenate([sha...]
    ppermute x1, waiting for transfers between devices: 0.01 us -> 3.14 us  [shards(): lax.ppermute(x[blocks_per_tile - 1, :, :, local_cols - LANES:], 'tx', for...]
    dot_general x1, matrix products: 3.22 us -> 0.96 us  [shards(): jnp.einsum('kc,bchw->bkhw', mixing, x, preferred_element_type=jnp.float32)]
    ppermute x1, waiting for transfers between devices: 7.56 us -> 9.17 us  [shards(): right = lax.ppermute(x[0, :, :, :LANES], 'tx', backward)]
    unnamed x13 -> x11, local copies, waits for them, and re-layouts: 8.82 us -> 7.21 us
    pallas_call x1, Pallas kernels: 19.5 us -> 21 us  [pair_maps(): pl.pallas_call(kernel, grid_spec=grid_spec, out_shape=[out_shape, out_sha...]
  transfers between devices with their start and end apart: 11 -> 11, of which waited for: 4 -> 4; matrix products, arithmetic and copies ran while one was open for 13% -> 12% of each run, Pallas kernels for 0% -> 0%
where the time goes in v15:
time: 140 us; the launch traced here: 139 us
  starting transfers between devices  68.8 us (49%)
  local copies, waits for them, and re-layouts  29.7 us (21%)
  Pallas kernels  21 us (15%)
  waiting for transfers between devices  13.4 us (10%)
  other arithmetic  3.89 us (3%)
    ppermute x8, starting transfers between devices, shards(): received.append(lax.ppermute(chunk, ('tx', 'ty'), pairs))  41.9 us
    pallas_call x1, Pallas kernels, pair_maps(): pl.pallas_call(kernel, grid_spec=grid_spec, out_shape=[out_shape, out_sha...  21 us
    ppermute x1, starting transfers between devices, shards(): lax.ppermute(share.reshape(-1, local_cols), 'ty', partners)  20.9 us
    ppermute x1, waiting for transfers between devices, shards(): right = lax.ppermute(x[0, :, :, :LANES], 'tx', backward)  9.17 us
    unnamed x11, local copies, waits for them, and re-layouts  7.21 us
    gather x2, local copies, waits for them, and re-layouts, shards(): x = jnp.take(received, order.reshape(-1), axis=0)  4.8 us
    dynamic_slice x1, local copies, waits for them, and re-layouts, shards(): chunk = lax.dynamic_slice_in_dim(x, first, sent_rows, axis=2)  4.77 us
    ppermute x1, starting transfers between devices, shards(): lax.ppermute(x[blocks_per_tile - 1, :, :, local_cols - LANES:], 'tx', for...  4.46 us
  transfers between devices with their start and end apart: 11, of which 4 were waited for; matrix products, arithmetic and copies ran while one was open for 12% of the time, Pallas kernels for 0%

profile of v15, /device:TPU:0, one launch (start us, length us, event | category | flops | bytes accessed | tf_op | source)
XLA Modules:
  0.0 139.2 jit_solution(16159583118507207791)
XLA Ops:
  0.9 4.8 %pad_dynamic-slice_fusion = (bf16[8,2,20,512]{3,2,1,0:T(8,128)(2,1)S(1)}, bf16[8,2,20,512]{3,2,1,0:T(8,128)(2,1)S(1)}, bf16[8,2,20,512]{3,2,1,0:T(8,128)(2,1)S(1...) fusion(s32[]{:T(128)S(6)} %select_n.180, ...), kind=kLoop, calls=%fused_computation.8 | loop fusion | bytes 4718624 | tf_op jit(solution)/shard_map/dynamic_slice | solution.py:163
  5.7 0.8 reshape.138
  6.5 4.0 %collective-permute-start = (bf16[320,512]{1,0:T(8,128)(2,1)}, bf16[320,512]{1,0:T(8,128)(2,1)}, u32[]{:S(2)}, u32[]{:S(2)}) collective-permute-start(bf16[320,512]{1,0:T(8,128)(2,1)} %reshape.138), channel_id=1, source_target_pairs={{0,0},{1,1},{2,8},{3,9},{4,16},{5,17},{6,24},{7,25},{8,2},{9,3},{1... | collective-permute-start | bytes 983048 | tf_op jit(solution)/shard_map/ppermute | solution.py:165
  10.5 5.2 %collective-permute-start.6 = (bf16[320,512]{1,0:T(8,128)(2,1)S(1)}, bf16[320,512]{1,0:T(8,128)(2,1)S(1)}, u32[]{:S(2)}, u32[]{:S(2)}) collective-permute-start(bf16[320,512]{1,0:T(8,128)(2,1)S(1)} %reshape.144), channel_id=1, source_target_pairs={{0,6},{1,7},{2,14},{3,15},{4,22},{5,23},{6,30},{7,31},{8,0},{9,1},... | collective-permute-start | bytes 983048 | tf_op jit(solution)/shard_map/ppermute | solution.py:165
  15.9 0.8 reshape.142
  16.7 0.8 collective-permute-start.4
  17.5 0.8 reshape.139
  18.3 2.2 %collective-permute-start.1 = (bf16[320,512]{1,0:T(8,128)(2,1)}, bf16[320,512]{1,0:T(8,128)(2,1)}, u32[]{:S(2)}, u32[]{:S(2)}) collective-permute-start(bf16[320,512]{1,0:T(8,128)(2,1)} %reshape.139), channel_id=1, source_target_pairs={{0,1},{1,2},{2,9},{3,10},{4,17},{5,18},{6,25},{7,26},{8,3},{9,4},{... | collective-permute-start | bytes 983048 | tf_op jit(solution)/shard_map/ppermute | solution.py:165
  21.1 14.5 %collective-permute-start.2 = (bf16[320,512]{1,0:T(8,128)(2,1)S(1)}, bf16[320,512]{1,0:T(8,128)(2,1)S(1)}, u32[]{:S(2)}, u32[]{:S(2)}) collective-permute-start(bf16[320,512]{1,0:T(8,128)(2,1)S(1)} %reshape.140), channel_id=1, source_target_pairs={{0,2},{1,3},{2,10},{3,11},{4,18},{5,19},{6,26},{7,27},{8,4},{9,5},... | collective-permute-start | bytes 983048 | tf_op jit(solution)/shard_map/ppermute | solution.py:165
  35.7 1.7 %bitcast_dynamic-update-slice_fusion.7 = bf16[8,320,512]{2,1,0:T(8,128)(2,1)} fusion(bf16[320,512]{1,0:T(8,128)(2,1)} %collective-permute-done), kind=kLoop, calls=%fused_computation.29 | loop fusion | bytes 655360
  37.4 5.6 %collective-permute-start.3 = (bf16[320,512]{1,0:T(8,128)(2,1)S(1)}, bf16[320,512]{1,0:T(8,128)(2,1)S(1)}, u32[]{:S(2)}, u32[]{:S(2)}) collective-permute-start(bf16[320,512]{1,0:T(8,128)(2,1)S(1)} %reshape.141), channel_id=1, source_target_pairs={{0,3},{1,4},{2,11},{3,12},{4,19},{5,20},{6,27},{7,28},{8,5},{9,6},... | collective-permute-start | bytes 983048 | tf_op jit(solution)/shard_map/ppermute | solution.py:165
  43.0 1.7 %bitcast_dynamic-update-slice_fusion.6 = bf16[8,320,512]{2,1,0:T(8,128)(2,1)} fusion(bf16[8,320,512]{2,1,0:T(8,128)(2,1)} %bitcast_dynamic-update-slice_fusion.7, bf16[320,512]{1,0:T(8,128)(2,1)} %collective-permute-done.1), kind=kLoop, calls=%fused_computation.28 | loop fusion | bytes 655360
  45.0 9.5 %collective-permute-start.7 = (bf16[320,512]{1,0:T(8,128)(2,1)S(1)}, bf16[320,512]{1,0:T(8,128)(2,1)S(1)}, u32[]{:S(2)}, u32[]{:S(2)}) collective-permute-start(bf16[320,512]{1,0:T(8,128)(2,1)S(1)} %reshape.145), channel_id=1, source_target_pairs={{0,7},{1,0},{2,15},{3,8},{4,23},{5,16},{6,31},{7,24},{8,1},{9,2},{... | collective-permute-start | bytes 983048 | tf_op jit(solution)/shard_map/ppermute | solution.py:165
  54.5 0.8 bitcast_dynamic-update-slice_fusion.5
  55.2 0.8 bitcast_dynamic-update-slice_fusion.4
  58.2 0.8 collective-permute-done.7
  59.8 2.5 %gather_fusion = bf16[8,320,512]{2,1,0:T(8,128)(2,1)S(1)} fusion(bf16[8,320,512]{2,1,0:T(8,128)(2,1)} %bitcast_dynamic-update-slice_fusion, s32[1024]{0:T(1024)S(1)} %pad_clamp_fusion), kind=kCustom, calls=%fused_computation | custom fusion | bytes 5242912 | tf_op jit(solution)/shard_map/jit(_take)/gather | solution.py:169
  62.3 2.3 %gather.7 = bf16[2,64,20,512]{3,2,1,0:T(8,128)(2,1)} reshape(bf16[8,320,512]{2,1,0:T(8,128)(2,1)S(1)} %gather_fusion) | data formatting | bytes 5242880 | tf_op jit(solution)/shard_map/jit(_take)/gather | solution.py:169
  64.6 2.8 %copy_select_fusion = bf16[2,64,20,512]{3,1,2,0:T(8,128)(2,1)S(1)} fusion(bf16[2,64,20,512]{3,2,1,0:T(8,128)(2,1)} %gather.7, pred[2,64]{1,0:T(4,128)(4,1)S(1)} %broadcast_in_dim.30), kind=kLoop, calls=%fused_computation.6 | loop fusion | flops 1310720 | bytes 5243008 | tf_op jit(solution)/shard_map/jit(_take)/select_n | solution.py:169
  67.9 0.9 reshape.146
  68.8 20.9 %collective-permute-start.8 = (bf16[512,512]{1,0:T(8,128)(2,1)}, bf16[512,512]{1,0:T(8,128)(2,1)}, u32[]{:S(2)}, u32[]{:S(2)}) collective-permute-start(bf16[512,512]{1,0:T(8,128)(2,1)} %reshape.146), channel_id=1, source_target_pairs={{0,1},{1,0},{2,3},{3,2},{4,5},{5,4},{6,7},{7,6},{8,9},{9,8},{10,11... | collective-permute-start | bytes 1572872 | tf_op jit(solution)/shard_map/ppermute | solution.py:175
  90.2 0.8 reshape.159
  91.0 0.8 reshape.160
  92.7 1.2 reshape.147
  94.2 4.5 %collective-permute-start.10 = (bf16[64,24,128]{2,0,1:T(8,128)(2,1)S(1)}, bf16[64,24,128]{2,0,1:T(8,128)(2,1)S(1)}, u32[]{:S(2)}, u32[]{:S(2)}) collective-permute-start(bf16[64,24,128]{2,0,1:T(8,128)(2,1)S(1)} %get-tuple-element.2), channel_id=1, source_target_pairs={{0,8},{8,16},{16,24},{1,9},{9,17},{17,25},{2,10},{10,18},{18,26},{... | collective-permute-start | bytes 1179656 | tf_op jit(solution)/shard_map/ppermute | solution.py:180
  98.6 1.5 %collective-permute-start.9 = (bf16[64,24,128]{2,0,1:T(8,128)(2,1)S(1)}, bf16[64,24,128]{2,0,1:T(8,128)(2,1)S(1)}, u32[]{:S(2)}, u32[]{:S(2)}) collective-permute-start(bf16[64,24,128]{2,0,1:T(8,128)(2,1)S(1)} %get-tuple-element.3), channel_id=1, source_target_pairs={{8,0},{16,8},{24,16},{9,1},{17,9},{25,17},{10,2},{18,10},{26,18},{... | collective-permute-start | bytes 1179656 | tf_op jit(solution)/shard_map/ppermute | solution.py:181
  100.1 1.0 convert_bitcast_fusion
  101.1 3.4 %copy.14 = bf16[2,64,24,512]{3,2,1,0:T(8,128)(2,1)} copy(bf16[2,64,24,512]{3,1,2,0:T(8,128)(2,1)S(1)} %convert_bitcast_fusion) | data formatting | bytes 6291456 | tf_op jit(solution)/shard_map/convert_element_type | solution.py:189
  104.5 3.1 %collective-permute-done.10 = bf16[64,24,128]{2,0,1:T(8,128)(2,1)S(1)} collective-permute-done((bf16[64,24,128]{2,0,1:T(8,128)(2,1)S(1)}, bf16[64,24,128]{2,0,1:T(8,128)(2,1)S(1)}, u32[]{:S(2)}, u32[]{:S(2)}) %collective-permute-start.10) | collective-permute-done | bytes 393248 | tf_op jit(solution)/shard_map/ppermute | solution.py:180
  107.6 9.2 %collective-permute-done.9 = bf16[64,24,128]{2,0,1:T(8,128)(2,1)S(1)} collective-permute-done((bf16[64,24,128]{2,0,1:T(8,128)(2,1)S(1)}, bf16[64,24,128]{2,0,1:T(8,128)(2,1)S(1)}, u32[]{:S(2)}, u32[]{:S(2)}) %collective-permute-start.9) | collective-permute-done | bytes 393248 | tf_op jit(solution)/shard_map/ppermute | solution.py:181
  117.1 1.0 copy.15
  118.1 21.0 %shard_map.68 = (f32[32,16,1024]{2,1,0:T(8,128)}, f32[32,16,1024]{2,1,0:T(8,128)}) custom-call(s32[32]{0:T(128)} %pre_ref.1, s32[32]{0:T(128)} %post_ref.1, s32[1]{0:T(128)} %bitcast.odd_ref, bf16[2,32,2,24,512]{4,3,2,1,0:T(8,128)(2,1)} %bitcast.43, bf16[32,2,24,128]{3,2,1,0:T(8,128)(2,1)} %bitcast.51, bf16[2,32,2,24,512]{4,3,2,1,0:T(8,128)(2,1)} %bitcast.44, ...), custom_call_target="tpu_custom_call" | custom-call | tf_op jit(solution)/shard_map/pallas_call | solution.py:132
  (43 shorter events, 6.3 us)
Async XLA Ops:
  5.7 15.2 %copy-start = (bf16[32,32]{1,0:T(8,128)(2,1)S(1)}, bf16[32,32]{1,0:T(8,128)(2,1)}, u32[]{:S(2)}) copy-start(bf16[32,32]{1,0:T(8,128)(2,1)} %param.7) | copy-start | bytes 6148
  6.5 14.6 %copy-start.1 = (bf16[32,32]{1,0:T(8,128)(2,1)S(1)}, bf16[32,32]{1,0:T(8,128)(2,1)}, u32[]{:S(2)}) copy-start(bf16[32,32]{1,0:T(8,128)(2,1)} %param.6) | copy-start | bytes 6148
  6.5 14.7 %collective-permute-start = (bf16[320,512]{1,0:T(8,128)(2,1)}, bf16[320,512]{1,0:T(8,128)(2,1)}, u32[]{:S(2)}, u32[]{:S(2)}) collective-permute-start(bf16[320,512]{1,0:T(8,128)(2,1)} %reshape.138), channel_id=1, source_target_pairs={{0,0},{1,1},{2,8},{3,9},{4,16},{5,17},{6,24},{7,25},{8,2},{9,3},{1... | collective-permute-start | bytes 983048 | tf_op jit(solution)/shard_map/ppermute | solution.py:165
  10.5 47.0 %collective-permute-start.6 = (bf16[320,512]{1,0:T(8,128)(2,1)S(1)}, bf16[320,512]{1,0:T(8,128)(2,1)S(1)}, u32[]{:S(2)}, u32[]{:S(2)}) collective-permute-start(bf16[320,512]{1,0:T(8,128)(2,1)S(1)} %reshape.144), channel_id=1, source_target_pairs={{0,6},{1,7},{2,14},{3,15},{4,22},{5,23},{6,30},{7,31},{8,0},{9,1},... | collective-permute-start | bytes 983048 | tf_op jit(solution)/shard_map/ppermute | solution.py:165
  15.8 40.9 %collective-permute-start.5 = (bf16[320,512]{1,0:T(8,128)(2,1)S(1)}, bf16[320,512]{1,0:T(8,128)(2,1)S(1)}, u32[]{:S(2)}, u32[]{:S(2)}) collective-permute-start(bf16[320,512]{1,0:T(8,128)(2,1)S(1)} %reshape.143), channel_id=1, source_target_pairs={{0,5},{1,6},{2,13},{3,14},{4,21},{5,22},{6,29},{7,30},{8,7},{9,0},... | collective-permute-start | bytes 983048 | tf_op jit(solution)/shard_map/ppermute | solution.py:165
  16.7 39.3 %collective-permute-start.4 = (bf16[320,512]{1,0:T(8,128)(2,1)}, bf16[320,512]{1,0:T(8,128)(2,1)S(1)}, u32[]{:S(2)}, u32[]{:S(2)}) collective-permute-start(bf16[320,512]{1,0:T(8,128)(2,1)} %reshape.142), channel_id=1, source_target_pairs={{0,4},{1,5},{2,12},{3,13},{4,20},{5,21},{6,28},{7,29},{8,6},{9,7},... | collective-permute-start | bytes 983048 | tf_op jit(solution)/shard_map/ppermute | solution.py:165
  18.3 19.1 %collective-permute-start.1 = (bf16[320,512]{1,0:T(8,128)(2,1)}, bf16[320,512]{1,0:T(8,128)(2,1)}, u32[]{:S(2)}, u32[]{:S(2)}) collective-permute-start(bf16[320,512]{1,0:T(8,128)(2,1)} %reshape.139), channel_id=1, source_target_pairs={{0,1},{1,2},{2,9},{3,10},{4,17},{5,18},{6,25},{7,26},{8,3},{9,4},{... | collective-permute-start | bytes 983048 | tf_op jit(solution)/shard_map/ppermute | solution.py:165
  21.1 23.8 %collective-permute-start.2 = (bf16[320,512]{1,0:T(8,128)(2,1)S(1)}, bf16[320,512]{1,0:T(8,128)(2,1)S(1)}, u32[]{:S(2)}, u32[]{:S(2)}) collective-permute-start(bf16[320,512]{1,0:T(8,128)(2,1)S(1)} %reshape.140), channel_id=1, source_target_pairs={{0,2},{1,3},{2,10},{3,11},{4,18},{5,19},{6,26},{7,27},{8,4},{9,5},... | collective-permute-start | bytes 983048 | tf_op jit(solution)/shard_map/ppermute | solution.py:165
  37.4 17.8 %collective-permute-start.3 = (bf16[320,512]{1,0:T(8,128)(2,1)S(1)}, bf16[320,512]{1,0:T(8,128)(2,1)S(1)}, u32[]{:S(2)}, u32[]{:S(2)}) collective-permute-start(bf16[320,512]{1,0:T(8,128)(2,1)S(1)} %reshape.141), channel_id=1, source_target_pairs={{0,3},{1,4},{2,11},{3,12},{4,19},{5,20},{6,27},{7,28},{8,5},{9,6},... | collective-permute-start | bytes 983048 | tf_op jit(solution)/shard_map/ppermute | solution.py:165
  45.0 14.1 %collective-permute-start.7 = (bf16[320,512]{1,0:T(8,128)(2,1)S(1)}, bf16[320,512]{1,0:T(8,128)(2,1)S(1)}, u32[]{:S(2)}, u32[]{:S(2)}) collective-permute-start(bf16[320,512]{1,0:T(8,128)(2,1)S(1)} %reshape.145), channel_id=1, source_target_pairs={{0,7},{1,0},{2,15},{3,8},{4,23},{5,16},{6,31},{7,24},{8,1},{9,2},{... | collective-permute-start | bytes 983048 | tf_op jit(solution)/shard_map/ppermute | solution.py:165
  68.8 23.9 %collective-permute-start.8 = (bf16[512,512]{1,0:T(8,128)(2,1)}, bf16[512,512]{1,0:T(8,128)(2,1)}, u32[]{:S(2)}, u32[]{:S(2)}) collective-permute-start(bf16[512,512]{1,0:T(8,128)(2,1)} %reshape.146), channel_id=1, source_target_pairs={{0,1},{1,0},{2,3},{3,2},{4,5},{5,4},{6,7},{7,6},{8,9},{9,8},{10,11... | collective-permute-start | bytes 1572872 | tf_op jit(solution)/shard_map/ppermute | solution.py:175
  94.2 13.5 %collective-permute-start.10 = (bf16[64,24,128]{2,0,1:T(8,128)(2,1)S(1)}, bf16[64,24,128]{2,0,1:T(8,128)(2,1)S(1)}, u32[]{:S(2)}, u32[]{:S(2)}) collective-permute-start(bf16[64,24,128]{2,0,1:T(8,128)(2,1)S(1)} %get-tuple-element.2), channel_id=1, source_target_pairs={{0,8},{8,16},{16,24},{1,9},{9,17},{17,25},{2,10},{10,18},{18,26},{... | collective-permute-start | bytes 1179656 | tf_op jit(solution)/shard_map/ppermute | solution.py:180
  98.6 18.2 %collective-permute-start.9 = (bf16[64,24,128]{2,0,1:T(8,128)(2,1)S(1)}, bf16[64,24,128]{2,0,1:T(8,128)(2,1)S(1)}, u32[]{:S(2)}, u32[]{:S(2)}) collective-permute-start(bf16[64,24,128]{2,0,1:T(8,128)(2,1)S(1)} %get-tuple-element.3), channel_id=1, source_target_pairs={{8,0},{16,8},{24,16},{9,1},{17,9},{25,17},{10,2},{18,10},{26,18},{... | collective-permute-start | bytes 1179656 | tf_op jit(solution)/shard_map/ppermute | solution.py:181

commit v16 on v12

--- a/solution.py
+++ b/solution.py
@@ -29,11 +29,14 @@
     return total
 
 
-def pair_kernel(pre_ref, post_ref, *refs, tile_rows, tile_cols):
-    del pre_ref, post_ref
+def pair_kernel(pre_ref, post_ref, main_ref, edge_ref, band_ref, coh_ref, chg_ref, field_ref, rows_ref, stack_ref, *, tile_rows, tile_cols):
     pp = PAIRS_PER_STEP
-    sides = refs[: 4 * pp]
-    band_ref, coh_ref, chg_ref, field_ref, rows_ref, stack_ref = refs[4 * pp :]
+    step = pl.program_id(0)
+    sides = []
+    for p in range(pp):
+        for ids in (pre_ref, post_ref):
+            at = ids[step * pp + p]
+            sides += [main_ref.at[:, pl.ds(at, 1)], edge_ref.at[pl.ds(at, 1)]]
     window = 2 * RADIUS + 1
     padded_cols = tile_cols + LANES
     rows = pp * FIELDS * tile_rows
@@ -89,27 +92,12 @@
     gap = lane_in - LANES - lane_out
     band = jnp.where((gap >= -RADIUS) & (gap <= RADIUS), 1.0, 0.0).astype(jnp.bfloat16)
     band = jnp.concatenate([band, band], axis=0)
-    main_block = (blocks_per_tile, 1, 2, padded_rows, block_cols)
-    edge_block = (1, 2, padded_rows, LANES)
-
-    def specs(p, which):
-        def main_index(i, pre, post):
-            ids = pre if which == 0 else post
-            return (0, ids[i * pp + p], 0, 0, 0)
-
-        def edge_index(i, pre, post):
-            ids = pre if which == 0 else post
-            return (ids[i * pp + p], 0, 0, 0)
-
-        return [pl.BlockSpec(main_block, main_index), pl.BlockSpec(edge_block, edge_index)]
-
-    in_specs = []
-    operands = []
-    for p in range(pp):
-        in_specs += specs(p, 0) + specs(p, 1)
-        operands += [main, edge, main, edge]
-    in_specs.append(pl.BlockSpec((2 * width, LANES), lambda i, pre, post: (0, 0)))
-    operands.append(band)
+    in_specs = [
+        pl.BlockSpec(main.shape, lambda i, pre, post: (0,) * main.ndim),
+        pl.BlockSpec(edge.shape, lambda i, pre, post: (0,) * edge.ndim),
+        pl.BlockSpec((2 * width, LANES), lambda i, pre, post: (0, 0)),
+    ]
+    operands = [main, edge, band]
     out_block = pl.BlockSpec((pp, tile_rows, tile_cols), lambda i, pre, post: (i, 0, 0))
     rows = pp * FIELDS * tile_rows
     blocks = tile_cols // LANES

time: 139 us -> 137 us (0.986)
  Pallas kernels: 19.5 us -> 17.4 us
    pallas_call x1, Pallas kernels: 19.5 us -> 17.4 us  [pair_maps(): pl.pallas_call(kernel, grid_spec=grid_spec, out_shape=[out_shape, out_sha...]
where the time goes in v16:
time: 137 us; the launch traced here: 136 us
  starting transfers between devices  60.4 us (44%)
  waiting for transfers between devices  27.6 us (20%)
  local copies, waits for them, and re-layouts  26 us (19%)
  Pallas kernels  17.4 us (13%)
  other arithmetic  2.01 us (1%)
  matrix products  1.64 us (1%)
    ppermute x8, starting transfers between devices, shards(): received.append(lax.ppermute(chunk, ('tx', 'ty'), pairs))  46.7 us
    ppermute x8, waiting for transfers between devices, shards(): received.append(lax.ppermute(chunk, ('tx', 'ty'), pairs))  18 us
    pallas_call x1, Pallas kernels, pair_maps(): pl.pallas_call(kernel, grid_spec=grid_spec, out_shape=[out_shape, out_sha...  17.4 us
    ppermute x1, starting transfers between devices, shards(): right = lax.ppermute(x[0, :, :, :LANES], 'tx', backward)  11.6 us
    unnamed x11, local copies, waits for them, and re-layouts  10.4 us
    ppermute x1, waiting for transfers between devices, shards(): lax.ppermute(x[blocks_per_tile - 1, :, :, local_cols - LANES:], 'tx', for...  8.27 us
    dynamic_slice x1, local copies, waits for them, and re-layouts, shards(): chunk = lax.dynamic_slice_in_dim(x, first, padded_rows, axis=2)  5.06 us
    convert_element_type x1, local copies, waits for them, and re-layouts, shards(): main.astype(jnp.bfloat16)  3.4 us
  transfers between devices with their start and end apart: 10, of which 4 were waited for; matrix products, arithmetic and copies ran while one was open for 14% of the time, Pallas kernels for 0%

profile of v16, /device:TPU:21, one launch (start us, length us, event | category | flops | bytes accessed | tf_op | source)
XLA Modules:
  0.0 136.0 jit_solution(8926695703949483790)
XLA Ops:
  0.8 5.1 %pad_dynamic-slice_fusion = (bf16[8,2,24,512]{3,2,1,0:T(8,128)(2,1)S(1)}, bf16[8,2,24,512]{3,2,1,0:T(8,128)(2,1)S(1)}, bf16[8,2,24,512]{3,2,1,0:T(8,128)(2,1)S(1...) fusion(s32[]{:T(128)S(6)} %select_n.146, ...), kind=kLoop, calls=%fused_computation.7 | loop fusion | bytes 5242912 | tf_op jit(solution)/shard_map/dynamic_slice | solution.py:147
  5.8 4.5 %collective-permute-start = (bf16[384,512]{1,0:T(8,128)(2,1)}, bf16[384,512]{1,0:T(8,128)(2,1)}, u32[]{:S(2)}, u32[]{:S(2)}) collective-permute-start(bf16[384,512]{1,0:T(8,128)(2,1)} %bitcast), channel_id=1, source_target_pairs={{0,0},{1,1},{2,8},{3,9},{4,16},{5,17},{6,24},{7,25},{8,2},{9,3},{1... | collective-permute-start | bytes 1179656 | tf_op jit(solution)/shard_map/ppermute | solution.py:149
  10.3 0.7 collective-permute-start.1
  11.0 2.3 %collective-permute-start.2 = (bf16[384,512]{1,0:T(8,128)(2,1)S(1)}, bf16[384,512]{1,0:T(8,128)(2,1)}, u32[]{:S(2)}, u32[]{:S(2)}) collective-permute-start(bf16[384,512]{1,0:T(8,128)(2,1)S(1)} %bitcast.61), channel_id=1, source_target_pairs={{0,2},{1,3},{2,10},{3,11},{4,18},{5,19},{6,26},{7,27},{8,4},{9,5},... | collective-permute-start | bytes 1179656 | tf_op jit(solution)/shard_map/ppermute | solution.py:149
  13.4 3.4 %collective-permute-start.3 = (bf16[384,512]{1,0:T(8,128)(2,1)S(1)}, bf16[384,512]{1,0:T(8,128)(2,1)}, u32[]{:S(2)}, u32[]{:S(2)}) collective-permute-start(bf16[384,512]{1,0:T(8,128)(2,1)S(1)} %bitcast.60), channel_id=1, source_target_pairs={{0,3},{1,4},{2,11},{3,12},{4,19},{5,20},{6,27},{7,28},{8,5},{9,6},... | collective-permute-start | bytes 1179656 | tf_op jit(solution)/shard_map/ppermute | solution.py:149
  17.1 0.5 copy.10
  17.6 0.8 reshape.168
  18.4 0.8 reshape.167
  19.6 0.7 pad_maximum_fusion.band_ref
  20.3 28.9 %collective-permute-start.5 = (bf16[384,512]{1,0:T(8,128)(2,1)S(1)}, bf16[384,512]{1,0:T(8,128)(2,1)S(1)}, u32[]{:S(2)}, u32[]{:S(2)}) collective-permute-start(bf16[384,512]{1,0:T(8,128)(2,1)S(1)} %bitcast.58), channel_id=1, source_target_pairs={{0,5},{1,6},{2,13},{3,14},{4,21},{5,22},{6,29},{7,30},{8,7},{9,0},... | collective-permute-start | bytes 1179656 | tf_op jit(solution)/shard_map/ppermute | solution.py:149
  49.1 1.8 %bitcast_dynamic-update-slice_fusion.7 = bf16[8,384,512]{2,1,0:T(8,128)(2,1)} fusion(bf16[384,512]{1,0:T(8,128)(2,1)} %collective-permute-done), kind=kLoop, calls=%fused_computation.24 | loop fusion | bytes 786432
  50.9 6.1 %collective-permute-start.6 = (bf16[384,512]{1,0:T(8,128)(2,1)S(1)}, bf16[384,512]{1,0:T(8,128)(2,1)S(1)}, u32[]{:S(2)}, u32[]{:S(2)}) collective-permute-start(bf16[384,512]{1,0:T(8,128)(2,1)S(1)} %bitcast.57), channel_id=1, source_target_pairs={{0,6},{1,7},{2,14},{3,15},{4,22},{5,23},{6,30},{7,31},{8,0},{9,1},... | collective-permute-start | bytes 1179656 | tf_op jit(solution)/shard_map/ppermute | solution.py:149
  57.0 1.8 %bitcast_dynamic-update-slice_fusion.6 = bf16[8,384,512]{2,1,0:T(8,128)(2,1)} fusion(bf16[8,384,512]{2,1,0:T(8,128)(2,1)} %bitcast_dynamic-update-slice_fusion.7, bf16[384,512]{1,0:T(8,128)(2,1)} %collective-permute-done.1), kind=kLoop, calls=%fused_computation.23 | loop fusion | bytes 786432
  58.8 0.9 collective-permute-start.7
  59.6 1.8 %bitcast_dynamic-update-slice_fusion.5 = bf16[8,384,512]{2,1,0:T(8,128)(2,1)} fusion(bf16[8,384,512]{2,1,0:T(8,128)(2,1)} %bitcast_dynamic-update-slice_fusion.6, bf16[384,512]{1,0:T(8,128)(2,1)} %collective-permute-done.2), kind=kLoop, calls=%fused_computation.22 | loop fusion | bytes 786432
  61.4 1.8 %bitcast_dynamic-update-slice_fusion.4 = bf16[8,384,512]{2,1,0:T(8,128)(2,1)} fusion(bf16[8,384,512]{2,1,0:T(8,128)(2,1)} %bitcast_dynamic-update-slice_fusion.5, bf16[384,512]{1,0:T(8,128)(2,1)} %collective-permute-done.3), kind=kLoop, calls=%fused_computation.21 | loop fusion | bytes 786432
  63.2 1.8 %bitcast_dynamic-update-slice_fusion.3 = bf16[8,384,512]{2,1,0:T(8,128)(2,1)} fusion(bf16[8,384,512]{2,1,0:T(8,128)(2,1)} %bitcast_dynamic-update-slice_fusion.4, bf16[384,512]{1,0:T(8,128)(2,1)} %collective-permute-done.4), kind=kLoop, calls=%fused_computation.20 | loop fusion | bytes 786432
  65.0 10.3 %collective-permute-done.5 = bf16[384,512]{1,0:T(8,128)(2,1)S(1)} collective-permute-done((bf16[384,512]{1,0:T(8,128)(2,1)S(1)}, bf16[384,512]{1,0:T(8,128)(2,1)S(1)}, u32[]{:S(2)}, u32[]{:S(2)}) %collective-permute-start.5) | collective-permute-done | bytes 393248 | tf_op jit(solution)/shard_map/ppermute | solution.py:149
  75.3 0.8 bitcast_dynamic-update-slice_fusion.2
  76.1 7.7 %collective-permute-done.6 = bf16[384,512]{1,0:T(8,128)(2,1)S(1)} collective-permute-done((bf16[384,512]{1,0:T(8,128)(2,1)S(1)}, bf16[384,512]{1,0:T(8,128)(2,1)S(1)}, u32[]{:S(2)}, u32[]{:S(2)}) %collective-permute-start.6) | collective-permute-done | bytes 393248 | tf_op jit(solution)/shard_map/ppermute | solution.py:149
  83.7 0.8 bitcast_dynamic-update-slice_fusion.1
  84.5 0.8 bitcast_dynamic-update-slice_fusion
  85.3 2.6 %gather_fusion = bf16[8,384,512]{2,1,0:T(8,128)(2,1)S(1)} fusion(bf16[8,384,512]{2,1,0:T(8,128)(2,1)} %bitcast_dynamic-update-slice_fusion, s32[1024]{0:T(1024)S(1)} %pad_clamp_fusion), kind=kCustom, calls=%fused_computation | custom fusion | bytes 6291488 | tf_op jit(solution)/shard_map/jit(_take)/gather | solution.py:153
  88.5 11.6 %collective-permute-start.8 = (bf16[64,24,128]{2,1,0:T(8,128)(2,1)S(1)}, bf16[64,24,128]{2,1,0:T(8,128)(2,1)S(1)}, u32[]{:S(2)}, u32[]{:S(2)}) collective-permute-start(bf16[64,24,128]{2,1,0:T(8,128)(2,1)S(1)} %get-tuple-element.3), channel_id=1, source_target_pairs={{8,0},{16,8},{24,16},{9,1},{17,9},{25,17},{10,2},{18,10},{26,18},{... | collective-permute-start | bytes 1179656 | tf_op jit(solution)/shard_map/ppermute | solution.py:159
  100.0 2.1 %collective-permute-start.9 = (bf16[64,24,128]{2,1,0:T(8,128)(2,1)S(1)}, bf16[64,24,128]{2,1,0:T(8,128)(2,1)S(1)}, u32[]{:S(2)}, u32[]{:S(2)}) collective-permute-start(bf16[64,24,128]{2,1,0:T(8,128)(2,1)S(1)} %get-tuple-element.2), channel_id=1, source_target_pairs={{0,8},{8,16},{16,24},{1,9},{9,17},{17,25},{2,10},{10,18},{18,26},{... | collective-permute-start | bytes 1179656 | tf_op jit(solution)/shard_map/ppermute | solution.py:158
  102.1 0.7 broadcast_select_fusion.1
  102.9 1.4 %convert_bitcast_fusion = bf16[2,64,24,512]{3,1,2,0:T(8,128)(2,1)S(1)} fusion(bf16[2,64,24,512]{3,2,1,0:T(8,128)(2,1)S(1)} %bitcast.54, bf16[64,64,1,1]{1,0,2,3:T(8,128)(2,1)S(1)} %reshape.167), kind=kOutput, calls=%fused_computation.3 | convolution fusion | flops 202899456 | bytes 6299648 | tf_op jit(solution)/shard_map/kc,bchw->bkhw/dot_general | solution.py:166
  104.2 3.4 %copy.12 = bf16[2,64,24,512]{3,2,1,0:T(8,128)(2,1)} copy(bf16[2,64,24,512]{3,1,2,0:T(8,128)(2,1)S(1)} %convert_bitcast_fusion) | data formatting | bytes 6291456 | tf_op jit(solution)/shard_map/convert_element_type | solution.py:167
  107.6 1.4 %collective-permute-done.8 = bf16[64,24,128]{2,1,0:T(8,128)(2,1)S(1)} collective-permute-done((bf16[64,24,128]{2,1,0:T(8,128)(2,1)S(1)}, bf16[64,24,128]{2,1,0:T(8,128)(2,1)S(1)}, u32[]{:S(2)}, u32[]{:S(2)}) %collective-permute-start.8) | collective-permute-done | bytes 393248 | tf_op jit(solution)/shard_map/ppermute | solution.py:159
  109.0 8.3 %collective-permute-done.9 = bf16[64,24,128]{2,1,0:T(8,128)(2,1)S(1)} collective-permute-done((bf16[64,24,128]{2,1,0:T(8,128)(2,1)S(1)}, bf16[64,24,128]{2,1,0:T(8,128)(2,1)S(1)}, u32[]{:S(2)}, u32[]{:S(2)}) %collective-permute-start.9) | collective-permute-done | bytes 393248 | tf_op jit(solution)/shard_map/ppermute | solution.py:158
  117.6 1.0 copy.14
  118.6 17.4 %shard_map.68 = (f32[32,16,1024]{2,1,0:T(8,128)}, f32[32,16,1024]{2,1,0:T(8,128)}) custom-call(s32[32]{0:T(128)} %pre_ref.1, s32[32]{0:T(128)} %post_ref.1, bf16[2,32,2,24,512]{4,3,2,1,0:T(8,128)(2,1)} %bitcast.53, bf16[32,2,24,128]{3,2,1,0:T(8,128)(2,1)} %bitcast.55, bf16[768,128]{1,0:T(8,128)(2,1)} %pad_maximum_fusion.band_ref), custom_call_target="tpu_custom_call" | custom-call | tf_op jit(solution)/shard_map/pallas_call | solution.py:118
  (31 shorter events, 1.5 us)
Async XLA Ops:
  0.6 16.3 %copy-start = (bf16[32,32]{1,0:T(8,128)(2,1)S(1)}, bf16[32,32]{1,0:T(8,128)(2,1)}, u32[]{:S(2)}) copy-start(bf16[32,32]{1,0:T(8,128)(2,1)} %param.7) | copy-start | bytes 6148
  0.6 16.4 %copy-start.1 = (bf16[32,32]{1,0:T(8,128)(2,1)S(1)}, bf16[32,32]{1,0:T(8,128)(2,1)}, u32[]{:S(2)}) copy-start(bf16[32,32]{1,0:T(8,128)(2,1)} %param.6) | copy-start | bytes 6148
  5.8 14.4 %collective-permute-start = (bf16[384,512]{1,0:T(8,128)(2,1)}, bf16[384,512]{1,0:T(8,128)(2,1)}, u32[]{:S(2)}, u32[]{:S(2)}) collective-permute-start(bf16[384,512]{1,0:T(8,128)(2,1)} %bitcast), channel_id=1, source_target_pairs={{0,0},{1,1},{2,8},{3,9},{4,16},{5,17},{6,24},{7,25},{8,2},{9,3},{1... | collective-permute-start | bytes 1179656 | tf_op jit(solution)/shard_map/ppermute | solution.py:149
  10.3 40.6 %collective-permute-start.1 = (bf16[384,512]{1,0:T(8,128)(2,1)S(1)}, bf16[384,512]{1,0:T(8,128)(2,1)}, u32[]{:S(2)}, u32[]{:S(2)}) collective-permute-start(bf16[384,512]{1,0:T(8,128)(2,1)S(1)} %bitcast.62), channel_id=1, source_target_pairs={{0,1},{1,2},{2,9},{3,10},{4,17},{5,18},{6,25},{7,26},{8,3},{9,4},{... | collective-permute-start | bytes 1179656 | tf_op jit(solution)/shard_map/ppermute | solution.py:149
  11.0 47.7 %collective-permute-start.2 = (bf16[384,512]{1,0:T(8,128)(2,1)S(1)}, bf16[384,512]{1,0:T(8,128)(2,1)}, u32[]{:S(2)}, u32[]{:S(2)}) collective-permute-start(bf16[384,512]{1,0:T(8,128)(2,1)S(1)} %bitcast.61), channel_id=1, source_target_pairs={{0,2},{1,3},{2,10},{3,11},{4,18},{5,19},{6,26},{7,27},{8,4},{9,5},... | collective-permute-start | bytes 1179656 | tf_op jit(solution)/shard_map/ppermute | solution.py:149
  13.4 48.0 %collective-permute-start.3 = (bf16[384,512]{1,0:T(8,128)(2,1)S(1)}, bf16[384,512]{1,0:T(8,128)(2,1)}, u32[]{:S(2)}, u32[]{:S(2)}) collective-permute-start(bf16[384,512]{1,0:T(8,128)(2,1)S(1)} %bitcast.60), channel_id=1, source_target_pairs={{0,3},{1,4},{2,11},{3,12},{4,19},{5,20},{6,27},{7,28},{8,5},{9,6},... | collective-permute-start | bytes 1179656 | tf_op jit(solution)/shard_map/ppermute | solution.py:149
  16.7 46.5 %collective-permute-start.4 = (bf16[384,512]{1,0:T(8,128)(2,1)S(1)}, bf16[384,512]{1,0:T(8,128)(2,1)}, u32[]{:S(2)}, u32[]{:S(2)}) collective-permute-start(bf16[384,512]{1,0:T(8,128)(2,1)S(1)} %bitcast.59), channel_id=1, source_target_pairs={{0,4},{1,5},{2,12},{3,13},{4,20},{5,21},{6,28},{7,29},{8,6},{9,7},... | collective-permute-start | bytes 1179656 | tf_op jit(solution)/shard_map/ppermute | solution.py:149
  20.3 55.0 %collective-permute-start.5 = (bf16[384,512]{1,0:T(8,128)(2,1)S(1)}, bf16[384,512]{1,0:T(8,128)(2,1)S(1)}, u32[]{:S(2)}, u32[]{:S(2)}) collective-permute-start(bf16[384,512]{1,0:T(8,128)(2,1)S(1)} %bitcast.58), channel_id=1, source_target_pairs={{0,5},{1,6},{2,13},{3,14},{4,21},{5,22},{6,29},{7,30},{8,7},{9,0},... | collective-permute-start | bytes 1179656 | tf_op jit(solution)/shard_map/ppermute | solution.py:149
  50.9 32.8 %collective-permute-start.6 = (bf16[384,512]{1,0:T(8,128)(2,1)S(1)}, bf16[384,512]{1,0:T(8,128)(2,1)S(1)}, u32[]{:S(2)}, u32[]{:S(2)}) collective-permute-start(bf16[384,512]{1,0:T(8,128)(2,1)S(1)} %bitcast.57), channel_id=1, source_target_pairs={{0,6},{1,7},{2,14},{3,15},{4,22},{5,23},{6,30},{7,31},{8,0},{9,1},... | collective-permute-start | bytes 1179656 | tf_op jit(solution)/shard_map/ppermute | solution.py:149
  58.8 25.7 %collective-permute-start.7 = (bf16[384,512]{1,0:T(8,128)(2,1)S(1)}, bf16[384,512]{1,0:T(8,128)(2,1)S(1)}, u32[]{:S(2)}, u32[]{:S(2)}) collective-permute-start(bf16[384,512]{1,0:T(8,128)(2,1)S(1)} %bitcast.56), channel_id=1, source_target_pairs={{0,7},{1,0},{2,15},{3,8},{4,23},{5,16},{6,31},{7,24},{8,1},{9,2},{... | collective-permute-start | bytes 1179656 | tf_op jit(solution)/shard_map/ppermute | solution.py:149
  88.5 20.6 %collective-permute-start.8 = (bf16[64,24,128]{2,1,0:T(8,128)(2,1)S(1)}, bf16[64,24,128]{2,1,0:T(8,128)(2,1)S(1)}, u32[]{:S(2)}, u32[]{:S(2)}) collective-permute-start(bf16[64,24,128]{2,1,0:T(8,128)(2,1)S(1)} %get-tuple-element.3), channel_id=1, source_target_pairs={{8,0},{16,8},{24,16},{9,1},{17,9},{25,17},{10,2},{18,10},{26,18},{... | collective-permute-start | bytes 1179656 | tf_op jit(solution)/shard_map/ppermute | solution.py:159
  100.0 17.2 %collective-permute-start.9 = (bf16[64,24,128]{2,1,0:T(8,128)(2,1)S(1)}, bf16[64,24,128]{2,1,0:T(8,128)(2,1)S(1)}, u32[]{:S(2)}, u32[]{:S(2)}) collective-permute-start(bf16[64,24,128]{2,1,0:T(8,128)(2,1)S(1)} %get-tuple-element.2), channel_id=1, source_target_pairs={{0,8},{8,16},{16,24},{1,9},{9,17},{17,25},{2,10},{10,18},{18,26},{... | collective-permute-start | bytes 1179656 | tf_op jit(solution)/shard_map/ppermute | solution.py:158

commit v17 on v16

--- a/solution.py
+++ b/solution.py
@@ -29,52 +29,74 @@
     return total
 
 
-def pair_kernel(pre_ref, post_ref, main_ref, edge_ref, band_ref, coh_ref, chg_ref, field_ref, rows_ref, stack_ref, *, tile_rows, tile_cols):
+def pair_kernel(pre_ref, post_ref, main_ref, edge_ref, band_ref, coh_ref, chg_ref, field_ref, rows_ref, stack_ref, power_ref, *, tile_rows, tile_cols):
     pp = PAIRS_PER_STEP
+    count = 2 * pp
     step = pl.program_id(0)
-    sides = []
-    for p in range(pp):
-        for ids in (pre_ref, post_ref):
-            at = ids[step * pp + p]
-            sides += [main_ref.at[:, pl.ds(at, 1)], edge_ref.at[pl.ds(at, 1)]]
     window = 2 * RADIUS + 1
     padded_cols = tile_cols + LANES
-    rows = pp * FIELDS * tile_rows
+    rows = count * tile_rows
     blocks = tile_cols // LANES
+    block_cols = main_ref.shape[-1]
+
+    def pieces(index):
+        parts = [(c * block_cols, main_ref[c, index]) for c in range(main_ref.shape[0])]
+        parts.append((tile_cols, edge_ref[index]))
+        return parts
+
+    def box_pass():
+        for f in range(count):
+            acc = window_rows(field_ref[f], window)[:tile_rows]
+            rows_ref[pl.ds(f * tile_rows, tile_rows), pl.ds(LANES, padded_cols)] = acc
+            rows_ref[pl.ds(f * tile_rows, tile_rows), pl.ds(0, LANES)] = acc[:, padded_cols - LANES :]
+        rowsum = rows_ref[...]
+        high = rowsum.astype(jnp.bfloat16)
+        low = (rowsum - high.astype(jnp.float32)).astype(jnp.bfloat16)
+        width = 3 * LANES
+        for j in range(blocks):
+            stack_ref[pl.ds(j * rows, rows), pl.ds(0, width)] = high[:, j * LANES : j * LANES + width]
+            stack_ref[pl.ds(j * rows, rows), pl.ds(width, width)] = low[:, j * LANES : j * LANES + width]
+        sums = jnp.dot(stack_ref[...], band_ref[...], preferred_element_type=jnp.float32)
+        return sums / float(window * window)
+
+    @pl.when(step == 0)
+    def _():
+        def chunk(k, carry):
+            for a in range(count):
+                for at, piece in pieces(k * count + a):
+                    re = piece[0].astype(jnp.float32)
+                    im = piece[1].astype(jnp.float32)
+                    field_ref[a, :, pl.ds(at, piece.shape[-1])] = re * re + im * im
+            means = box_pass()
+            for j in range(blocks):
+                for a in range(count):
+                    base = j * rows + a * tile_rows
+                    power_ref[k * count + a, :, pl.ds(j * LANES, LANES)] = (
+                        means[base : base + tile_rows] + 1e-06
+                    )
+            return carry
+
+        lax.fori_loop(0, main_ref.shape[1] // count, chunk, 0)
+
+    pre_at = [pre_ref[step * pp + p] for p in range(pp)]
+    post_at = [post_ref[step * pp + p] for p in range(pp)]
     for p in range(pp):
-        a_main, a_edge, b_main, b_edge = sides[4 * p : 4 * p + 4]
-        pieces = [(c * a_main.shape[-1], a_main[c, 0], b_main[c, 0]) for c in range(a_main.shape[0])]
-        pieces.append((tile_cols, a_edge[0], b_edge[0]))
-        for at, a, b in pieces:
+        for (at, a), (_, b) in zip(pieces(pre_at[p]), pieces(post_at[p])):
             width = a.shape[-1]
             pr = a[0].astype(jnp.float32)
             pi = a[1].astype(jnp.float32)
             qr = b[0].astype(jnp.float32)
             qi = b[1].astype(jnp.float32)
-            fields = (pr * pr + pi * pi, qr * qr + qi * qi, pr * qr + pi * qi, pi * qr - pr * qi)
-            for f, value in enumerate(fields):
-                field_ref[f, :, pl.ds(at, width)] = value
-        for f in range(FIELDS):
-            acc = window_rows(field_ref[f], window)[:tile_rows]
-            at = (p * FIELDS + f) * tile_rows
-            rows_ref[pl.ds(at, tile_rows), pl.ds(LANES, padded_cols)] = acc
-            rows_ref[pl.ds(at, tile_rows), pl.ds(0, LANES)] = acc[:, padded_cols - LANES :]
-    rowsum = rows_ref[...]
-    high = rowsum.astype(jnp.bfloat16)
-    low = (rowsum - high.astype(jnp.float32)).astype(jnp.bfloat16)
-    width = 3 * LANES
-    for j in range(blocks):
-        stack_ref[pl.ds(j * rows, rows), pl.ds(0, width)] = high[:, j * LANES : j * LANES + width]
-        stack_ref[pl.ds(j * rows, rows), pl.ds(width, width)] = low[:, j * LANES : j * LANES + width]
-    sums = jnp.dot(stack_ref[...], band_ref[...], preferred_element_type=jnp.float32)
-    means = sums / float(window * window)
+            field_ref[2 * p, :, pl.ds(at, width)] = pr * qr + pi * qi
+            field_ref[2 * p + 1, :, pl.ds(at, width)] = pi * qr - pr * qi
+    means = box_pass()
     for j in range(blocks):
         for p in range(pp):
-            base = j * rows + p * FIELDS * tile_rows
-            pre_power = means[base : base + tile_rows] + 1e-06
-            post_power = means[base + tile_rows : base + 2 * tile_rows] + 1e-06
-            real_mean = means[base + 2 * tile_rows : base + 3 * tile_rows]
-            imag_mean = means[base + 3 * tile_rows : base + 4 * tile_rows]
+            pre_power = power_ref[pre_at[p], :, pl.ds(j * LANES, LANES)]
+            post_power = power_ref[post_at[p], :, pl.ds(j * LANES, LANES)]
+            base = j * rows + 2 * p * tile_rows
+            real_mean = means[base : base + tile_rows]
+            imag_mean = means[base + tile_rows : base + 2 * tile_rows]
             coh = jnp.sqrt(real_mean * real_mean + imag_mean * imag_mean) / jnp.sqrt(
                 pre_power * post_power
             )
@@ -99,7 +121,7 @@
     ]
     operands = [main, edge, band]
     out_block = pl.BlockSpec((pp, tile_rows, tile_cols), lambda i, pre, post: (i, 0, 0))
-    rows = pp * FIELDS * tile_rows
+    rows = 2 * pp * tile_rows
     blocks = tile_cols // LANES
     padded_cols = tile_cols + LANES
     grid_spec = pltpu.PrefetchScalarGridSpec(
@@ -108,9 +130,10 @@
         in_specs=in_specs,
         out_specs=[out_block, out_block],
         scratch_shapes=[
-            pltpu.VMEM((FIELDS, padded_rows, padded_cols), jnp.float32),
+            pltpu.VMEM((2 * pp, padded_rows, padded_cols), jnp.float32),
             pltpu.VMEM((rows, padded_cols + LANES), jnp.float32),
             pltpu.VMEM((blocks * rows, 2 * width), jnp.bfloat16),
+            pltpu.VMEM((main.shape[1], tile_rows, tile_cols), jnp.float32),
         ],
     )
     out_shape = jax.ShapeDtypeStruct((count_pairs, tile_rows, tile_cols), jnp.float32)

time: 137 us -> 135 us (0.985)
  Pallas kernels: 17.4 us -> 15.8 us
    pallas_call x1, Pallas kernels: 17.4 us -> 15.8 us  [pair_maps(): pl.pallas_call(kernel, grid_spec=grid_spec, out_shape=[out_shape, out_sha...]
where the time goes in v17:
time: 135 us; the launch traced here: 134 us
  starting transfers between devices  60.4 us (45%)
  waiting for transfers between devices  27.6 us (20%)
  local copies, waits for them, and re-layouts  26 us (19%)
  Pallas kernels  15.8 us (12%)
  other arithmetic  2.01 us (1%)
  matrix products  1.64 us (1%)
    ppermute x8, starting transfers between devices, shards(): received.append(lax.ppermute(chunk, ('tx', 'ty'), pairs))  46.7 us
    ppermute x8, waiting for transfers between devices, shards(): received.append(lax.ppermute(chunk, ('tx', 'ty'), pairs))  18 us
    pallas_call x1, Pallas kernels, pair_maps(): pl.pallas_call(kernel, grid_spec=grid_spec, out_shape=[out_shape, out_sha...  15.8 us
    ppermute x1, starting transfers between devices, shards(): right = lax.ppermute(x[0, :, :, :LANES], 'tx', backward)  11.6 us
    unnamed x11, local copies, waits for them, and re-layouts  10.4 us
    ppermute x1, waiting for transfers between devices, shards(): lax.ppermute(x[blocks_per_tile - 1, :, :, local_cols - LANES:], 'tx', for...  8.27 us
    dynamic_slice x1, local copies, waits for them, and re-layouts, shards(): chunk = lax.dynamic_slice_in_dim(x, first, padded_rows, axis=2)  5.06 us
    convert_element_type x1, local copies, waits for them, and re-layouts, shards(): main.astype(jnp.bfloat16)  3.4 us
  transfers between devices with their start and end apart: 10, of which 4 were waited for; matrix products, arithmetic and copies ran while one was open for 14% of the time, Pallas kernels for 0%

profile of v17, /device:TPU:21, one launch (start us, length us, event | category | flops | bytes accessed | tf_op | source)
XLA Modules:
  0.0 134.4 jit_solution(6548858563205953476)
XLA Ops:
  0.8 5.1 %pad_dynamic-slice_fusion = (bf16[8,2,24,512]{3,2,1,0:T(8,128)(2,1)S(1)}, bf16[8,2,24,512]{3,2,1,0:T(8,128)(2,1)S(1)}, bf16[8,2,24,512]{3,2,1,0:T(8,128)(2,1)S(1...) fusion(s32[]{:T(128)S(6)} %select_n.146, ...), kind=kLoop, calls=%fused_computation.7 | loop fusion | bytes 5242912 | tf_op jit(solution)/shard_map/dynamic_slice | solution.py:170
  5.8 4.5 %collective-permute-start = (bf16[384,512]{1,0:T(8,128)(2,1)}, bf16[384,512]{1,0:T(8,128)(2,1)}, u32[]{:S(2)}, u32[]{:S(2)}) collective-permute-start(bf16[384,512]{1,0:T(8,128)(2,1)} %bitcast), channel_id=1, source_target_pairs={{0,0},{1,1},{2,8},{3,9},{4,16},{5,17},{6,24},{7,25},{8,2},{9,3},{1... | collective-permute-start | bytes 1179656 | tf_op jit(solution)/shard_map/ppermute | solution.py:172
  10.3 0.7 collective-permute-start.1
  11.0 2.3 %collective-permute-start.2 = (bf16[384,512]{1,0:T(8,128)(2,1)S(1)}, bf16[384,512]{1,0:T(8,128)(2,1)}, u32[]{:S(2)}, u32[]{:S(2)}) collective-permute-start(bf16[384,512]{1,0:T(8,128)(2,1)S(1)} %bitcast.61), channel_id=1, source_target_pairs={{0,2},{1,3},{2,10},{3,11},{4,18},{5,19},{6,26},{7,27},{8,4},{9,5},... | collective-permute-start | bytes 1179656 | tf_op jit(solution)/shard_map/ppermute | solution.py:172
  13.4 3.4 %collective-permute-start.3 = (bf16[384,512]{1,0:T(8,128)(2,1)S(1)}, bf16[384,512]{1,0:T(8,128)(2,1)}, u32[]{:S(2)}, u32[]{:S(2)}) collective-permute-start(bf16[384,512]{1,0:T(8,128)(2,1)S(1)} %bitcast.60), channel_id=1, source_target_pairs={{0,3},{1,4},{2,11},{3,12},{4,19},{5,20},{6,27},{7,28},{8,5},{9,6},... | collective-permute-start | bytes 1179656 | tf_op jit(solution)/shard_map/ppermute | solution.py:172
  17.1 0.5 copy.10
  17.6 0.8 reshape.168
  18.4 0.8 reshape.167
  19.6 0.7 pad_maximum_fusion.band_ref
  20.3 28.9 %collective-permute-start.5 = (bf16[384,512]{1,0:T(8,128)(2,1)S(1)}, bf16[384,512]{1,0:T(8,128)(2,1)S(1)}, u32[]{:S(2)}, u32[]{:S(2)}) collective-permute-start(bf16[384,512]{1,0:T(8,128)(2,1)S(1)} %bitcast.58), channel_id=1, source_target_pairs={{0,5},{1,6},{2,13},{3,14},{4,21},{5,22},{6,29},{7,30},{8,7},{9,0},... | collective-permute-start | bytes 1179656 | tf_op jit(solution)/shard_map/ppermute | solution.py:172
  49.1 1.8 %bitcast_dynamic-update-slice_fusion.7 = bf16[8,384,512]{2,1,0:T(8,128)(2,1)} fusion(bf16[384,512]{1,0:T(8,128)(2,1)} %collective-permute-done), kind=kLoop, calls=%fused_computation.24 | loop fusion | bytes 786432
  50.9 6.1 %collective-permute-start.6 = (bf16[384,512]{1,0:T(8,128)(2,1)S(1)}, bf16[384,512]{1,0:T(8,128)(2,1)S(1)}, u32[]{:S(2)}, u32[]{:S(2)}) collective-permute-start(bf16[384,512]{1,0:T(8,128)(2,1)S(1)} %bitcast.57), channel_id=1, source_target_pairs={{0,6},{1,7},{2,14},{3,15},{4,22},{5,23},{6,30},{7,31},{8,0},{9,1},... | collective-permute-start | bytes 1179656 | tf_op jit(solution)/shard_map/ppermute | solution.py:172
  57.0 1.8 %bitcast_dynamic-update-slice_fusion.6 = bf16[8,384,512]{2,1,0:T(8,128)(2,1)} fusion(bf16[8,384,512]{2,1,0:T(8,128)(2,1)} %bitcast_dynamic-update-slice_fusion.7, bf16[384,512]{1,0:T(8,128)(2,1)} %collective-permute-done.1), kind=kLoop, calls=%fused_computation.23 | loop fusion | bytes 786432
  58.8 0.9 collective-permute-start.7
  59.6 1.8 %bitcast_dynamic-update-slice_fusion.5 = bf16[8,384,512]{2,1,0:T(8,128)(2,1)} fusion(bf16[8,384,512]{2,1,0:T(8,128)(2,1)} %bitcast_dynamic-update-slice_fusion.6, bf16[384,512]{1,0:T(8,128)(2,1)} %collective-permute-done.2), kind=kLoop, calls=%fused_computation.22 | loop fusion | bytes 786432
  61.4 1.8 %bitcast_dynamic-update-slice_fusion.4 = bf16[8,384,512]{2,1,0:T(8,128)(2,1)} fusion(bf16[8,384,512]{2,1,0:T(8,128)(2,1)} %bitcast_dynamic-update-slice_fusion.5, bf16[384,512]{1,0:T(8,128)(2,1)} %collective-permute-done.3), kind=kLoop, calls=%fused_computation.21 | loop fusion | bytes 786432
  63.2 1.8 %bitcast_dynamic-update-slice_fusion.3 = bf16[8,384,512]{2,1,0:T(8,128)(2,1)} fusion(bf16[8,384,512]{2,1,0:T(8,128)(2,1)} %bitcast_dynamic-update-slice_fusion.4, bf16[384,512]{1,0:T(8,128)(2,1)} %collective-permute-done.4), kind=kLoop, calls=%fused_computation.20 | loop fusion | bytes 786432
  65.0 10.3 %collective-permute-done.5 = bf16[384,512]{1,0:T(8,128)(2,1)S(1)} collective-permute-done((bf16[384,512]{1,0:T(8,128)(2,1)S(1)}, bf16[384,512]{1,0:T(8,128)(2,1)S(1)}, u32[]{:S(2)}, u32[]{:S(2)}) %collective-permute-start.5) | collective-permute-done | bytes 393248 | tf_op jit(solution)/shard_map/ppermute | solution.py:172
  75.3 0.8 bitcast_dynamic-update-slice_fusion.2
  76.1 7.7 %collective-permute-done.6 = bf16[384,512]{1,0:T(8,128)(2,1)S(1)} collective-permute-done((bf16[384,512]{1,0:T(8,128)(2,1)S(1)}, bf16[384,512]{1,0:T(8,128)(2,1)S(1)}, u32[]{:S(2)}, u32[]{:S(2)}) %collective-permute-start.6) | collective-permute-done | bytes 393248 | tf_op jit(solution)/shard_map/ppermute | solution.py:172
  83.7 0.8 bitcast_dynamic-update-slice_fusion.1
  84.5 0.8 bitcast_dynamic-update-slice_fusion
  85.3 2.6 %gather_fusion = bf16[8,384,512]{2,1,0:T(8,128)(2,1)S(1)} fusion(bf16[8,384,512]{2,1,0:T(8,128)(2,1)} %bitcast_dynamic-update-slice_fusion, s32[1024]{0:T(1024)S(1)} %pad_clamp_fusion), kind=kCustom, calls=%fused_computation | custom fusion | bytes 6291488 | tf_op jit(solution)/shard_map/jit(_take)/gather | solution.py:176
  88.5 11.6 %collective-permute-start.8 = (bf16[64,24,128]{2,1,0:T(8,128)(2,1)S(1)}, bf16[64,24,128]{2,1,0:T(8,128)(2,1)S(1)}, u32[]{:S(2)}, u32[]{:S(2)}) collective-permute-start(bf16[64,24,128]{2,1,0:T(8,128)(2,1)S(1)} %get-tuple-element.3), channel_id=1, source_target_pairs={{8,0},{16,8},{24,16},{9,1},{17,9},{25,17},{10,2},{18,10},{26,18},{... | collective-permute-start | bytes 1179656 | tf_op jit(solution)/shard_map/ppermute | solution.py:182
  100.0 2.1 %collective-permute-start.9 = (bf16[64,24,128]{2,1,0:T(8,128)(2,1)S(1)}, bf16[64,24,128]{2,1,0:T(8,128)(2,1)S(1)}, u32[]{:S(2)}, u32[]{:S(2)}) collective-permute-start(bf16[64,24,128]{2,1,0:T(8,128)(2,1)S(1)} %get-tuple-element.2), channel_id=1, source_target_pairs={{0,8},{8,16},{16,24},{1,9},{9,17},{17,25},{2,10},{10,18},{18,26},{... | collective-permute-start | bytes 1179656 | tf_op jit(solution)/shard_map/ppermute | solution.py:181
  102.1 0.7 broadcast_select_fusion.1
  102.9 1.4 %convert_bitcast_fusion = bf16[2,64,24,512]{3,1,2,0:T(8,128)(2,1)S(1)} fusion(bf16[2,64,24,512]{3,2,1,0:T(8,128)(2,1)S(1)} %bitcast.54, bf16[64,64,1,1]{1,0,2,3:T(8,128)(2,1)S(1)} %reshape.167), kind=kOutput, calls=%fused_computation.3 | convolution fusion | flops 202899456 | bytes 6299648 | tf_op jit(solution)/shard_map/kc,bchw->bkhw/dot_general | solution.py:189
  104.2 3.4 %copy.12 = bf16[2,64,24,512]{3,2,1,0:T(8,128)(2,1)} copy(bf16[2,64,24,512]{3,1,2,0:T(8,128)(2,1)S(1)} %convert_bitcast_fusion) | data formatting | bytes 6291456 | tf_op jit(solution)/shard_map/convert_element_type | solution.py:190
  107.6 1.4 %collective-permute-done.8 = bf16[64,24,128]{2,1,0:T(8,128)(2,1)S(1)} collective-permute-done((bf16[64,24,128]{2,1,0:T(8,128)(2,1)S(1)}, bf16[64,24,128]{2,1,0:T(8,128)(2,1)S(1)}, u32[]{:S(2)}, u32[]{:S(2)}) %collective-permute-start.8) | collective-permute-done | bytes 393248 | tf_op jit(solution)/shard_map/ppermute | solution.py:182
  109.0 8.3 %collective-permute-done.9 = bf16[64,24,128]{2,1,0:T(8,128)(2,1)S(1)} collective-permute-done((bf16[64,24,128]{2,1,0:T(8,128)(2,1)S(1)}, bf16[64,24,128]{2,1,0:T(8,128)(2,1)S(1)}, u32[]{:S(2)}, u32[]{:S(2)}) %collective-permute-start.9) | collective-permute-done | bytes 393248 | tf_op jit(solution)/shard_map/ppermute | solution.py:181
  117.6 1.0 copy.14
  118.6 15.8 %shard_map.68 = (f32[32,16,1024]{2,1,0:T(8,128)}, f32[32,16,1024]{2,1,0:T(8,128)}) custom-call(s32[32]{0:T(128)} %pre_ref.1, s32[32]{0:T(128)} %post_ref.1, bf16[2,32,2,24,512]{4,3,2,1,0:T(8,128)(2,1)} %bitcast.53, bf16[32,2,24,128]{3,2,1,0:T(8,128)(2,1)} %bitcast.55, bf16[768,128]{1,0:T(8,128)(2,1)} %pad_maximum_fusion.band_ref), custom_call_target="tpu_custom_call" | custom-call | tf_op jit(solution)/shard_map/pallas_call | solution.py:141
  (31 shorter events, 1.5 us)
Async XLA Ops:
  0.6 16.3 %copy-start = (bf16[32,32]{1,0:T(8,128)(2,1)S(1)}, bf16[32,32]{1,0:T(8,128)(2,1)}, u32[]{:S(2)}) copy-start(bf16[32,32]{1,0:T(8,128)(2,1)} %param.7) | copy-start | bytes 6148
  0.6 16.4 %copy-start.1 = (bf16[32,32]{1,0:T(8,128)(2,1)S(1)}, bf16[32,32]{1,0:T(8,128)(2,1)}, u32[]{:S(2)}) copy-start(bf16[32,32]{1,0:T(8,128)(2,1)} %param.6) | copy-start | bytes 6148
  5.8 14.4 %collective-permute-start = (bf16[384,512]{1,0:T(8,128)(2,1)}, bf16[384,512]{1,0:T(8,128)(2,1)}, u32[]{:S(2)}, u32[]{:S(2)}) collective-permute-start(bf16[384,512]{1,0:T(8,128)(2,1)} %bitcast), channel_id=1, source_target_pairs={{0,0},{1,1},{2,8},{3,9},{4,16},{5,17},{6,24},{7,25},{8,2},{9,3},{1... | collective-permute-start | bytes 1179656 | tf_op jit(solution)/shard_map/ppermute | solution.py:172
  10.3 40.6 %collective-permute-start.1 = (bf16[384,512]{1,0:T(8,128)(2,1)S(1)}, bf16[384,512]{1,0:T(8,128)(2,1)}, u32[]{:S(2)}, u32[]{:S(2)}) collective-permute-start(bf16[384,512]{1,0:T(8,128)(2,1)S(1)} %bitcast.62), channel_id=1, source_target_pairs={{0,1},{1,2},{2,9},{3,10},{4,17},{5,18},{6,25},{7,26},{8,3},{9,4},{... | collective-permute-start | bytes 1179656 | tf_op jit(solution)/shard_map/ppermute | solution.py:172
  11.0 47.7 %collective-permute-start.2 = (bf16[384,512]{1,0:T(8,128)(2,1)S(1)}, bf16[384,512]{1,0:T(8,128)(2,1)}, u32[]{:S(2)}, u32[]{:S(2)}) collective-permute-start(bf16[384,512]{1,0:T(8,128)(2,1)S(1)} %bitcast.61), channel_id=1, source_target_pairs={{0,2},{1,3},{2,10},{3,11},{4,18},{5,19},{6,26},{7,27},{8,4},{9,5},... | collective-permute-start | bytes 1179656 | tf_op jit(solution)/shard_map/ppermute | solution.py:172
  13.4 48.0 %collective-permute-start.3 = (bf16[384,512]{1,0:T(8,128)(2,1)S(1)}, bf16[384,512]{1,0:T(8,128)(2,1)}, u32[]{:S(2)}, u32[]{:S(2)}) collective-permute-start(bf16[384,512]{1,0:T(8,128)(2,1)S(1)} %bitcast.60), channel_id=1, source_target_pairs={{0,3},{1,4},{2,11},{3,12},{4,19},{5,20},{6,27},{7,28},{8,5},{9,6},... | collective-permute-start | bytes 1179656 | tf_op jit(solution)/shard_map/ppermute | solution.py:172
  16.7 46.5 %collective-permute-start.4 = (bf16[384,512]{1,0:T(8,128)(2,1)S(1)}, bf16[384,512]{1,0:T(8,128)(2,1)}, u32[]{:S(2)}, u32[]{:S(2)}) collective-permute-start(bf16[384,512]{1,0:T(8,128)(2,1)S(1)} %bitcast.59), channel_id=1, source_target_pairs={{0,4},{1,5},{2,12},{3,13},{4,20},{5,21},{6,28},{7,29},{8,6},{9,7},... | collective-permute-start | bytes 1179656 | tf_op jit(solution)/shard_map/ppermute | solution.py:172
  20.3 55.0 %collective-permute-start.5 = (bf16[384,512]{1,0:T(8,128)(2,1)S(1)}, bf16[384,512]{1,0:T(8,128)(2,1)S(1)}, u32[]{:S(2)}, u32[]{:S(2)}) collective-permute-start(bf16[384,512]{1,0:T(8,128)(2,1)S(1)} %bitcast.58), channel_id=1, source_target_pairs={{0,5},{1,6},{2,13},{3,14},{4,21},{5,22},{6,29},{7,30},{8,7},{9,0},... | collective-permute-start | bytes 1179656 | tf_op jit(solution)/shard_map/ppermute | solution.py:172
  50.9 32.8 %collective-permute-start.6 = (bf16[384,512]{1,0:T(8,128)(2,1)S(1)}, bf16[384,512]{1,0:T(8,128)(2,1)S(1)}, u32[]{:S(2)}, u32[]{:S(2)}) collective-permute-start(bf16[384,512]{1,0:T(8,128)(2,1)S(1)} %bitcast.57), channel_id=1, source_target_pairs={{0,6},{1,7},{2,14},{3,15},{4,22},{5,23},{6,30},{7,31},{8,0},{9,1},... | collective-permute-start | bytes 1179656 | tf_op jit(solution)/shard_map/ppermute | solution.py:172
  58.8 25.7 %collective-permute-start.7 = (bf16[384,512]{1,0:T(8,128)(2,1)S(1)}, bf16[384,512]{1,0:T(8,128)(2,1)S(1)}, u32[]{:S(2)}, u32[]{:S(2)}) collective-permute-start(bf16[384,512]{1,0:T(8,128)(2,1)S(1)} %bitcast.56), channel_id=1, source_target_pairs={{0,7},{1,0},{2,15},{3,8},{4,23},{5,16},{6,31},{7,24},{8,1},{9,2},{... | collective-permute-start | bytes 1179656 | tf_op jit(solution)/shard_map/ppermute | solution.py:172
  88.5 20.6 %collective-permute-start.8 = (bf16[64,24,128]{2,1,0:T(8,128)(2,1)S(1)}, bf16[64,24,128]{2,1,0:T(8,128)(2,1)S(1)}, u32[]{:S(2)}, u32[]{:S(2)}) collective-permute-start(bf16[64,24,128]{2,1,0:T(8,128)(2,1)S(1)} %get-tuple-element.3), channel_id=1, source_target_pairs={{8,0},{16,8},{24,16},{9,1},{17,9},{25,17},{10,2},{18,10},{26,18},{... | collective-permute-start | bytes 1179656 | tf_op jit(solution)/shard_map/ppermute | solution.py:182
  100.0 17.2 %collective-permute-start.9 = (bf16[64,24,128]{2,1,0:T(8,128)(2,1)S(1)}, bf16[64,24,128]{2,1,0:T(8,128)(2,1)S(1)}, u32[]{:S(2)}, u32[]{:S(2)}) collective-permute-start(bf16[64,24,128]{2,1,0:T(8,128)(2,1)S(1)} %get-tuple-element.2), channel_id=1, source_target_pairs={{0,8},{8,16},{16,24},{1,9},{9,17},{17,25},{2,10},{10,18},{18,26},{... | collective-permute-start | bytes 1179656 | tf_op jit(solution)/shard_map/ppermute | solution.py:181

commit v18 on v17

--- a/solution.py
+++ b/solution.py
@@ -9,7 +9,7 @@
 
 RADIUS = 4
 LANES = 128
-PAIRS_PER_STEP = 4
+PAIRS_PER_STEP = 8
 FIELDS = 4
 
 

time: 135 us -> 135 us (level)
  no operation moved by 1% of the time
where the time goes in v18:
time: 135 us; the launch traced here: 134 us
  starting transfers between devices  60.4 us (45%)
  waiting for transfers between devices  27.6 us (20%)
  local copies, waits for them, and re-layouts  26 us (19%)
  Pallas kernels  15.6 us (12%)
  other arithmetic  2.01 us (1%)
  matrix products  1.64 us (1%)
    ppermute x8, starting transfers between devices, shards(): received.append(lax.ppermute(chunk, ('tx', 'ty'), pairs))  46.7 us
    ppermute x8, waiting for transfers between devices, shards(): received.append(lax.ppermute(chunk, ('tx', 'ty'), pairs))  18 us
    pallas_call x1, Pallas kernels, pair_maps(): pl.pallas_call(kernel, grid_spec=grid_spec, out_shape=[out_shape, out_sha...  15.6 us
    ppermute x1, starting transfers between devices, shards(): right = lax.ppermute(x[0, :, :, :LANES], 'tx', backward)  11.6 us
    unnamed x11, local copies, waits for them, and re-layouts  10.4 us
    ppermute x1, waiting for transfers between devices, shards(): lax.ppermute(x[blocks_per_tile - 1, :, :, local_cols - LANES:], 'tx', for...  8.27 us
    dynamic_slice x1, local copies, waits for them, and re-layouts, shards(): chunk = lax.dynamic_slice_in_dim(x, first, padded_rows, axis=2)  5.06 us
    convert_element_type x1, local copies, waits for them, and re-layouts, shards(): main.astype(jnp.bfloat16)  3.4 us
  transfers between devices with their start and end apart: 10, of which 4 were waited for; matrix products, arithmetic and copies ran while one was open for 14% of the time, Pallas kernels for 0%

profile of v18, /device:TPU:21, one launch (start us, length us, event | category | flops | bytes accessed | tf_op | source)
XLA Modules:
  0.0 134.2 jit_solution(6064232188736070352)
XLA Ops:
  0.8 5.1 %pad_dynamic-slice_fusion = (bf16[8,2,24,512]{3,2,1,0:T(8,128)(2,1)S(1)}, bf16[8,2,24,512]{3,2,1,0:T(8,128)(2,1)S(1)}, bf16[8,2,24,512]{3,2,1,0:T(8,128)(2,1)S(1...) fusion(s32[]{:T(128)S(6)} %select_n.146, ...), kind=kLoop, calls=%fused_computation.7 | loop fusion | bytes 5242912 | tf_op jit(solution)/shard_map/dynamic_slice | solution.py:170
  5.8 4.5 %collective-permute-start = (bf16[384,512]{1,0:T(8,128)(2,1)}, bf16[384,512]{1,0:T(8,128)(2,1)}, u32[]{:S(2)}, u32[]{:S(2)}) collective-permute-start(bf16[384,512]{1,0:T(8,128)(2,1)} %bitcast), channel_id=1, source_target_pairs={{0,0},{1,1},{2,8},{3,9},{4,16},{5,17},{6,24},{7,25},{8,2},{9,3},{1... | collective-permute-start | bytes 1179656 | tf_op jit(solution)/shard_map/ppermute | solution.py:172
  10.3 0.7 collective-permute-start.1
  11.0 2.3 %collective-permute-start.2 = (bf16[384,512]{1,0:T(8,128)(2,1)S(1)}, bf16[384,512]{1,0:T(8,128)(2,1)}, u32[]{:S(2)}, u32[]{:S(2)}) collective-permute-start(bf16[384,512]{1,0:T(8,128)(2,1)S(1)} %bitcast.61), channel_id=1, source_target_pairs={{0,2},{1,3},{2,10},{3,11},{4,18},{5,19},{6,26},{7,27},{8,4},{9,5},... | collective-permute-start | bytes 1179656 | tf_op jit(solution)/shard_map/ppermute | solution.py:172
  13.4 3.4 %collective-permute-start.3 = (bf16[384,512]{1,0:T(8,128)(2,1)S(1)}, bf16[384,512]{1,0:T(8,128)(2,1)}, u32[]{:S(2)}, u32[]{:S(2)}) collective-permute-start(bf16[384,512]{1,0:T(8,128)(2,1)S(1)} %bitcast.60), channel_id=1, source_target_pairs={{0,3},{1,4},{2,11},{3,12},{4,19},{5,20},{6,27},{7,28},{8,5},{9,6},... | collective-permute-start | bytes 1179656 | tf_op jit(solution)/shard_map/ppermute | solution.py:172
  17.1 0.5 copy.10
  17.6 0.8 reshape.168
  18.4 0.8 reshape.167
  19.6 0.7 pad_maximum_fusion.band_ref
  20.3 28.9 %collective-permute-start.5 = (bf16[384,512]{1,0:T(8,128)(2,1)S(1)}, bf16[384,512]{1,0:T(8,128)(2,1)S(1)}, u32[]{:S(2)}, u32[]{:S(2)}) collective-permute-start(bf16[384,512]{1,0:T(8,128)(2,1)S(1)} %bitcast.58), channel_id=1, source_target_pairs={{0,5},{1,6},{2,13},{3,14},{4,21},{5,22},{6,29},{7,30},{8,7},{9,0},... | collective-permute-start | bytes 1179656 | tf_op jit(solution)/shard_map/ppermute | solution.py:172
  49.1 1.8 %bitcast_dynamic-update-slice_fusion.7 = bf16[8,384,512]{2,1,0:T(8,128)(2,1)} fusion(bf16[384,512]{1,0:T(8,128)(2,1)} %collective-permute-done), kind=kLoop, calls=%fused_computation.24 | loop fusion | bytes 786432
  50.9 6.1 %collective-permute-start.6 = (bf16[384,512]{1,0:T(8,128)(2,1)S(1)}, bf16[384,512]{1,0:T(8,128)(2,1)S(1)}, u32[]{:S(2)}, u32[]{:S(2)}) collective-permute-start(bf16[384,512]{1,0:T(8,128)(2,1)S(1)} %bitcast.57), channel_id=1, source_target_pairs={{0,6},{1,7},{2,14},{3,15},{4,22},{5,23},{6,30},{7,31},{8,0},{9,1},... | collective-permute-start | bytes 1179656 | tf_op jit(solution)/shard_map/ppermute | solution.py:172
  57.0 1.8 %bitcast_dynamic-update-slice_fusion.6 = bf16[8,384,512]{2,1,0:T(8,128)(2,1)} fusion(bf16[8,384,512]{2,1,0:T(8,128)(2,1)} %bitcast_dynamic-update-slice_fusion.7, bf16[384,512]{1,0:T(8,128)(2,1)} %collective-permute-done.1), kind=kLoop, calls=%fused_computation.23 | loop fusion | bytes 786432
  58.8 0.9 collective-permute-start.7
  59.6 1.8 %bitcast_dynamic-update-slice_fusion.5 = bf16[8,384,512]{2,1,0:T(8,128)(2,1)} fusion(bf16[8,384,512]{2,1,0:T(8,128)(2,1)} %bitcast_dynamic-update-slice_fusion.6, bf16[384,512]{1,0:T(8,128)(2,1)} %collective-permute-done.2), kind=kLoop, calls=%fused_computation.22 | loop fusion | bytes 786432
  61.4 1.8 %bitcast_dynamic-update-slice_fusion.4 = bf16[8,384,512]{2,1,0:T(8,128)(2,1)} fusion(bf16[8,384,512]{2,1,0:T(8,128)(2,1)} %bitcast_dynamic-update-slice_fusion.5, bf16[384,512]{1,0:T(8,128)(2,1)} %collective-permute-done.3), kind=kLoop, calls=%fused_computation.21 | loop fusion | bytes 786432
  63.2 1.8 %bitcast_dynamic-update-slice_fusion.3 = bf16[8,384,512]{2,1,0:T(8,128)(2,1)} fusion(bf16[8,384,512]{2,1,0:T(8,128)(2,1)} %bitcast_dynamic-update-slice_fusion.4, bf16[384,512]{1,0:T(8,128)(2,1)} %collective-permute-done.4), kind=kLoop, calls=%fused_computation.20 | loop fusion | bytes 786432
  65.0 10.3 %collective-permute-done.5 = bf16[384,512]{1,0:T(8,128)(2,1)S(1)} collective-permute-done((bf16[384,512]{1,0:T(8,128)(2,1)S(1)}, bf16[384,512]{1,0:T(8,128)(2,1)S(1)}, u32[]{:S(2)}, u32[]{:S(2)}) %collective-permute-start.5) | collective-permute-done | bytes 393248 | tf_op jit(solution)/shard_map/ppermute | solution.py:172
  75.3 0.8 bitcast_dynamic-update-slice_fusion.2
  76.1 7.7 %collective-permute-done.6 = bf16[384,512]{1,0:T(8,128)(2,1)S(1)} collective-permute-done((bf16[384,512]{1,0:T(8,128)(2,1)S(1)}, bf16[384,512]{1,0:T(8,128)(2,1)S(1)}, u32[]{:S(2)}, u32[]{:S(2)}) %collective-permute-start.6) | collective-permute-done | bytes 393248 | tf_op jit(solution)/shard_map/ppermute | solution.py:172
  83.7 0.8 bitcast_dynamic-update-slice_fusion.1
  84.5 0.8 bitcast_dynamic-update-slice_fusion
  85.3 2.6 %gather_fusion = bf16[8,384,512]{2,1,0:T(8,128)(2,1)S(1)} fusion(bf16[8,384,512]{2,1,0:T(8,128)(2,1)} %bitcast_dynamic-update-slice_fusion, s32[1024]{0:T(1024)S(1)} %pad_clamp_fusion), kind=kCustom, calls=%fused_computation | custom fusion | bytes 6291488 | tf_op jit(solution)/shard_map/jit(_take)/gather | solution.py:176
  88.5 11.6 %collective-permute-start.8 = (bf16[64,24,128]{2,1,0:T(8,128)(2,1)S(1)}, bf16[64,24,128]{2,1,0:T(8,128)(2,1)S(1)}, u32[]{:S(2)}, u32[]{:S(2)}) collective-permute-start(bf16[64,24,128]{2,1,0:T(8,128)(2,1)S(1)} %get-tuple-element.3), channel_id=1, source_target_pairs={{8,0},{16,8},{24,16},{9,1},{17,9},{25,17},{10,2},{18,10},{26,18},{... | collective-permute-start | bytes 1179656 | tf_op jit(solution)/shard_map/ppermute | solution.py:182
  100.0 2.1 %collective-permute-start.9 = (bf16[64,24,128]{2,1,0:T(8,128)(2,1)S(1)}, bf16[64,24,128]{2,1,0:T(8,128)(2,1)S(1)}, u32[]{:S(2)}, u32[]{:S(2)}) collective-permute-start(bf16[64,24,128]{2,1,0:T(8,128)(2,1)S(1)} %get-tuple-element.2), channel_id=1, source_target_pairs={{0,8},{8,16},{16,24},{1,9},{9,17},{17,25},{2,10},{10,18},{18,26},{... | collective-permute-start | bytes 1179656 | tf_op jit(solution)/shard_map/ppermute | solution.py:181
  102.1 0.7 broadcast_select_fusion.1
  102.9 1.4 %convert_bitcast_fusion = bf16[2,64,24,512]{3,1,2,0:T(8,128)(2,1)S(1)} fusion(bf16[2,64,24,512]{3,2,1,0:T(8,128)(2,1)S(1)} %bitcast.54, bf16[64,64,1,1]{1,0,2,3:T(8,128)(2,1)S(1)} %reshape.167), kind=kOutput, calls=%fused_computation.3 | convolution fusion | flops 202899456 | bytes 6299648 | tf_op jit(solution)/shard_map/kc,bchw->bkhw/dot_general | solution.py:189
  104.2 3.4 %copy.12 = bf16[2,64,24,512]{3,2,1,0:T(8,128)(2,1)} copy(bf16[2,64,24,512]{3,1,2,0:T(8,128)(2,1)S(1)} %convert_bitcast_fusion) | data formatting | bytes 6291456 | tf_op jit(solution)/shard_map/convert_element_type | solution.py:190
  107.6 1.4 %collective-permute-done.8 = bf16[64,24,128]{2,1,0:T(8,128)(2,1)S(1)} collective-permute-done((bf16[64,24,128]{2,1,0:T(8,128)(2,1)S(1)}, bf16[64,24,128]{2,1,0:T(8,128)(2,1)S(1)}, u32[]{:S(2)}, u32[]{:S(2)}) %collective-permute-start.8) | collective-permute-done | bytes 393248 | tf_op jit(solution)/shard_map/ppermute | solution.py:182
  109.0 8.3 %collective-permute-done.9 = bf16[64,24,128]{2,1,0:T(8,128)(2,1)S(1)} collective-permute-done((bf16[64,24,128]{2,1,0:T(8,128)(2,1)S(1)}, bf16[64,24,128]{2,1,0:T(8,128)(2,1)S(1)}, u32[]{:S(2)}, u32[]{:S(2)}) %collective-permute-start.9) | collective-permute-done | bytes 393248 | tf_op jit(solution)/shard_map/ppermute | solution.py:181
  117.6 1.0 copy.14
  118.6 15.6 %shard_map.68 = (f32[32,16,1024]{2,1,0:T(8,128)}, f32[32,16,1024]{2,1,0:T(8,128)}) custom-call(s32[32]{0:T(128)} %pre_ref.1, s32[32]{0:T(128)} %post_ref.1, bf16[2,32,2,24,512]{4,3,2,1,0:T(8,128)(2,1)} %bitcast.53, bf16[32,2,24,128]{3,2,1,0:T(8,128)(2,1)} %bitcast.55, bf16[768,128]{1,0:T(8,128)(2,1)} %pad_maximum_fusion.band_ref), custom_call_target="tpu_custom_call" | custom-call | tf_op jit(solution)/shard_map/pallas_call | solution.py:141
  (31 shorter events, 1.5 us)
Async XLA Ops:
  0.6 16.3 %copy-start = (bf16[32,32]{1,0:T(8,128)(2,1)S(1)}, bf16[32,32]{1,0:T(8,128)(2,1)}, u32[]{:S(2)}) copy-start(bf16[32,32]{1,0:T(8,128)(2,1)} %param.7) | copy-start | bytes 6148
  0.6 16.4 %copy-start.1 = (bf16[32,32]{1,0:T(8,128)(2,1)S(1)}, bf16[32,32]{1,0:T(8,128)(2,1)}, u32[]{:S(2)}) copy-start(bf16[32,32]{1,0:T(8,128)(2,1)} %param.6) | copy-start | bytes 6148
  5.8 14.4 %collective-permute-start = (bf16[384,512]{1,0:T(8,128)(2,1)}, bf16[384,512]{1,0:T(8,128)(2,1)}, u32[]{:S(2)}, u32[]{:S(2)}) collective-permute-start(bf16[384,512]{1,0:T(8,128)(2,1)} %bitcast), channel_id=1, source_target_pairs={{0,0},{1,1},{2,8},{3,9},{4,16},{5,17},{6,24},{7,25},{8,2},{9,3},{1... | collective-permute-start | bytes 1179656 | tf_op jit(solution)/shard_map/ppermute | solution.py:172
  10.3 40.6 %collective-permute-start.1 = (bf16[384,512]{1,0:T(8,128)(2,1)S(1)}, bf16[384,512]{1,0:T(8,128)(2,1)}, u32[]{:S(2)}, u32[]{:S(2)}) collective-permute-start(bf16[384,512]{1,0:T(8,128)(2,1)S(1)} %bitcast.62), channel_id=1, source_target_pairs={{0,1},{1,2},{2,9},{3,10},{4,17},{5,18},{6,25},{7,26},{8,3},{9,4},{... | collective-permute-start | bytes 1179656 | tf_op jit(solution)/shard_map/ppermute | solution.py:172
  11.0 47.7 %collective-permute-start.2 = (bf16[384,512]{1,0:T(8,128)(2,1)S(1)}, bf16[384,512]{1,0:T(8,128)(2,1)}, u32[]{:S(2)}, u32[]{:S(2)}) collective-permute-start(bf16[384,512]{1,0:T(8,128)(2,1)S(1)} %bitcast.61), channel_id=1, source_target_pairs={{0,2},{1,3},{2,10},{3,11},{4,18},{5,19},{6,26},{7,27},{8,4},{9,5},... | collective-permute-start | bytes 1179656 | tf_op jit(solution)/shard_map/ppermute | solution.py:172
  13.4 48.0 %collective-permute-start.3 = (bf16[384,512]{1,0:T(8,128)(2,1)S(1)}, bf16[384,512]{1,0:T(8,128)(2,1)}, u32[]{:S(2)}, u32[]{:S(2)}) collective-permute-start(bf16[384,512]{1,0:T(8,128)(2,1)S(1)} %bitcast.60), channel_id=1, source_target_pairs={{0,3},{1,4},{2,11},{3,12},{4,19},{5,20},{6,27},{7,28},{8,5},{9,6},... | collective-permute-start | bytes 1179656 | tf_op jit(solution)/shard_map/ppermute | solution.py:172
  16.7 46.5 %collective-permute-start.4 = (bf16[384,512]{1,0:T(8,128)(2,1)S(1)}, bf16[384,512]{1,0:T(8,128)(2,1)}, u32[]{:S(2)}, u32[]{:S(2)}) collective-permute-start(bf16[384,512]{1,0:T(8,128)(2,1)S(1)} %bitcast.59), channel_id=1, source_target_pairs={{0,4},{1,5},{2,12},{3,13},{4,20},{5,21},{6,28},{7,29},{8,6},{9,7},... | collective-permute-start | bytes 1179656 | tf_op jit(solution)/shard_map/ppermute | solution.py:172
  20.3 55.0 %collective-permute-start.5 = (bf16[384,512]{1,0:T(8,128)(2,1)S(1)}, bf16[384,512]{1,0:T(8,128)(2,1)S(1)}, u32[]{:S(2)}, u32[]{:S(2)}) collective-permute-start(bf16[384,512]{1,0:T(8,128)(2,1)S(1)} %bitcast.58), channel_id=1, source_target_pairs={{0,5},{1,6},{2,13},{3,14},{4,21},{5,22},{6,29},{7,30},{8,7},{9,0},... | collective-permute-start | bytes 1179656 | tf_op jit(solution)/shard_map/ppermute | solution.py:172
  50.9 32.8 %collective-permute-start.6 = (bf16[384,512]{1,0:T(8,128)(2,1)S(1)}, bf16[384,512]{1,0:T(8,128)(2,1)S(1)}, u32[]{:S(2)}, u32[]{:S(2)}) collective-permute-start(bf16[384,512]{1,0:T(8,128)(2,1)S(1)} %bitcast.57), channel_id=1, source_target_pairs={{0,6},{1,7},{2,14},{3,15},{4,22},{5,23},{6,30},{7,31},{8,0},{9,1},... | collective-permute-start | bytes 1179656 | tf_op jit(solution)/shard_map/ppermute | solution.py:172
  58.8 25.7 %collective-permute-start.7 = (bf16[384,512]{1,0:T(8,128)(2,1)S(1)}, bf16[384,512]{1,0:T(8,128)(2,1)S(1)}, u32[]{:S(2)}, u32[]{:S(2)}) collective-permute-start(bf16[384,512]{1,0:T(8,128)(2,1)S(1)} %bitcast.56), channel_id=1, source_target_pairs={{0,7},{1,0},{2,15},{3,8},{4,23},{5,16},{6,31},{7,24},{8,1},{9,2},{... | collective-permute-start | bytes 1179656 | tf_op jit(solution)/shard_map/ppermute | solution.py:172
  88.5 20.6 %collective-permute-start.8 = (bf16[64,24,128]{2,1,0:T(8,128)(2,1)S(1)}, bf16[64,24,128]{2,1,0:T(8,128)(2,1)S(1)}, u32[]{:S(2)}, u32[]{:S(2)}) collective-permute-start(bf16[64,24,128]{2,1,0:T(8,128)(2,1)S(1)} %get-tuple-element.3), channel_id=1, source_target_pairs={{8,0},{16,8},{24,16},{9,1},{17,9},{25,17},{10,2},{18,10},{26,18},{... | collective-permute-start | bytes 1179656 | tf_op jit(solution)/shard_map/ppermute | solution.py:182
  100.0 17.2 %collective-permute-start.9 = (bf16[64,24,128]{2,1,0:T(8,128)(2,1)S(1)}, bf16[64,24,128]{2,1,0:T(8,128)(2,1)S(1)}, u32[]{:S(2)}, u32[]{:S(2)}) collective-permute-start(bf16[64,24,128]{2,1,0:T(8,128)(2,1)S(1)} %get-tuple-element.2), channel_id=1, source_target_pairs={{0,8},{8,16},{16,24},{1,9},{9,17},{17,25},{2,10},{10,18},{18,26},{... | collective-permute-start | bytes 1179656 | tf_op jit(solution)/shard_map/ppermute | solution.py:181

commit v19 on v18

--- a/solution.py
+++ b/solution.py
@@ -157,7 +157,6 @@
 
     me_col = lax.axis_index("tx")
     me_row = lax.axis_index("ty")
-    x = jnp.pad(stack, ((0, 0), (0, 0), (RADIUS, RADIUS), (0, 0)))
     start = me_col * blocks_per_tile + me_row % blocks_per_tile
     received = []
     for m in range(n_rows):
@@ -166,8 +165,16 @@
             for row in range(n_rows):
                 to_row = (m + col * blocks_per_tile + row % blocks_per_tile) % n_rows
                 pairs.append((col * n_rows + row, (row // blocks_per_tile) * n_rows + to_row))
-        first = ((start + m) % n_rows) * tile_rows
-        chunk = lax.dynamic_slice_in_dim(x, first, padded_rows, axis=2)
+        block = (start + m) % n_rows
+        first = block * tile_rows
+        top = lax.dynamic_slice_in_dim(stack, jnp.maximum(first - RADIUS, 0), RADIUS, axis=2)
+        top = jnp.where(block > 0, top, jnp.zeros_like(top))
+        bottom = lax.dynamic_slice_in_dim(
+            stack, jnp.minimum(first + tile_rows, height - RADIUS), RADIUS, axis=2
+        )
+        bottom = jnp.where(block < n_rows - 1, bottom, jnp.zeros_like(bottom))
+        middle = lax.dynamic_slice_in_dim(stack, first, tile_rows, axis=2)
+        chunk = jnp.concatenate([top, middle, bottom], axis=2)
         chunk = chunk.reshape(local_acq * 2 * padded_rows, local_cols)
         received.append(lax.ppermute(chunk, ("tx", "ty"), pairs))
     received = jnp.stack(received, axis=0)

time: 135 us -> 140 us (1.037)
  other arithmetic: 2.01 us -> 13.1 us
  local copies, waits for them, and re-layouts: 26 us -> 23.3 us
  waiting for transfers between devices: 27.6 us -> 25.2 us
    concatenate x0 -> x8, other arithmetic: none -> 7.09 us  [shards(): chunk = jnp.concatenate([top, middle, bottom], axis=2)]
    ppermute x1, starting transfers between devices: 11.6 us -> 7.32 us  [shards(): right = lax.ppermute(x[0, :, :, :LANES], 'tx', backward)]
    ppermute x8, starting transfers between devices: 46.7 us -> 49.8 us  [shards(): received.append(lax.ppermute(chunk, ('tx', 'ty'), pairs))]
    unnamed x11 -> x25, local copies, waits for them, and re-layouts: 10.4 us -> 7.51 us
    dynamic_slice x1, local copies, waits for them, and re-layouts: 5.06 us -> 2.57 us  [shards(): middle = lax.dynamic_slice_in_dim(stack, first, tile_rows, axis=2)]
    ppermute x1, waiting for transfers between devices: 8.27 us -> 6.07 us  [shards(): lax.ppermute(x[blocks_per_tile - 1, :, :, local_cols - LANES:], 'tx', for...]
    select_n x0 -> x2, other arithmetic: none -> 1.62 us  [the longest x1 1.21 us: shards(): top = jnp.where(block > 0, top, jnp.zeros_like(top))]
  transfers between devices with their start and end apart: 10 -> 10, of which waited for: 4 -> 4; matrix products, arithmetic and copies ran while one was open for 14% -> 20% of each run, Pallas kernels for 0% -> 0%
where the time goes in v19:
time: 140 us; the launch traced here: 139 us
  starting transfers between devices  59.2 us (42%)
  waiting for transfers between devices  25.2 us (18%)
  local copies, waits for them, and re-layouts  23.3 us (17%)
  Pallas kernels  15.6 us (11%)
  other arithmetic  13.1 us (9%)
  matrix products  1.63 us (1%)
    ppermute x8, starting transfers between devices, shards(): received.append(lax.ppermute(chunk, ('tx', 'ty'), pairs))  49.8 us
    ppermute x8, waiting for transfers between devices, shards(): received.append(lax.ppermute(chunk, ('tx', 'ty'), pairs))  17.8 us
    pallas_call x1, Pallas kernels, pair_maps(): pl.pallas_call(kernel, grid_spec=grid_spec, out_shape=[out_shape, out_sha...  15.6 us
    unnamed x25, local copies, waits for them, and re-layouts  7.51 us
    ppermute x1, starting transfers between devices, shards(): right = lax.ppermute(x[0, :, :, :LANES], 'tx', backward)  7.32 us
    concatenate x8, other arithmetic, shards(): chunk = jnp.concatenate([top, middle, bottom], axis=2)  7.09 us
    ppermute x1, waiting for transfers between devices, shards(): lax.ppermute(x[blocks_per_tile - 1, :, :, local_cols - LANES:], 'tx', for...  6.07 us
    convert_element_type x1, local copies, waits for them, and re-layouts, shards(): main.astype(jnp.bfloat16)  3.39 us
  transfers between devices with their start and end apart: 10, of which 4 were waited for; matrix products, arithmetic and copies ran while one was open for 20% of the time, Pallas kernels for 0%

profile of v19, /device:TPU:21, one launch (start us, length us, event | category | flops | bytes accessed | tf_op | source)
XLA Modules:
  0.0 139.1 jit_solution(14207423024577083811)
XLA Ops:
  0.8 2.6 %constant_dynamic-slice_fusion = (bf16[8,2,16,512]{3,2,1,0:T(8,128)(2,1)S(1)}, bf16[8,2,16,512]{3,2,1,0:T(8,128)(2,1)S(1)}, bf16[8,2,16,512]{3,2,1,0:T(8,128)(2,...) fusion(bf16[8,2,128,512]{3,2,1,0:T(8,128)(2,1)} %param.5, ...), kind=kLoop, calls=%fused_computation.54 | loop fusion | bytes 4194336 | tf_op jit(solution)/shard_map/dynamic_slice | solution.py:176
  3.4 1.2 dynamic-slice_select_fusion.1
  4.6 0.9 pad_maximum_fusion.4
  5.6 0.9 pad_maximum_fusion.3
  7.5 1.9 %pad_maximum_fusion = bf16[8,2,24,512]{3,2,1,0:T(8,128)(2,1)} fusion(bf16[8,2,4,512]{3,2,1,0:T(4,128)(2,1)S(1)} %get-tuple-element.26, bf16[8,2,16,512]{3,2,1,0:T(8,128)(2,1)} %get-tuple-element.20, bf16[8,2,4,512]{3,2,1,0:T(4,128)(2,1)S(1)} %get-tuple-element.27), kind=kLoop, calls=%fused_computation.9 | loop fusion | flops 1179648 | bytes 786432 | tf_op jit(solution)/shard_map/concatenate | solution.py:177
  9.4 1.6 %collective-permute-start = (bf16[384,512]{1,0:T(8,128)(2,1)}, bf16[384,512]{1,0:T(8,128)(2,1)S(1)}, u32[]{:S(2)}, u32[]{:S(2)}) collective-permute-start(bf16[384,512]{1,0:T(8,128)(2,1)} %bitcast), channel_id=1, source_target_pairs={{0,0},{1,1},{2,8},{3,9},{4,16},{5,17},{6,24},{7,25},{8,2},{9,3},{1... | collective-permute-start | bytes 1179656 | tf_op jit(solution)/shard_map/ppermute | solution.py:179
  11.0 0.9 pad_maximum_fusion.1
  12.0 3.3 %collective-permute-start.1 = (bf16[384,512]{1,0:T(8,128)(2,1)}, bf16[384,512]{1,0:T(8,128)(2,1)S(1)}, u32[]{:S(2)}, u32[]{:S(2)}) collective-permute-start(bf16[384,512]{1,0:T(8,128)(2,1)} %bitcast.2), channel_id=1, source_target_pairs={{0,1},{1,2},{2,9},{3,10},{4,17},{5,18},{6,25},{7,26},{8,3},{9,4},{... | collective-permute-start | bytes 1179656 | tf_op jit(solution)/shard_map/ppermute | solution.py:179
  15.4 0.8 collective-permute-start.2
  18.5 1.0 pad_maximum_fusion.5
  20.1 1.0 pad_maximum_fusion.6
  21.7 1.2 copy.10
  23.0 1.4 %reshape.168 = bf16[64,64,1]{1,0,2:T(8,128)(2,1)} reshape(bf16[32,2,32,2]{3,2,1,0:T(8,128)(2,1)S(1)} %copy.10) | data formatting | bytes 16384 | tf_op jit(solution)/shard_map/reshape | solution.py:195
  24.4 0.8 reshape.167
  27.0 35.4 %collective-permute-start.5 = (bf16[384,512]{1,0:T(8,128)(2,1)S(1)}, bf16[384,512]{1,0:T(8,128)(2,1)S(1)}, u32[]{:S(2)}, u32[]{:S(2)}) collective-permute-start(bf16[384,512]{1,0:T(8,128)(2,1)S(1)} %bitcast.58), channel_id=1, source_target_pairs={{0,5},{1,6},{2,13},{3,14},{4,21},{5,22},{6,29},{7,30},{8,7},{9,0},... | collective-permute-start | bytes 1179656 | tf_op jit(solution)/shard_map/ppermute | solution.py:179
  63.2 0.8 collective-permute-start.6
  64.8 7.2 %collective-permute-start.7 = (bf16[384,512]{1,0:T(8,128)(2,1)S(1)}, bf16[384,512]{1,0:T(8,128)(2,1)S(1)}, u32[]{:S(2)}, u32[]{:S(2)}) collective-permute-start(bf16[384,512]{1,0:T(8,128)(2,1)S(1)} %bitcast.59), channel_id=1, source_target_pairs={{0,7},{1,0},{2,15},{3,8},{4,23},{5,16},{6,31},{7,24},{8,1},{9,2},{... | collective-permute-start | bytes 1179656 | tf_op jit(solution)/shard_map/ppermute | solution.py:179
  72.0 0.8 bitcast_dynamic-update-slice_fusion.5
  72.8 1.8 %bitcast_dynamic-update-slice_fusion.4 = bf16[8,384,512]{2,1,0:T(8,128)(2,1)} fusion(bf16[8,384,512]{2,1,0:T(8,128)(2,1)} %bitcast_dynamic-update-slice_fusion.5, bf16[384,512]{1,0:T(8,128)(2,1)} %collective-permute-done.3), kind=kLoop, calls=%fused_computation.21 | loop fusion | bytes 786432
  74.6 1.8 %bitcast_dynamic-update-slice_fusion.3 = bf16[8,384,512]{2,1,0:T(8,128)(2,1)} fusion(bf16[8,384,512]{2,1,0:T(8,128)(2,1)} %bitcast_dynamic-update-slice_fusion.4, bf16[384,512]{1,0:T(8,128)(2,1)} %collective-permute-done.4), kind=kLoop, calls=%fused_computation.20 | loop fusion | bytes 786432
  76.4 10.1 %collective-permute-done.5 = bf16[384,512]{1,0:T(8,128)(2,1)S(1)} collective-permute-done((bf16[384,512]{1,0:T(8,128)(2,1)S(1)}, bf16[384,512]{1,0:T(8,128)(2,1)S(1)}, u32[]{:S(2)}, u32[]{:S(2)}) %collective-permute-start.5) | collective-permute-done | bytes 393248 | tf_op jit(solution)/shard_map/ppermute | solution.py:179
  87.2 7.7 %collective-permute-done.6 = bf16[384,512]{1,0:T(8,128)(2,1)S(1)} collective-permute-done((bf16[384,512]{1,0:T(8,128)(2,1)S(1)}, bf16[384,512]{1,0:T(8,128)(2,1)S(1)}, u32[]{:S(2)}, u32[]{:S(2)}) %collective-permute-start.6) | collective-permute-done | bytes 393248 | tf_op jit(solution)/shard_map/ppermute | solution.py:179
  94.9 0.8 bitcast_dynamic-update-slice_fusion.1
  96.5 2.8 %gather_fusion = bf16[8,384,512]{2,1,0:T(8,128)(2,1)S(1)} fusion(bf16[8,384,512]{2,1,0:T(8,128)(2,1)} %bitcast_dynamic-update-slice_fusion, s32[1024]{0:T(1024)} %pad_clamp_fusion), kind=kCustom, calls=%fused_computation | custom fusion | bytes 6291488 | tf_op jit(solution)/shard_map/jit(_take)/gather | solution.py:183
  99.8 7.3 %collective-permute-start.8 = (bf16[64,24,128]{2,1,0:T(8,128)(2,1)S(1)}, bf16[64,24,128]{2,1,0:T(8,128)(2,1)S(1)}, u32[]{:S(2)}, u32[]{:S(2)}) collective-permute-start(bf16[64,24,128]{2,1,0:T(8,128)(2,1)S(1)} %get-tuple-element.3), channel_id=1, source_target_pairs={{8,0},{16,8},{24,16},{9,1},{17,9},{25,17},{10,2},{18,10},{26,18},{... | collective-permute-start | bytes 1179656 | tf_op jit(solution)/shard_map/ppermute | solution.py:189
  107.1 2.1 %collective-permute-start.9 = (bf16[64,24,128]{2,1,0:T(8,128)(2,1)S(1)}, bf16[64,24,128]{2,1,0:T(8,128)(2,1)S(1)}, u32[]{:S(2)}, u32[]{:S(2)}) collective-permute-start(bf16[64,24,128]{2,1,0:T(8,128)(2,1)S(1)} %get-tuple-element.2), channel_id=1, source_target_pairs={{0,8},{8,16},{16,24},{1,9},{9,17},{17,25},{2,10},{10,18},{18,26},{... | collective-permute-start | bytes 1179656 | tf_op jit(solution)/shard_map/ppermute | solution.py:188
  110.0 1.4 convert_bitcast_fusion
  111.4 3.4 %copy.12 = bf16[2,64,24,512]{3,2,1,0:T(8,128)(2,1)} copy(bf16[2,64,24,512]{3,1,2,0:T(8,128)(2,1)S(1)} %convert_bitcast_fusion) | data formatting | bytes 6291456 | tf_op jit(solution)/shard_map/convert_element_type | solution.py:197
  114.8 1.3 collective-permute-done.8
  116.1 6.1 %collective-permute-done.9 = bf16[64,24,128]{2,1,0:T(8,128)(2,1)S(1)} collective-permute-done((bf16[64,24,128]{2,1,0:T(8,128)(2,1)S(1)}, bf16[64,24,128]{2,1,0:T(8,128)(2,1)S(1)}, u32[]{:S(2)}, u32[]{:S(2)}) %collective-permute-start.9) | collective-permute-done | bytes 393248 | tf_op jit(solution)/shard_map/ppermute | solution.py:188
  122.5 1.0 copy.14
  123.5 15.6 %shard_map.68 = (f32[32,16,1024]{2,1,0:T(8,128)}, f32[32,16,1024]{2,1,0:T(8,128)}) custom-call(s32[32]{0:T(128)} %pre_ref.1, s32[32]{0:T(128)} %post_ref.1, bf16[2,32,2,24,512]{4,3,2,1,0:T(8,128)(2,1)} %bitcast.53, bf16[32,2,24,128]{3,2,1,0:T(8,128)(2,1)} %bitcast.55, bf16[768,128]{1,0:T(8,128)(2,1)} %pad_maximum_fusion.8.band_ref), custom_call_target="tpu_custom_call" | custom-call | tf_op jit(solution)/shard_map/pallas_call | solution.py:141
  (55 shorter events, 11.0 us)
Async XLA Ops:
  0.6 2.8 %copy-start = (bf16[8,2,128,512]{3,2,1,0:T(8,128)(2,1)S(1)}, bf16[8,2,128,512]{3,2,1,0:T(8,128)(2,1)}, u32[]{:S(2)}) copy-start(bf16[8,2,128,512]{3,2,1,0:T(8,128)(2,1)} %param.5) | copy-start | bytes 6291460
  3.4 13.6 %copy-start.2 = (bf16[32,32]{1,0:T(8,128)(2,1)S(1)}, bf16[32,32]{1,0:T(8,128)(2,1)}, u32[]{:S(2)}) copy-start(bf16[32,32]{1,0:T(8,128)(2,1)} %param.7) | copy-start | bytes 6148
  3.4 14.4 %copy-start.4 = (bf16[32,32]{1,0:T(8,128)(2,1)S(1)}, bf16[32,32]{1,0:T(8,128)(2,1)}, u32[]{:S(2)}) copy-start(bf16[32,32]{1,0:T(8,128)(2,1)} %param.6) | copy-start | bytes 6148
  5.5 69.0 %collective-permute-start.4 = (bf16[384,512]{1,0:T(8,128)(2,1)}, bf16[384,512]{1,0:T(8,128)(2,1)}, u32[]{:S(2)}, u32[]{:S(2)}) collective-permute-start(bf16[384,512]{1,0:T(8,128)(2,1)} %bitcast.8), channel_id=1, source_target_pairs={{0,4},{1,5},{2,12},{3,13},{4,20},{5,21},{6,28},{7,29},{8,6},{9,7},... | collective-permute-start | bytes 1179656 | tf_op jit(solution)/shard_map/ppermute | solution.py:179
  6.5 66.2 %collective-permute-start.3 = (bf16[384,512]{1,0:T(8,128)(2,1)}, bf16[384,512]{1,0:T(8,128)(2,1)}, u32[]{:S(2)}, u32[]{:S(2)}) collective-permute-start(bf16[384,512]{1,0:T(8,128)(2,1)} %bitcast.6), channel_id=1, source_target_pairs={{0,3},{1,4},{2,11},{3,12},{4,19},{5,20},{6,27},{7,28},{8,5},{9,6},... | collective-permute-start | bytes 1179656 | tf_op jit(solution)/shard_map/ppermute | solution.py:179
  9.4 17.6 %collective-permute-start = (bf16[384,512]{1,0:T(8,128)(2,1)}, bf16[384,512]{1,0:T(8,128)(2,1)S(1)}, u32[]{:S(2)}, u32[]{:S(2)}) collective-permute-start(bf16[384,512]{1,0:T(8,128)(2,1)} %bitcast), channel_id=1, source_target_pairs={{0,0},{1,1},{2,8},{3,9},{4,16},{5,17},{6,24},{7,25},{8,2},{9,3},{1... | collective-permute-start | bytes 1179656 | tf_op jit(solution)/shard_map/ppermute | solution.py:179
  12.0 51.2 %collective-permute-start.1 = (bf16[384,512]{1,0:T(8,128)(2,1)}, bf16[384,512]{1,0:T(8,128)(2,1)S(1)}, u32[]{:S(2)}, u32[]{:S(2)}) collective-permute-start(bf16[384,512]{1,0:T(8,128)(2,1)} %bitcast.2), channel_id=1, source_target_pairs={{0,1},{1,2},{2,9},{3,10},{4,17},{5,18},{6,25},{7,26},{8,3},{9,4},{... | collective-permute-start | bytes 1179656 | tf_op jit(solution)/shard_map/ppermute | solution.py:179
  15.4 49.4 %collective-permute-start.2 = (bf16[384,512]{1,0:T(8,128)(2,1)S(1)}, bf16[384,512]{1,0:T(8,128)(2,1)S(1)}, u32[]{:S(2)}, u32[]{:S(2)}) collective-permute-start(bf16[384,512]{1,0:T(8,128)(2,1)S(1)} %bitcast.56), channel_id=1, source_target_pairs={{0,2},{1,3},{2,10},{3,11},{4,18},{5,19},{6,26},{7,27},{8,4},{9,5},... | collective-permute-start | bytes 1179656 | tf_op jit(solution)/shard_map/ppermute | solution.py:179
  26.1 1.0 copy-start.5
  27.0 59.4 %collective-permute-start.5 = (bf16[384,512]{1,0:T(8,128)(2,1)S(1)}, bf16[384,512]{1,0:T(8,128)(2,1)S(1)}, u32[]{:S(2)}, u32[]{:S(2)}) collective-permute-start(bf16[384,512]{1,0:T(8,128)(2,1)S(1)} %bitcast.58), channel_id=1, source_target_pairs={{0,5},{1,6},{2,13},{3,14},{4,21},{5,22},{6,29},{7,30},{8,7},{9,0},... | collective-permute-start | bytes 1179656 | tf_op jit(solution)/shard_map/ppermute | solution.py:179
  63.2 31.7 %collective-permute-start.6 = (bf16[384,512]{1,0:T(8,128)(2,1)S(1)}, bf16[384,512]{1,0:T(8,128)(2,1)S(1)}, u32[]{:S(2)}, u32[]{:S(2)}) collective-permute-start(bf16[384,512]{1,0:T(8,128)(2,1)S(1)} %bitcast.57), channel_id=1, source_target_pairs={{0,6},{1,7},{2,14},{3,15},{4,22},{5,23},{6,30},{7,31},{8,0},{9,1},... | collective-permute-start | bytes 1179656 | tf_op jit(solution)/shard_map/ppermute | solution.py:179
  64.8 30.9 %collective-permute-start.7 = (bf16[384,512]{1,0:T(8,128)(2,1)S(1)}, bf16[384,512]{1,0:T(8,128)(2,1)S(1)}, u32[]{:S(2)}, u32[]{:S(2)}) collective-permute-start(bf16[384,512]{1,0:T(8,128)(2,1)S(1)} %bitcast.59), channel_id=1, source_target_pairs={{0,7},{1,0},{2,15},{3,8},{4,23},{5,16},{6,31},{7,24},{8,1},{9,2},{... | collective-permute-start | bytes 1179656 | tf_op jit(solution)/shard_map/ppermute | solution.py:179
  96.5 2.8 %copy-start.6 = (pred[2,64]{1,0:T(4,128)(4,1)S(1)}, pred[2,64]{1,0:T(4,128)(4,1)}, u32[]{:S(2)}) copy-start(pred[2,64]{1,0:T(4,128)(4,1)} %copy-done.5) | copy-start | bytes 388
  99.3 10.0 %copy-start.3 = (pred[8,384]{1,0:T(8,128)(4,1)S(1)}, pred[8,384]{1,0:T(8,128)(4,1)}, u32[]{:S(2)}) copy-start(pred[8,384]{1,0:T(8,128)(4,1)} %broadcast_in_dim.40) | copy-start | bytes 9220
  99.8 16.3 %collective-permute-start.8 = (bf16[64,24,128]{2,1,0:T(8,128)(2,1)S(1)}, bf16[64,24,128]{2,1,0:T(8,128)(2,1)S(1)}, u32[]{:S(2)}, u32[]{:S(2)}) collective-permute-start(bf16[64,24,128]{2,1,0:T(8,128)(2,1)S(1)} %get-tuple-element.3), channel_id=1, source_target_pairs={{8,0},{16,8},{24,16},{9,1},{17,9},{25,17},{10,2},{18,10},{26,18},{... | collective-permute-start | bytes 1179656 | tf_op jit(solution)/shard_map/ppermute | solution.py:189
  107.1 15.0 %collective-permute-start.9 = (bf16[64,24,128]{2,1,0:T(8,128)(2,1)S(1)}, bf16[64,24,128]{2,1,0:T(8,128)(2,1)S(1)}, u32[]{:S(2)}, u32[]{:S(2)}) collective-permute-start(bf16[64,24,128]{2,1,0:T(8,128)(2,1)S(1)} %get-tuple-element.2), channel_id=1, source_target_pairs={{0,8},{8,16},{16,24},{1,9},{9,17},{17,25},{2,10},{10,18},{18,26},{... | collective-permute-start | bytes 1179656 | tf_op jit(solution)/shard_map/ppermute | solution.py:188
  111.3 10.8 %copy-start.7 = (pred[128]{0:T(512)(128)(4,1)S(1)}, pred[128]{0:T(512)(128)(4,1)}, u32[]{:S(2)}) copy-start(pred[128]{0:T(512)(128)(4,1)} %get-tuple-element.30) | copy-start | bytes 388
  111.3 10.8 %copy-start.8 = (pred[128]{0:T(512)(128)(4,1)S(1)}, pred[128]{0:T(512)(128)(4,1)}, u32[]{:S(2)}) copy-start(pred[128]{0:T(512)(128)(4,1)} %get-tuple-element.31) | copy-start | bytes 388
  111.4 10.9 %copy-start.1 = (bf16[64,64,1]{1,0,2:T(8,128)(2,1)S(1)}, bf16[64,64,1]{1,0,2:T(8,128)(2,1)}, u32[]{:S(2)}) copy-start(bf16[64,64,1]{1,0,2:T(8,128)(2,1)} %reshape.168) | copy-start | bytes 24580

commit v20 on v18

--- a/solution.py
+++ b/solution.py
@@ -178,8 +178,11 @@
 
     forward = [(i, i + 1) for i in range(n_cols - 1)]
     backward = [(target, source) for source, target in forward]
-    left = lax.ppermute(x[blocks_per_tile - 1, :, :, local_cols - LANES :], "tx", forward)
-    right = lax.ppermute(x[0, :, :, :LANES], "tx", backward)
+    halo_shape = (2 * count_acq, padded_rows, LANES)
+    left = jnp.take(received, order[blocks_per_tile - 1], axis=0)[:, :, local_cols - LANES :]
+    right = jnp.take(received, order[0], axis=0)[:, :, :LANES]
+    left = lax.ppermute(left, "tx", forward).reshape(halo_shape)
+    right = lax.ppermute(right, "tx", backward).reshape(halo_shape)
     lane = lax.broadcasted_iota(jnp.int32, right.shape, 2)
     zeros = jnp.zeros_like(right)
     edge = jnp.where(lane < RADIUS, right, jnp.where(lane >= LANES - RADIUS, left, zeros))

time: 135 us -> 139 us (1.030)
  the two profiles are of different devices: /device:TPU:21 before, /device:TPU:26 now
where the time goes in v20:
time: 139 us
  waiting for transfers between devices  68.7 us (49%)
  local copies, waits for them, and re-layouts  25.4 us (18%)
  starting transfers between devices  15.7 us (11%)
  Pallas kernels  15.6 us (11%)
  other arithmetic  10.8 us (8%)
  matrix products  1.62 us (1%)
    ppermute x8, waiting for transfers between devices, shards(): received.append(lax.ppermute(chunk, ('tx', 'ty'), pairs))  68.7 us
    pallas_call x1, Pallas kernels, pair_maps(): pl.pallas_call(kernel, grid_spec=grid_spec, out_shape=[out_shape, out_sha...  15.6 us
    ppermute x8, starting transfers between devices, shards(): received.append(lax.ppermute(chunk, ('tx', 'ty'), pairs))  8.77 us
    unnamed x19, local copies, waits for them, and re-layouts  5.96 us
    ppermute x1, starting transfers between devices, shards(): left = lax.ppermute(left, 'tx', forward).reshape(halo_shape)  4.99 us
    dynamic_slice x1, local copies, waits for them, and re-layouts, shards(): chunk = lax.dynamic_slice_in_dim(x, first, padded_rows, axis=2)  4.9 us
    convert_element_type x1, local copies, waits for them, and re-layouts, shards(): main.astype(jnp.bfloat16)  3.41 us
  transfers between devices with their start and end apart: 10, of which 7 were waited for; matrix products, arithmetic and copies ran while one was open for 19% of the time, Pallas kernels for 0%

profile of v20, /device:TPU:26, one launch (start us, length us, event | category | flops | bytes accessed | tf_op | source)
XLA Modules:
  0.0 138.7 jit_solution(7099978445992790491)
XLA Ops:
  0.8 4.9 %pad_dynamic-slice_fusion = (bf16[8,2,24,512]{3,2,1,0:T(8,128)(2,1)S(1)}, bf16[8,2,24,512]{3,2,1,0:T(8,128)(2,1)}, bf16[8,2,24,512]{3,2,1,0:T(8,128)(2,1)}, bf16...) fusion(s32[]{:T(128)S(6)} %select_n.155, ...), kind=kLoop, calls=%fused_computation.8 | loop fusion | bytes 5242912 | tf_op jit(solution)/shard_map/dynamic_slice | solution.py:170
  5.7 3.2 %collective-permute-start = (bf16[384,512]{1,0:T(8,128)(2,1)S(1)}, bf16[384,512]{1,0:T(8,128)(2,1)S(1)}, u32[]{:S(2)}, u32[]{:S(2)}) collective-permute-start(bf16[384,512]{1,0:T(8,128)(2,1)S(1)} %bitcast.60), channel_id=1, source_target_pairs={{0,0},{1,1},{2,8},{3,9},{4,16},{5,17},{6,24},{7,25},{8,2},{9,3},{1... | collective-permute-start | bytes 1179656 | tf_op jit(solution)/shard_map/ppermute | solution.py:172
  8.9 1.7 %collective-permute-start.1 = (bf16[384,512]{1,0:T(8,128)(2,1)}, bf16[384,512]{1,0:T(8,128)(2,1)}, u32[]{:S(2)}, u32[]{:S(2)}) collective-permute-start(bf16[384,512]{1,0:T(8,128)(2,1)} %bitcast.2), channel_id=1, source_target_pairs={{0,1},{1,2},{2,9},{3,10},{4,17},{5,18},{6,25},{7,26},{8,3},{9,4},{... | collective-permute-start | bytes 1179656 | tf_op jit(solution)/shard_map/ppermute | solution.py:172
  11.1 3.3 %collective-permute-start.3 = (bf16[384,512]{1,0:T(8,128)(2,1)}, bf16[384,512]{1,0:T(8,128)(2,1)}, u32[]{:S(2)}, u32[]{:S(2)}) collective-permute-start(bf16[384,512]{1,0:T(8,128)(2,1)} %bitcast.6), channel_id=1, source_target_pairs={{0,3},{1,4},{2,11},{3,12},{4,19},{5,20},{6,27},{7,28},{8,5},{9,6},... | collective-permute-start | bytes 1179656 | tf_op jit(solution)/shard_map/ppermute | solution.py:172
  18.2 1.4 %reshape.198 = bf16[64,64,1]{1,0,2:T(8,128)(2,1)} reshape(bf16[32,2,32,2]{3,2,1,0:T(8,128)(2,1)S(1)} %copy.10) | data formatting | bytes 16384 | tf_op jit(solution)/shard_map/reshape | solution.py:191
  19.6 0.8 reshape.197
  22.1 10.9 %collective-permute-done = bf16[384,512]{1,0:T(8,128)(2,1)S(1)} collective-permute-done((bf16[384,512]{1,0:T(8,128)(2,1)S(1)}, bf16[384,512]{1,0:T(8,128)(2,1)S(1)}, u32[]{:S(2)}, u32[]{:S(2)}) %collective-permute-start) | collective-permute-done | bytes 393248 | tf_op jit(solution)/shard_map/ppermute | solution.py:172
  33.0 0.8 copy-done
  33.7 1.0 bitcast_dynamic-update-slice_fusion.7
  34.8 23.2 %collective-permute-done.1 = bf16[384,512]{1,0:T(8,128)(2,1)} collective-permute-done((bf16[384,512]{1,0:T(8,128)(2,1)}, bf16[384,512]{1,0:T(8,128)(2,1)}, u32[]{:S(2)}, u32[]{:S(2)}) %collective-permute-start.1) | collective-permute-done | bytes 393248 | tf_op jit(solution)/shard_map/ppermute | solution.py:172
  58.0 1.0 bitcast_dynamic-update-slice_fusion.6
  59.0 7.5 %collective-permute-done.2 = bf16[384,512]{1,0:T(8,128)(2,1)} collective-permute-done((bf16[384,512]{1,0:T(8,128)(2,1)}, bf16[384,512]{1,0:T(8,128)(2,1)}, u32[]{:S(2)}, u32[]{:S(2)}) %collective-permute-start.2) | collective-permute-done | bytes 393248 | tf_op jit(solution)/shard_map/ppermute | solution.py:172
  66.5 1.0 bitcast_dynamic-update-slice_fusion.5
  67.6 1.4 collective-permute-done.3
  68.9 1.0 bitcast_dynamic-update-slice_fusion.4
  70.0 3.5 %collective-permute-done.4 = bf16[384,512]{1,0:T(8,128)(2,1)} collective-permute-done((bf16[384,512]{1,0:T(8,128)(2,1)}, bf16[384,512]{1,0:T(8,128)(2,1)}, u32[]{:S(2)}, u32[]{:S(2)}) %collective-permute-start.4) | collective-permute-done | bytes 393248 | tf_op jit(solution)/shard_map/ppermute | solution.py:172
  73.4 1.0 bitcast_dynamic-update-slice_fusion.3
  74.5 4.9 %collective-permute-done.6 = bf16[384,512]{1,0:T(8,128)(2,1)S(1)} collective-permute-done((bf16[384,512]{1,0:T(8,128)(2,1)}, bf16[384,512]{1,0:T(8,128)(2,1)S(1)}, u32[]{:S(2)}, u32[]{:S(2)}) %collective-permute-start.6) | collective-permute-done | bytes 393248 | tf_op jit(solution)/shard_map/ppermute | solution.py:172
  79.4 17.3 %collective-permute-done.7 = bf16[384,512]{1,0:T(8,128)(2,1)S(1)} collective-permute-done((bf16[384,512]{1,0:T(8,128)(2,1)S(1)}, bf16[384,512]{1,0:T(8,128)(2,1)S(1)}, u32[]{:S(2)}, u32[]{:S(2)}) %collective-permute-start.7) | collective-permute-done | bytes 393248 | tf_op jit(solution)/shard_map/ppermute | solution.py:172
  96.8 1.9 %gather_fusion.1 = bf16[4,384,512]{2,1,0:T(8,128)(2,1)} fusion(bf16[8,384,512]{2,1,0:T(8,128)(2,1)S(1)} %bitcast_dynamic-update-slice_fusion, s32[1024]{0:T(1024)} %pad_clamp_fusion.1), kind=kCustom, calls=%fused_computation.clone | custom fusion | bytes 3145744 | tf_op jit(solution)/shard_map/jit(_take)/gather | solution.py:183
  98.7 1.8 %slice_select_fusion.1 = bf16[4,384,128]{2,1,0:T(8,128)(2,1)} fusion(bf16[4,384,512]{2,1,0:T(8,128)(2,1)} %gather_fusion.1, pred[4]{0:T(512)(128)(4,1)} %get-tuple-element.17), kind=kLoop, calls=%fused_computation.17 | loop fusion | flops 196608 | bytes 786436 | tf_op jit(solution)/shard_map/jit(_take)/select_n | solution.py:183
  100.5 1.9 %collective-permute-start.8 = (bf16[4,384,128]{2,1,0:T(8,128)(2,1)}, bf16[4,384,128]{2,1,0:T(8,128)(2,1)S(1)}, u32[]{:S(2)}, u32[]{:S(2)}) collective-permute-start(bf16[4,384,128]{2,1,0:T(8,128)(2,1)} %slice_select_fusion.1), channel_id=1, source_target_pairs={{8,0},{16,8},{24,16},{9,1},{17,9},{25,17},{10,2},{18,10},{26,18},{... | collective-permute-start | bytes 1179656 | tf_op jit(solution)/shard_map/ppermute | solution.py:185
  102.5 1.9 %gather_fusion.2 = bf16[4,384,512]{2,1,0:T(8,128)(2,1)} fusion(bf16[8,384,512]{2,1,0:T(8,128)(2,1)S(1)} %bitcast_dynamic-update-slice_fusion, s32[1024]{0:T(1024)} %pad_clamp_fusion), kind=kCustom, calls=%fused_computation.1.clone | custom fusion | bytes 3145744 | tf_op jit(solution)/shard_map/jit(_take)/gather | solution.py:182
  104.4 1.8 %slice_select_fusion = bf16[4,384,128]{2,1,0:T(8,128)(2,1)} fusion(bf16[4,384,512]{2,1,0:T(8,128)(2,1)} %gather_fusion.2, pred[4]{0:T(512)(128)(4,1)} %get-tuple-element.3), kind=kLoop, calls=%fused_computation.16 | loop fusion | flops 196608 | bytes 786436 | tf_op jit(solution)/shard_map/jit(_take)/select_n | solution.py:182
  106.2 5.0 %collective-permute-start.9 = (bf16[4,384,128]{2,1,0:T(8,128)(2,1)}, bf16[4,384,128]{2,1,0:T(8,128)(2,1)}, u32[]{:S(2)}, u32[]{:S(2)}) collective-permute-start(bf16[4,384,128]{2,1,0:T(8,128)(2,1)} %slice_select_fusion), channel_id=1, source_target_pairs={{0,8},{8,16},{16,24},{1,9},{9,17},{17,25},{2,10},{10,18},{18,26},{... | collective-permute-start | bytes 1179656 | tf_op jit(solution)/shard_map/ppermute | solution.py:184
  111.2 2.5 %gather_fusion = bf16[8,384,512]{2,1,0:T(8,128)(2,1)} fusion(bf16[8,384,512]{2,1,0:T(8,128)(2,1)S(1)} %bitcast_dynamic-update-slice_fusion, s32[1024]{0:T(1024)} %pad_clamp_fusion.2), kind=kCustom, calls=%fused_computation.2 | custom fusion | bytes 6291488 | tf_op jit(solution)/shard_map/jit(_take)/gather | solution.py:176
  113.7 2.2 %broadcast_select_fusion = bf16[8,384,512]{2,1,0:T(8,128)(2,1)S(1)} fusion(bf16[8,384,512]{2,1,0:T(8,128)(2,1)} %gather_fusion, pred[8,384]{1,0:T(8,128)(4,1)} %broadcast_in_dim.45), kind=kLoop, calls=%fused_computation.6 | loop fusion | flops 1572864 | bytes 6294528 | tf_op jit(solution)/shard_map/jit(_take)/select_n | solution.py:176
  116.0 1.4 convert_bitcast_fusion
  117.4 3.4 %copy.12 = bf16[2,64,24,512]{3,2,1,0:T(8,128)(2,1)} copy(bf16[2,64,24,512]{3,1,2,0:T(8,128)(2,1)S(1)} %convert_bitcast_fusion) | data formatting | bytes 6291456 | tf_op jit(solution)/shard_map/convert_element_type | solution.py:193
  120.8 1.0 select_select_fusion
  122.1 1.0 copy.14
  123.2 15.6 %shard_map.68 = (f32[32,16,1024]{2,1,0:T(8,128)}, f32[32,16,1024]{2,1,0:T(8,128)}) custom-call(s32[32]{0:T(128)} %pre_ref.1, s32[32]{0:T(128)} %post_ref.1, bf16[2,32,2,24,512]{4,3,2,1,0:T(8,128)(2,1)} %bitcast.54, bf16[32,2,24,128]{3,2,1,0:T(8,128)(2,1)} %bitcast.57, bf16[768,128]{1,0:T(8,128)(2,1)} %pad_maximum_fusion.band_ref), custom_call_target="tpu_custom_call" | custom-call | tf_op jit(solution)/shard_map/pallas_call | solution.py:141
  (44 shorter events, 6.3 us)
Async XLA Ops:
  0.6 15.7 %copy-start.2 = (bf16[32,32]{1,0:T(8,128)(2,1)S(1)}, bf16[32,32]{1,0:T(8,128)(2,1)}, u32[]{:S(2)}) copy-start(bf16[32,32]{1,0:T(8,128)(2,1)} %param.9) | copy-start | bytes 6148
  0.6 15.9 %copy-start.3 = (bf16[32,32]{1,0:T(8,128)(2,1)S(1)}, bf16[32,32]{1,0:T(8,128)(2,1)}, u32[]{:S(2)}) copy-start(bf16[32,32]{1,0:T(8,128)(2,1)} %param.8) | copy-start | bytes 6148
  5.7 27.3 %collective-permute-start = (bf16[384,512]{1,0:T(8,128)(2,1)S(1)}, bf16[384,512]{1,0:T(8,128)(2,1)S(1)}, u32[]{:S(2)}, u32[]{:S(2)}) collective-permute-start(bf16[384,512]{1,0:T(8,128)(2,1)S(1)} %bitcast.60), channel_id=1, source_target_pairs={{0,0},{1,1},{2,8},{3,9},{4,16},{5,17},{6,24},{7,25},{8,2},{9,3},{1... | collective-permute-start | bytes 1179656 | tf_op jit(solution)/shard_map/ppermute | solution.py:172
  8.9 49.1 %collective-permute-start.1 = (bf16[384,512]{1,0:T(8,128)(2,1)}, bf16[384,512]{1,0:T(8,128)(2,1)}, u32[]{:S(2)}, u32[]{:S(2)}) collective-permute-start(bf16[384,512]{1,0:T(8,128)(2,1)} %bitcast.2), channel_id=1, source_target_pairs={{0,1},{1,2},{2,9},{3,10},{4,17},{5,18},{6,25},{7,26},{8,3},{9,4},{... | collective-permute-start | bytes 1179656 | tf_op jit(solution)/shard_map/ppermute | solution.py:172
  10.6 55.9 %collective-permute-start.2 = (bf16[384,512]{1,0:T(8,128)(2,1)}, bf16[384,512]{1,0:T(8,128)(2,1)}, u32[]{:S(2)}, u32[]{:S(2)}) collective-permute-start(bf16[384,512]{1,0:T(8,128)(2,1)} %bitcast.4), channel_id=1, source_target_pairs={{0,2},{1,3},{2,10},{3,11},{4,18},{5,19},{6,26},{7,27},{8,4},{9,5},... | collective-permute-start | bytes 1179656 | tf_op jit(solution)/shard_map/ppermute | solution.py:172
  11.1 57.8 %collective-permute-start.3 = (bf16[384,512]{1,0:T(8,128)(2,1)}, bf16[384,512]{1,0:T(8,128)(2,1)}, u32[]{:S(2)}, u32[]{:S(2)}) collective-permute-start(bf16[384,512]{1,0:T(8,128)(2,1)} %bitcast.6), channel_id=1, source_target_pairs={{0,3},{1,4},{2,11},{3,12},{4,19},{5,20},{6,27},{7,28},{8,5},{9,6},... | collective-permute-start | bytes 1179656 | tf_op jit(solution)/shard_map/ppermute | solution.py:172
  14.5 59.0 %collective-permute-start.4 = (bf16[384,512]{1,0:T(8,128)(2,1)}, bf16[384,512]{1,0:T(8,128)(2,1)}, u32[]{:S(2)}, u32[]{:S(2)}) collective-permute-start(bf16[384,512]{1,0:T(8,128)(2,1)} %bitcast.8), channel_id=1, source_target_pairs={{0,4},{1,5},{2,12},{3,13},{4,20},{5,21},{6,28},{7,29},{8,6},{9,7},... | collective-permute-start | bytes 1179656 | tf_op jit(solution)/shard_map/ppermute | solution.py:172
  33.0 0.8 copy-start
  33.7 40.7 %collective-permute-start.5 = (bf16[384,512]{1,0:T(8,128)(2,1)}, bf16[384,512]{1,0:T(8,128)(2,1)S(1)}, u32[]{:S(2)}, u32[]{:S(2)}) collective-permute-start(bf16[384,512]{1,0:T(8,128)(2,1)} %bitcast.10), channel_id=1, source_target_pairs={{0,5},{1,6},{2,13},{3,14},{4,21},{5,22},{6,29},{7,30},{8,7},{9,0},... | collective-permute-start | bytes 1179656 | tf_op jit(solution)/shard_map/ppermute | solution.py:172
  58.0 21.4 %collective-permute-start.6 = (bf16[384,512]{1,0:T(8,128)(2,1)}, bf16[384,512]{1,0:T(8,128)(2,1)S(1)}, u32[]{:S(2)}, u32[]{:S(2)}) collective-permute-start(bf16[384,512]{1,0:T(8,128)(2,1)} %bitcast.59), channel_id=1, source_target_pairs={{0,6},{1,7},{2,14},{3,15},{4,22},{5,23},{6,30},{7,31},{8,0},{9,1},... | collective-permute-start | bytes 1179656 | tf_op jit(solution)/shard_map/ppermute | solution.py:172
  66.5 30.2 %collective-permute-start.7 = (bf16[384,512]{1,0:T(8,128)(2,1)S(1)}, bf16[384,512]{1,0:T(8,128)(2,1)S(1)}, u32[]{:S(2)}, u32[]{:S(2)}) collective-permute-start(bf16[384,512]{1,0:T(8,128)(2,1)S(1)} %bitcast.58), channel_id=1, source_target_pairs={{0,7},{1,0},{2,15},{3,8},{4,23},{5,16},{6,31},{7,24},{8,1},{9,2},{... | collective-permute-start | bytes 1179656 | tf_op jit(solution)/shard_map/ppermute | solution.py:172
  100.5 20.3 %collective-permute-start.8 = (bf16[4,384,128]{2,1,0:T(8,128)(2,1)}, bf16[4,384,128]{2,1,0:T(8,128)(2,1)S(1)}, u32[]{:S(2)}, u32[]{:S(2)}) collective-permute-start(bf16[4,384,128]{2,1,0:T(8,128)(2,1)} %slice_select_fusion.1), channel_id=1, source_target_pairs={{8,0},{16,8},{24,16},{9,1},{17,9},{25,17},{10,2},{18,10},{26,18},{... | collective-permute-start | bytes 1179656 | tf_op jit(solution)/shard_map/ppermute | solution.py:185
  106.2 14.6 %collective-permute-start.9 = (bf16[4,384,128]{2,1,0:T(8,128)(2,1)}, bf16[4,384,128]{2,1,0:T(8,128)(2,1)}, u32[]{:S(2)}, u32[]{:S(2)}) collective-permute-start(bf16[4,384,128]{2,1,0:T(8,128)(2,1)} %slice_select_fusion), channel_id=1, source_target_pairs={{0,8},{8,16},{16,24},{1,9},{9,17},{17,25},{2,10},{10,18},{18,26},{... | collective-permute-start | bytes 1179656 | tf_op jit(solution)/shard_map/ppermute | solution.py:184
  117.4 3.4 %copy-start.4 = (pred[128]{0:T(512)(128)(4,1)S(1)}, pred[128]{0:T(512)(128)(4,1)}, u32[]{:S(2)}) copy-start(pred[128]{0:T(512)(128)(4,1)} %get-tuple-element.21) | copy-start | bytes 388
  117.4 3.4 %copy-start.5 = (pred[128]{0:T(512)(128)(4,1)S(1)}, pred[128]{0:T(512)(128)(4,1)}, u32[]{:S(2)}) copy-start(pred[128]{0:T(512)(128)(4,1)} %get-tuple-element.22) | copy-start | bytes 388
  117.4 4.5 %copy-start.1 = (bf16[64,64,1]{1,0,2:T(8,128)(2,1)S(1)}, bf16[64,64,1]{1,0,2:T(8,128)(2,1)}, u32[]{:S(2)}) copy-start(bf16[64,64,1]{1,0,2:T(8,128)(2,1)} %reshape.198) | copy-start | bytes 24580

commit v21 on v18

--- a/solution.py
+++ b/solution.py
@@ -170,10 +170,10 @@
         chunk = lax.dynamic_slice_in_dim(x, first, padded_rows, axis=2)
         chunk = chunk.reshape(local_acq * 2 * padded_rows, local_cols)
         received.append(lax.ppermute(chunk, ("tx", "ty"), pairs))
-    received = jnp.stack(received, axis=0)
-    source = jnp.arange(blocks_per_tile)[:, None] + blocks_per_tile * jnp.arange(n_cols)[None, :]
-    order = (me_row - source) % n_rows
-    x = jnp.take(received, order.reshape(-1), axis=0)
+    x = jnp.zeros((n_rows,) + received[0].shape, received[0].dtype)
+    for m, chunk in enumerate(received):
+        s = (me_row - m) % n_rows
+        x = lax.dynamic_update_index_in_dim(x, chunk, (s % blocks_per_tile) * n_cols + s // blocks_per_tile, 0)
     x = x.reshape(blocks_per_tile, 2 * count_acq, padded_rows, local_cols)
 
     forward = [(i, i + 1) for i in range(n_cols - 1)]

time: 135 us -> 135 us (level); the launches traced: 134 us -> 133 us
  local copies, waits for them, and re-layouts: 26 us -> 22.5 us
  starting transfers between devices: 60.4 us -> 62.5 us
    unnamed x11 -> x16, local copies, waits for them, and re-layouts: 10.4 us -> 1.5 us
    ppermute x8, waiting for transfers between devices: 18 us -> 22.4 us  [shards(): received.append(lax.ppermute(chunk, ('tx', 'ty'), pairs))]
    dynamic_update_slice x0 -> x8, local copies, waits for them, and re-layouts: none -> 4.22 us  [shards(): lax.dynamic_update_index_in_dim(x, chunk, s % blocks_per_tile * n_cols +...]
    ppermute x1, waiting for transfers between devices: 8.27 us -> 4.13 us  [shards(): lax.ppermute(x[blocks_per_tile - 1, :, :, local_cols - LANES:], 'tx', for...]
    gather x1 -> x0, local copies, waits for them, and re-layouts: 2.64 us -> none  [shards(): x = jnp.take(received, order.reshape(-1), axis=0)]
    reshape x2, local copies, waits for them, and re-layouts: 1.62 us -> 4.22 us  [shards(): mixing = mixing.reshape(2 * count_acq, 2 * count_acq)]
    ppermute x8, starting transfers between devices: 46.7 us -> 48.7 us  [shards(): received.append(lax.ppermute(chunk, ('tx', 'ty'), pairs))]
    another operation x1, local copies, waits for them, and re-layouts: 0.5 us -> 2.01 us  [shards(): jnp.stack([jnp.stack([filt_re, -filt_im], -1), jnp.stack([filt_im, filt_r...]
  transfers between devices with their start and end apart: 10 -> 10, of which waited for: 4 -> 3; matrix products, arithmetic and copies ran while one was open for 14% -> 13% of each run, Pallas kernels for 0% -> 0%
where the time goes in v21:
time: 135 us; the launch traced here: 133 us
  starting transfers between devices  62.5 us (46%)
  waiting for transfers between devices  26.5 us (20%)
  local copies, waits for them, and re-layouts  22.5 us (17%)
  Pallas kernels  15.6 us (12%)
  other arithmetic  3.01 us (2%)
  matrix products  1.59 us (1%)
    ppermute x8, starting transfers between devices, shards(): received.append(lax.ppermute(chunk, ('tx', 'ty'), pairs))  48.7 us
    ppermute x8, waiting for transfers between devices, shards(): received.append(lax.ppermute(chunk, ('tx', 'ty'), pairs))  22.4 us
    pallas_call x1, Pallas kernels, pair_maps(): pl.pallas_call(kernel, grid_spec=grid_spec, out_shape=[out_shape, out_sha...  15.6 us
    ppermute x1, starting transfers between devices, shards(): right = lax.ppermute(x[0, :, :, :LANES], 'tx', backward)  11.7 us
    dynamic_slice x1, local copies, waits for them, and re-layouts, shards(): chunk = lax.dynamic_slice_in_dim(x, first, padded_rows, axis=2)  4.9 us
    dynamic_update_slice x8, local copies, waits for them, and re-layouts, shards(): lax.dynamic_update_index_in_dim(x, chunk, s % blocks_per_tile * n_cols +...  4.22 us
    reshape x2, local copies, waits for them, and re-layouts, shards(): mixing = mixing.reshape(2 * count_acq, 2 * count_acq)  4.22 us
    ppermute x1, waiting for transfers between devices, shards(): lax.ppermute(x[blocks_per_tile - 1, :, :, local_cols - LANES:], 'tx', for...  4.13 us
  transfers between devices with their start and end apart: 10, of which 3 were waited for; matrix products, arithmetic and copies ran while one was open for 13% of the time, Pallas kernels for 0%

profile of v21, /device:TPU:21, one launch (start us, length us, event | category | flops | bytes accessed | tf_op | source)
XLA Modules:
  0.0 132.6 jit_solution(15405522418619380790)
XLA Ops:
  0.8 4.9 %pad_dynamic-slice_fusion = (bf16[8,2,24,512]{3,2,1,0:T(8,128)(2,1)S(1)}, bf16[8,2,24,512]{3,2,1,0:T(8,128)(2,1)}, bf16[8,2,24,512]{3,2,1,0:T(8,128)(2,1)}, bf16...) fusion(s32[]{:T(128)S(6)} %select_n.234, ...), kind=kLoop, calls=%fused_computation.4 | loop fusion | bytes 5242912 | tf_op jit(solution)/shard_map/dynamic_slice | solution.py:170
  5.7 0.7 collective-permute-start
  6.4 4.5 %collective-permute-start.1 = (bf16[384,512]{1,0:T(8,128)(2,1)}, bf16[384,512]{1,0:T(8,128)(2,1)}, u32[]{:S(2)}, u32[]{:S(2)}) collective-permute-start(bf16[384,512]{1,0:T(8,128)(2,1)} %bitcast.2), channel_id=1, source_target_pairs={{0,1},{1,2},{2,9},{3,10},{4,17},{5,18},{6,25},{7,26},{8,3},{9,4},{... | collective-permute-start | bytes 1179656 | tf_op jit(solution)/shard_map/ppermute | solution.py:172
  10.9 5.7 %collective-permute-start.3 = (bf16[384,512]{1,0:T(8,128)(2,1)}, bf16[384,512]{1,0:T(8,128)(2,1)}, u32[]{:S(2)}, u32[]{:S(2)}) collective-permute-start(bf16[384,512]{1,0:T(8,128)(2,1)} %bitcast.6), channel_id=1, source_target_pairs={{0,3},{1,4},{2,11},{3,12},{4,19},{5,20},{6,27},{7,28},{8,5},{9,6},... | collective-permute-start | bytes 1179656 | tf_op jit(solution)/shard_map/ppermute | solution.py:172
  16.8 0.6 pad_maximum_fusion.1
  17.4 0.7 pad_maximum_fusion.band_ref
  18.1 0.7 copy-done.1
  18.8 30.6 %collective-permute-start.5 = (bf16[384,512]{1,0:T(8,128)(2,1)}, bf16[384,512]{1,0:T(8,128)(2,1)S(1)}, u32[]{:S(2)}, u32[]{:S(2)}) collective-permute-start(bf16[384,512]{1,0:T(8,128)(2,1)} %bitcast.10), channel_id=1, source_target_pairs={{0,5},{1,6},{2,13},{3,14},{4,21},{5,22},{6,29},{7,30},{8,7},{9,0},... | collective-permute-start | bytes 1179656 | tf_op jit(solution)/shard_map/ppermute | solution.py:172
  49.4 0.3 broadcast_in_dim.41
  49.7 0.7 copy-done.2
  50.5 6.3 %collective-permute-start.6 = (bf16[384,512]{1,0:T(8,128)(2,1)S(1)}, bf16[384,512]{1,0:T(8,128)(2,1)S(1)}, u32[]{:S(2)}, u32[]{:S(2)}) collective-permute-start(bf16[384,512]{1,0:T(8,128)(2,1)S(1)} %bitcast.54), channel_id=1, source_target_pairs={{0,6},{1,7},{2,14},{3,15},{4,22},{5,23},{6,30},{7,31},{8,0},{9,1},... | collective-permute-start | bytes 1179656 | tf_op jit(solution)/shard_map/ppermute | solution.py:172
  56.7 1.0 bitcast_dynamic-update-slice_fusion.6
  57.8 0.9 collective-permute-start.7
  58.7 1.0 bitcast_dynamic-update-slice_fusion.5
  59.7 1.0 bitcast_dynamic-update-slice_fusion.4
  60.8 1.0 bitcast_dynamic-update-slice_fusion.3
  61.8 14.1 %collective-permute-done.5 = bf16[384,512]{1,0:T(8,128)(2,1)S(1)} collective-permute-done((bf16[384,512]{1,0:T(8,128)(2,1)}, bf16[384,512]{1,0:T(8,128)(2,1)S(1)}, u32[]{:S(2)}, u32[]{:S(2)}) %collective-permute-start.5) | collective-permute-done | bytes 393248 | tf_op jit(solution)/shard_map/ppermute | solution.py:172
  75.9 8.3 %collective-permute-done.6 = bf16[384,512]{1,0:T(8,128)(2,1)S(1)} collective-permute-done((bf16[384,512]{1,0:T(8,128)(2,1)S(1)}, bf16[384,512]{1,0:T(8,128)(2,1)S(1)}, u32[]{:S(2)}, u32[]{:S(2)}) %collective-permute-start.6) | collective-permute-done | bytes 393248 | tf_op jit(solution)/shard_map/ppermute | solution.py:172
  84.3 1.0 slice_bitcast_fusion
  85.3 11.7 %collective-permute-start.8 = (bf16[64,24,128]{2,1,0:T(8,128)(2,1)}, bf16[64,24,128]{2,1,0:T(8,128)(2,1)S(1)}, u32[]{:S(2)}, u32[]{:S(2)}) collective-permute-start(bf16[64,24,128]{2,1,0:T(8,128)(2,1)} %get-tuple-element.3), channel_id=1, source_target_pairs={{8,0},{16,8},{24,16},{9,1},{17,9},{25,17},{10,2},{18,10},{26,18},{... | collective-permute-start | bytes 1179656 | tf_op jit(solution)/shard_map/ppermute | solution.py:182
  97.0 2.1 %collective-permute-start.9 = (bf16[64,24,128]{2,1,0:T(8,128)(2,1)}, bf16[64,24,128]{2,1,0:T(8,128)(2,1)}, u32[]{:S(2)}, u32[]{:S(2)}) collective-permute-start(bf16[64,24,128]{2,1,0:T(8,128)(2,1)} %get-tuple-element.2), channel_id=1, source_target_pairs={{0,8},{8,16},{16,24},{1,9},{9,17},{17,25},{2,10},{10,18},{18,26},{... | collective-permute-start | bytes 1179656 | tf_op jit(solution)/shard_map/ppermute | solution.py:181
  99.1 0.5 iota_compare_fusion
  99.6 2.0 %copy.10 = bf16[32,2,32,2]{3,2,1,0:T(8,128)(2,1)} copy(bf16[32,2,32,2]{2,0,3,1:T(8,128)(2,1)} %pad_maximum_fusion.1) | data formatting | bytes 16384 | tf_op jit(solution)/shard_map/stack | solution.py:187
  101.6 2.4 %reshape.58 = bf16[64,64,1]{1,0,2:T(8,128)(2,1)} reshape(bf16[32,2,32,2]{3,2,1,0:T(8,128)(2,1)} %copy.10) | data formatting | bytes 16384 | tf_op jit(solution)/shard_map/reshape | solution.py:188
  104.0 1.8 %reshape.57 = bf16[64,64,1,1]{1,0,2,3:T(8,128)(2,1)S(1)} reshape(bf16[32,2,32,2]{3,2,1,0:T(8,128)(2,1)} %copy.10) | data formatting | bytes 16384 | tf_op jit(solution)/shard_map/reshape | solution.py:188
  105.9 1.3 %convert_bitcast_fusion = bf16[2,64,24,512]{3,1,2,0:T(8,128)(2,1)S(1)} fusion(bf16[2,64,24,512]{3,2,1,0:T(8,128)(2,1)S(1)} %bitcast.50, bf16[64,64,1,1]{1,0,2,3:T(8,128)(2,1)S(1)} %reshape.57), kind=kOutput, calls=%fused_computation.2 | convolution fusion | flops 202899456 | bytes 6299648 | tf_op jit(solution)/shard_map/kc,bchw->bkhw/dot_general | solution.py:189
  107.2 3.4 %copy.12 = bf16[2,64,24,512]{3,2,1,0:T(8,128)(2,1)} copy(bf16[2,64,24,512]{3,1,2,0:T(8,128)(2,1)S(1)} %convert_bitcast_fusion) | data formatting | bytes 6291456 | tf_op jit(solution)/shard_map/convert_element_type | solution.py:190
  110.6 4.1 %collective-permute-done.9 = bf16[64,24,128]{2,1,0:T(8,128)(2,1)} collective-permute-done((bf16[64,24,128]{2,1,0:T(8,128)(2,1)}, bf16[64,24,128]{2,1,0:T(8,128)(2,1)}, u32[]{:S(2)}, u32[]{:S(2)}) %collective-permute-start.9) | collective-permute-done | bytes 393248 | tf_op jit(solution)/shard_map/ppermute | solution.py:181
  114.8 1.0 select_select_fusion
  115.8 0.2 convolution_convert_fusion
  116.1 1.0 copy.14
  117.1 15.6 %shard_map.68 = (f32[32,16,1024]{2,1,0:T(8,128)}, f32[32,16,1024]{2,1,0:T(8,128)}) custom-call(s32[32]{0:T(128)} %pre_ref.1, s32[32]{0:T(128)} %post_ref.1, bf16[2,32,2,24,512]{4,3,2,1,0:T(8,128)(2,1)} %bitcast.51, bf16[32,2,24,128]{3,2,1,0:T(8,128)(2,1)} %bitcast.52, bf16[768,128]{1,0:T(8,128)(2,1)} %pad_maximum_fusion.band_ref), custom_call_target="tpu_custom_call" | custom-call | tf_op jit(solution)/shard_map/pallas_call | solution.py:141
  (31 shorter events, 0.3 us)
Async XLA Ops:
  0.6 16.1 %copy-start.4 = (bf16[32,32]{1,0:T(8,128)(2,1)S(1)}, bf16[32,32]{1,0:T(8,128)(2,1)}, u32[]{:S(2)}) copy-start(bf16[32,32]{1,0:T(8,128)(2,1)} %param.7) | copy-start | bytes 6148
  0.6 16.1 %copy-start.5 = (bf16[32,32]{1,0:T(8,128)(2,1)S(1)}, bf16[32,32]{1,0:T(8,128)(2,1)}, u32[]{:S(2)}) copy-start(bf16[32,32]{1,0:T(8,128)(2,1)} %param.6) | copy-start | bytes 6148
  5.7 12.4 %collective-permute-start = (bf16[384,512]{1,0:T(8,128)(2,1)S(1)}, bf16[384,512]{1,0:T(8,128)(2,1)S(1)}, u32[]{:S(2)}, u32[]{:S(2)}) collective-permute-start(bf16[384,512]{1,0:T(8,128)(2,1)S(1)} %bitcast.55), channel_id=1, source_target_pairs={{0,0},{1,1},{2,8},{3,9},{4,16},{5,17},{6,24},{7,25},{8,2},{9,3},{1... | collective-permute-start | bytes 1179656 | tf_op jit(solution)/shard_map/ppermute | solution.py:172
  6.4 44.1 %collective-permute-start.1 = (bf16[384,512]{1,0:T(8,128)(2,1)}, bf16[384,512]{1,0:T(8,128)(2,1)}, u32[]{:S(2)}, u32[]{:S(2)}) collective-permute-start(bf16[384,512]{1,0:T(8,128)(2,1)} %bitcast.2), channel_id=1, source_target_pairs={{0,1},{1,2},{2,9},{3,10},{4,17},{5,18},{6,25},{7,26},{8,3},{9,4},{... | collective-permute-start | bytes 1179656 | tf_op jit(solution)/shard_map/ppermute | solution.py:172
  10.9 46.9 %collective-permute-start.2 = (bf16[384,512]{1,0:T(8,128)(2,1)}, bf16[384,512]{1,0:T(8,128)(2,1)}, u32[]{:S(2)}, u32[]{:S(2)}) collective-permute-start(bf16[384,512]{1,0:T(8,128)(2,1)} %bitcast.4), channel_id=1, source_target_pairs={{0,2},{1,3},{2,10},{3,11},{4,18},{5,19},{6,26},{7,27},{8,4},{9,5},... | collective-permute-start | bytes 1179656 | tf_op jit(solution)/shard_map/ppermute | solution.py:172
  10.9 48.8 %collective-permute-start.3 = (bf16[384,512]{1,0:T(8,128)(2,1)}, bf16[384,512]{1,0:T(8,128)(2,1)}, u32[]{:S(2)}, u32[]{:S(2)}) collective-permute-start(bf16[384,512]{1,0:T(8,128)(2,1)} %bitcast.6), channel_id=1, source_target_pairs={{0,3},{1,4},{2,11},{3,12},{4,19},{5,20},{6,27},{7,28},{8,5},{9,6},... | collective-permute-start | bytes 1179656 | tf_op jit(solution)/shard_map/ppermute | solution.py:172
  16.6 44.2 %collective-permute-start.4 = (bf16[384,512]{1,0:T(8,128)(2,1)}, bf16[384,512]{1,0:T(8,128)(2,1)}, u32[]{:S(2)}, u32[]{:S(2)}) collective-permute-start(bf16[384,512]{1,0:T(8,128)(2,1)} %bitcast.8), channel_id=1, source_target_pairs={{0,4},{1,5},{2,12},{3,13},{4,20},{5,21},{6,28},{7,29},{8,6},{9,7},... | collective-permute-start | bytes 1179656 | tf_op jit(solution)/shard_map/ppermute | solution.py:172
  17.4 33.1 %copy-start = (bf16[8,2,24,512]{3,2,1,0:T(8,128)(2,1)S(1)}, bf16[8,2,24,512]{3,2,1,0:T(8,128)(2,1)}, u32[]{:S(2)}) copy-start(bf16[8,2,24,512]{3,2,1,0:T(8,128)(2,1)} %get-tuple-element.10) | copy-start | bytes 1179652
  18.1 0.8 copy-start.1
  18.8 57.1 %collective-permute-start.5 = (bf16[384,512]{1,0:T(8,128)(2,1)}, bf16[384,512]{1,0:T(8,128)(2,1)S(1)}, u32[]{:S(2)}, u32[]{:S(2)}) collective-permute-start(bf16[384,512]{1,0:T(8,128)(2,1)} %bitcast.10), channel_id=1, source_target_pairs={{0,5},{1,6},{2,13},{3,14},{4,21},{5,22},{6,29},{7,30},{8,7},{9,0},... | collective-permute-start | bytes 1179656 | tf_op jit(solution)/shard_map/ppermute | solution.py:172
  49.4 1.0 copy-start.2
  50.5 33.7 %collective-permute-start.6 = (bf16[384,512]{1,0:T(8,128)(2,1)S(1)}, bf16[384,512]{1,0:T(8,128)(2,1)S(1)}, u32[]{:S(2)}, u32[]{:S(2)}) collective-permute-start(bf16[384,512]{1,0:T(8,128)(2,1)S(1)} %bitcast.54), channel_id=1, source_target_pairs={{0,6},{1,7},{2,14},{3,15},{4,22},{5,23},{6,30},{7,31},{8,0},{9,1},... | collective-permute-start | bytes 1179656 | tf_op jit(solution)/shard_map/ppermute | solution.py:172
  57.8 26.5 %collective-permute-start.7 = (bf16[384,512]{1,0:T(8,128)(2,1)S(1)}, bf16[384,512]{1,0:T(8,128)(2,1)S(1)}, u32[]{:S(2)}, u32[]{:S(2)}) collective-permute-start(bf16[384,512]{1,0:T(8,128)(2,1)S(1)} %bitcast.53), channel_id=1, source_target_pairs={{0,7},{1,0},{2,15},{3,8},{4,23},{5,16},{6,31},{7,24},{8,1},{9,2},{... | collective-permute-start | bytes 1179656 | tf_op jit(solution)/shard_map/ppermute | solution.py:172
  85.3 25.3 %collective-permute-start.8 = (bf16[64,24,128]{2,1,0:T(8,128)(2,1)}, bf16[64,24,128]{2,1,0:T(8,128)(2,1)S(1)}, u32[]{:S(2)}, u32[]{:S(2)}) collective-permute-start(bf16[64,24,128]{2,1,0:T(8,128)(2,1)} %get-tuple-element.3), channel_id=1, source_target_pairs={{8,0},{16,8},{24,16},{9,1},{17,9},{25,17},{10,2},{18,10},{26,18},{... | collective-permute-start | bytes 1179656 | tf_op jit(solution)/shard_map/ppermute | solution.py:182
  97.0 17.8 %collective-permute-start.9 = (bf16[64,24,128]{2,1,0:T(8,128)(2,1)}, bf16[64,24,128]{2,1,0:T(8,128)(2,1)}, u32[]{:S(2)}, u32[]{:S(2)}) collective-permute-start(bf16[64,24,128]{2,1,0:T(8,128)(2,1)} %get-tuple-element.2), channel_id=1, source_target_pairs={{0,8},{8,16},{16,24},{1,9},{9,17},{17,25},{2,10},{10,18},{18,26},{... | collective-permute-start | bytes 1179656 | tf_op jit(solution)/shard_map/ppermute | solution.py:181
  107.2 7.5 %copy-start.6 = (pred[128]{0:T(512)(128)(4,1)S(1)}, pred[128]{0:T(512)(128)(4,1)}, u32[]{:S(2)}) copy-start(pred[128]{0:T(512)(128)(4,1)} %get-tuple-element.14) | copy-start | bytes 388
  107.2 7.5 %copy-start.7 = (pred[128]{0:T(512)(128)(4,1)S(1)}, pred[128]{0:T(512)(128)(4,1)}, u32[]{:S(2)}) copy-start(pred[128]{0:T(512)(128)(4,1)} %get-tuple-element.15) | copy-start | bytes 388
  107.2 8.6 %copy-start.3 = (bf16[64,64,1]{1,0,2:T(8,128)(2,1)S(1)}, bf16[64,64,1]{1,0,2:T(8,128)(2,1)}, u32[]{:S(2)}) copy-start(bf16[64,64,1]{1,0,2:T(8,128)(2,1)} %reshape.58) | copy-start | bytes 24580

commit v22 on v18

--- a/solution.py
+++ b/solution.py
@@ -9,7 +9,7 @@
 
 RADIUS = 4
 LANES = 128
-PAIRS_PER_STEP = 8
+PAIRS_PER_STEP = 16
 FIELDS = 4
 
 

time: 135 us -> 135 us (level)
  no operation moved by 1% of the time
where the time goes in v22:
time: 135 us
  starting transfers between devices  60.4 us (45%)
  waiting for transfers between devices  27.6 us (20%)
  local copies, waits for them, and re-layouts  26 us (19%)
  Pallas kernels  16 us (12%)
  other arithmetic  2.01 us (1%)
  matrix products  1.64 us (1%)
    ppermute x8, starting transfers between devices, shards(): received.append(lax.ppermute(chunk, ('tx', 'ty'), pairs))  46.7 us
    ppermute x8, waiting for transfers between devices, shards(): received.append(lax.ppermute(chunk, ('tx', 'ty'), pairs))  18 us
    pallas_call x1, Pallas kernels, pair_maps(): pl.pallas_call(kernel, grid_spec=grid_spec, out_shape=[out_shape, out_sha...  16 us
    ppermute x1, starting transfers between devices, shards(): right = lax.ppermute(x[0, :, :, :LANES], 'tx', backward)  11.6 us
    unnamed x11, local copies, waits for them, and re-layouts  10.4 us
    ppermute x1, waiting for transfers between devices, shards(): lax.ppermute(x[blocks_per_tile - 1, :, :, local_cols - LANES:], 'tx', for...  8.27 us
    dynamic_slice x1, local copies, waits for them, and re-layouts, shards(): chunk = lax.dynamic_slice_in_dim(x, first, padded_rows, axis=2)  5.06 us
    convert_element_type x1, local copies, waits for them, and re-layouts, shards(): main.astype(jnp.bfloat16)  3.4 us
  transfers between devices with their start and end apart: 10, of which 4 were waited for; matrix products, arithmetic and copies ran while one was open for 14% of the time, Pallas kernels for 0%

profile of v22, /device:TPU:21, one launch (start us, length us, event | category | flops | bytes accessed | tf_op | source)
XLA Modules:
  0.0 134.6 jit_solution(15727228233095167118)
XLA Ops:
  0.8 5.1 %pad_dynamic-slice_fusion = (bf16[8,2,24,512]{3,2,1,0:T(8,128)(2,1)S(1)}, bf16[8,2,24,512]{3,2,1,0:T(8,128)(2,1)S(1)}, bf16[8,2,24,512]{3,2,1,0:T(8,128)(2,1)S(1...) fusion(s32[]{:T(128)S(6)} %select_n.146, ...), kind=kLoop, calls=%fused_computation.7 | loop fusion | bytes 5242912 | tf_op jit(solution)/shard_map/dynamic_slice | solution.py:170
  5.8 4.5 %collective-permute-start = (bf16[384,512]{1,0:T(8,128)(2,1)}, bf16[384,512]{1,0:T(8,128)(2,1)}, u32[]{:S(2)}, u32[]{:S(2)}) collective-permute-start(bf16[384,512]{1,0:T(8,128)(2,1)} %bitcast), channel_id=1, source_target_pairs={{0,0},{1,1},{2,8},{3,9},{4,16},{5,17},{6,24},{7,25},{8,2},{9,3},{1... | collective-permute-start | bytes 1179656 | tf_op jit(solution)/shard_map/ppermute | solution.py:172
  10.3 0.7 collective-permute-start.1
  11.0 2.3 %collective-permute-start.2 = (bf16[384,512]{1,0:T(8,128)(2,1)S(1)}, bf16[384,512]{1,0:T(8,128)(2,1)}, u32[]{:S(2)}, u32[]{:S(2)}) collective-permute-start(bf16[384,512]{1,0:T(8,128)(2,1)S(1)} %bitcast.61), channel_id=1, source_target_pairs={{0,2},{1,3},{2,10},{3,11},{4,18},{5,19},{6,26},{7,27},{8,4},{9,5},... | collective-permute-start | bytes 1179656 | tf_op jit(solution)/shard_map/ppermute | solution.py:172
  13.4 3.4 %collective-permute-start.3 = (bf16[384,512]{1,0:T(8,128)(2,1)S(1)}, bf16[384,512]{1,0:T(8,128)(2,1)}, u32[]{:S(2)}, u32[]{:S(2)}) collective-permute-start(bf16[384,512]{1,0:T(8,128)(2,1)S(1)} %bitcast.60), channel_id=1, source_target_pairs={{0,3},{1,4},{2,11},{3,12},{4,19},{5,20},{6,27},{7,28},{8,5},{9,6},... | collective-permute-start | bytes 1179656 | tf_op jit(solution)/shard_map/ppermute | solution.py:172
  17.1 0.5 copy.10
  17.6 0.8 reshape.168
  18.4 0.8 reshape.167
  19.6 0.7 pad_maximum_fusion.band_ref
  20.3 28.9 %collective-permute-start.5 = (bf16[384,512]{1,0:T(8,128)(2,1)S(1)}, bf16[384,512]{1,0:T(8,128)(2,1)S(1)}, u32[]{:S(2)}, u32[]{:S(2)}) collective-permute-start(bf16[384,512]{1,0:T(8,128)(2,1)S(1)} %bitcast.58), channel_id=1, source_target_pairs={{0,5},{1,6},{2,13},{3,14},{4,21},{5,22},{6,29},{7,30},{8,7},{9,0},... | collective-permute-start | bytes 1179656 | tf_op jit(solution)/shard_map/ppermute | solution.py:172
  49.1 1.8 %bitcast_dynamic-update-slice_fusion.7 = bf16[8,384,512]{2,1,0:T(8,128)(2,1)} fusion(bf16[384,512]{1,0:T(8,128)(2,1)} %collective-permute-done), kind=kLoop, calls=%fused_computation.24 | loop fusion | bytes 786432
  50.9 6.1 %collective-permute-start.6 = (bf16[384,512]{1,0:T(8,128)(2,1)S(1)}, bf16[384,512]{1,0:T(8,128)(2,1)S(1)}, u32[]{:S(2)}, u32[]{:S(2)}) collective-permute-start(bf16[384,512]{1,0:T(8,128)(2,1)S(1)} %bitcast.57), channel_id=1, source_target_pairs={{0,6},{1,7},{2,14},{3,15},{4,22},{5,23},{6,30},{7,31},{8,0},{9,1},... | collective-permute-start | bytes 1179656 | tf_op jit(solution)/shard_map/ppermute | solution.py:172
  57.0 1.8 %bitcast_dynamic-update-slice_fusion.6 = bf16[8,384,512]{2,1,0:T(8,128)(2,1)} fusion(bf16[8,384,512]{2,1,0:T(8,128)(2,1)} %bitcast_dynamic-update-slice_fusion.7, bf16[384,512]{1,0:T(8,128)(2,1)} %collective-permute-done.1), kind=kLoop, calls=%fused_computation.23 | loop fusion | bytes 786432
  58.8 0.9 collective-permute-start.7
  59.6 1.8 %bitcast_dynamic-update-slice_fusion.5 = bf16[8,384,512]{2,1,0:T(8,128)(2,1)} fusion(bf16[8,384,512]{2,1,0:T(8,128)(2,1)} %bitcast_dynamic-update-slice_fusion.6, bf16[384,512]{1,0:T(8,128)(2,1)} %collective-permute-done.2), kind=kLoop, calls=%fused_computation.22 | loop fusion | bytes 786432
  61.4 1.8 %bitcast_dynamic-update-slice_fusion.4 = bf16[8,384,512]{2,1,0:T(8,128)(2,1)} fusion(bf16[8,384,512]{2,1,0:T(8,128)(2,1)} %bitcast_dynamic-update-slice_fusion.5, bf16[384,512]{1,0:T(8,128)(2,1)} %collective-permute-done.3), kind=kLoop, calls=%fused_computation.21 | loop fusion | bytes 786432
  63.2 1.8 %bitcast_dynamic-update-slice_fusion.3 = bf16[8,384,512]{2,1,0:T(8,128)(2,1)} fusion(bf16[8,384,512]{2,1,0:T(8,128)(2,1)} %bitcast_dynamic-update-slice_fusion.4, bf16[384,512]{1,0:T(8,128)(2,1)} %collective-permute-done.4), kind=kLoop, calls=%fused_computation.20 | loop fusion | bytes 786432
  65.0 10.3 %collective-permute-done.5 = bf16[384,512]{1,0:T(8,128)(2,1)S(1)} collective-permute-done((bf16[384,512]{1,0:T(8,128)(2,1)S(1)}, bf16[384,512]{1,0:T(8,128)(2,1)S(1)}, u32[]{:S(2)}, u32[]{:S(2)}) %collective-permute-start.5) | collective-permute-done | bytes 393248 | tf_op jit(solution)/shard_map/ppermute | solution.py:172
  75.3 0.8 bitcast_dynamic-update-slice_fusion.2
  76.1 7.7 %collective-permute-done.6 = bf16[384,512]{1,0:T(8,128)(2,1)S(1)} collective-permute-done((bf16[384,512]{1,0:T(8,128)(2,1)S(1)}, bf16[384,512]{1,0:T(8,128)(2,1)S(1)}, u32[]{:S(2)}, u32[]{:S(2)}) %collective-permute-start.6) | collective-permute-done | bytes 393248 | tf_op jit(solution)/shard_map/ppermute | solution.py:172
  83.7 0.8 bitcast_dynamic-update-slice_fusion.1
  84.5 0.8 bitcast_dynamic-update-slice_fusion
  85.3 2.6 %gather_fusion = bf16[8,384,512]{2,1,0:T(8,128)(2,1)S(1)} fusion(bf16[8,384,512]{2,1,0:T(8,128)(2,1)} %bitcast_dynamic-update-slice_fusion, s32[1024]{0:T(1024)S(1)} %pad_clamp_fusion), kind=kCustom, calls=%fused_computation | custom fusion | bytes 6291488 | tf_op jit(solution)/shard_map/jit(_take)/gather | solution.py:176
  88.5 11.6 %collective-permute-start.8 = (bf16[64,24,128]{2,1,0:T(8,128)(2,1)S(1)}, bf16[64,24,128]{2,1,0:T(8,128)(2,1)S(1)}, u32[]{:S(2)}, u32[]{:S(2)}) collective-permute-start(bf16[64,24,128]{2,1,0:T(8,128)(2,1)S(1)} %get-tuple-element.3), channel_id=1, source_target_pairs={{8,0},{16,8},{24,16},{9,1},{17,9},{25,17},{10,2},{18,10},{26,18},{... | collective-permute-start | bytes 1179656 | tf_op jit(solution)/shard_map/ppermute | solution.py:182
  100.0 2.1 %collective-permute-start.9 = (bf16[64,24,128]{2,1,0:T(8,128)(2,1)S(1)}, bf16[64,24,128]{2,1,0:T(8,128)(2,1)S(1)}, u32[]{:S(2)}, u32[]{:S(2)}) collective-permute-start(bf16[64,24,128]{2,1,0:T(8,128)(2,1)S(1)} %get-tuple-element.2), channel_id=1, source_target_pairs={{0,8},{8,16},{16,24},{1,9},{9,17},{17,25},{2,10},{10,18},{18,26},{... | collective-permute-start | bytes 1179656 | tf_op jit(solution)/shard_map/ppermute | solution.py:181
  102.1 0.7 broadcast_select_fusion.1
  102.9 1.4 %convert_bitcast_fusion = bf16[2,64,24,512]{3,1,2,0:T(8,128)(2,1)S(1)} fusion(bf16[2,64,24,512]{3,2,1,0:T(8,128)(2,1)S(1)} %bitcast.54, bf16[64,64,1,1]{1,0,2,3:T(8,128)(2,1)S(1)} %reshape.167), kind=kOutput, calls=%fused_computation.3 | convolution fusion | flops 202899456 | bytes 6299648 | tf_op jit(solution)/shard_map/kc,bchw->bkhw/dot_general | solution.py:189
  104.2 3.4 %copy.12 = bf16[2,64,24,512]{3,2,1,0:T(8,128)(2,1)} copy(bf16[2,64,24,512]{3,1,2,0:T(8,128)(2,1)S(1)} %convert_bitcast_fusion) | data formatting | bytes 6291456 | tf_op jit(solution)/shard_map/convert_element_type | solution.py:190
  107.6 1.4 %collective-permute-done.8 = bf16[64,24,128]{2,1,0:T(8,128)(2,1)S(1)} collective-permute-done((bf16[64,24,128]{2,1,0:T(8,128)(2,1)S(1)}, bf16[64,24,128]{2,1,0:T(8,128)(2,1)S(1)}, u32[]{:S(2)}, u32[]{:S(2)}) %collective-permute-start.8) | collective-permute-done | bytes 393248 | tf_op jit(solution)/shard_map/ppermute | solution.py:182
  109.0 8.3 %collective-permute-done.9 = bf16[64,24,128]{2,1,0:T(8,128)(2,1)S(1)} collective-permute-done((bf16[64,24,128]{2,1,0:T(8,128)(2,1)S(1)}, bf16[64,24,128]{2,1,0:T(8,128)(2,1)S(1)}, u32[]{:S(2)}, u32[]{:S(2)}) %collective-permute-start.9) | collective-permute-done | bytes 393248 | tf_op jit(solution)/shard_map/ppermute | solution.py:181
  117.6 1.0 copy.14
  118.6 16.0 %shard_map.68 = (f32[32,16,1024]{2,1,0:T(8,128)}, f32[32,16,1024]{2,1,0:T(8,128)}) custom-call(s32[32]{0:T(128)} %pre_ref.1, s32[32]{0:T(128)} %post_ref.1, bf16[2,32,2,24,512]{4,3,2,1,0:T(8,128)(2,1)} %bitcast.53, bf16[32,2,24,128]{3,2,1,0:T(8,128)(2,1)} %bitcast.55, bf16[768,128]{1,0:T(8,128)(2,1)} %pad_maximum_fusion.band_ref), custom_call_target="tpu_custom_call" | custom-call | tf_op jit(solution)/shard_map/pallas_call | solution.py:141
  (31 shorter events, 1.5 us)
Async XLA Ops:
  0.6 16.3 %copy-start = (bf16[32,32]{1,0:T(8,128)(2,1)S(1)}, bf16[32,32]{1,0:T(8,128)(2,1)}, u32[]{:S(2)}) copy-start(bf16[32,32]{1,0:T(8,128)(2,1)} %param.7) | copy-start | bytes 6148
  0.6 16.4 %copy-start.1 = (bf16[32,32]{1,0:T(8,128)(2,1)S(1)}, bf16[32,32]{1,0:T(8,128)(2,1)}, u32[]{:S(2)}) copy-start(bf16[32,32]{1,0:T(8,128)(2,1)} %param.6) | copy-start | bytes 6148
  5.8 14.4 %collective-permute-start = (bf16[384,512]{1,0:T(8,128)(2,1)}, bf16[384,512]{1,0:T(8,128)(2,1)}, u32[]{:S(2)}, u32[]{:S(2)}) collective-permute-start(bf16[384,512]{1,0:T(8,128)(2,1)} %bitcast), channel_id=1, source_target_pairs={{0,0},{1,1},{2,8},{3,9},{4,16},{5,17},{6,24},{7,25},{8,2},{9,3},{1... | collective-permute-start | bytes 1179656 | tf_op jit(solution)/shard_map/ppermute | solution.py:172
  10.3 40.6 %collective-permute-start.1 = (bf16[384,512]{1,0:T(8,128)(2,1)S(1)}, bf16[384,512]{1,0:T(8,128)(2,1)}, u32[]{:S(2)}, u32[]{:S(2)}) collective-permute-start(bf16[384,512]{1,0:T(8,128)(2,1)S(1)} %bitcast.62), channel_id=1, source_target_pairs={{0,1},{1,2},{2,9},{3,10},{4,17},{5,18},{6,25},{7,26},{8,3},{9,4},{... | collective-permute-start | bytes 1179656 | tf_op jit(solution)/shard_map/ppermute | solution.py:172
  11.0 47.7 %collective-permute-start.2 = (bf16[384,512]{1,0:T(8,128)(2,1)S(1)}, bf16[384,512]{1,0:T(8,128)(2,1)}, u32[]{:S(2)}, u32[]{:S(2)}) collective-permute-start(bf16[384,512]{1,0:T(8,128)(2,1)S(1)} %bitcast.61), channel_id=1, source_target_pairs={{0,2},{1,3},{2,10},{3,11},{4,18},{5,19},{6,26},{7,27},{8,4},{9,5},... | collective-permute-start | bytes 1179656 | tf_op jit(solution)/shard_map/ppermute | solution.py:172
  13.4 48.0 %collective-permute-start.3 = (bf16[384,512]{1,0:T(8,128)(2,1)S(1)}, bf16[384,512]{1,0:T(8,128)(2,1)}, u32[]{:S(2)}, u32[]{:S(2)}) collective-permute-start(bf16[384,512]{1,0:T(8,128)(2,1)S(1)} %bitcast.60), channel_id=1, source_target_pairs={{0,3},{1,4},{2,11},{3,12},{4,19},{5,20},{6,27},{7,28},{8,5},{9,6},... | collective-permute-start | bytes 1179656 | tf_op jit(solution)/shard_map/ppermute | solution.py:172
  16.7 46.5 %collective-permute-start.4 = (bf16[384,512]{1,0:T(8,128)(2,1)S(1)}, bf16[384,512]{1,0:T(8,128)(2,1)}, u32[]{:S(2)}, u32[]{:S(2)}) collective-permute-start(bf16[384,512]{1,0:T(8,128)(2,1)S(1)} %bitcast.59), channel_id=1, source_target_pairs={{0,4},{1,5},{2,12},{3,13},{4,20},{5,21},{6,28},{7,29},{8,6},{9,7},... | collective-permute-start | bytes 1179656 | tf_op jit(solution)/shard_map/ppermute | solution.py:172
  20.3 55.0 %collective-permute-start.5 = (bf16[384,512]{1,0:T(8,128)(2,1)S(1)}, bf16[384,512]{1,0:T(8,128)(2,1)S(1)}, u32[]{:S(2)}, u32[]{:S(2)}) collective-permute-start(bf16[384,512]{1,0:T(8,128)(2,1)S(1)} %bitcast.58), channel_id=1, source_target_pairs={{0,5},{1,6},{2,13},{3,14},{4,21},{5,22},{6,29},{7,30},{8,7},{9,0},... | collective-permute-start | bytes 1179656 | tf_op jit(solution)/shard_map/ppermute | solution.py:172
  50.9 32.8 %collective-permute-start.6 = (bf16[384,512]{1,0:T(8,128)(2,1)S(1)}, bf16[384,512]{1,0:T(8,128)(2,1)S(1)}, u32[]{:S(2)}, u32[]{:S(2)}) collective-permute-start(bf16[384,512]{1,0:T(8,128)(2,1)S(1)} %bitcast.57), channel_id=1, source_target_pairs={{0,6},{1,7},{2,14},{3,15},{4,22},{5,23},{6,30},{7,31},{8,0},{9,1},... | collective-permute-start | bytes 1179656 | tf_op jit(solution)/shard_map/ppermute | solution.py:172
  58.8 25.7 %collective-permute-start.7 = (bf16[384,512]{1,0:T(8,128)(2,1)S(1)}, bf16[384,512]{1,0:T(8,128)(2,1)S(1)}, u32[]{:S(2)}, u32[]{:S(2)}) collective-permute-start(bf16[384,512]{1,0:T(8,128)(2,1)S(1)} %bitcast.56), channel_id=1, source_target_pairs={{0,7},{1,0},{2,15},{3,8},{4,23},{5,16},{6,31},{7,24},{8,1},{9,2},{... | collective-permute-start | bytes 1179656 | tf_op jit(solution)/shard_map/ppermute | solution.py:172
  88.5 20.6 %collective-permute-start.8 = (bf16[64,24,128]{2,1,0:T(8,128)(2,1)S(1)}, bf16[64,24,128]{2,1,0:T(8,128)(2,1)S(1)}, u32[]{:S(2)}, u32[]{:S(2)}) collective-permute-start(bf16[64,24,128]{2,1,0:T(8,128)(2,1)S(1)} %get-tuple-element.3), channel_id=1, source_target_pairs={{8,0},{16,8},{24,16},{9,1},{17,9},{25,17},{10,2},{18,10},{26,18},{... | collective-permute-start | bytes 1179656 | tf_op jit(solution)/shard_map/ppermute | solution.py:182
  100.0 17.2 %collective-permute-start.9 = (bf16[64,24,128]{2,1,0:T(8,128)(2,1)S(1)}, bf16[64,24,128]{2,1,0:T(8,128)(2,1)S(1)}, u32[]{:S(2)}, u32[]{:S(2)}) collective-permute-start(bf16[64,24,128]{2,1,0:T(8,128)(2,1)S(1)} %get-tuple-element.2), channel_id=1, source_target_pairs={{0,8},{8,16},{16,24},{1,9},{9,17},{17,25},{2,10},{10,18},{18,26},{... | collective-permute-start | bytes 1179656 | tf_op jit(solution)/shard_map/ppermute | solution.py:181
